TPU v7x, 32 devices: a whole 2x2x4 slice. The times are simulated.
32 devices in a mesh: kv: 4 (over x, core), blk: 8 (over z, y).
Axes of the slice: x: 2, y: 2, z: 4, core: 2. Of those that a mesh axis runs over, the one named last changes fastest.
Arguments:
- hidden_in: bfloat16 [512, 2560], P('blk', 'kv'), may hold values from -33 to 33
- queries: bfloat16 [512, 2560], P('blk', 'kv'), may hold values from -240 to 240
- new_kv: bfloat16 [512, 4, 2, 128], P('blk', 'kv'), may hold values from -6 to 6
- cache_pool: bfloat16 [32, 16, 4, 2, 128], P('blk', None, 'kv'), may hold values from -6 to 6
- cache_len: int32 [8], replicated, may hold values from 0 to 128, as said below
- block_holder: int32 [8, 8], replicated, may hold values from 0 to 7, as said below
- block_slot: int32 [8, 8], replicated, may hold values from 0 to 3, as said below
- decode_holder: int32 [8, 12], replicated, may hold values from 0 to 7, as said below
- decode_slot: int32 [8, 12], replicated, may hold values from 0 to 7, as said below
- out_weight: bfloat16 [2560, 2560], P('kv', 'blk'), may hold values from -0.125 to 0.125
- norm_gain: bfloat16 [2560], P('kv'), may hold values from 0.5 to 1.5
- router_weight: float32 [2560, 64], P('kv'), may hold values from -0.125 to 0.125
- expert_routes: int32 [512, 6], P('blk'), may hold values from 0 to 63, all different within a row; in each aligned block of 64 rows (0 to 63, 64 to 127, ...) at most 8 rows name the same one
- w_gate: bfloat16 [128, 2560, 768], P('blk', 'kv'), may hold values from -0.125 to 0.125
- w_up: bfloat16 [128, 2560, 768], P('blk', 'kv'), may hold values from -0.125 to 0.125
- w_down: bfloat16 [128, 768, 2560], P('blk', None, 'kv'), may hold values from -0.15625 to 0.15625
Outputs:
- layer_out: bfloat16 [512, 2560], P('blk', 'kv')
- decode_pool: bfloat16 [64, 16, 4, 2, 128], P('blk', None, 'kv')
Inputs may be any that keep to these rules, and one draw needn't show every extreme that they name: `cache_len`: every value is a multiple of 16; half of the requests have 0, the others at least 16. `block_holder`: the entries of one request are distinct devices; entries beyond cache_len / 16 are unused. `block_slot`: the used blocks held by one device have distinct slots. `decode_holder`: the used blocks that one device sends, those it holds and the 4 new blocks of its own request, go to distinct decoding devices. `decode_slot`: no two used blocks share a decoding device and slot.
All inputs are finite; a program needn't handle non-finite values.
Results may differ from a plain program's by a relative error of at most 0.008.
Values may be sent and summed in bfloat16 or wider, within the bound.
No kernel may reach another device: no remote copies, remote signals or barrier semaphores. Data moves between devices by JAX's collectives and lax.ppermute only.
A program may use at most 128 MiB of HBM per device.

v0:
```python
import math

import jax
import jax.numpy as jnp
from jax import lax
from jax.sharding import PartitionSpec as P

D = 2560
CAP = 8


EPSILON = 1e-05
MASKED = -1e30


def head_rows(asked_rows, head_count, head_dim):
    stretch_len = asked_rows.shape[0]
    return (
        asked_rows.reshape(stretch_len, head_count, head_dim)
        .transpose(1, 0, 2)
        .reshape(head_count * stretch_len, head_dim)
    )


def absorb(carried, scores, value_rows):
    running_max, denominator, accumulated = carried
    new_max = jnp.maximum(running_max, jnp.max(scores, axis=1))
    decay = jnp.exp(running_max - new_max)
    raised = jnp.exp(scores - new_max[:, None])
    denominator = denominator * decay + jnp.sum(raised, axis=1)
    accumulated = accumulated * decay[:, None] + jnp.dot(
        raised.astype(jnp.bfloat16), value_rows, preferred_element_type=jnp.float32
    )
    return (new_max, denominator, accumulated)


def attend_blocks(carried, query_rows, blocks, present, scale):
    block_count = blocks.shape[0]
    block_len = blocks.shape[1]
    head_dim = blocks.shape[3]
    tile_blocks = min(32, block_count)
    span = tile_blocks * block_len
    flags = present.astype(jnp.int32)
    live_count = jnp.sum(flags)
    order_rank = jnp.cumsum(flags) - 1
    positions = jnp.arange(block_count)
    chosen = present[None, :] & (order_rank[None, :] == positions[:, None])
    packing = jnp.sum(jnp.where(chosen, positions[None, :], 0), axis=1)
    packed = blocks[packing]

    def advance(turn, state_now):
        segment = lax.dynamic_slice_in_dim(packed, turn * tile_blocks, tile_blocks, 0)
        key_rows = segment[:, :, 0].reshape(span, head_dim)
        value_rows = segment[:, :, 1].reshape(span, head_dim)
        scores = (
            jnp.einsum("qd,kd->qk", query_rows, key_rows, preferred_element_type=jnp.float32)
            * scale
        )
        is_live = turn * tile_blocks + jnp.arange(span) // block_len < live_count
        scores = jnp.where(is_live[None, :], scores, MASKED)
        return absorb(state_now, scores, value_rows)

    return lax.fori_loop(0, (live_count + tile_blocks - 1) // tile_blocks, advance, carried)


def per_device(
    hidden_in,
    queries,
    new_kv,
    cache_pool,
    cache_len,
    block_holder,
    block_slot,
    decode_holder,
    decode_slot,
    out_weight,
    norm_gain,
    router_weight,
    expert_routes,
    w_gate,
    w_up,
    w_down,
):
    blk_count = lax.axis_size("blk")
    own_index = lax.axis_index("blk")
    stretch_len = queries.shape[0]
    head_dim = new_kv.shape[3]
    head_count = queries.shape[1] // head_dim
    pool_size = cache_pool.shape[0]
    block_len = cache_pool.shape[1]
    max_blocks = block_holder.shape[1]
    fresh_count = stretch_len // block_len
    scale = 1.0 / math.sqrt(head_dim)
    devices = jnp.arange(blk_count)
    in_use = jnp.arange(max_blocks)[None, :] < (cache_len // block_len)[:, None]
    pool_rows = cache_pool[:, :, 0]
    fresh_rows = new_kv[:, 0]
    sources = jnp.concatenate(
        [pool_rows, fresh_rows.reshape(fresh_count, block_len, 2, head_dim)], axis=0
    )
    held_here = in_use & (block_holder == own_index)
    old_target = jnp.where(held_here, decode_holder[:, :max_blocks], blk_count).reshape(-1)
    pick_old = jax.ops.segment_sum((block_slot + 1).reshape(-1), old_target, num_segments=blk_count)
    pick_new = jax.ops.segment_sum(
        pool_size + 1 + jnp.arange(fresh_count),
        decode_holder[own_index, max_blocks:],
        num_segments=blk_count,
    )
    picked = pick_old + pick_new
    sending = jnp.where(
        (picked > 0)[:, None, None, None],
        sources[jnp.maximum(picked - 1, 0)],
        jnp.zeros((), jnp.bfloat16),
    )
    landed = lax.all_to_all(sending, "blk", split_axis=0, concat_axis=0, tiled=True)
    source_request = jnp.zeros_like(devices) + own_index
    match_here = (block_holder[devices] == own_index) & in_use[devices]
    outgoing = pool_rows[jnp.sum(jnp.where(match_here, block_slot[devices], 0), axis=1)]
    arrived = lax.all_to_all(outgoing, "blk", split_axis=0, concat_axis=0, tiled=True)
    present = jnp.any(
        (block_holder[source_request] == devices[:, None]) & in_use[source_request], axis=1
    )
    own_rows = head_rows(queries, head_count, head_dim)
    row_count = head_count * stretch_len
    start_state = (
        jnp.full((row_count,), MASKED, jnp.float32),
        jnp.zeros((row_count,), jnp.float32),
        jnp.zeros((row_count, head_dim), jnp.float32),
    )
    query_pos = jnp.arange(row_count) % stretch_len
    allowed = jnp.arange(stretch_len)[None, :] <= query_pos[:, None]
    local_scores = (
        jnp.einsum("qd,kd->qk", own_rows, fresh_rows[:, 0], preferred_element_type=jnp.float32)
        * scale
    )
    carried = absorb(start_state, jnp.where(allowed, local_scores, MASKED), fresh_rows[:, 1])
    carried = attend_blocks(carried, own_rows, arrived, present, scale)
    running_max, denominator, accumulated = carried
    attended = (
        (accumulated / denominator[:, None])
        .reshape(head_count, stretch_len, head_dim)
        .transpose(1, 0, 2)
    )
    attended = attended.reshape(stretch_len, head_count * head_dim).astype(jnp.bfloat16)
    projected = jnp.dot(
        attended,
        lax.all_gather(out_weight, "blk", axis=1, tiled=True),
        preferred_element_type=jnp.float32,
    )
    head_total = lax.psum_scatter(
        projected.astype(jnp.bfloat16), "kv", scatter_dimension=1, tiled=True
    ).astype(jnp.float32)
    residual = (hidden_in.astype(jnp.float32) + head_total).astype(jnp.bfloat16)
    resid_float = residual.astype(jnp.float32)
    scaled = resid_float * norm_gain.astype(jnp.float32)[None, :]
    square_sum, raw_logits = lax.psum(
        (
            jnp.sum(resid_float * resid_float, axis=1),
            jnp.dot(scaled, router_weight, precision=lax.Precision.HIGHEST),
        ),
        "kv",
    )
    inverse = lax.rsqrt(square_sum / D + EPSILON)
    logits = raw_logits * inverse[:, None]
    normed = (scaled * inverse[:, None]).astype(jnp.bfloat16)
    expert_count = router_weight.shape[1]
    top_count = expert_routes.shape[1]
    chosen_logit = jnp.sum(
        jnp.where(
            expert_routes[:, :, None] == jnp.arange(expert_count)[None, None, :],
            logits[:, None, :],
            0.0,
        ),
        axis=2,
    )
    lifted = jnp.exp(chosen_logit)
    gates = lifted / jnp.sum(lifted, axis=1, keepdims=True)
    capacity = CAP
    flat_routes = expert_routes.reshape(-1)
    assign_count = flat_routes.shape[0]
    onehot = (flat_routes[:, None] == jnp.arange(expert_count)[None, :]).astype(jnp.int32)
    earlier = jnp.cumsum(onehot, axis=0) - onehot
    slot_rank = jnp.sum(earlier * onehot, axis=1)
    target = flat_routes * capacity + slot_rank
    slot_total = expert_count * capacity
    source_item = jax.ops.segment_sum(jnp.arange(assign_count) + 1, target, num_segments=slot_total)
    packed_rows = jnp.where(
        (source_item > 0)[:, None],
        normed[jnp.maximum(source_item - 1, 0) // top_count],
        jnp.zeros((), jnp.bfloat16),
    )
    pieces_here = w_gate.shape[0]
    feature_part = normed.shape[1]
    doubled = jnp.broadcast_to(
        packed_rows.reshape(expert_count, 1, capacity, feature_part),
        (expert_count, 2, capacity, feature_part),
    )
    doubled = doubled.reshape(blk_count, pieces_here, capacity, feature_part)
    rows_in = lax.all_to_all(doubled, "blk", split_axis=0, concat_axis=0, tiled=True)
    gate_part = jnp.einsum("spkd,pdu->spku", rows_in, w_gate, preferred_element_type=jnp.float32)
    up_part = jnp.einsum("spkd,pdu->spku", rows_in, w_up, preferred_element_type=jnp.float32)
    both_parts = jnp.stack([gate_part, up_part], axis=3)
    whole = lax.psum(both_parts.astype(jnp.bfloat16), "kv").astype(jnp.float32)
    hidden = (jax.nn.silu(whole[:, :, :, 0]) * whole[:, :, :, 1]).astype(jnp.bfloat16)
    piece_out = jnp.einsum(
        "spku,pud->spkd", hidden, w_down, preferred_element_type=jnp.float32
    ).astype(jnp.bfloat16)
    returned = lax.all_to_all(piece_out, "blk", split_axis=0, concat_axis=0, tiled=True)
    per_piece = returned.reshape(expert_count, 2, capacity, feature_part).astype(jnp.float32)
    per_slot = (per_piece[:, 0] + per_piece[:, 1]).reshape(slot_total, feature_part)
    routed = per_slot[target].reshape(stretch_len, top_count, feature_part)
    moe_out = jnp.sum(routed * gates[:, :, None], axis=1)
    layer_out = (resid_float + moe_out).astype(jnp.bfloat16)
    here_old = in_use & (decode_holder[:, :max_blocks] == own_index)
    from_old = jnp.where(here_old, block_holder, blk_count).reshape(-1)
    put_old = jax.ops.segment_sum(
        (decode_slot[:, :max_blocks] + 1).reshape(-1), from_old, num_segments=blk_count
    )
    here_new = decode_holder[:, max_blocks:] == own_index
    request_ids = jnp.broadcast_to(jnp.arange(decode_holder.shape[0])[:, None], here_new.shape)
    from_new = jnp.where(here_new, request_ids, blk_count).reshape(-1)
    put_new = jax.ops.segment_sum(
        (decode_slot[:, max_blocks:] + 1).reshape(-1), from_new, num_segments=blk_count
    )
    placing = put_old + put_new
    decode_size = pool_size + fresh_count
    placement = (placing[None, :] - 1 == jnp.arange(decode_size)[:, None]).astype(jnp.bfloat16)
    decoded = jnp.dot(
        placement, landed.reshape(blk_count, -1), preferred_element_type=jnp.float32
    ).astype(jnp.bfloat16)
    decode_pool = decoded.reshape(decode_size, block_len, 1, 2, head_dim)
    return (layer_out, decode_pool)


def solution(mesh):
    in_specs = (
        P("blk", "kv"),
        P("blk", "kv"),
        P("blk", "kv", None, None),
        P("blk", None, "kv", None, None),
        P(),
        P(),
        P(),
        P(),
        P(),
        P("kv", "blk"),
        P("kv"),
        P("kv", None),
        P("blk", None),
        P("blk", "kv", None),
        P("blk", "kv", None),
        P("blk", None, "kv"),
    )
    out_specs = (P("blk", "kv"), P("blk", None, "kv", None, None))
    return jax.shard_map(
        per_device, mesh=mesh, in_specs=in_specs, out_specs=out_specs, check_vma=False
    )
```

profile of v0, /device:TPU:0, one launch (start us, length us, event | category | flops | bytes accessed | tf_op | source)
XLA Modules:
  0.0 305.2 jit_solution(9065691189428837269)
XLA Ops:
  8.5 1.2 gather_fusion.2
  9.8 1.2 gather_fusion.4
  12.7 1.2 gather_fusion.5
  13.9 7.3 %all-to-all-start = ((bf16[8,16,2,128]{3,1,2,0:T(8,128)(2,1)}), bf16[8,16,2,128]{3,1,2,0:T(8,128)(2,1)S(1)}, u32[]{:S(2)}, u32[]{:S(2)}) async-start(bf16[8,16,2,128]{3,1,2,0:T(8,128)(2,1)} %gather_fusion.5), calls=%async_computation | async-start | bytes 131072 | tf_op jit(solution)/shard_map/all_to_all | solution.py:119
  22.5 1.2 gather_fusion
  32.6 55.0 %all-gather.2.cloned.1.call-done = bf16[640,2560]{0,1:T(8,128)(2,1)} async-done(((bf16[640,320]{0,1:T(8,128)(2,1)}), bf16[640,2560]{0,1:T(8,128)(2,1)}) %all-gather.2.cloned.1.call-update) | async-done | bytes 3276816 | tf_op jit(solution)/shard_map/all_gather | solution.py:147
  87.6 3.0 convolution_convert_fusion.1
  91.8 3.9 %scatter_custom_fusion = s32[512]{0:T(512)S(1)} fusion(s32[384]{0:T(512)S(1)} %get-tuple-element.165, s32[384]{0:T(512)S(1)} %iota_add_fusion, s32[]{:T(128)} %constant.152.clone.1), kind=kCustom, calls=%fused_computation.145 | custom fusion | flops 384 | bytes 2052 | tf_op jit(solution)/shard_map/scatter-add | solution.py:186
  95.8 17.1 %reduce-scatter.4.cloned.1.call-done = bf16[640,64]{1,0:T(8,128)(2,1)} async-done(((bf16[2560,64]{1,0:T(8,128)(2,1)}), bf16[640,64]{1,0:T(8,128)(2,1)}) %reduce-scatter.4.cloned.1.call-update) | async-done | bytes 81936
  114.4 10.5 %all-reduce = (f32[64]{0:T(128)S(1)}, f32[64,64]{1,0:T(8,128)S(1)}) all-reduce(f32[64]{0:T(128)S(1)} %get-tuple-element.186, f32[64,64]{1,0:T(8,128)S(1)} %fusion.41), channel_id=1, replica_groups=mesh['kv'=4,'blk'=8] {'kv'}, use_global_device_ids=true, to_apply=%region_17.18 | all-reduce | flops 4160 | bytes 33280 | tf_op jit(solution)/shard_map/psum | solution.py:156
  125.0 2.7 gather_fusion.7
  127.7 1.2 bitcast_select_fusion
  129.1 37.4 %all_to_all.20 = bf16[8,16,8,640]{3,2,1,0:T(8,128)(2,1)S(1)} all-to-all(bf16[8,16,8,640]{3,2,1,0:T(8,128)(2,1)S(1)} %bitcast.141), channel_id=1, replica_groups=mesh['kv'=4,'blk'=8] {'blk'}, dimensions={0} | all-to-all | bytes 2621440 | tf_op jit(solution)/shard_map/all_to_all | solution.py:199
  166.5 8.3 %fusion.26 = bf16[8,16,8,1,768]{4,2,0,1,3:T(8,128)(2,1)S(1)} fusion(bf16[16,640,768]{2,1,0:T(8,128)(2,1)} %param.32, bf16[8,16,8,640]{3,2,1,0:T(8,128)(2,1)S(1)} %all_to_all.20), kind=kOutput, calls=%fused_computation.47 | convolution fusion | flops 1007419392 | bytes 18612224 | tf_op jit(solution)/shard_map/spkd,pdu->spku/dot_general | solution.py:201
  174.9 2.7 fusion.29
  177.6 2.0 pad_maximum_fusion
  183.3 3.8 %all-to-all-start.3 = ((bf16[8,16,2,128]{3,1,2,0:T(8,128)(2,1)}), bf16[8,16,2,128]{3,1,2,0:T(8,128)(2,1)S(1)}, u32[]{:S(2)}, u32[]{:S(2)}) async-start(bf16[8,16,2,128]{3,1,2,0:T(8,128)(2,1)} %broadcast_select_fusion), calls=%async_computation.3 | async-start | bytes 131072 | tf_op jit(solution)/shard_map/all_to_all | solution.py:115
  187.1 59.1 %all-reduce.3.cloned.1.call-done = bf16[8,16,8,2,768]{4,2,0,1,3:T(8,128)(2,1)} async-done(((bf16[8,16,8,2,768]{4,2,0,1,3:T(8,128)(2,1)}), bf16[8,16,8,2,768]{4,2,0,1,3:T(8,128)(2,1)}) %all-reduce.3.cloned.1.call-update) | async-done | bytes 3145744 | tf_op jit(solution)/shard_map/psum | solution.py:203
  246.3 2.7 convert_element_type.109
  248.9 8.3 %fusion.32 = bf16[8,16,8,640]{3,2,0,1:T(8,128)(2,1)S(1)} fusion(bf16[16,768,640]{2,1,0:T(8,128)(2,1)} %param.33, f32[8,16,8,2,768]{4,2,0,1,3:T(8,128)S(1)} %convert_element_type.109), kind=kOutput, calls=%fused_computation.49 | convolution fusion | flops 1012006912 | bytes 23330816 | tf_op jit(solution)/shard_map/spku,pud->spkd/dot_general | solution.py:205
  257.2 1.2 copy.100
  258.4 5.5 %all-to-all-start.2 = ((bf16[8,16,8,640]{3,2,1,0:T(8,128)(2,1)}), bf16[8,16,8,640]{3,2,1,0:T(8,128)(2,1)S(1)}, u32[]{:S(2)}, u32[]{:S(2)}) async-start(bf16[8,16,8,640]{3,2,1,0:T(8,128)(2,1)} %copy.100), calls=%async_computation.2 | async-start | bytes 2621440 | tf_op jit(solution)/shard_map/all_to_all | solution.py:208
  267.6 27.6 %all-to-all-done.2 = bf16[8,16,8,640]{3,2,1,0:T(8,128)(2,1)S(1)} async-done(((bf16[8,16,8,640]{3,2,1,0:T(8,128)(2,1)}), bf16[8,16,8,640]{3,2,1,0:T(8,128)(2,1)S(1)}, u32[]{:S(2)}, u32[]{:S(2)}) %all-to-all-start.2) | async-done | bytes 1310752 | tf_op jit(solution)/shard_map/all_to_all | solution.py:208
  295.6 1.9 gather_fusion.8
  (131 shorter events, 24.3 us)
Async XLA Ops:
  7.2 106.9 %copy-start = (f32[640,64]{0,1:T(8,128)S(1)}, f32[640,64]{0,1:T(8,128)}, u32[]{:S(2)}) copy-start(f32[640,64]{0,1:T(8,128)} %param.29) | copy-start | bytes 491524
  13.9 17.9 %all-to-all-start = ((bf16[8,16,2,128]{3,1,2,0:T(8,128)(2,1)}), bf16[8,16,2,128]{3,1,2,0:T(8,128)(2,1)S(1)}, u32[]{:S(2)}, u32[]{:S(2)}) async-start(bf16[8,16,2,128]{3,1,2,0:T(8,128)(2,1)} %gather_fusion.5), calls=%async_computation | async-start | bytes 131072 | tf_op jit(solution)/shard_map/all_to_all | solution.py:119
  21.2 66.4 %all-gather.2.cloned.1.call-start = ((), (), s32[]{:S(2)}) async-start(), calls=%async_computation.5 | async-start | bytes 3686400 | tf_op jit(solution)/shard_map/all_gather | solution.py:147
  21.9 91.0 %reduce-scatter.4.cloned.1.call-start = ((), (), s32[]{:S(2)}) async-start(), calls=%async_computation.7 | async-start | bytes 819200
  32.4 81.6 %copy-start.4 = (bf16[64,640]{1,0:T(8,128)(2,1)S(1)}, bf16[64,640]{1,0:T(8,128)(2,1)}, u32[]{:S(2)}) copy-start(bf16[64,640]{1,0:T(8,128)(2,1)} %param.18) | copy-start | bytes 245764
  91.8 154.5 %all-reduce.3.cloned.1.call-start = ((), (), s32[]{:S(2)}) async-start(), calls=%async_computation.6 | async-start | bytes 6291456 | tf_op jit(solution)/shard_map/psum | solution.py:203
  125.0 49.8 %slice-start = ((s8[15728640]{0:T(1024)(128)(4,1)}), s8[3145728]{0:T(1024)(128)(4,1)S(1)}, s32[]{:S(2)}) async-start(s8[15728640]{0:T(1024)(128)(4,1)} %bitcast.139), calls=%async_computation.8 | async-start | bytes 6291456
  129.0 45.8 %slice-start.1 = ((s8[15728640]{0:T(1024)(128)(4,1)}), s8[4194304]{0:T(1024)(128)(4,1)S(1)}, s32[]{:S(2)}) async-start(s8[15728640]{0:T(1024)(128)(4,1)} %bitcast.139), calls=%async_computation.9 | async-start | bytes 8388608
  166.5 8.4 %slice-start.2 = ((s8[15728640]{0:T(1024)(128)(4,1)}), s8[4194304]{0:T(1024)(128)(4,1)S(1)}, s32[]{:S(2)}) async-start(s8[15728640]{0:T(1024)(128)(4,1)} %bitcast.139), calls=%async_computation.10 | async-start | bytes 8388608
  166.5 8.4 %slice-start.3 = ((s8[15728640]{0:T(1024)(128)(4,1)}), s8[4194304]{0:T(1024)(128)(4,1)S(1)}, s32[]{:S(2)}) async-start(s8[15728640]{0:T(1024)(128)(4,1)} %bitcast.139), calls=%async_computation.11 | async-start | bytes 8388608
  179.5 0.7 copy-start.2
  179.5 0.8 copy-start.3
  179.5 1.8 copy-start.7
  183.3 75.1 %all-to-all-start.3 = ((bf16[8,16,2,128]{3,1,2,0:T(8,128)(2,1)}), bf16[8,16,2,128]{3,1,2,0:T(8,128)(2,1)S(1)}, u32[]{:S(2)}, u32[]{:S(2)}) async-start(bf16[8,16,2,128]{3,1,2,0:T(8,128)(2,1)} %broadcast_select_fusion), calls=%async_computation.3 | async-start | bytes 131072 | tf_op jit(solution)/shard_map/all_to_all | solution.py:115
  257.2 6.8 %copy-start.6 = (s32[8,12]{1,0:T(8,128)S(1)}, s32[8,12]{1,0:T(8,128)}, u32[]{:S(2)}) copy-start(s32[8,12]{1,0:T(8,128)} %param.26) | copy-start | bytes 1156
  257.2 10.0 %copy-start.5 = (s32[64,6]{0,1:T(8,128)S(1)}, s32[64,6]{0,1:T(8,128)}, u32[]{:S(2)}) copy-start(s32[64,6]{0,1:T(8,128)} %param.30) | copy-start | bytes 4612
  258.4 36.8 %all-to-all-start.2 = ((bf16[8,16,8,640]{3,2,1,0:T(8,128)(2,1)}), bf16[8,16,8,640]{3,2,1,0:T(8,128)(2,1)S(1)}, u32[]{:S(2)}, u32[]{:S(2)}) async-start(bf16[8,16,8,640]{3,2,1,0:T(8,128)(2,1)} %copy.100), calls=%async_computation.2 | async-start | bytes 2621440 | tf_op jit(solution)/shard_map/all_to_all | solution.py:208
  295.6 3.1 %copy-start.1 = (f32[640,64]{0,1:T(8,128)S(1)}, f32[640,64]{0,1:T(8,128)}, u32[]{:S(2)}) copy-start(f32[640,64]{0,1:T(8,128)} %param.29) | copy-start | bytes 491524
Sparse Core Ops, SparseCore 0:
  24.2 63.3 all-gather.1
  91.9 21.0 reduce-scatter.3
  179.7 66.5 all-reduce.2
where the time goes:
time: 306 us; the launch traced here: 305 us
  waiting for transfers between devices  160 us (52%)
  blocking collectives  47.9 us (16%)
  matrix products  23.2 us (8%)
  local copies, waits for them, and re-layouts  21.6 us (7%)
  other arithmetic  21.4 us (7%)
  starting transfers between devices  16.7 us (5%)
  between operations  14.8 us (5%)
    psum x1, waiting for transfers between devices, per_device(): whole = lax.psum(both_parts.astype(jnp.bfloat16), 'kv').astype(jnp.float32)  59.1 us
    all_gather x1, waiting for transfers between devices, per_device(): lax.all_gather(out_weight, 'blk', axis=1, tiled=True)  55 us
    all_to_all x1, blocking collectives, per_device(): lax.all_to_all(doubled, 'blk', split_axis=0, concat_axis=0, tiled=True)  37.4 us
    all_to_all x1, waiting for transfers between devices, per_device(): lax.all_to_all(piece_out, 'blk', split_axis=0, concat_axis=0, tiled=True)  27.6 us
    unnamed x4, waiting for transfers between devices  17.8 us
    psum x1, blocking collectives, per_device(): lax.psum((jnp.sum(resid_float * resid_float, axis=1), jnp.dot(scaled, rou...  10.5 us
    dot_general x1, matrix products, per_device(): jnp.einsum('spkd,pdu->spku', rows_in, w_up, preferred_element_type=jnp.fl...  8.32 us
    dot_general x1, matrix products, per_device(): jnp.einsum('spku,pud->spkd', hidden, w_down, preferred_element_type=jnp.f...  8.29 us
  transfers between devices with their start and end apart: 6, of which 4 were waited for; matrix products, arithmetic and copies ran while one was open for 11% of the time, Pallas kernels for 0%

commit v1 on v0

--- a/solution.py
+++ b/solution.py
@@ -142,13 +142,13 @@
         .transpose(1, 0, 2)
     )
     attended = attended.reshape(stretch_len, head_count * head_dim).astype(jnp.bfloat16)
-    projected = jnp.dot(
-        attended,
-        lax.all_gather(out_weight, "blk", axis=1, tiled=True),
-        preferred_element_type=jnp.float32,
-    )
+    every_token = lax.all_gather(attended, "blk", axis=0, tiled=True)
+    column_part = jnp.dot(
+        every_token, out_weight, preferred_element_type=jnp.float32
+    ).astype(jnp.bfloat16)
+    projected = lax.all_to_all(column_part, "blk", split_axis=0, concat_axis=1, tiled=True)
     head_total = lax.psum_scatter(
-        projected.astype(jnp.bfloat16), "kv", scatter_dimension=1, tiled=True
+        projected, "kv", scatter_dimension=1, tiled=True
     ).astype(jnp.float32)
     residual = (hidden_in.astype(jnp.float32) + head_total).astype(jnp.bfloat16)
     resid_float = residual.astype(jnp.float32)

time: 306 us -> 294 us (0.961)
  waiting for transfers between devices: 160 us -> 111 us
  blocking collectives: 47.9 us -> 81.7 us
  starting transfers between devices: 16.7 us -> 20.3 us
    all_gather x1 -> x0, waiting for transfers between devices: 55 us -> none  [per_device(): lax.all_gather(out_weight, 'blk', axis=1, tiled=True)]
    all_gather x0 -> x1, blocking collectives: none -> 33.9 us  [per_device(): every_token = lax.all_gather(attended, 'blk', axis=0, tiled=True)]
    all_to_all x0 -> x1, waiting for transfers between devices: none -> 6.82 us  [per_device(): lax.all_to_all(column_part, 'blk', split_axis=0, concat_axis=1, tiled=True)]
    all_to_all x0 -> x1, starting transfers between devices: none -> 3.79 us  [per_device(): lax.all_to_all(column_part, 'blk', split_axis=0, concat_axis=1, tiled=True)]
    unnamed x4 -> x3, waiting for transfers between devices: 17.8 us -> 17.3 us
    unnamed x30 -> x51, local copies, waits for them, and re-layouts: 5.77 us -> 6.18 us
where the time goes in v1:
time: 294 us; the launch traced here: 293 us
  waiting for transfers between devices  111 us (38%)
  blocking collectives  81.7 us (28%)
  local copies, waits for them, and re-layouts  22.9 us (8%)
  other arithmetic  21.5 us (7%)
  matrix products  20.6 us (7%)
  starting transfers between devices  20.3 us (7%)
  between operations  15.4 us (5%)
    psum x1, waiting for transfers between devices, per_device(): whole = lax.psum(both_parts.astype(jnp.bfloat16), 'kv').astype(jnp.float32)  59.1 us
    all_to_all x1, blocking collectives, per_device(): lax.all_to_all(doubled, 'blk', split_axis=0, concat_axis=0, tiled=True)  37.3 us
    all_gather x1, blocking collectives, per_device(): every_token = lax.all_gather(attended, 'blk', axis=0, tiled=True)  33.9 us
    all_to_all x1, waiting for transfers between devices, per_device(): lax.all_to_all(piece_out, 'blk', split_axis=0, concat_axis=0, tiled=True)  27.6 us
    unnamed x3, waiting for transfers between devices  17.3 us
    psum x1, blocking collectives, per_device(): lax.psum((jnp.sum(resid_float * resid_float, axis=1), jnp.dot(scaled, rou...  10.5 us
    dot_general x1, matrix products, per_device(): jnp.einsum('spkd,pdu->spku', rows_in, w_up, preferred_element_type=jnp.fl...  8.31 us
    dot_general x1, matrix products, per_device(): jnp.einsum('spku,pud->spkd', hidden, w_down, preferred_element_type=jnp.f...  8.29 us
  transfers between devices with their start and end apart: 6, of which 4 were waited for; matrix products, arithmetic and copies ran while one was open for 11% of the time, Pallas kernels for 0%

profile of v1, /device:TPU:0, one launch (start us, length us, event | category | flops | bytes accessed | tf_op | source)
XLA Modules:
  0.0 293.3 jit_solution(17245542163544495511)
XLA Ops:
  8.6 1.2 gather_fusion.2
  9.8 1.2 gather_fusion.4
  11.0 1.5 and_select_fusion.2
  14.5 7.3 %all-to-all-start = ((bf16[8,16,2,128]{3,1,2,0:T(8,128)(2,1)}), bf16[8,16,2,128]{3,1,2,0:T(8,128)(2,1)S(1)}, u32[]{:S(2)}, u32[]{:S(2)}) async-start(bf16[8,16,2,128]{3,1,2,0:T(8,128)(2,1)} %gather_fusion.5), calls=%async_computation | async-start | bytes 131072 | tf_op jit(solution)/shard_map/all_to_all | solution.py:119
  22.4 1.2 gather_fusion
  29.6 33.9 %all_gather.3 = bf16[512,640]{1,0:T(8,128)(2,1)S(1)} all-gather(bf16[64,640]{1,0:T(8,128)(2,1)S(1)} %bitcast.159), channel_id=1, replica_groups=mesh['kv'=4,'blk'=8] {'blk'}, dimensions={0}, use_global_device_ids=true | all-gather | bytes 737280 | tf_op jit(solution)/shard_map/all_gather | solution.py:145
  64.8 3.8 %all-to-all-start.1 = ((bf16[8,64,320]{2,1,0:T(8,128)(2,1)}), bf16[8,64,320]{2,1,0:T(8,128)(2,1)S(1)}, u32[]{:S(2)}, u32[]{:S(2)}) async-start(bf16[8,64,320]{2,1,0:T(8,128)(2,1)} %bitcast.16), calls=%async_computation.1 | async-start | bytes 786432 | tf_op jit(solution)/shard_map/all_to_all | solution.py:149
  71.0 6.8 %all-to-all-done.1 = bf16[8,64,320]{2,1,0:T(8,128)(2,1)S(1)} async-done(((bf16[8,64,320]{2,1,0:T(8,128)(2,1)}), bf16[8,64,320]{2,1,0:T(8,128)(2,1)S(1)}, u32[]{:S(2)}, u32[]{:S(2)}) %all-to-all-start.1) | async-done | bytes 327712 | tf_op jit(solution)/shard_map/all_to_all | solution.py:149
  79.0 3.9 %scatter_custom_fusion = s32[512]{0:T(512)S(1)} fusion(s32[384]{0:T(512)S(1)} %get-tuple-element.175, s32[384]{0:T(512)S(1)} %iota_add_fusion, s32[]{:T(128)} %constant.152.clone.1), kind=kCustom, calls=%fused_computation.144 | custom fusion | flops 384 | bytes 2052 | tf_op jit(solution)/shard_map/scatter-add | solution.py:186
  83.1 17.3 %reduce-scatter.4.cloned.1.call-done = bf16[640,64]{1,0:T(8,128)(2,1)} async-done(((bf16[2560,64]{1,0:T(8,128)(2,1)}), bf16[640,64]{1,0:T(8,128)(2,1)}) %reduce-scatter.4.cloned.1.call-update) | async-done | bytes 81936
  101.9 10.5 %all-reduce = (f32[64]{0:T(128)S(1)}, f32[64,64]{1,0:T(8,128)S(1)}) all-reduce(f32[64]{0:T(128)S(1)} %get-tuple-element.196, f32[64,64]{1,0:T(8,128)S(1)} %fusion.41), channel_id=1, replica_groups=mesh['kv'=4,'blk'=8] {'kv'}, use_global_device_ids=true, to_apply=%region_17.18 | all-reduce | flops 4160 | bytes 33280 | tf_op jit(solution)/shard_map/psum | solution.py:156
  112.5 2.7 gather_fusion.7
  115.2 1.2 bitcast_select_fusion
  116.6 37.3 %all_to_all.39 = bf16[8,16,8,640]{3,2,1,0:T(8,128)(2,1)S(1)} all-to-all(bf16[8,16,8,640]{3,2,1,0:T(8,128)(2,1)S(1)} %bitcast.146), channel_id=1, replica_groups=mesh['kv'=4,'blk'=8] {'blk'}, dimensions={0} | all-to-all | bytes 2621440 | tf_op jit(solution)/shard_map/all_to_all | solution.py:199
  153.9 8.3 %fusion.26 = bf16[8,16,8,1,768]{4,2,0,1,3:T(8,128)(2,1)S(1)} fusion(bf16[16,640,768]{2,1,0:T(8,128)(2,1)} %param.32, bf16[8,16,8,640]{3,2,1,0:T(8,128)(2,1)S(1)} %all_to_all.39), kind=kOutput, calls=%fused_computation.46 | convolution fusion | flops 1007419392 | bytes 18612224 | tf_op jit(solution)/shard_map/spkd,pdu->spku/dot_general | solution.py:201
  162.3 2.7 fusion.29
  165.0 2.0 pad_maximum_fusion
  171.0 3.7 %all-to-all-start.4 = ((bf16[8,16,2,128]{3,1,2,0:T(8,128)(2,1)}), bf16[8,16,2,128]{3,1,2,0:T(8,128)(2,1)S(1)}, u32[]{:S(2)}, u32[]{:S(2)}) async-start(bf16[8,16,2,128]{3,1,2,0:T(8,128)(2,1)} %broadcast_select_fusion), calls=%async_computation.4 | async-start | bytes 131072 | tf_op jit(solution)/shard_map/all_to_all | solution.py:115
  174.7 59.1 %all-reduce.3.cloned.1.call-done = bf16[8,16,8,2,768]{4,2,0,1,3:T(8,128)(2,1)} async-done(((bf16[8,16,8,2,768]{4,2,0,1,3:T(8,128)(2,1)}), bf16[8,16,8,2,768]{4,2,0,1,3:T(8,128)(2,1)}) %all-reduce.3.cloned.1.call-update) | async-done | bytes 3145744 | tf_op jit(solution)/shard_map/psum | solution.py:203
  233.7 2.7 convert_element_type.109
  236.4 8.3 %fusion.32 = bf16[8,16,8,640]{3,2,0,1:T(8,128)(2,1)S(1)} fusion(bf16[16,768,640]{2,1,0:T(8,128)(2,1)} %param.33, f32[8,16,8,2,768]{4,2,0,1,3:T(8,128)S(1)} %convert_element_type.109), kind=kOutput, calls=%fused_computation.48 | convolution fusion | flops 1012006912 | bytes 23330816 | tf_op jit(solution)/shard_map/spku,pud->spkd/dot_general | solution.py:205
  245.9 5.5 %all-to-all-start.3 = ((bf16[8,16,8,640]{3,2,1,0:T(8,128)(2,1)}), bf16[8,16,8,640]{3,2,1,0:T(8,128)(2,1)S(1)}, u32[]{:S(2)}, u32[]{:S(2)}) async-start(bf16[8,16,8,640]{3,2,1,0:T(8,128)(2,1)} %copy.131), calls=%async_computation.3 | async-start | bytes 2621440 | tf_op jit(solution)/shard_map/all_to_all | solution.py:208
  255.1 27.6 %all-to-all-done.3 = bf16[8,16,8,640]{3,2,1,0:T(8,128)(2,1)S(1)} async-done(((bf16[8,16,8,640]{3,2,1,0:T(8,128)(2,1)}), bf16[8,16,8,640]{3,2,1,0:T(8,128)(2,1)S(1)}, u32[]{:S(2)}, u32[]{:S(2)}) %all-to-all-start.3) | async-done | bytes 1310752 | tf_op jit(solution)/shard_map/all_to_all | solution.py:208
  283.1 1.9 gather_fusion.8
  (153 shorter events, 26.3 us)
Async XLA Ops:
  7.2 56.3 %copy-start = (bf16[640,320]{0,1:T(8,128)(2,1)S(1)}, bf16[640,320]{0,1:T(8,128)(2,1)}, u32[]{:S(2)}) copy-start(bf16[640,320]{0,1:T(8,128)(2,1)} %param.27) | copy-start | bytes 1228804
  13.3 11.8 %copy-start.4 = (bf16[4,16,1,2,128]{4,1,3,0,2:T(8,128)(2,1)}, bf16[4,16,1,2,128]{4,1,3,0,2:T(8,128)(2,1)S(1)}, u32[]{:S(2)}) copy-start(bf16[4,16,1,2,128]{4,1,3,0,2:T(8,128)(2,1)S(1)} %copy.157) | copy-start | bytes 98308
  14.5 14.2 %all-to-all-start = ((bf16[8,16,2,128]{3,1,2,0:T(8,128)(2,1)}), bf16[8,16,2,128]{3,1,2,0:T(8,128)(2,1)S(1)}, u32[]{:S(2)}, u32[]{:S(2)}) async-start(bf16[8,16,2,128]{3,1,2,0:T(8,128)(2,1)} %gather_fusion.5), calls=%async_computation | async-start | bytes 131072 | tf_op jit(solution)/shard_map/all_to_all | solution.py:119
  29.3 39.5 %copy-start.17 = (bf16[640]{0:T(1024)(128)(2,1)S(1)}, bf16[640]{0:T(1024)(128)(2,1)}, u32[]{:S(2)}) copy-start(bf16[640]{0:T(1024)(128)(2,1)} %param.28) | copy-start | bytes 3844
  29.3 40.7 %copy-start.10 = (s32[64,6]{0,1:T(8,128)S(1)}, s32[64,6]{0,1:T(8,128)}, u32[]{:S(2)}) copy-start(s32[64,6]{0,1:T(8,128)} %param.30) | copy-start | bytes 4612
  63.5 37.9 %copy-start.9 = (bf16[64,640]{1,0:T(8,128)(2,1)S(1)}, bf16[64,640]{1,0:T(8,128)(2,1)}, u32[]{:S(2)}) copy-start(bf16[64,640]{1,0:T(8,128)(2,1)} %param.18) | copy-start | bytes 245764
  63.5 38.1 %copy-start.7 = (f32[640,64]{0,1:T(8,128)S(1)}, f32[640,64]{0,1:T(8,128)}, u32[]{:S(2)}) copy-start(f32[640,64]{0,1:T(8,128)} %param.29) | copy-start | bytes 491524
  64.8 13.0 %all-to-all-start.1 = ((bf16[8,64,320]{2,1,0:T(8,128)(2,1)}), bf16[8,64,320]{2,1,0:T(8,128)(2,1)S(1)}, u32[]{:S(2)}, u32[]{:S(2)}) async-start(bf16[8,64,320]{2,1,0:T(8,128)(2,1)} %bitcast.16), calls=%async_computation.1 | async-start | bytes 786432 | tf_op jit(solution)/shard_map/all_to_all | solution.py:149
  68.6 31.7 %reduce-scatter.4.cloned.1.call-start = ((), (), s32[]{:S(2)}) async-start(), calls=%async_computation.7 | async-start | bytes 819200
  79.0 154.8 %all-reduce.3.cloned.1.call-start = ((), (), s32[]{:S(2)}) async-start(), calls=%async_computation.6 | async-start | bytes 6291456 | tf_op jit(solution)/shard_map/psum | solution.py:203
  101.5 13.6 %copy-start.2 = (bf16[64,640]{1,0:T(8,128)(2,1)}, bf16[64,640]{1,0:T(8,128)(2,1)S(1)}, u32[]{:S(2)}) copy-start(bf16[64,640]{1,0:T(8,128)(2,1)S(1)} %get-tuple-element.197) | copy-start | bytes 245764
  112.5 49.7 %slice-start = ((s8[15728640]{0:T(1024)(128)(4,1)}), s8[3145728]{0:T(1024)(128)(4,1)S(1)}, s32[]{:S(2)}) async-start(s8[15728640]{0:T(1024)(128)(4,1)} %bitcast.144), calls=%async_computation.8 | async-start | bytes 6291456
  116.4 45.8 %slice-start.1 = ((s8[15728640]{0:T(1024)(128)(4,1)}), s8[4194304]{0:T(1024)(128)(4,1)S(1)}, s32[]{:S(2)}) async-start(s8[15728640]{0:T(1024)(128)(4,1)} %bitcast.144), calls=%async_computation.9 | async-start | bytes 8388608
  153.9 8.3 %slice-start.2 = ((s8[15728640]{0:T(1024)(128)(4,1)}), s8[4194304]{0:T(1024)(128)(4,1)S(1)}, s32[]{:S(2)}) async-start(s8[15728640]{0:T(1024)(128)(4,1)} %bitcast.144), calls=%async_computation.10 | async-start | bytes 8388608
  153.9 8.4 %slice-start.3 = ((s8[15728640]{0:T(1024)(128)(4,1)}), s8[4194304]{0:T(1024)(128)(4,1)S(1)}, s32[]{:S(2)}) async-start(s8[15728640]{0:T(1024)(128)(4,1)} %bitcast.144), calls=%async_computation.11 | async-start | bytes 8388608
  166.9 2.0 copy-start.13
  166.9 2.7 copy-start.5
  171.0 74.9 %all-to-all-start.4 = ((bf16[8,16,2,128]{3,1,2,0:T(8,128)(2,1)}), bf16[8,16,2,128]{3,1,2,0:T(8,128)(2,1)S(1)}, u32[]{:S(2)}, u32[]{:S(2)}) async-start(bf16[8,16,2,128]{3,1,2,0:T(8,128)(2,1)} %broadcast_select_fusion), calls=%async_computation.4 | async-start | bytes 131072 | tf_op jit(solution)/shard_map/all_to_all | solution.py:115
  244.7 6.8 %copy-start.14 = (s32[8,8]{1,0:T(8,128)S(1)}, s32[8,8]{1,0:T(8,128)}, u32[]{:S(2)}) copy-start(s32[8,8]{1,0:T(8,128)} %get-tuple-element.202) | copy-start | bytes 772
  244.7 6.8 %copy-start.12 = (s32[8,12]{1,0:T(8,128)S(1)}, s32[8,12]{1,0:T(8,128)}, u32[]{:S(2)}) copy-start(s32[8,12]{1,0:T(8,128)} %param.26) | copy-start | bytes 1156
  244.7 9.0 %copy-start.16 = (s32[384]{0:T(512)S(1)}, s32[384]{0:T(512)}, u32[]{:S(2)}) copy-start(s32[384]{0:T(512)} %get-tuple-element.174) | copy-start | bytes 4612
  244.7 10.0 %copy-start.11 = (s32[64,6]{0,1:T(8,128)S(1)}, s32[64,6]{0,1:T(8,128)}, u32[]{:S(2)}) copy-start(s32[64,6]{0,1:T(8,128)} %param.30) | copy-start | bytes 4612
  245.9 36.8 %all-to-all-start.3 = ((bf16[8,16,8,640]{3,2,1,0:T(8,128)(2,1)}), bf16[8,16,8,640]{3,2,1,0:T(8,128)(2,1)S(1)}, u32[]{:S(2)}, u32[]{:S(2)}) async-start(bf16[8,16,8,640]{3,2,1,0:T(8,128)(2,1)} %copy.131), calls=%async_computation.3 | async-start | bytes 2621440 | tf_op jit(solution)/shard_map/all_to_all | solution.py:208
  283.1 3.4 %copy-start.1 = (bf16[640,320]{0,1:T(8,128)(2,1)S(1)}, bf16[640,320]{0,1:T(8,128)(2,1)}, u32[]{:S(2)}) copy-start(bf16[640,320]{0,1:T(8,128)(2,1)} %param.27) | copy-start | bytes 1228804
  (4 other events, 3.1 us)
Sparse Core Ops, SparseCore 0:
  79.1 21.2 reduce-scatter.3
  167.1 66.5 all-reduce.2

commit v2 on v1

--- a/solution.py
+++ b/solution.py
@@ -142,7 +142,9 @@
         .transpose(1, 0, 2)
     )
     attended = attended.reshape(stretch_len, head_count * head_dim).astype(jnp.bfloat16)
-    every_token = lax.all_gather(attended, "blk", axis=0, tiled=True)
+    every_token = lax.all_to_all(
+        jnp.broadcast_to(attended[None], (blk_count,) + attended.shape), "blk", 0, 0, tiled=True
+    ).reshape(-1, attended.shape[1])
     column_part = jnp.dot(
         every_token, out_weight, preferred_element_type=jnp.float32
     ).astype(jnp.bfloat16)
@@ -191,23 +193,49 @@
     )
     pieces_here = w_gate.shape[0]
     feature_part = normed.shape[1]
-    doubled = jnp.broadcast_to(
-        packed_rows.reshape(expert_count, 1, capacity, feature_part),
-        (expert_count, 2, capacity, feature_part),
-    )
-    doubled = doubled.reshape(blk_count, pieces_here, capacity, feature_part)
-    rows_in = lax.all_to_all(doubled, "blk", split_axis=0, concat_axis=0, tiled=True)
-    gate_part = jnp.einsum("spkd,pdu->spku", rows_in, w_gate, preferred_element_type=jnp.float32)
-    up_part = jnp.einsum("spkd,pdu->spku", rows_in, w_up, preferred_element_type=jnp.float32)
-    both_parts = jnp.stack([gate_part, up_part], axis=3)
-    whole = lax.psum(both_parts.astype(jnp.bfloat16), "kv").astype(jnp.float32)
-    hidden = (jax.nn.silu(whole[:, :, :, 0]) * whole[:, :, :, 1]).astype(jnp.bfloat16)
+    kv_count = lax.axis_size("kv")
+    hidden_len = w_gate.shape[2]
+    hidden_part = hidden_len // kv_count
+    paired = pieces_here % 2 == 0
+    if paired:
+        experts_here = pieces_here // 2
+        sent = packed_rows.reshape(blk_count, experts_here, capacity, feature_part)
+        landed_rows = lax.all_to_all(sent, "blk", split_axis=0, concat_axis=0, tiled=True)
+        rows_in = jnp.broadcast_to(
+            landed_rows[:, :, None], (blk_count, experts_here, 2, capacity, feature_part)
+        ).reshape(blk_count, pieces_here, capacity, feature_part)
+    else:
+        doubled = jnp.broadcast_to(
+            packed_rows.reshape(expert_count, 1, capacity, feature_part),
+            (expert_count, 2, capacity, feature_part),
+        )
+        doubled = doubled.reshape(blk_count, pieces_here, capacity, feature_part)
+        rows_in = lax.all_to_all(doubled, "blk", split_axis=0, concat_axis=0, tiled=True)
+    gate_w = w_gate.reshape(pieces_here, feature_part, kv_count, hidden_part)
+    up_w = w_up.reshape(pieces_here, feature_part, kv_count, hidden_part)
+    gate_part = jnp.einsum("spkd,pdcv->cspkv", rows_in, gate_w, preferred_element_type=jnp.float32)
+    up_part = jnp.einsum("spkd,pdcv->cspkv", rows_in, up_w, preferred_element_type=jnp.float32)
+    both_parts = jnp.stack([gate_part, up_part], axis=1).astype(jnp.bfloat16)
+    share_shape = both_parts.shape[1:]
+    own_share = lax.psum_scatter(
+        both_parts.reshape(-1, hidden_part), "kv", scatter_dimension=0, tiled=True
+    )
+    own_share = own_share.reshape(share_shape).astype(jnp.float32)
+    hidden_share = (jax.nn.silu(own_share[0]) * own_share[1]).astype(jnp.bfloat16)
+    hidden = lax.all_gather(hidden_share, "kv", axis=0)
+    down_w = w_down.reshape(pieces_here, kv_count, hidden_part, feature_part)
     piece_out = jnp.einsum(
-        "spku,pud->spkd", hidden, w_down, preferred_element_type=jnp.float32
+        "cspkv,pcvd->spkd", hidden, down_w, preferred_element_type=jnp.float32
     ).astype(jnp.bfloat16)
-    returned = lax.all_to_all(piece_out, "blk", split_axis=0, concat_axis=0, tiled=True)
-    per_piece = returned.reshape(expert_count, 2, capacity, feature_part).astype(jnp.float32)
-    per_slot = (per_piece[:, 0] + per_piece[:, 1]).reshape(slot_total, feature_part)
+    if paired:
+        half_sum = piece_out.reshape(blk_count, experts_here, 2, capacity, feature_part)
+        half_sum = jnp.sum(half_sum.astype(jnp.float32), axis=2).astype(jnp.bfloat16)
+        returned = lax.all_to_all(half_sum, "blk", split_axis=0, concat_axis=0, tiled=True)
+        per_slot = returned.reshape(slot_total, feature_part).astype(jnp.float32)
+    else:
+        returned = lax.all_to_all(piece_out, "blk", split_axis=0, concat_axis=0, tiled=True)
+        per_piece = returned.reshape(expert_count, 2, capacity, feature_part).astype(jnp.float32)
+        per_slot = (per_piece[:, 0] + per_piece[:, 1]).reshape(slot_total, feature_part)
     routed = per_slot[target].reshape(stretch_len, top_count, feature_part)
     moe_out = jnp.sum(routed * gates[:, :, None], axis=1)
     layer_out = (resid_float + moe_out).astype(jnp.bfloat16)

time: 294 us -> 301 us (1.024)
  blocking collectives: 81.7 us -> 10.5 us
  local copies, waits for them, and re-layouts: 22.9 us -> 64.1 us
  matrix products: 20.6 us -> 35.7 us
  starting transfers between devices: 20.3 us -> 34.7 us
  waiting for transfers between devices: 111 us -> 119 us
    psum x1 -> x0, waiting for transfers between devices: 59.1 us -> none  [per_device(): whole = lax.psum(both_parts.astype(jnp.bfloat16), 'kv').astype(jnp.float32)]
    reduce_scatter x0 -> x1, waiting for transfers between devices: none -> 45.9 us  [per_device(): lax.psum_scatter(both_parts.reshape(-1, hidden_part), 'kv', scatter_dimen...]
    unnamed x51 -> x29, local copies, waits for them, and re-layouts: 6.18 us -> 43.5 us
    all_to_all x1 -> x0, blocking collectives: 37.3 us -> none  [per_device(): lax.all_to_all(doubled, 'blk', split_axis=0, concat_axis=0, tiled=True)]
    all_gather x1 -> x0, blocking collectives: 33.9 us -> none  [per_device(): every_token = lax.all_gather(attended, 'blk', axis=0, tiled=True)]
    dot_general x3, matrix products: 19.3 us -> 34.4 us  [the longest x1 12.8 us: per_device(): jnp.einsum('spkd,pdcv->cspkv', rows_in, up_w, preferred_element_type=jnp....]
    all_gather x0 -> x1, waiting for transfers between devices: none -> 14.1 us  [per_device(): hidden = lax.all_gather(hidden_share, 'kv', axis=0)]
    all_to_all x1 -> x3, starting transfers between devices: 5.52 us -> 18 us  [the longest x1 6.77 us: per_device(): lax.all_to_all(jnp.broadcast_to(attended[None], (blk_count,) + attended.s...]
  transfers between devices with their start and end apart: 6 -> 9, of which waited for: 4 -> 7; matrix products, arithmetic and copies ran while one was open for 11% -> 22% of each run, Pallas kernels for 0% -> 0%
where the time goes in v2:
time: 301 us; the launch traced here: 299 us
  waiting for transfers between devices  119 us (40%)
  local copies, waits for them, and re-layouts  64.1 us (21%)
  matrix products  35.7 us (12%)
  starting transfers between devices  34.7 us (12%)
  other arithmetic  19.2 us (6%)
  between operations  14.9 us (5%)
  blocking collectives  10.5 us (3%)
    reduce_scatter x1, waiting for transfers between devices, per_device(): lax.psum_scatter(both_parts.reshape(-1, hidden_part), 'kv', scatter_dimen...  45.9 us
    unnamed x29, local copies, waits for them, and re-layouts  43.5 us
    unnamed x4, waiting for transfers between devices  17.7 us
    all_to_all x1, waiting for transfers between devices, per_device(): lax.all_to_all(jnp.broadcast_to(attended[None], (blk_count,) + attended.s...  16.5 us
    all_to_all x1, waiting for transfers between devices, per_device(): lax.all_to_all(half_sum, 'blk', split_axis=0, concat_axis=0, tiled=True)  14.2 us
    all_gather x1, waiting for transfers between devices, per_device(): hidden = lax.all_gather(hidden_share, 'kv', axis=0)  14.1 us
    dot_general x1, matrix products, per_device(): jnp.einsum('spkd,pdcv->cspkv', rows_in, up_w, preferred_element_type=jnp....  12.8 us
    dot_general x1, matrix products, per_device(): jnp.einsum('spkd,pdcv->cspkv', rows_in, gate_w, preferred_element_type=jn...  12.8 us
  transfers between devices with their start and end apart: 9, of which 7 were waited for; matrix products, arithmetic and copies ran while one was open for 22% of the time, Pallas kernels for 0%

profile of v2, /device:TPU:0, one launch (start us, length us, event | category | flops | bytes accessed | tf_op | source)
XLA Modules:
  0.0 298.7 jit_solution(15214036862400287935)
XLA Ops:
  13.9 7.3 %all-to-all-start = ((bf16[8,16,2,128]{3,1,2,0:T(8,128)(2,1)}), bf16[8,16,2,128]{3,1,2,0:T(8,128)(2,1)S(1)}, u32[]{:S(2)}, u32[]{:S(2)}) async-start(bf16[8,16,2,128]{3,1,2,0:T(8,128)(2,1)} %gather_fusion.5), calls=%async_computation | async-start | bytes 131072 | tf_op jit(solution)/shard_map/all_to_all | solution.py:119
  29.8 6.8 %all-to-all-start.1 = ((bf16[8,64,640]{2,1,0:T(8,128)(2,1)}), bf16[8,64,640]{2,1,0:T(8,128)(2,1)S(1)}, u32[]{:S(2)}, u32[]{:S(2)}) async-start(bf16[8,64,640]{2,1,0:T(8,128)(2,1)} %broadcast_in_dim.156), calls=%async_computation.1 | async-start | bytes 1310720 | tf_op jit(solution)/shard_map/all_to_all | solution.py:145
  36.8 16.5 %all-to-all-done.1 = bf16[8,64,640]{2,1,0:T(8,128)(2,1)S(1)} async-done(((bf16[8,64,640]{2,1,0:T(8,128)(2,1)}), bf16[8,64,640]{2,1,0:T(8,128)(2,1)S(1)}, u32[]{:S(2)}, u32[]{:S(2)}) %all-to-all-start.1) | async-done | bytes 655392 | tf_op jit(solution)/shard_map/all_to_all | solution.py:145
  54.7 3.6 %all-to-all-start.2 = ((bf16[8,64,320]{2,1,0:T(8,128)(2,1)}), bf16[8,64,320]{2,1,0:T(8,128)(2,1)S(1)}, u32[]{:S(2)}, u32[]{:S(2)}) async-start(bf16[8,64,320]{2,1,0:T(8,128)(2,1)} %bitcast.17), calls=%async_computation.2 | async-start | bytes 786432 | tf_op jit(solution)/shard_map/all_to_all | solution.py:151
  60.2 10.0 %all-to-all-done.2 = bf16[8,64,320]{2,1,0:T(8,128)(2,1)S(1)} async-done(((bf16[8,64,320]{2,1,0:T(8,128)(2,1)}), bf16[8,64,320]{2,1,0:T(8,128)(2,1)S(1)}, u32[]{:S(2)}, u32[]{:S(2)}) %all-to-all-start.2) | async-done | bytes 327712 | tf_op jit(solution)/shard_map/all_to_all | solution.py:151
  71.3 3.9 %scatter_custom_fusion = s32[512]{0:T(512)S(1)} fusion(s32[384]{0:T(512)S(1)} %get-tuple-element.185, s32[384]{0:T(512)S(1)} %iota_add_fusion, s32[]{:T(128)} %constant.153.clone.1), kind=kCustom, calls=%fused_computation.130 | custom fusion | flops 384 | bytes 2052 | tf_op jit(solution)/shard_map/scatter-add | solution.py:188
  75.3 17.6 %reduce-scatter.7.cloned.1.call-done = bf16[640,64]{1,0:T(8,128)(2,1)} async-done(((bf16[2560,64]{1,0:T(8,128)(2,1)}), bf16[640,64]{1,0:T(8,128)(2,1)}) %reduce-scatter.7.cloned.1.call-update) | async-done | bytes 81936
  94.5 10.5 %all-reduce = (f32[64]{0:T(128)S(1)}, f32[64,64]{1,0:T(8,128)S(1)}) all-reduce(f32[64]{0:T(128)S(1)} %get-tuple-element.206, f32[64,64]{1,0:T(8,128)S(1)} %fusion.9), channel_id=1, replica_groups=mesh['kv'=4,'blk'=8] {'kv'}, use_global_device_ids=true, to_apply=%region_17.18 | all-reduce | flops 4160 | bytes 33280 | tf_op jit(solution)/shard_map/psum | solution.py:158
  105.1 2.0 gather_fusion.7
  108.1 5.7 %all-to-all-start.3 = ((bf16[8,8,8,640]{3,2,1,0:T(8,128)(2,1)}), bf16[8,8,8,640]{3,2,1,0:T(8,128)(2,1)S(1)}, u32[]{:S(2)}, u32[]{:S(2)}) async-start(bf16[8,8,8,640]{3,2,1,0:T(8,128)(2,1)} %broadcast_select_fusion), calls=%async_computation.3 | async-start | bytes 1310720 | tf_op jit(solution)/shard_map/all_to_all | solution.py:203
  114.0 19.5 %copy.188 = bf16[16,640,768]{1,2,0:T(8,128)(2,1)} copy(bf16[16,640,768]{2,1,0:T(8,128)(2,1)} %param.32) | data formatting | bytes 31457280 | tf_op args[14]
  133.5 19.5 %copy.187 = bf16[16,640,768]{1,2,0:T(8,128)(2,1)} copy(bf16[16,640,768]{2,1,0:T(8,128)(2,1)} %param.31) | data formatting | bytes 31457280 | tf_op args[13]
  153.2 12.8 %convert_bitcast_fusion = bf16[4,1,8,16,8,192]{5,4,0,2,3,1:T(8,128)(2,1)} fusion(bf16[8,16,8,640,1]{3,2,4,0,1:T(8,128)(2,1)S(1)} %bitcast.135, bf16[16,640,4,192,1]{1,3,2,4,0:T(8,128)(2,1)} %bitcast.134), kind=kOutput, calls=%fused_computation.33 | convolution fusion | flops 1007419392 | bytes 18612224 | tf_op jit(solution)/shard_map/spkd,pdcv->cspkv/dot_general | solution.py:217
  166.1 12.8 %convert_bitcast_fusion.1 = bf16[4,1,8,16,8,192]{5,4,0,2,3,1:T(8,128)(2,1)} fusion(bf16[8,16,8,640,1]{3,2,4,0,1:T(8,128)(2,1)S(1)} %bitcast.136, bf16[16,640,4,192,1]{1,3,2,4,0:T(8,128)(2,1)} %bitcast.133), kind=kOutput, calls=%fused_computation.34 | convolution fusion | flops 1007419392 | bytes 18612224 | tf_op jit(solution)/shard_map/spkd,pdcv->cspkv/dot_general | solution.py:216
  178.9 3.0 %pad_maximum_fusion = bf16[4,2,8,16,8,192]{5,4,0,2,3,1:T(8,128)(2,1)S(1)} fusion(bf16[4,1,8,16,8,192]{5,4,0,2,3,1:T(8,128)(2,1)} %convert_bitcast_fusion, bf16[4,1,8,16,8,192]{5,4,0,2,3,1:T(8,128)(2,1)} %convert_bitcast_fusion.1), kind=kLoop, calls=%fused_computation.31 | loop fusion | flops 1572864 | bytes 6291456 | tf_op jit(solution)/shard_map/stack | solution.py:218
  182.0 2.5 copy.189
  184.5 45.9 %reduce-scatter.5.cloned.1.call-done = bf16[2048,192]{1,0:T(8,128)(2,1)} async-done(((bf16[8192,192]{1,0:T(8,128)(2,1)}), bf16[2048,192]{1,0:T(8,128)(2,1)}) %reduce-scatter.5.cloned.1.call-update) | async-done | bytes 786448 | tf_op jit(solution)/shard_map/reduce_scatter | solution.py:220
  230.4 1.4 fusion.48
  236.2 5.5 %all-to-all-start.5 = ((bf16[8,16,2,128]{3,1,2,0:T(8,128)(2,1)}), bf16[8,16,2,128]{3,1,2,0:T(8,128)(2,1)S(1)}, u32[]{:S(2)}, u32[]{:S(2)}) async-start(bf16[8,16,2,128]{3,1,2,0:T(8,128)(2,1)} %broadcast_select_fusion.1), calls=%async_computation.6 | async-start | bytes 131072 | tf_op jit(solution)/shard_map/all_to_all | solution.py:115
  241.8 14.1 %all-gather.2.cloned.1.call-done = bf16[4,8,16,8,192]{4,3,0,1,2:T(8,128)(2,1)} async-done(((bf16[1,8,16,8,192]{4,3,0,1,2:T(8,128)(2,1)}), bf16[4,8,16,8,192]{4,3,0,1,2:T(8,128)(2,1)}) %all-gather.2.cloned.1.call-update) | async-done | bytes 1572880 | tf_op jit(solution)/shard_map/all_gather | solution.py:225
  256.0 8.7 %bitcast_reduce_fusion = bf16[8,8,8,640]{3,2,0,1:T(8,128)(2,1)S(1)} fusion(bf16[4,8,16,8,192]{4,3,0,1,2:T(8,128)(2,1)} %all-gather.2.cloned.1.call-done, bf16[16,4,192,640,1]{3,2,1,4,0:T(8,128)(2,1)} %bitcast.137), kind=kOutput, calls=%fused_computation.35 | convolution fusion | flops 1007616000 | bytes 17956864 | tf_op jit(solution)/shard_map/cspkv,pcvd->spkd/dot_general | solution.py:227
  265.6 5.6 %all-to-all-start.4 = ((bf16[8,8,8,640]{3,2,1,0:T(8,128)(2,1)}), bf16[8,8,8,640]{3,2,1,0:T(8,128)(2,1)S(1)}, u32[]{:S(2)}, u32[]{:S(2)}) async-start(bf16[8,8,8,640]{3,2,1,0:T(8,128)(2,1)} %copy.193), calls=%async_computation.5 | async-start | bytes 1310720 | tf_op jit(solution)/shard_map/all_to_all | solution.py:233
  274.7 14.2 %all-to-all-done.4 = bf16[8,8,8,640]{3,2,1,0:T(8,128)(2,1)S(1)} async-done(((bf16[8,8,8,640]{3,2,1,0:T(8,128)(2,1)}), bf16[8,8,8,640]{3,2,1,0:T(8,128)(2,1)S(1)}, u32[]{:S(2)}, u32[]{:S(2)}) %all-to-all-start.4) | async-done | bytes 655392 | tf_op jit(solution)/shard_map/all_to_all | solution.py:233
  289.1 1.9 gather_fusion.8
  (138 shorter events, 32.3 us)
Async XLA Ops:
  7.2 46.2 %copy-start = (bf16[640,320]{0,1:T(8,128)(2,1)S(1)}, bf16[640,320]{0,1:T(8,128)(2,1)}, u32[]{:S(2)}) copy-start(bf16[640,320]{0,1:T(8,128)(2,1)} %param.27) | copy-start | bytes 1228804
  13.9 14.2 %all-to-all-start = ((bf16[8,16,2,128]{3,1,2,0:T(8,128)(2,1)}), bf16[8,16,2,128]{3,1,2,0:T(8,128)(2,1)S(1)}, u32[]{:S(2)}, u32[]{:S(2)}) async-start(bf16[8,16,2,128]{3,1,2,0:T(8,128)(2,1)} %gather_fusion.5), calls=%async_computation | async-start | bytes 131072 | tf_op jit(solution)/shard_map/all_to_all | solution.py:119
  28.7 7.9 %copy-start.6 = (s32[64,6]{0,1:T(8,128)S(1)}, s32[64,6]{0,1:T(8,128)}, u32[]{:S(2)}) copy-start(s32[64,6]{0,1:T(8,128)} %param.30) | copy-start | bytes 4612
  29.8 28.8 %copy-start.9 = (bf16[640]{0:T(1024)(128)(2,1)S(1)}, bf16[640]{0:T(1024)(128)(2,1)}, u32[]{:S(2)}) copy-start(bf16[640]{0:T(1024)(128)(2,1)} %param.28) | copy-start | bytes 3844
  29.8 23.5 %all-to-all-start.1 = ((bf16[8,64,640]{2,1,0:T(8,128)(2,1)}), bf16[8,64,640]{2,1,0:T(8,128)(2,1)S(1)}, u32[]{:S(2)}, u32[]{:S(2)}) async-start(bf16[8,64,640]{2,1,0:T(8,128)(2,1)} %broadcast_in_dim.156), calls=%async_computation.1 | async-start | bytes 1310720 | tf_op jit(solution)/shard_map/all_to_all | solution.py:145
  53.8 40.2 %copy-start.5 = (bf16[64,640]{1,0:T(8,128)(2,1)S(1)}, bf16[64,640]{1,0:T(8,128)(2,1)}, u32[]{:S(2)}) copy-start(bf16[64,640]{1,0:T(8,128)(2,1)} %param.18) | copy-start | bytes 245764
  53.8 40.3 %copy-start.3 = (f32[640,64]{0,1:T(8,128)S(1)}, f32[640,64]{0,1:T(8,128)}, u32[]{:S(2)}) copy-start(f32[640,64]{0,1:T(8,128)} %param.29) | copy-start | bytes 491524
  54.7 15.4 %all-to-all-start.2 = ((bf16[8,64,320]{2,1,0:T(8,128)(2,1)}), bf16[8,64,320]{2,1,0:T(8,128)(2,1)S(1)}, u32[]{:S(2)}, u32[]{:S(2)}) async-start(bf16[8,64,320]{2,1,0:T(8,128)(2,1)} %bitcast.17), calls=%async_computation.2 | async-start | bytes 786432 | tf_op jit(solution)/shard_map/all_to_all | solution.py:151
  58.4 34.6 %reduce-scatter.7.cloned.1.call-start = ((), (), s32[]{:S(2)}) async-start(), calls=%async_computation.10 | async-start | bytes 819200
  108.1 44.9 %all-to-all-start.3 = ((bf16[8,8,8,640]{3,2,1,0:T(8,128)(2,1)}), bf16[8,8,8,640]{3,2,1,0:T(8,128)(2,1)S(1)}, u32[]{:S(2)}, u32[]{:S(2)}) async-start(bf16[8,8,8,640]{3,2,1,0:T(8,128)(2,1)} %broadcast_select_fusion), calls=%async_computation.3 | async-start | bytes 1310720 | tf_op jit(solution)/shard_map/all_to_all | solution.py:203
  113.8 116.7 %reduce-scatter.5.cloned.1.call-start = ((), (), s32[]{:S(2)}) async-start(), calls=%async_computation.8 | async-start | bytes 5242880 | tf_op jit(solution)/shard_map/reduce_scatter | solution.py:220
  184.5 71.5 %all-gather.2.cloned.1.call-start = ((), (), s32[]{:S(2)}) async-start(), calls=%async_computation.9 | async-start | bytes 2621440 | tf_op jit(solution)/shard_map/all_gather | solution.py:225
  231.8 1.2 copy-start.2
  231.8 1.3 copy-start.4
  231.8 2.3 copy-start.8
  231.8 9.9 %copy-start.7 = (s32[8,12]{1,0:T(8,128)S(1)}, s32[8,12]{1,0:T(8,128)}, u32[]{:S(2)}) copy-start(s32[8,12]{1,0:T(8,128)} %param.26) | copy-start | bytes 1156
  236.2 29.5 %all-to-all-start.5 = ((bf16[8,16,2,128]{3,1,2,0:T(8,128)(2,1)}), bf16[8,16,2,128]{3,1,2,0:T(8,128)(2,1)S(1)}, u32[]{:S(2)}, u32[]{:S(2)}) async-start(bf16[8,16,2,128]{3,1,2,0:T(8,128)(2,1)} %broadcast_select_fusion.1), calls=%async_computation.6 | async-start | bytes 131072 | tf_op jit(solution)/shard_map/all_to_all | solution.py:115
  265.6 23.3 %all-to-all-start.4 = ((bf16[8,8,8,640]{3,2,1,0:T(8,128)(2,1)}), bf16[8,8,8,640]{3,2,1,0:T(8,128)(2,1)S(1)}, u32[]{:S(2)}, u32[]{:S(2)}) async-start(bf16[8,8,8,640]{3,2,1,0:T(8,128)(2,1)} %copy.193), calls=%async_computation.5 | async-start | bytes 1310720 | tf_op jit(solution)/shard_map/all_to_all | solution.py:233
  289.1 3.1 %copy-start.1 = (bf16[640,320]{0,1:T(8,128)(2,1)S(1)}, bf16[640,320]{0,1:T(8,128)(2,1)}, u32[]{:S(2)}) copy-start(bf16[640,320]{0,1:T(8,128)(2,1)} %param.27) | copy-start | bytes 1228804
Sparse Core Ops, SparseCore 0:
  71.4 21.5 reduce-scatter.6
  184.6 45.8 reduce-scatter.4
  233.1 22.8 all-gather.1

commit v3 on v2

--- a/solution.py
+++ b/solution.py
@@ -193,9 +193,6 @@
     )
     pieces_here = w_gate.shape[0]
     feature_part = normed.shape[1]
-    kv_count = lax.axis_size("kv")
-    hidden_len = w_gate.shape[2]
-    hidden_part = hidden_len // kv_count
     paired = pieces_here % 2 == 0
     if paired:
         experts_here = pieces_here // 2
@@ -211,21 +208,13 @@
         )
         doubled = doubled.reshape(blk_count, pieces_here, capacity, feature_part)
         rows_in = lax.all_to_all(doubled, "blk", split_axis=0, concat_axis=0, tiled=True)
-    gate_w = w_gate.reshape(pieces_here, feature_part, kv_count, hidden_part)
-    up_w = w_up.reshape(pieces_here, feature_part, kv_count, hidden_part)
-    gate_part = jnp.einsum("spkd,pdcv->cspkv", rows_in, gate_w, preferred_element_type=jnp.float32)
-    up_part = jnp.einsum("spkd,pdcv->cspkv", rows_in, up_w, preferred_element_type=jnp.float32)
-    both_parts = jnp.stack([gate_part, up_part], axis=1).astype(jnp.bfloat16)
-    share_shape = both_parts.shape[1:]
-    own_share = lax.psum_scatter(
-        both_parts.reshape(-1, hidden_part), "kv", scatter_dimension=0, tiled=True
-    )
-    own_share = own_share.reshape(share_shape).astype(jnp.float32)
-    hidden_share = (jax.nn.silu(own_share[0]) * own_share[1]).astype(jnp.bfloat16)
-    hidden = lax.all_gather(hidden_share, "kv", axis=0)
-    down_w = w_down.reshape(pieces_here, kv_count, hidden_part, feature_part)
+    gate_part = jnp.einsum("spkd,pdu->spku", rows_in, w_gate, preferred_element_type=jnp.float32)
+    up_part = jnp.einsum("spkd,pdu->spku", rows_in, w_up, preferred_element_type=jnp.float32)
+    both_parts = jnp.stack([gate_part, up_part], axis=3)
+    whole = lax.psum(both_parts.astype(jnp.bfloat16), "kv").astype(jnp.float32)
+    hidden = (jax.nn.silu(whole[:, :, :, 0]) * whole[:, :, :, 1]).astype(jnp.bfloat16)
     piece_out = jnp.einsum(
-        "cspkv,pcvd->spkd", hidden, down_w, preferred_element_type=jnp.float32
+        "spku,pud->spkd", hidden, w_down, preferred_element_type=jnp.float32
     ).astype(jnp.bfloat16)
     if paired:
         half_sum = piece_out.reshape(blk_count, experts_here, 2, capacity, feature_part)

time: 301 us -> 262 us (0.87)
  local copies, waits for them, and re-layouts: 64.1 us -> 21.3 us
  waiting for transfers between devices: 119 us -> 136 us
  matrix products: 35.7 us -> 26.8 us
  starting transfers between devices: 34.7 us -> 30.1 us
    psum x0 -> x1, waiting for transfers between devices: none -> 61.6 us  [per_device(): whole = lax.psum(both_parts.astype(jnp.bfloat16), 'kv').astype(jnp.float32)]
    reduce_scatter x1 -> x0, waiting for transfers between devices: 45.9 us -> none  [per_device(): lax.psum_scatter(both_parts.reshape(-1, hidden_part), 'kv', scatter_dimen...]
    unnamed x29 -> x27, local copies, waits for them, and re-layouts: 43.5 us -> 4.54 us
    all_to_all x1, waiting for transfers between devices: 0.01 us -> 15.5 us  [per_device(): lax.all_to_all(sent, 'blk', split_axis=0, concat_axis=0, tiled=True)]
    all_gather x1 -> x0, waiting for transfers between devices: 14.1 us -> none  [per_device(): hidden = lax.all_gather(hidden_share, 'kv', axis=0)]
    dot_general x3 -> x4, matrix products: 34.4 us -> 25.3 us  [the longest x1 8.33 us: per_device(): jnp.einsum('spkd,pdu->spku', rows_in, w_gate, preferred_element_type=jnp....]
    unnamed x4 -> x3, waiting for transfers between devices: 17.7 us -> 17.7 us
  transfers between devices with their start and end apart: 9 -> 8, of which waited for: 7 -> 7; matrix products, arithmetic and copies ran while one was open for 22% -> 11% of each run, Pallas kernels for 0% -> 0%
where the time goes in v3:
time: 262 us; the launch traced here: 261 us
  waiting for transfers between devices  136 us (52%)
  starting transfers between devices  30.1 us (11%)
  matrix products  26.8 us (10%)
  local copies, waits for them, and re-layouts  21.3 us (8%)
  other arithmetic  20.9 us (8%)
  between operations  15.2 us (6%)
  blocking collectives  10.5 us (4%)
    psum x1, waiting for transfers between devices, per_device(): whole = lax.psum(both_parts.astype(jnp.bfloat16), 'kv').astype(jnp.float32)  61.6 us
    unnamed x3, waiting for transfers between devices  17.7 us
    all_to_all x1, waiting for transfers between devices, per_device(): lax.all_to_all(jnp.broadcast_to(attended[None], (blk_count,) + attended.s...  16.5 us
    all_to_all x1, waiting for transfers between devices, per_device(): lax.all_to_all(sent, 'blk', split_axis=0, concat_axis=0, tiled=True)  15.5 us
    all_to_all x1, waiting for transfers between devices, per_device(): lax.all_to_all(half_sum, 'blk', split_axis=0, concat_axis=0, tiled=True)  13.7 us
    psum x1, blocking collectives, per_device(): lax.psum((jnp.sum(resid_float * resid_float, axis=1), jnp.dot(scaled, rou...  10.5 us
    all_to_all x1, waiting for transfers between devices, per_device(): lax.all_to_all(column_part, 'blk', split_axis=0, concat_axis=1, tiled=True)  9.99 us
    dot_general x1, matrix products, per_device(): jnp.einsum('spkd,pdu->spku', rows_in, w_gate, preferred_element_type=jnp....  8.33 us
  transfers between devices with their start and end apart: 8, of which 7 were waited for; matrix products, arithmetic and copies ran while one was open for 11% of the time, Pallas kernels for 0%

profile of v3, /device:TPU:0, one launch (start us, length us, event | category | flops | bytes accessed | tf_op | source)
XLA Modules:
  0.0 260.8 jit_solution(300913456292242412)
XLA Ops:
  8.6 1.2 gather_fusion.2
  9.8 1.2 gather_fusion.4
  13.9 7.3 %all-to-all-start = ((bf16[8,16,2,128]{3,1,2,0:T(8,128)(2,1)}), bf16[8,16,2,128]{3,1,2,0:T(8,128)(2,1)S(1)}, u32[]{:S(2)}, u32[]{:S(2)}) async-start(bf16[8,16,2,128]{3,1,2,0:T(8,128)(2,1)} %gather_fusion.5), calls=%async_computation | async-start | bytes 131072 | tf_op jit(solution)/shard_map/all_to_all | solution.py:119
  28.7 1.6 while.16
  31.4 4.3 %all-to-all-start.1 = ((bf16[8,64,640]{2,1,0:T(8,128)(2,1)}), bf16[8,64,640]{2,1,0:T(8,128)(2,1)S(1)}, u32[]{:S(2)}, u32[]{:S(2)}) async-start(bf16[8,64,640]{2,1,0:T(8,128)(2,1)} %broadcast_in_dim.156), calls=%async_computation.1 | async-start | bytes 1310720 | tf_op jit(solution)/shard_map/all_to_all | solution.py:145
  35.9 16.5 %all-to-all-done.1 = bf16[8,64,640]{2,1,0:T(8,128)(2,1)S(1)} async-done(((bf16[8,64,640]{2,1,0:T(8,128)(2,1)}), bf16[8,64,640]{2,1,0:T(8,128)(2,1)S(1)}, u32[]{:S(2)}, u32[]{:S(2)}) %all-to-all-start.1) | async-done | bytes 655392 | tf_op jit(solution)/shard_map/all_to_all | solution.py:145
  53.8 3.6 %all-to-all-start.2 = ((bf16[8,64,320]{2,1,0:T(8,128)(2,1)}), bf16[8,64,320]{2,1,0:T(8,128)(2,1)S(1)}, u32[]{:S(2)}, u32[]{:S(2)}) async-start(bf16[8,64,320]{2,1,0:T(8,128)(2,1)} %bitcast.17), calls=%async_computation.2 | async-start | bytes 786432 | tf_op jit(solution)/shard_map/all_to_all | solution.py:151
  59.3 10.0 %all-to-all-done.2 = bf16[8,64,320]{2,1,0:T(8,128)(2,1)S(1)} async-done(((bf16[8,64,320]{2,1,0:T(8,128)(2,1)}), bf16[8,64,320]{2,1,0:T(8,128)(2,1)S(1)}, u32[]{:S(2)}, u32[]{:S(2)}) %all-to-all-start.2) | async-done | bytes 327712 | tf_op jit(solution)/shard_map/all_to_all | solution.py:151
  70.4 3.9 %scatter_custom_fusion = s32[512]{0:T(512)S(1)} fusion(s32[384]{0:T(512)S(1)} %get-tuple-element.185, s32[384]{0:T(512)S(1)} %iota_add_fusion, s32[]{:T(128)} %constant.153.clone.1), kind=kCustom, calls=%fused_computation.141 | custom fusion | flops 384 | bytes 2052 | tf_op jit(solution)/shard_map/scatter-add | solution.py:188
  74.4 17.6 %reduce-scatter.4.cloned.1.call-done = bf16[640,64]{1,0:T(8,128)(2,1)} async-done(((bf16[2560,64]{1,0:T(8,128)(2,1)}), bf16[640,64]{1,0:T(8,128)(2,1)}) %reduce-scatter.4.cloned.1.call-update) | async-done | bytes 81936
  93.6 10.5 %all-reduce = (f32[64]{0:T(128)S(1)}, f32[64,64]{1,0:T(8,128)S(1)}) all-reduce(f32[64]{0:T(128)S(1)} %get-tuple-element.206, f32[64,64]{1,0:T(8,128)S(1)} %fusion.33), channel_id=1, replica_groups=mesh['kv'=4,'blk'=8] {'kv'}, use_global_device_ids=true, to_apply=%region_17.18 | all-reduce | flops 4160 | bytes 33280 | tf_op jit(solution)/shard_map/psum | solution.py:158
  104.2 2.0 gather_fusion.7
  107.2 5.7 %all-to-all-start.3 = ((bf16[8,8,8,640]{3,2,1,0:T(8,128)(2,1)}), bf16[8,8,8,640]{3,2,1,0:T(8,128)(2,1)S(1)}, u32[]{:S(2)}, u32[]{:S(2)}) async-start(bf16[8,8,8,640]{3,2,1,0:T(8,128)(2,1)} %broadcast_select_fusion), calls=%async_computation.3 | async-start | bytes 1310720 | tf_op jit(solution)/shard_map/all_to_all | solution.py:200
  115.0 15.5 %all-to-all-done.3 = bf16[8,8,8,640]{3,2,1,0:T(8,128)(2,1)S(1)} async-done(((bf16[8,8,8,640]{3,2,1,0:T(8,128)(2,1)}), bf16[8,8,8,640]{3,2,1,0:T(8,128)(2,1)S(1)}, u32[]{:S(2)}, u32[]{:S(2)}) %all-to-all-start.3) | async-done | bytes 655392 | tf_op jit(solution)/shard_map/all_to_all | solution.py:200
  130.7 8.3 %fusion.26 = bf16[8,16,8,1,768]{4,2,0,1,3:T(8,128)(2,1)S(1)} fusion(bf16[8,16,8,640]{3,2,0,1:T(8,128)(2,1)S(1)} %bitcast.147, bf16[16,640,768]{2,1,0:T(8,128)(2,1)} %param.32), kind=kOutput, calls=%fused_computation.46 | convolution fusion | flops 1007419392 | bytes 18612224 | tf_op jit(solution)/shard_map/spkd,pdu->spku/dot_general | solution.py:212
  139.0 8.3 %fusion.29 = bf16[8,16,8,1,768]{4,2,0,1,3:T(8,128)(2,1)S(1)} fusion(bf16[8,16,8,640]{3,2,0,1:T(8,128)(2,1)S(1)} %bitcast.148, bf16[16,640,768]{2,1,0:T(8,128)(2,1)} %param.31), kind=kOutput, calls=%fused_computation.47 | convolution fusion | flops 1007419392 | bytes 18612224 | tf_op jit(solution)/shard_map/spkd,pdu->spku/dot_general | solution.py:211
  147.3 2.0 pad_maximum_fusion
  150.7 3.7 %all-to-all-start.5 = ((bf16[8,16,2,128]{3,1,2,0:T(8,128)(2,1)}), bf16[8,16,2,128]{3,1,2,0:T(8,128)(2,1)S(1)}, u32[]{:S(2)}, u32[]{:S(2)}) async-start(bf16[8,16,2,128]{3,1,2,0:T(8,128)(2,1)} %broadcast_select_fusion.1), calls=%async_computation.5 | async-start | bytes 131072 | tf_op jit(solution)/shard_map/all_to_all | solution.py:115
  154.5 61.6 %all-reduce.3.cloned.1.call-done = bf16[8,16,8,2,768]{4,2,0,1,3:T(8,128)(2,1)} async-done(((bf16[8,16,8,2,768]{4,2,0,1,3:T(8,128)(2,1)}), bf16[8,16,8,2,768]{4,2,0,1,3:T(8,128)(2,1)}) %all-reduce.3.cloned.1.call-update) | async-done | bytes 3145744 | tf_op jit(solution)/shard_map/psum | solution.py:214
  216.1 2.7 %convert_element_type.115 = f32[8,16,8,2,768]{4,2,0,1,3:T(8,128)S(1)} convert(bf16[8,16,8,2,768]{4,2,0,1,3:T(8,128)(2,1)} %all-reduce.3.cloned.1.call-done) | non-fusion elementwise | flops 1572864 | bytes 9437184 | tf_op jit(solution)/shard_map/convert_element_type | solution.py:214
  218.7 8.3 %bitcast_reduce_fusion = bf16[8,8,8,640]{3,2,0,1:T(8,128)(2,1)S(1)} fusion(bf16[16,768,640]{2,1,0:T(8,128)(2,1)} %param.33, f32[8,16,8,2,768]{4,2,0,1,3:T(8,128)S(1)} %convert_element_type.115), kind=kOutput, calls=%fused_computation.48 | convolution fusion | flops 1012334592 | bytes 22675456 | tf_op jit(solution)/shard_map/spku,pud->spkd/dot_general | solution.py:216
  228.0 5.5 %all-to-all-start.4 = ((bf16[8,8,8,640]{3,2,1,0:T(8,128)(2,1)}), bf16[8,8,8,640]{3,2,1,0:T(8,128)(2,1)S(1)}, u32[]{:S(2)}, u32[]{:S(2)}) async-start(bf16[8,8,8,640]{3,2,1,0:T(8,128)(2,1)} %copy.143), calls=%async_computation.4 | async-start | bytes 1310720 | tf_op jit(solution)/shard_map/all_to_all | solution.py:222
  237.0 13.7 %all-to-all-done.4 = bf16[8,8,8,640]{3,2,1,0:T(8,128)(2,1)S(1)} async-done(((bf16[8,8,8,640]{3,2,1,0:T(8,128)(2,1)}), bf16[8,8,8,640]{3,2,1,0:T(8,128)(2,1)S(1)}, u32[]{:S(2)}, u32[]{:S(2)}) %all-to-all-start.4) | async-done | bytes 655392 | tf_op jit(solution)/shard_map/all_to_all | solution.py:222
  250.8 1.9 gather_fusion.8
  (139 shorter events, 30.2 us)
Async XLA Ops:
  7.2 45.3 %copy-start = (bf16[640,320]{0,1:T(8,128)(2,1)S(1)}, bf16[640,320]{0,1:T(8,128)(2,1)}, u32[]{:S(2)}) copy-start(bf16[640,320]{0,1:T(8,128)(2,1)} %param.27) | copy-start | bytes 1228804
  13.9 14.2 %all-to-all-start = ((bf16[8,16,2,128]{3,1,2,0:T(8,128)(2,1)}), bf16[8,16,2,128]{3,1,2,0:T(8,128)(2,1)S(1)}, u32[]{:S(2)}, u32[]{:S(2)}) async-start(bf16[8,16,2,128]{3,1,2,0:T(8,128)(2,1)} %gather_fusion.5), calls=%async_computation | async-start | bytes 131072 | tf_op jit(solution)/shard_map/all_to_all | solution.py:119
  28.7 7.0 %copy-start.6 = (s32[64,6]{0,1:T(8,128)S(1)}, s32[64,6]{0,1:T(8,128)}, u32[]{:S(2)}) copy-start(s32[64,6]{0,1:T(8,128)} %param.30) | copy-start | bytes 4612
  30.3 27.4 %copy-start.9 = (bf16[640]{0:T(1024)(128)(2,1)S(1)}, bf16[640]{0:T(1024)(128)(2,1)}, u32[]{:S(2)}) copy-start(bf16[640]{0:T(1024)(128)(2,1)} %param.28) | copy-start | bytes 3844
  31.4 61.7 %copy-start.5 = (bf16[64,640]{1,0:T(8,128)(2,1)S(1)}, bf16[64,640]{1,0:T(8,128)(2,1)}, u32[]{:S(2)}) copy-start(bf16[64,640]{1,0:T(8,128)(2,1)} %param.18) | copy-start | bytes 245764
  31.4 21.1 %all-to-all-start.1 = ((bf16[8,64,640]{2,1,0:T(8,128)(2,1)}), bf16[8,64,640]{2,1,0:T(8,128)(2,1)S(1)}, u32[]{:S(2)}, u32[]{:S(2)}) async-start(bf16[8,64,640]{2,1,0:T(8,128)(2,1)} %broadcast_in_dim.156), calls=%async_computation.1 | async-start | bytes 1310720 | tf_op jit(solution)/shard_map/all_to_all | solution.py:145
  35.7 57.6 %copy-start.3 = (f32[640,64]{0,1:T(8,128)S(1)}, f32[640,64]{0,1:T(8,128)}, u32[]{:S(2)}) copy-start(f32[640,64]{0,1:T(8,128)} %param.29) | copy-start | bytes 491524
  53.8 15.4 %all-to-all-start.2 = ((bf16[8,64,320]{2,1,0:T(8,128)(2,1)}), bf16[8,64,320]{2,1,0:T(8,128)(2,1)S(1)}, u32[]{:S(2)}, u32[]{:S(2)}) async-start(bf16[8,64,320]{2,1,0:T(8,128)(2,1)} %bitcast.17), calls=%async_computation.2 | async-start | bytes 786432 | tf_op jit(solution)/shard_map/all_to_all | solution.py:151
  57.5 34.6 %reduce-scatter.4.cloned.1.call-start = ((), (), s32[]{:S(2)}) async-start(), calls=%async_computation.8 | async-start | bytes 819200
  104.2 8.8 %copy-start.2 = (s32[8,8]{1,0:T(8,128)S(1)}, s32[8,8]{1,0:T(8,128)}, u32[]{:S(2)}) copy-start(s32[8,8]{1,0:T(8,128)} %param.24) | copy-start | bytes 772
  104.2 8.9 %copy-start.4 = (bf16[64,1,2,128]{3,2,1,0:T(2,128)(2,1)S(1)}, bf16[64,1,2,128]{3,2,1,0:T(2,128)(2,1)}, u32[]{:S(2)}) copy-start(bf16[64,1,2,128]{3,2,1,0:T(2,128)(2,1)} %param.20) | copy-start | bytes 98308
  104.2 9.9 %copy-start.8 = (s32[8,12]{1,0:T(8,128)S(1)}, s32[8,12]{1,0:T(8,128)}, u32[]{:S(2)}) copy-start(s32[8,12]{1,0:T(8,128)} %param.25) | copy-start | bytes 1156
  107.2 23.2 %all-to-all-start.3 = ((bf16[8,8,8,640]{3,2,1,0:T(8,128)(2,1)}), bf16[8,8,8,640]{3,2,1,0:T(8,128)(2,1)S(1)}, u32[]{:S(2)}, u32[]{:S(2)}) async-start(bf16[8,8,8,640]{3,2,1,0:T(8,128)(2,1)} %broadcast_select_fusion), calls=%async_computation.3 | async-start | bytes 1310720 | tf_op jit(solution)/shard_map/all_to_all | solution.py:200
  112.9 103.2 %all-reduce.3.cloned.1.call-start = ((), (), s32[]{:S(2)}) async-start(), calls=%async_computation.7 | async-start | bytes 6291456 | tf_op jit(solution)/shard_map/psum | solution.py:214
  149.3 5.1 %copy-start.7 = (s32[8,12]{1,0:T(8,128)S(1)}, s32[8,12]{1,0:T(8,128)}, u32[]{:S(2)}) copy-start(s32[8,12]{1,0:T(8,128)} %param.26) | copy-start | bytes 1156
  150.7 77.3 %all-to-all-start.5 = ((bf16[8,16,2,128]{3,1,2,0:T(8,128)(2,1)}), bf16[8,16,2,128]{3,1,2,0:T(8,128)(2,1)S(1)}, u32[]{:S(2)}, u32[]{:S(2)}) async-start(bf16[8,16,2,128]{3,1,2,0:T(8,128)(2,1)} %broadcast_select_fusion.1), calls=%async_computation.5 | async-start | bytes 131072 | tf_op jit(solution)/shard_map/all_to_all | solution.py:115
  228.0 22.7 %all-to-all-start.4 = ((bf16[8,8,8,640]{3,2,1,0:T(8,128)(2,1)}), bf16[8,8,8,640]{3,2,1,0:T(8,128)(2,1)S(1)}, u32[]{:S(2)}, u32[]{:S(2)}) async-start(bf16[8,8,8,640]{3,2,1,0:T(8,128)(2,1)} %copy.143), calls=%async_computation.4 | async-start | bytes 1310720 | tf_op jit(solution)/shard_map/all_to_all | solution.py:222
  250.8 3.1 %copy-start.1 = (bf16[640,320]{0,1:T(8,128)(2,1)S(1)}, bf16[640,320]{0,1:T(8,128)(2,1)}, u32[]{:S(2)}) copy-start(bf16[640,320]{0,1:T(8,128)(2,1)} %param.27) | copy-start | bytes 1228804
Sparse Core Ops, SparseCore 0:
  70.5 21.5 reduce-scatter.3
  149.4 66.5 all-reduce.2

commit v4 on v3

--- a/solution.py
+++ b/solution.py
@@ -149,9 +149,28 @@
         every_token, out_weight, preferred_element_type=jnp.float32
     ).astype(jnp.bfloat16)
     projected = lax.all_to_all(column_part, "blk", split_axis=0, concat_axis=1, tiled=True)
-    head_total = lax.psum_scatter(
-        projected, "kv", scatter_dimension=1, tiled=True
-    ).astype(jnp.float32)
+    kv_index = lax.axis_index("kv")
+    if lax.axis_size("kv") == 4:
+        chip_bit = kv_index // 2
+        core_low = kv_index % 2
+        swap_core = [(i, i ^ 1) for i in range(4)]
+        swap_chip = [(i, i ^ 2) for i in range(4)]
+        chip_cols = projected.shape[1] // 2
+        chip_kept = lax.dynamic_slice_in_dim(projected, chip_bit * chip_cols, chip_cols, 1)
+        chip_given = lax.dynamic_slice_in_dim(projected, (1 - chip_bit) * chip_cols, chip_cols, 1)
+        chip_sum = chip_kept.astype(jnp.float32) + lax.ppermute(
+            chip_given, "kv", swap_chip
+        ).astype(jnp.float32)
+        own_cols = chip_cols // 2
+        core_kept = lax.dynamic_slice_in_dim(chip_sum, core_low * own_cols, own_cols, 1)
+        core_given = lax.dynamic_slice_in_dim(
+            chip_sum, (1 - core_low) * own_cols, own_cols, 1
+        ).astype(jnp.bfloat16)
+        head_total = core_kept + lax.ppermute(core_given, "kv", swap_core).astype(jnp.float32)
+    else:
+        head_total = lax.psum_scatter(
+            projected, "kv", scatter_dimension=1, tiled=True
+        ).astype(jnp.float32)
     residual = (hidden_in.astype(jnp.float32) + head_total).astype(jnp.bfloat16)
     resid_float = residual.astype(jnp.float32)
     scaled = resid_float * norm_gain.astype(jnp.float32)[None, :]
@@ -210,9 +229,24 @@
         rows_in = lax.all_to_all(doubled, "blk", split_axis=0, concat_axis=0, tiled=True)
     gate_part = jnp.einsum("spkd,pdu->spku", rows_in, w_gate, preferred_element_type=jnp.float32)
     up_part = jnp.einsum("spkd,pdu->spku", rows_in, w_up, preferred_element_type=jnp.float32)
-    both_parts = jnp.stack([gate_part, up_part], axis=3)
-    whole = lax.psum(both_parts.astype(jnp.bfloat16), "kv").astype(jnp.float32)
-    hidden = (jax.nn.silu(whole[:, :, :, 0]) * whole[:, :, :, 1]).astype(jnp.bfloat16)
+    both_parts = jnp.stack([gate_part, up_part], axis=3).astype(jnp.bfloat16)
+    kv_count = lax.axis_size("kv")
+    core_bit = lax.axis_index("kv") % 2
+    flip_core = [(i, i ^ 1) for i in range(kv_count)]
+    flip_chip = [(i, i ^ 2) for i in range(kv_count)]
+    half = both_parts.shape[0] // 2
+    kept = lax.dynamic_slice_in_dim(both_parts, core_bit * half, half, 0)
+    given = lax.dynamic_slice_in_dim(both_parts, (1 - core_bit) * half, half, 0)
+    pair_sum = kept.astype(jnp.float32) + lax.ppermute(given, "kv", flip_core).astype(jnp.float32)
+    pair_sum = pair_sum.astype(jnp.bfloat16)
+    whole = pair_sum.astype(jnp.float32) + lax.ppermute(pair_sum, "kv", flip_chip).astype(jnp.float32)
+    hidden_half = (jax.nn.silu(whole[:, :, :, 0]) * whole[:, :, :, 1]).astype(jnp.bfloat16)
+    hidden_other = lax.ppermute(hidden_half, "kv", flip_core)
+    hidden = jnp.where(
+        core_bit == 0,
+        jnp.concatenate([hidden_half, hidden_other], axis=0),
+        jnp.concatenate([hidden_other, hidden_half], axis=0),
+    )
     piece_out = jnp.einsum(
         "spku,pud->spkd", hidden, w_down, preferred_element_type=jnp.float32
     ).astype(jnp.bfloat16)

time: 262 us -> 212 us (0.81)
  waiting for transfers between devices: 136 us -> 94.4 us
  between operations: 15.2 us -> 2 us
  starting transfers between devices: 30.1 us -> 33.3 us
    psum x1 -> x0, waiting for transfers between devices: 61.6 us -> none  [per_device(): whole = lax.psum(both_parts.astype(jnp.bfloat16), 'kv').astype(jnp.float32)]
    ppermute x0 -> x5, waiting for transfers between devices: none -> 41.2 us  [the longest x1 32.5 us: per_device(): lax.ppermute(pair_sum, 'kv', flip_chip).astype(jnp.float32)]
    unnamed x3 -> x0, waiting for transfers between devices: 17.7 us -> none
    all_to_all x1, waiting for transfers between devices: 9.99 us -> 6.33 us  [per_device(): lax.all_to_all(column_part, 'blk', split_axis=0, concat_axis=1, tiled=True)]
    ppermute x0 -> x5, starting transfers between devices: none -> 3.44 us  [the longest x1 1.73 us: per_device(): lax.ppermute(pair_sum, 'kv', flip_chip).astype(jnp.float32)]
    add x0 -> x2, other arithmetic: none -> 2.68 us  [the longest x1 2.65 us: per_device(): pair_sum.astype(jnp.float32)]
  transfers between devices with their start and end apart: 8 -> 11, of which waited for: 7 -> 9; matrix products, arithmetic and copies ran while one was open for 11% -> 13% of each run, Pallas kernels for 0% -> 0%
where the time goes in v4:
time: 212 us
  waiting for transfers between devices  94.4 us (45%)
  starting transfers between devices  33.3 us (16%)
  matrix products  26.5 us (12%)
  other arithmetic  23.5 us (11%)
  local copies, waits for them, and re-layouts  20.4 us (10%)
  blocking collectives  11.7 us (6%)
    ppermute x1, waiting for transfers between devices, per_device(): lax.ppermute(pair_sum, 'kv', flip_chip).astype(jnp.float32)  32.5 us
    all_to_all x1, waiting for transfers between devices, per_device(): lax.all_to_all(sent, 'blk', split_axis=0, concat_axis=0, tiled=True)  16.4 us
    all_to_all x1, waiting for transfers between devices, per_device(): lax.all_to_all(jnp.broadcast_to(attended[None], (blk_count,) + attended.s...  15.6 us
    all_to_all x1, waiting for transfers between devices, per_device(): lax.all_to_all(half_sum, 'blk', split_axis=0, concat_axis=0, tiled=True)  13.9 us
    psum x1, blocking collectives, per_device(): lax.psum((jnp.sum(resid_float * resid_float, axis=1), jnp.dot(scaled, rou...  11.7 us
    dot_general x1, matrix products, per_device(): jnp.einsum('spkd,pdu->spku', rows_in, w_gate, preferred_element_type=jnp....  8.3 us
    dot_general x1, matrix products, per_device(): jnp.einsum('spkd,pdu->spku', rows_in, w_up, preferred_element_type=jnp.fl...  8.3 us
    dot_general x1, matrix products, per_device(): jnp.einsum('spku,pud->spkd', hidden, w_down, preferred_element_type=jnp.f...  8.07 us
  transfers between devices with their start and end apart: 11, of which 9 were waited for; matrix products, arithmetic and copies ran while one was open for 13% of the time, Pallas kernels for 0%

profile of v4, /device:TPU:0, one launch (start us, length us, event | category | flops | bytes accessed | tf_op | source)
XLA Modules:
  0.0 211.9 jit_solution(12792886233527939173)
XLA Ops:
  7.0 7.3 %all-to-all-start = ((bf16[8,16,2,128]{3,1,2,0:T(8,128)(2,1)}), bf16[8,16,2,128]{3,1,2,0:T(8,128)(2,1)S(1)}, u32[]{:S(2)}, u32[]{:S(2)}) async-start(bf16[8,16,2,128]{3,1,2,0:T(8,128)(2,1)} %gather_fusion.5), calls=%async_computation | async-start | bytes 131072 | tf_op jit(solution)/shard_map/all_to_all | solution.py:119
  24.5 5.1 %all-to-all-start.1 = ((bf16[8,64,640]{2,1,0:T(8,128)(2,1)}), bf16[8,64,640]{2,1,0:T(8,128)(2,1)S(1)}, u32[]{:S(2)}, u32[]{:S(2)}) async-start(bf16[8,64,640]{2,1,0:T(8,128)(2,1)} %broadcast_in_dim.156), calls=%async_computation.1 | async-start | bytes 1310720 | tf_op jit(solution)/shard_map/all_to_all | solution.py:145
  30.7 15.6 %all-to-all-done.1 = bf16[8,64,640]{2,1,0:T(8,128)(2,1)S(1)} async-done(((bf16[8,64,640]{2,1,0:T(8,128)(2,1)}), bf16[8,64,640]{2,1,0:T(8,128)(2,1)S(1)}, u32[]{:S(2)}, u32[]{:S(2)}) %all-to-all-start.1) | async-done | bytes 655392 | tf_op jit(solution)/shard_map/all_to_all | solution.py:145
  47.7 3.6 %all-to-all-start.2 = ((bf16[8,64,320]{2,1,0:T(8,128)(2,1)}), bf16[8,64,320]{2,1,0:T(8,128)(2,1)S(1)}, u32[]{:S(2)}, u32[]{:S(2)}) async-start(bf16[8,64,320]{2,1,0:T(8,128)(2,1)} %bitcast.17), calls=%async_computation.2 | async-start | bytes 786432 | tf_op jit(solution)/shard_map/all_to_all | solution.py:151
  52.7 3.9 %scatter_custom_fusion = s32[512]{0:T(512)S(1)} fusion(s32[384]{0:T(512)S(1)} %get-tuple-element.175, s32[384]{0:T(512)S(1)} %iota_add_fusion, s32[]{:T(128)} %constant.180.clone.1), kind=kCustom, calls=%fused_computation.157 | custom fusion | flops 384 | bytes 2052 | tf_op jit(solution)/shard_map/scatter-add | solution.py:207
  56.7 6.3 %all-to-all-done.2 = bf16[8,64,320]{2,1,0:T(8,128)(2,1)S(1)} async-done(((bf16[8,64,320]{2,1,0:T(8,128)(2,1)}), bf16[8,64,320]{2,1,0:T(8,128)(2,1)S(1)}, u32[]{:S(2)}, u32[]{:S(2)}) %all-to-all-start.2) | async-done | bytes 327712 | tf_op jit(solution)/shard_map/all_to_all | solution.py:151
  63.6 1.6 collective-permute-start
  65.2 3.8 %collective-permute-done = bf16[64,1280]{1,0:T(8,128)(2,1)S(1)} collective-permute-done((bf16[64,1280]{1,0:T(8,128)(2,1)S(1)}, bf16[64,1280]{1,0:T(8,128)(2,1)S(1)}, u32[]{:S(2)}, u32[]{:S(2)}) %collective-permute-start) | collective-permute-done | bytes 163872 | tf_op jit(solution)/shard_map/ppermute | solution.py:161
  70.9 11.7 %all-reduce = (f32[64]{0:T(128)S(1)}, f32[64,64]{1,0:T(8,128)S(1)}) all-reduce(f32[64]{0:T(128)S(1)} %get-tuple-element.196, f32[64,64]{1,0:T(8,128)S(1)} %fusion.39), channel_id=1, replica_groups=mesh['kv'=4,'blk'=8] {'kv'}, use_global_device_ids=true, to_apply=%region_16.17 | all-reduce | flops 4160 | bytes 33280 | tf_op jit(solution)/shard_map/psum | solution.py:177
  82.7 2.0 gather_fusion.7
  85.7 4.3 %all-to-all-start.3 = ((bf16[8,8,8,640]{3,2,1,0:T(8,128)(2,1)}), bf16[8,8,8,640]{3,2,1,0:T(8,128)(2,1)S(1)}, u32[]{:S(2)}, u32[]{:S(2)}) async-start(bf16[8,8,8,640]{3,2,1,0:T(8,128)(2,1)} %broadcast_select_fusion), calls=%async_computation.3 | async-start | bytes 1310720 | tf_op jit(solution)/shard_map/all_to_all | solution.py:219
  90.0 16.4 %all-to-all-done.3 = bf16[8,8,8,640]{3,2,1,0:T(8,128)(2,1)S(1)} async-done(((bf16[8,8,8,640]{3,2,1,0:T(8,128)(2,1)}), bf16[8,8,8,640]{3,2,1,0:T(8,128)(2,1)S(1)}, u32[]{:S(2)}, u32[]{:S(2)}) %all-to-all-start.3) | async-done | bytes 655392 | tf_op jit(solution)/shard_map/all_to_all | solution.py:219
  106.6 8.3 %fusion.32 = bf16[8,16,8,1,768]{4,2,0,1,3:T(8,128)(2,1)S(1)} fusion(bf16[8,16,8,640]{3,2,0,1:T(8,128)(2,1)S(1)} %bitcast.137, bf16[16,640,768]{2,1,0:T(8,128)(2,1)} %param.32), kind=kOutput, calls=%fused_computation.59 | convolution fusion | flops 1007419392 | bytes 18612224 | tf_op jit(solution)/shard_map/spkd,pdu->spku/dot_general | solution.py:231
  114.9 8.3 %fusion.35 = bf16[8,16,8,1,768]{4,2,0,1,3:T(8,128)(2,1)S(1)} fusion(bf16[8,16,8,640]{3,2,0,1:T(8,128)(2,1)S(1)} %bitcast.138, bf16[16,640,768]{2,1,0:T(8,128)(2,1)} %param.31), kind=kOutput, calls=%fused_computation.60 | convolution fusion | flops 1007419392 | bytes 18612224 | tf_op jit(solution)/shard_map/spkd,pdu->spku/dot_general | solution.py:230
  124.6 3.7 %collective-permute-done.2 = bf16[4,16,8,2,768]{4,2,0,1,3:T(8,128)(2,1)} collective-permute-done((bf16[4,16,8,2,768]{4,2,0,1,3:T(8,128)(2,1)}, bf16[4,16,8,2,768]{4,2,0,1,3:T(8,128)(2,1)}, u32[]{:S(2)}, u32[]{:S(2)}) %collective-permute-start.2) | collective-permute-done | bytes 1572896 | tf_op jit(solution)/shard_map/ppermute | solution.py:240
  128.3 3.1 %add_convert_fusion = bf16[4,16,8,2,768]{4,2,0,1,3:T(8,128)(2,1)} fusion(bf16[4,16,8,2,768]{4,2,0,1,3:T(8,128)(2,1)} %collective-permute-done.2, s32[]{:T(128)S(6)} %select_n.179, bf16[8,16,8,1,768]{4,2,0,1,3:T(8,128)(2,1)S(1)} %fusion.35, bf16[8,16,8,1,768]{4,2,0,1,3:T(8,128)(2,1)S(1)} %fusion.32), kind=kLoop, calls=%fused_computation.42 | loop fusion | flops 3932160 | bytes 6291460 | tf_op jit(solution)/shard_map/convert_element_type | solution.py:241
  131.4 1.7 collective-permute-start.3
  135.7 32.5 %collective-permute-done.3 = bf16[4,16,8,2,768]{4,2,0,1,3:T(8,128)(2,1)} collective-permute-done((bf16[4,16,8,2,768]{4,2,0,1,3:T(8,128)(2,1)}, bf16[4,16,8,2,768]{4,2,0,1,3:T(8,128)(2,1)}, u32[]{:S(2)}, u32[]{:S(2)}) %collective-permute-start.3) | collective-permute-done | bytes 1572896 | tf_op jit(solution)/shard_map/ppermute | solution.py:242
  168.1 2.6 %convert_add_fusion = f32[4,16,8,2,768]{4,2,0,1,3:T(8,128)S(1)} fusion(bf16[4,16,8,2,768]{4,2,0,1,3:T(8,128)(2,1)} %collective-permute-done.3, bf16[4,16,8,2,768]{4,2,0,1,3:T(8,128)(2,1)} %collective-permute-done.2, s32[]{:T(128)S(6)} %select_n.179, bf16[8,16,8,1,768]{4,2,0,1,3:T(8,128)(2,1)S(1)} %fusion.32, bf16[8,16,8,1,768]{4,2,0,1,3:T(8,128)(2,1)S(1)} %fusion.35), kind=kLoop, calls=%fused_computation.41 | loop fusion | flops 6291456 | bytes 9437188 | tf_op jit(solution)/shard_map/add | solution.py:242
  172.1 3.6 %all-to-all-start.5 = ((bf16[8,16,2,128]{3,1,2,0:T(8,128)(2,1)}), bf16[8,16,2,128]{3,1,2,0:T(8,128)(2,1)S(1)}, u32[]{:S(2)}, u32[]{:S(2)}) async-start(bf16[8,16,2,128]{3,1,2,0:T(8,128)(2,1)} %broadcast_select_fusion.1), calls=%async_computation.5 | async-start | bytes 131072 | tf_op jit(solution)/shard_map/all_to_all | solution.py:115
  175.9 8.1 %bitcast_reduce_fusion = bf16[8,8,8,640]{3,2,0,1:T(8,128)(2,1)S(1)} fusion(bf16[16,768,640]{2,1,0:T(8,128)(2,1)} %param.33, bf16[4,16,8,768]{3,2,0,1:T(8,128)(2,1)S(1)} %collective-permute-done.4, bf16[4,16,8,768]{3,2,0,1:T(8,128)(2,1)S(1)} %fusion.25, pred[]{:T(512)S(6)} %eq.107), kind=kOutput, calls=%fused_computation.61 | convolution fusion | flops 1009975296 | bytes 17956864 | tf_op jit(solution)/shard_map/spku,pud->spkd/dot_general | solution.py:250
  184.9 6.0 %all-to-all-start.4 = ((bf16[8,8,8,640]{3,2,1,0:T(8,128)(2,1)}), bf16[8,8,8,640]{3,2,1,0:T(8,128)(2,1)S(1)}, u32[]{:S(2)}, u32[]{:S(2)}) async-start(bf16[8,8,8,640]{3,2,1,0:T(8,128)(2,1)} %copy.126), calls=%async_computation.4 | async-start | bytes 1310720 | tf_op jit(solution)/shard_map/all_to_all | solution.py:256
  194.4 13.9 %all-to-all-done.4 = bf16[8,8,8,640]{3,2,1,0:T(8,128)(2,1)S(1)} async-done(((bf16[8,8,8,640]{3,2,1,0:T(8,128)(2,1)}), bf16[8,8,8,640]{3,2,1,0:T(8,128)(2,1)S(1)}, u32[]{:S(2)}, u32[]{:S(2)}) %all-to-all-start.4) | async-done | bytes 655392 | tf_op jit(solution)/shard_map/all_to_all | solution.py:256
  208.4 1.9 gather_fusion.8
  (167 shorter events, 36.1 us)
Async XLA Ops:
  0.6 45.7 %copy-start = (bf16[640,320]{0,1:T(8,128)(2,1)S(1)}, bf16[640,320]{0,1:T(8,128)(2,1)}, u32[]{:S(2)}) copy-start(bf16[640,320]{0,1:T(8,128)(2,1)} %param.27) | copy-start | bytes 1228804
  5.8 12.8 %copy-start.5 = (bf16[4,16,1,2,128]{4,1,3,0,2:T(8,128)(2,1)}, bf16[4,16,1,2,128]{4,1,3,0,2:T(8,128)(2,1)S(1)}, u32[]{:S(2)}) copy-start(bf16[4,16,1,2,128]{4,1,3,0,2:T(8,128)(2,1)S(1)} %copy.144) | copy-start | bytes 98308
  7.0 14.2 %all-to-all-start = ((bf16[8,16,2,128]{3,1,2,0:T(8,128)(2,1)}), bf16[8,16,2,128]{3,1,2,0:T(8,128)(2,1)S(1)}, u32[]{:S(2)}, u32[]{:S(2)}) async-start(bf16[8,16,2,128]{3,1,2,0:T(8,128)(2,1)} %gather_fusion.5), calls=%async_computation | async-start | bytes 131072 | tf_op jit(solution)/shard_map/all_to_all | solution.py:119
  24.5 21.8 %all-to-all-start.1 = ((bf16[8,64,640]{2,1,0:T(8,128)(2,1)}), bf16[8,64,640]{2,1,0:T(8,128)(2,1)S(1)}, u32[]{:S(2)}, u32[]{:S(2)}) async-start(bf16[8,64,640]{2,1,0:T(8,128)(2,1)} %broadcast_in_dim.156), calls=%async_computation.1 | async-start | bytes 1310720 | tf_op jit(solution)/shard_map/all_to_all | solution.py:145
  30.7 21.0 %copy-start.16 = (bf16[640]{0:T(1024)(128)(2,1)S(1)}, bf16[640]{0:T(1024)(128)(2,1)}, u32[]{:S(2)}) copy-start(bf16[640]{0:T(1024)(128)(2,1)} %param.28) | copy-start | bytes 3844
  47.7 15.4 %all-to-all-start.2 = ((bf16[8,64,320]{2,1,0:T(8,128)(2,1)}), bf16[8,64,320]{2,1,0:T(8,128)(2,1)S(1)}, u32[]{:S(2)}, u32[]{:S(2)}) async-start(bf16[8,64,320]{2,1,0:T(8,128)(2,1)} %bitcast.17), calls=%async_computation.2 | async-start | bytes 786432 | tf_op jit(solution)/shard_map/all_to_all | solution.py:151
  51.3 19.1 %copy-start.10 = (bf16[64,640]{1,0:T(8,128)(2,1)S(1)}, bf16[64,640]{1,0:T(8,128)(2,1)}, u32[]{:S(2)}) copy-start(bf16[64,640]{1,0:T(8,128)(2,1)} %param.18) | copy-start | bytes 245764
  52.1 18.5 %copy-start.8 = (f32[640,64]{0,1:T(8,128)S(1)}, f32[640,64]{0,1:T(8,128)}, u32[]{:S(2)}) copy-start(f32[640,64]{0,1:T(8,128)} %param.29) | copy-start | bytes 491524
  63.6 5.4 %collective-permute-start = (bf16[64,1280]{1,0:T(8,128)(2,1)S(1)}, bf16[64,1280]{1,0:T(8,128)(2,1)S(1)}, u32[]{:S(2)}, u32[]{:S(2)}) collective-permute-start(bf16[64,1280]{1,0:T(8,128)(2,1)S(1)} %constant_dynamic-slice_fusion), channel_id=1, source_target_pairs={{0,16},{8,24},{16,0},{24,8},{1,17},{9,25},{17,1},{25,9},{2,18},{10... | collective-permute-start | bytes 491528 | tf_op jit(solution)/shard_map/ppermute | solution.py:161
  69.1 1.3 collective-permute-start.1
  70.6 14.1 %copy-start.2 = (bf16[64,640]{1,0:T(8,128)(2,1)}, bf16[64,640]{1,0:T(8,128)(2,1)S(1)}, u32[]{:S(2)}) copy-start(bf16[64,640]{1,0:T(8,128)(2,1)S(1)} %get-tuple-element.197) | copy-start | bytes 245764
  85.7 20.7 %all-to-all-start.3 = ((bf16[8,8,8,640]{3,2,1,0:T(8,128)(2,1)}), bf16[8,8,8,640]{3,2,1,0:T(8,128)(2,1)S(1)}, u32[]{:S(2)}, u32[]{:S(2)}) async-start(bf16[8,8,8,640]{3,2,1,0:T(8,128)(2,1)} %broadcast_select_fusion), calls=%async_computation.3 | async-start | bytes 1310720 | tf_op jit(solution)/shard_map/all_to_all | solution.py:219
  124.5 3.8 %collective-permute-start.2 = (bf16[4,16,8,2,768]{4,2,0,1,3:T(8,128)(2,1)}, bf16[4,16,8,2,768]{4,2,0,1,3:T(8,128)(2,1)}, u32[]{:S(2)}, u32[]{:S(2)}) collective-permute-start(bf16[4,16,8,2,768]{4,2,0,1,3:T(8,128)(2,1)} %fusion.22), channel_id=1, source_target_pairs={{0,8},{8,0},{16,24},{24,16},{1,9},{9,1},{17,25},{25,17},{2,10},{10... | collective-permute-start | bytes 4718600 | tf_op jit(solution)/shard_map/ppermute | solution.py:240
  124.5 8.6 %copy-start.4 = (s32[8,8]{1,0:T(8,128)S(1)}, s32[8,8]{1,0:T(8,128)}, u32[]{:S(2)}) copy-start(s32[8,8]{1,0:T(8,128)} %param.23) | copy-start | bytes 772
  124.5 8.6 %copy-start.13 = (s32[8,12]{1,0:T(8,128)S(1)}, s32[8,12]{1,0:T(8,128)}, u32[]{:S(2)}) copy-start(s32[8,12]{1,0:T(8,128)} %param.25) | copy-start | bytes 1156
  124.5 8.6 %copy-start.18 = (s32[8]{0:T(128)S(1)}, s32[8]{0:T(128)}, u32[]{:S(2)}) copy-start(s32[8]{0:T(128)} %copy-done.17) | copy-start | bytes 100
  124.5 8.7 %copy-start.7 = (s32[8,8]{1,0:T(8,128)S(1)}, s32[8,8]{1,0:T(8,128)}, u32[]{:S(2)}) copy-start(s32[8,8]{1,0:T(8,128)} %param.24) | copy-start | bytes 772
  124.5 8.8 %copy-start.9 = (bf16[64,1,2,128]{3,2,1,0:T(2,128)(2,1)S(1)}, bf16[64,1,2,128]{3,2,1,0:T(2,128)(2,1)}, u32[]{:S(2)}) copy-start(bf16[64,1,2,128]{3,2,1,0:T(2,128)(2,1)} %param.20) | copy-start | bytes 98308
  124.6 10.5 %copy-start.6 = (bf16[4,16,1,2,128]{4,1,3,0,2:T(8,128)(2,1)S(1)}, bf16[4,16,1,2,128]{4,1,3,0,2:T(8,128)(2,1)}, u32[]{:S(2)}) copy-start(bf16[4,16,1,2,128]{4,1,3,0,2:T(8,128)(2,1)} %copy-done.5) | copy-start | bytes 98308
  131.4 36.8 %collective-permute-start.3 = (bf16[4,16,8,2,768]{4,2,0,1,3:T(8,128)(2,1)}, bf16[4,16,8,2,768]{4,2,0,1,3:T(8,128)(2,1)}, u32[]{:S(2)}, u32[]{:S(2)}) collective-permute-start(bf16[4,16,8,2,768]{4,2,0,1,3:T(8,128)(2,1)} %add_convert_fusion), channel_id=1, source_target_pairs={{0,16},{8,24},{16,0},{24,8},{1,17},{9,25},{17,1},{25,9},{2,18},{10... | collective-permute-start | bytes 4718600 | tf_op jit(solution)/shard_map/ppermute | solution.py:242
  171.3 4.6 %collective-permute-start.4 = (bf16[4,16,8,768]{3,2,0,1:T(8,128)(2,1)S(1)}, bf16[4,16,8,768]{3,2,0,1:T(8,128)(2,1)S(1)}, u32[]{:S(2)}, u32[]{:S(2)}) collective-permute-start(bf16[4,16,8,768]{3,2,0,1:T(8,128)(2,1)S(1)} %fusion.25), channel_id=1, source_target_pairs={{0,8},{8,0},{16,24},{24,16},{1,9},{9,1},{17,25},{25,17},{2,10},{10... | collective-permute-start | bytes 2359304 | tf_op jit(solution)/shard_map/ppermute | solution.py:244
  172.1 12.8 %all-to-all-start.5 = ((bf16[8,16,2,128]{3,1,2,0:T(8,128)(2,1)}), bf16[8,16,2,128]{3,1,2,0:T(8,128)(2,1)S(1)}, u32[]{:S(2)}, u32[]{:S(2)}) async-start(bf16[8,16,2,128]{3,1,2,0:T(8,128)(2,1)} %broadcast_select_fusion.1), calls=%async_computation.5 | async-start | bytes 131072 | tf_op jit(solution)/shard_map/all_to_all | solution.py:115
  184.0 10.0 %copy-start.12 = (s32[64,6]{0,1:T(8,128)S(1)}, s32[64,6]{0,1:T(8,128)}, u32[]{:S(2)}) copy-start(s32[64,6]{0,1:T(8,128)} %param.30) | copy-start | bytes 4612
  184.9 23.4 %all-to-all-start.4 = ((bf16[8,8,8,640]{3,2,1,0:T(8,128)(2,1)}), bf16[8,8,8,640]{3,2,1,0:T(8,128)(2,1)S(1)}, u32[]{:S(2)}, u32[]{:S(2)}) async-start(bf16[8,8,8,640]{3,2,1,0:T(8,128)(2,1)} %copy.126), calls=%async_computation.4 | async-start | bytes 1310720 | tf_op jit(solution)/shard_map/all_to_all | solution.py:256
  (6 other events, 22.9 us)

commit v5 on v4

--- a/solution.py
+++ b/solution.py
@@ -112,11 +112,14 @@
         sources[jnp.maximum(picked - 1, 0)],
         jnp.zeros((), jnp.bfloat16),
     )
-    landed = lax.all_to_all(sending, "blk", split_axis=0, concat_axis=0, tiled=True)
     source_request = jnp.zeros_like(devices) + own_index
     match_here = (block_holder[devices] == own_index) & in_use[devices]
     outgoing = pool_rows[jnp.sum(jnp.where(match_here, block_slot[devices], 0), axis=1)]
-    arrived = lax.all_to_all(outgoing, "blk", split_axis=0, concat_axis=0, tiled=True)
+    both_blocks = lax.all_to_all(
+        jnp.stack([sending, outgoing], axis=1), "blk", split_axis=0, concat_axis=0, tiled=True
+    )
+    landed = both_blocks[:, 0]
+    arrived = both_blocks[:, 1]
     present = jnp.any(
         (block_holder[source_request] == devices[:, None]) & in_use[source_request], axis=1
     )
@@ -174,13 +177,20 @@
     residual = (hidden_in.astype(jnp.float32) + head_total).astype(jnp.bfloat16)
     resid_float = residual.astype(jnp.float32)
     scaled = resid_float * norm_gain.astype(jnp.float32)[None, :]
-    square_sum, raw_logits = lax.psum(
-        (
-            jnp.sum(resid_float * resid_float, axis=1),
+    stats = jnp.concatenate(
+        [
+            jnp.sum(resid_float * resid_float, axis=1, keepdims=True),
             jnp.dot(scaled, router_weight, precision=lax.Precision.HIGHEST),
-        ),
-        "kv",
-    )
+        ],
+        axis=1,
+    )
+    if lax.axis_size("kv") == 4:
+        stats = stats + lax.ppermute(stats, "kv", [(i, i ^ 1) for i in range(4)])
+        stats = stats + lax.ppermute(stats, "kv", [(i, i ^ 2) for i in range(4)])
+    else:
+        stats = lax.psum(stats, "kv")
+    square_sum = stats[:, 0]
+    raw_logits = stats[:, 1:]
     inverse = lax.rsqrt(square_sum / D + EPSILON)
     logits = raw_logits * inverse[:, None]
     normed = (scaled * inverse[:, None]).astype(jnp.bfloat16)

time: 212 us -> 206 us (0.972)
  waiting for transfers between devices: 94.4 us -> 108 us
  blocking collectives: 11.7 us -> 0 us
  starting transfers between devices: 33.3 us -> 26.2 us
    psum x1 -> x0, blocking collectives: 11.7 us -> none  [per_device(): lax.psum((jnp.sum(resid_float * resid_float, axis=1), jnp.dot(scaled, rou...]
    all_to_all x2 -> x1, waiting for transfers between devices: 0.95 us -> 5.76 us  [per_device(): lax.all_to_all(jnp.stack([sending, outgoing], axis=1), 'blk', split_axis=...]
    ppermute x1, waiting for transfers between devices: 3.8 us -> 0.01 us  [per_device(): lax.ppermute(chip_given, 'kv', swap_chip).astype(jnp.float32)]
    ppermute x0 -> x2, waiting for transfers between devices: none -> 3.72 us  [the longest x1 2.67 us: per_device(): stats = stats + lax.ppermute(stats, 'kv', [(i, i ^ 2) for i in range(4)])]
    all_to_all x2 -> x1, starting transfers between devices: 10.9 us -> 7.28 us  [per_device(): lax.all_to_all(jnp.stack([sending, outgoing], axis=1), 'blk', split_axis=...]
    all_to_all x1, waiting for transfers between devices: 6.33 us -> 9.85 us  [per_device(): lax.all_to_all(column_part, 'blk', split_axis=0, concat_axis=1, tiled=True)]
    ppermute x1, waiting for transfers between devices: 32.5 us -> 35.3 us  [per_device(): lax.ppermute(pair_sum, 'kv', flip_chip).astype(jnp.float32)]
    all_to_all x1, starting transfers between devices: 6.01 us -> 3.61 us  [per_device(): lax.all_to_all(half_sum, 'blk', split_axis=0, concat_axis=0, tiled=True)]
  transfers between devices with their start and end apart: 11 -> 12, of which waited for: 9 -> 11; matrix products, arithmetic and copies ran while one was open for 13% -> 5% of each run, Pallas kernels for 0% -> 0%
where the time goes in v5:
time: 206 us; the launch traced here: 205 us
  waiting for transfers between devices  108 us (52%)
  starting transfers between devices  26.2 us (13%)
  matrix products  26 us (13%)
  other arithmetic  21.9 us (11%)
  local copies, waits for them, and re-layouts  20.6 us (10%)
    ppermute x1, waiting for transfers between devices, per_device(): lax.ppermute(pair_sum, 'kv', flip_chip).astype(jnp.float32)  35.3 us
    all_to_all x1, waiting for transfers between devices, per_device(): lax.all_to_all(sent, 'blk', split_axis=0, concat_axis=0, tiled=True)  16.5 us
    all_to_all x1, waiting for transfers between devices, per_device(): lax.all_to_all(jnp.broadcast_to(attended[None], (blk_count,) + attended.s...  15.8 us
    all_to_all x1, waiting for transfers between devices, per_device(): lax.all_to_all(half_sum, 'blk', split_axis=0, concat_axis=0, tiled=True)  14.2 us
    all_to_all x1, waiting for transfers between devices, per_device(): lax.all_to_all(column_part, 'blk', split_axis=0, concat_axis=1, tiled=True)  9.85 us
    dot_general x1, matrix products, per_device(): jnp.einsum('spkd,pdu->spku', rows_in, w_gate, preferred_element_type=jnp....  8.3 us
    dot_general x1, matrix products, per_device(): jnp.einsum('spkd,pdu->spku', rows_in, w_up, preferred_element_type=jnp.fl...  8.3 us
    dot_general x1, matrix products, per_device(): jnp.einsum('spku,pud->spkd', hidden, w_down, preferred_element_type=jnp.f...  8.07 us
  transfers between devices with their start and end apart: 12, of which 11 were waited for; matrix products, arithmetic and copies ran while one was open for 5% of the time, Pallas kernels for 0%

profile of v5, /device:TPU:0, one launch (start us, length us, event | category | flops | bytes accessed | tf_op | source)
XLA Modules:
  0.0 204.8 jit_solution(18388819698261509326)
XLA Ops:
  7.8 1.4 and_select_fusion.1
  15.3 7.3 %all-to-all-start = ((bf16[8,2,16,2,128]{4,2,3,1,0:T(8,128)(2,1)}), bf16[8,2,16,2,128]{4,2,3,1,0:T(8,128)(2,1)S(1)}, u32[]{:S(2)}, u32[]{:S(2)}) async-start(bf16[8,2,16,2,128]{4,2,3,1,0:T(8,128)(2,1)} %copy.131), calls=%async_computation | async-start | bytes 262144 | tf_op jit(solution)/shard_map/all_to_all | solution.py:118
  24.1 5.8 %all-to-all-done = bf16[8,2,16,2,128]{4,2,3,1,0:T(8,128)(2,1)S(1)} async-done(((bf16[8,2,16,2,128]{4,2,3,1,0:T(8,128)(2,1)}), bf16[8,2,16,2,128]{4,2,3,1,0:T(8,128)(2,1)S(1)}, u32[]{:S(2)}, u32[]{:S(2)}) %all-to-all-start) | async-done | bytes 131104 | tf_op jit(solution)/shard_map/all_to_all | solution.py:118
  32.3 3.8 %all-to-all-start.1 = ((bf16[8,64,640]{2,1,0:T(8,128)(2,1)}), bf16[8,64,640]{2,1,0:T(8,128)(2,1)S(1)}, u32[]{:S(2)}, u32[]{:S(2)}) async-start(bf16[8,64,640]{2,1,0:T(8,128)(2,1)} %broadcast_in_dim.163), calls=%async_computation.1 | async-start | bytes 1310720 | tf_op jit(solution)/shard_map/all_to_all | solution.py:148
  36.4 15.8 %all-to-all-done.1 = bf16[8,64,640]{2,1,0:T(8,128)(2,1)S(1)} async-done(((bf16[8,64,640]{2,1,0:T(8,128)(2,1)}), bf16[8,64,640]{2,1,0:T(8,128)(2,1)S(1)}, u32[]{:S(2)}, u32[]{:S(2)}) %all-to-all-start.1) | async-done | bytes 655392 | tf_op jit(solution)/shard_map/all_to_all | solution.py:148
  53.6 3.6 %all-to-all-start.2 = ((bf16[8,64,320]{2,1,0:T(8,128)(2,1)}), bf16[8,64,320]{2,1,0:T(8,128)(2,1)S(1)}, u32[]{:S(2)}, u32[]{:S(2)}) async-start(bf16[8,64,320]{2,1,0:T(8,128)(2,1)} %bitcast.22), calls=%async_computation.2 | async-start | bytes 786432 | tf_op jit(solution)/shard_map/all_to_all | solution.py:154
  58.6 9.8 %all-to-all-done.2 = bf16[8,64,320]{2,1,0:T(8,128)(2,1)S(1)} async-done(((bf16[8,64,320]{2,1,0:T(8,128)(2,1)}), bf16[8,64,320]{2,1,0:T(8,128)(2,1)S(1)}, u32[]{:S(2)}, u32[]{:S(2)}) %all-to-all-start.2) | async-done | bytes 327712 | tf_op jit(solution)/shard_map/all_to_all | solution.py:154
  69.0 1.5 collective-permute-start
  70.8 3.9 %scatter_custom_fusion.2 = s32[512]{0:T(512)S(1)} fusion(s32[384]{0:T(512)S(1)} %get-tuple-element.175, s32[384]{0:T(512)S(1)} %iota_add_fusion, s32[]{:T(128)} %constant.180.clone.1), kind=kCustom, calls=%fused_computation.164 | custom fusion | flops 384 | bytes 2052 | tf_op jit(solution)/shard_map/scatter-add | solution.py:217
  79.3 2.7 %collective-permute-done.3 = f32[64,65]{1,0:T(8,128)S(1)} collective-permute-done((f32[64,65]{1,0:T(8,128)S(1)}, f32[64,65]{1,0:T(8,128)S(1)}, u32[]{:S(2)}, u32[]{:S(2)}) %collective-permute-start.3) | collective-permute-done | bytes 16672 | tf_op jit(solution)/shard_map/ppermute | solution.py:189
  82.2 2.0 gather_fusion.8
  85.2 3.7 %all-to-all-start.3 = ((bf16[8,8,8,640]{3,2,1,0:T(8,128)(2,1)}), bf16[8,8,8,640]{3,2,1,0:T(8,128)(2,1)S(1)}, u32[]{:S(2)}, u32[]{:S(2)}) async-start(bf16[8,8,8,640]{3,2,1,0:T(8,128)(2,1)} %broadcast_select_fusion), calls=%async_computation.3 | async-start | bytes 1310720 | tf_op jit(solution)/shard_map/all_to_all | solution.py:229
  89.0 16.5 %all-to-all-done.3 = bf16[8,8,8,640]{3,2,1,0:T(8,128)(2,1)S(1)} async-done(((bf16[8,8,8,640]{3,2,1,0:T(8,128)(2,1)}), bf16[8,8,8,640]{3,2,1,0:T(8,128)(2,1)S(1)}, u32[]{:S(2)}, u32[]{:S(2)}) %all-to-all-start.3) | async-done | bytes 655392 | tf_op jit(solution)/shard_map/all_to_all | solution.py:229
  105.7 8.3 %fusion.32 = bf16[8,16,8,1,768]{4,2,0,1,3:T(8,128)(2,1)S(1)} fusion(bf16[8,16,8,640]{3,2,0,1:T(8,128)(2,1)S(1)} %bitcast.147, bf16[16,640,768]{2,1,0:T(8,128)(2,1)} %param.32), kind=kOutput, calls=%fused_computation.59 | convolution fusion | flops 1007419392 | bytes 18612224 | tf_op jit(solution)/shard_map/spkd,pdu->spku/dot_general | solution.py:241
  114.1 8.3 %fusion.35 = bf16[8,16,8,1,768]{4,2,0,1,3:T(8,128)(2,1)S(1)} fusion(bf16[8,16,8,640]{3,2,0,1:T(8,128)(2,1)S(1)} %bitcast.148, bf16[16,640,768]{2,1,0:T(8,128)(2,1)} %param.31), kind=kOutput, calls=%fused_computation.60 | convolution fusion | flops 1007419392 | bytes 18612224 | tf_op jit(solution)/shard_map/spkd,pdu->spku/dot_general | solution.py:240
  123.7 3.7 %collective-permute-done.4 = bf16[4,16,8,2,768]{4,2,0,1,3:T(8,128)(2,1)} collective-permute-done((bf16[4,16,8,2,768]{4,2,0,1,3:T(8,128)(2,1)}, bf16[4,16,8,2,768]{4,2,0,1,3:T(8,128)(2,1)}, u32[]{:S(2)}, u32[]{:S(2)}) %collective-permute-start.4) | collective-permute-done | bytes 1572896 | tf_op jit(solution)/shard_map/ppermute | solution.py:250
  127.4 2.0 add_convert_fusion
  130.6 35.3 %collective-permute-done.5 = bf16[4,16,8,2,768]{4,2,0,1,3:T(8,128)(2,1)S(1)} collective-permute-done((bf16[4,16,8,2,768]{4,2,0,1,3:T(8,128)(2,1)S(1)}, bf16[4,16,8,2,768]{4,2,0,1,3:T(8,128)(2,1)S(1)}, u32[]{:S(2)}, u32[]{:S(2)}) %collective-permute-start.5) | collective-permute-done | bytes 1572896 | tf_op jit(solution)/shard_map/ppermute | solution.py:252
  165.9 2.2 %convert_add_fusion = f32[4,16,8,2,768]{4,2,0,1,3:T(8,128)S(1)} fusion(bf16[4,16,8,2,768]{4,2,0,1,3:T(8,128)(2,1)S(1)} %collective-permute-done.5, bf16[4,16,8,2,768]{4,2,0,1,3:T(8,128)(2,1)} %collective-permute-done.4, s32[]{:T(128)S(6)} %select_n.188, bf16[8,16,8,1,768]{4,2,0,1,3:T(8,128)(2,1)S(1)} %fusion.32, bf16[8,16,8,1,768]{4,2,0,1,3:T(8,128)(2,1)S(1)} %fusion.35), kind=kLoop, calls=%fused_computation.41 | loop fusion | flops 6291456 | bytes 9437188 | tf_op jit(solution)/shard_map/add | solution.py:252
  168.9 2.0 collective-permute-done.6
  170.9 8.1 %bitcast_reduce_fusion = bf16[8,8,8,640]{3,2,0,1:T(8,128)(2,1)S(1)} fusion(bf16[16,768,640]{2,1,0:T(8,128)(2,1)} %param.33, bf16[4,16,8,768]{3,2,0,1:T(8,128)(2,1)S(1)} %collective-permute-done.6, bf16[4,16,8,768]{3,2,0,1:T(8,128)(2,1)S(1)} %fusion.25, pred[]{:T(512)S(6)} %eq.108), kind=kOutput, calls=%fused_computation.61 | convolution fusion | flops 1009975296 | bytes 17956864 | tf_op jit(solution)/shard_map/spku,pud->spkd/dot_general | solution.py:260
  179.9 3.6 %all-to-all-start.4 = ((bf16[8,8,8,640]{3,2,1,0:T(8,128)(2,1)}), bf16[8,8,8,640]{3,2,1,0:T(8,128)(2,1)S(1)}, u32[]{:S(2)}, u32[]{:S(2)}) async-start(bf16[8,8,8,640]{3,2,1,0:T(8,128)(2,1)} %copy.143), calls=%async_computation.4 | async-start | bytes 1310720 | tf_op jit(solution)/shard_map/all_to_all | solution.py:266
  187.0 14.2 %all-to-all-done.4 = bf16[8,8,8,640]{3,2,1,0:T(8,128)(2,1)S(1)} async-done(((bf16[8,8,8,640]{3,2,1,0:T(8,128)(2,1)}), bf16[8,8,8,640]{3,2,1,0:T(8,128)(2,1)S(1)}, u32[]{:S(2)}, u32[]{:S(2)}) %all-to-all-start.4) | async-done | bytes 655392 | tf_op jit(solution)/shard_map/all_to_all | solution.py:266
  201.4 1.9 gather_fusion.9
  (158 shorter events, 35.5 us)
Async XLA Ops:
  0.6 51.6 %copy-start = (bf16[640,320]{0,1:T(8,128)(2,1)S(1)}, bf16[640,320]{0,1:T(8,128)(2,1)}, u32[]{:S(2)}) copy-start(bf16[640,320]{0,1:T(8,128)(2,1)} %param.27) | copy-start | bytes 1228804
  0.6 22.5 %copy-start.6 = (bf16[64,1,2,128]{3,2,1,0:T(2,128)(2,1)S(1)}, bf16[64,1,2,128]{3,2,1,0:T(2,128)(2,1)}, u32[]{:S(2)}) copy-start(bf16[64,1,2,128]{3,2,1,0:T(2,128)(2,1)} %param.20) | copy-start | bytes 98308
  0.7 22.8 %copy-start.7 = (bf16[64,640]{1,0:T(8,128)(2,1)S(1)}, bf16[64,640]{1,0:T(8,128)(2,1)}, u32[]{:S(2)}) copy-start(bf16[64,640]{1,0:T(8,128)(2,1)} %param.19) | copy-start | bytes 245764
  15.3 14.6 %all-to-all-start = ((bf16[8,2,16,2,128]{4,2,3,1,0:T(8,128)(2,1)}), bf16[8,2,16,2,128]{4,2,3,1,0:T(8,128)(2,1)S(1)}, u32[]{:S(2)}, u32[]{:S(2)}) async-start(bf16[8,2,16,2,128]{4,2,3,1,0:T(8,128)(2,1)} %copy.131), calls=%async_computation | async-start | bytes 262144 | tf_op jit(solution)/shard_map/all_to_all | solution.py:118
  31.1 4.9 %copy-start.9 = (s32[64,6]{0,1:T(8,128)S(1)}, s32[64,6]{0,1:T(8,128)}, u32[]{:S(2)}) copy-start(s32[64,6]{0,1:T(8,128)} %param.30) | copy-start | bytes 4612
  32.3 20.0 %all-to-all-start.1 = ((bf16[8,64,640]{2,1,0:T(8,128)(2,1)}), bf16[8,64,640]{2,1,0:T(8,128)(2,1)S(1)}, u32[]{:S(2)}, u32[]{:S(2)}) async-start(bf16[8,64,640]{2,1,0:T(8,128)(2,1)} %broadcast_in_dim.163), calls=%async_computation.1 | async-start | bytes 1310720 | tf_op jit(solution)/shard_map/all_to_all | solution.py:148
  53.6 14.8 %all-to-all-start.2 = ((bf16[8,64,320]{2,1,0:T(8,128)(2,1)}), bf16[8,64,320]{2,1,0:T(8,128)(2,1)S(1)}, u32[]{:S(2)}, u32[]{:S(2)}) async-start(bf16[8,64,320]{2,1,0:T(8,128)(2,1)} %bitcast.22), calls=%async_computation.2 | async-start | bytes 786432 | tf_op jit(solution)/shard_map/all_to_all | solution.py:154
  57.3 17.6 %copy-start.14 = (bf16[640]{0:T(1024)(128)(2,1)S(1)}, bf16[640]{0:T(1024)(128)(2,1)}, u32[]{:S(2)}) copy-start(bf16[640]{0:T(1024)(128)(2,1)} %param.28) | copy-start | bytes 3844
  57.3 18.9 %copy-start.8 = (bf16[64,640]{1,0:T(8,128)(2,1)S(1)}, bf16[64,640]{1,0:T(8,128)(2,1)}, u32[]{:S(2)}) copy-start(bf16[64,640]{1,0:T(8,128)(2,1)} %param.18) | copy-start | bytes 245764
  68.4 7.9 %copy-start.5 = (f32[640,64]{0,1:T(8,128)S(1)}, f32[640,64]{0,1:T(8,128)}, u32[]{:S(2)}) copy-start(f32[640,64]{0,1:T(8,128)} %param.29) | copy-start | bytes 491524
  69.0 5.7 %collective-permute-start = (bf16[64,1280]{1,0:T(8,128)(2,1)S(1)}, bf16[64,1280]{1,0:T(8,128)(2,1)S(1)}, u32[]{:S(2)}, u32[]{:S(2)}) collective-permute-start(bf16[64,1280]{1,0:T(8,128)(2,1)S(1)} %constant_dynamic-slice_fusion), channel_id=1, source_target_pairs={{0,16},{8,24},{16,0},{24,8},{1,17},{9,25},{17,1},{25,9},{2,18},{10... | collective-permute-start | bytes 491528 | tf_op jit(solution)/shard_map/ppermute | solution.py:164
  74.8 1.3 collective-permute-start.1
  76.3 8.0 %copy-start.2 = (bf16[64,640]{1,0:T(8,128)(2,1)}, bf16[64,640]{1,0:T(8,128)(2,1)S(1)}, u32[]{:S(2)}) copy-start(bf16[64,640]{1,0:T(8,128)(2,1)S(1)} %get-tuple-element.195) | copy-start | bytes 245764
  76.8 1.2 collective-permute-start.2
  78.1 3.9 %collective-permute-start.3 = (f32[64,65]{1,0:T(8,128)S(1)}, f32[64,65]{1,0:T(8,128)S(1)}, u32[]{:S(2)}, u32[]{:S(2)}) collective-permute-start(f32[64,65]{1,0:T(8,128)S(1)} %fusion.96), channel_id=1, source_target_pairs={{0,16},{8,24},{16,0},{24,8},{1,17},{9,25},{17,1},{25,9},{2,18},{10... | collective-permute-start | bytes 49928 | tf_op jit(solution)/shard_map/ppermute | solution.py:189
  85.2 20.3 %all-to-all-start.3 = ((bf16[8,8,8,640]{3,2,1,0:T(8,128)(2,1)}), bf16[8,8,8,640]{3,2,1,0:T(8,128)(2,1)S(1)}, u32[]{:S(2)}, u32[]{:S(2)}) async-start(bf16[8,8,8,640]{3,2,1,0:T(8,128)(2,1)} %broadcast_select_fusion), calls=%async_computation.3 | async-start | bytes 1310720 | tf_op jit(solution)/shard_map/all_to_all | solution.py:229
  123.7 3.8 %collective-permute-start.4 = (bf16[4,16,8,2,768]{4,2,0,1,3:T(8,128)(2,1)}, bf16[4,16,8,2,768]{4,2,0,1,3:T(8,128)(2,1)}, u32[]{:S(2)}, u32[]{:S(2)}) collective-permute-start(bf16[4,16,8,2,768]{4,2,0,1,3:T(8,128)(2,1)} %fusion.22), channel_id=1, source_target_pairs={{0,8},{8,0},{16,24},{24,16},{1,9},{9,1},{17,25},{25,17},{2,10},{10... | collective-permute-start | bytes 4718600 | tf_op jit(solution)/shard_map/ppermute | solution.py:250
  129.4 36.5 %collective-permute-start.5 = (bf16[4,16,8,2,768]{4,2,0,1,3:T(8,128)(2,1)S(1)}, bf16[4,16,8,2,768]{4,2,0,1,3:T(8,128)(2,1)S(1)}, u32[]{:S(2)}, u32[]{:S(2)}) collective-permute-start(bf16[4,16,8,2,768]{4,2,0,1,3:T(8,128)(2,1)S(1)} %add_convert_fusion), channel_id=1, source_target_pairs={{0,16},{8,24},{16,0},{24,8},{1,17},{9,25},{17,1},{25,9},{2,18},{10... | collective-permute-start | bytes 4718600 | tf_op jit(solution)/shard_map/ppermute | solution.py:252
  168.6 2.4 %collective-permute-start.6 = (bf16[4,16,8,768]{3,2,0,1:T(8,128)(2,1)S(1)}, bf16[4,16,8,768]{3,2,0,1:T(8,128)(2,1)S(1)}, u32[]{:S(2)}, u32[]{:S(2)}) collective-permute-start(bf16[4,16,8,768]{3,2,0,1:T(8,128)(2,1)S(1)} %fusion.25), channel_id=1, source_target_pairs={{0,8},{8,0},{16,24},{24,16},{1,9},{9,1},{17,25},{25,17},{2,10},{10... | collective-permute-start | bytes 2359304 | tf_op jit(solution)/shard_map/ppermute | solution.py:254
  179.0 4.8 %copy-start.12 = (s32[8,8]{1,0:T(8,128)S(1)}, s32[8,8]{1,0:T(8,128)}, u32[]{:S(2)}) copy-start(s32[8,8]{1,0:T(8,128)} %get-tuple-element.202) | copy-start | bytes 772
  179.0 6.6 %copy-start.4 = (bf16[8,1,16,2,128]{4,2,3,1,0:T(8,128)(2,1)S(1)}, bf16[8,1,16,2,128]{4,2,3,1,0:T(8,128)(2,1)}, u32[]{:S(2)}) copy-start(bf16[8,1,16,2,128]{4,2,3,1,0:T(8,128)(2,1)} %get-tuple-element.200) | copy-start | bytes 196612
  179.0 7.7 %copy-start.10 = (s32[64,6]{0,1:T(8,128)S(1)}, s32[64,6]{0,1:T(8,128)}, u32[]{:S(2)}) copy-start(s32[64,6]{0,1:T(8,128)} %param.30) | copy-start | bytes 4612
  179.9 21.3 %all-to-all-start.4 = ((bf16[8,8,8,640]{3,2,1,0:T(8,128)(2,1)}), bf16[8,8,8,640]{3,2,1,0:T(8,128)(2,1)S(1)}, u32[]{:S(2)}, u32[]{:S(2)}) async-start(bf16[8,8,8,640]{3,2,1,0:T(8,128)(2,1)} %copy.143), calls=%async_computation.4 | async-start | bytes 1310720 | tf_op jit(solution)/shard_map/all_to_all | solution.py:266
  201.4 3.4 %copy-start.1 = (bf16[640,320]{0,1:T(8,128)(2,1)S(1)}, bf16[640,320]{0,1:T(8,128)(2,1)}, u32[]{:S(2)}) copy-start(bf16[640,320]{0,1:T(8,128)(2,1)} %param.27) | copy-start | bytes 1228804
  (3 other events, 2.3 us)

commit v6 on v5

--- a/solution.py
+++ b/solution.py
@@ -7,6 +7,7 @@
 
 D = 2560
 CAP = 8
+CHUNKS = 2
 
 
 EPSILON = 1e-05
@@ -223,52 +224,63 @@
     pieces_here = w_gate.shape[0]
     feature_part = normed.shape[1]
     paired = pieces_here % 2 == 0
-    if paired:
-        experts_here = pieces_here // 2
-        sent = packed_rows.reshape(blk_count, experts_here, capacity, feature_part)
-        landed_rows = lax.all_to_all(sent, "blk", split_axis=0, concat_axis=0, tiled=True)
-        rows_in = jnp.broadcast_to(
-            landed_rows[:, :, None], (blk_count, experts_here, 2, capacity, feature_part)
-        ).reshape(blk_count, pieces_here, capacity, feature_part)
-    else:
-        doubled = jnp.broadcast_to(
-            packed_rows.reshape(expert_count, 1, capacity, feature_part),
-            (expert_count, 2, capacity, feature_part),
-        )
-        doubled = doubled.reshape(blk_count, pieces_here, capacity, feature_part)
-        rows_in = lax.all_to_all(doubled, "blk", split_axis=0, concat_axis=0, tiled=True)
-    gate_part = jnp.einsum("spkd,pdu->spku", rows_in, w_gate, preferred_element_type=jnp.float32)
-    up_part = jnp.einsum("spkd,pdu->spku", rows_in, w_up, preferred_element_type=jnp.float32)
-    both_parts = jnp.stack([gate_part, up_part], axis=3).astype(jnp.bfloat16)
     kv_count = lax.axis_size("kv")
     core_bit = lax.axis_index("kv") % 2
     flip_core = [(i, i ^ 1) for i in range(kv_count)]
     flip_chip = [(i, i ^ 2) for i in range(kv_count)]
-    half = both_parts.shape[0] // 2
-    kept = lax.dynamic_slice_in_dim(both_parts, core_bit * half, half, 0)
-    given = lax.dynamic_slice_in_dim(both_parts, (1 - core_bit) * half, half, 0)
-    pair_sum = kept.astype(jnp.float32) + lax.ppermute(given, "kv", flip_core).astype(jnp.float32)
-    pair_sum = pair_sum.astype(jnp.bfloat16)
-    whole = pair_sum.astype(jnp.float32) + lax.ppermute(pair_sum, "kv", flip_chip).astype(jnp.float32)
-    hidden_half = (jax.nn.silu(whole[:, :, :, 0]) * whole[:, :, :, 1]).astype(jnp.bfloat16)
-    hidden_other = lax.ppermute(hidden_half, "kv", flip_core)
-    hidden = jnp.where(
-        core_bit == 0,
-        jnp.concatenate([hidden_half, hidden_other], axis=0),
-        jnp.concatenate([hidden_other, hidden_half], axis=0),
-    )
-    piece_out = jnp.einsum(
-        "spku,pud->spkd", hidden, w_down, preferred_element_type=jnp.float32
-    ).astype(jnp.bfloat16)
     if paired:
-        half_sum = piece_out.reshape(blk_count, experts_here, 2, capacity, feature_part)
-        half_sum = jnp.sum(half_sum.astype(jnp.float32), axis=2).astype(jnp.bfloat16)
-        returned = lax.all_to_all(half_sum, "blk", split_axis=0, concat_axis=0, tiled=True)
-        per_slot = returned.reshape(slot_total, feature_part).astype(jnp.float32)
+        experts_here = pieces_here // 2
+        outgoing_rows = packed_rows.reshape(blk_count, experts_here, capacity, feature_part)
     else:
+        outgoing_rows = jnp.broadcast_to(
+            packed_rows.reshape(expert_count, 1, capacity, feature_part),
+            (expert_count, 2, capacity, feature_part),
+        ).reshape(blk_count, pieces_here, capacity, feature_part)
+
+    def expert_chunk(chunk_rows):
+        chunk_len = chunk_rows.shape[2]
+        landed_rows = lax.all_to_all(chunk_rows, "blk", split_axis=0, concat_axis=0, tiled=True)
+        if paired:
+            rows_in = jnp.broadcast_to(
+                landed_rows[:, :, None], (blk_count, experts_here, 2, chunk_len, feature_part)
+            ).reshape(blk_count, pieces_here, chunk_len, feature_part)
+        else:
+            rows_in = landed_rows
+        gate_part = jnp.einsum("spkd,pdu->spku", rows_in, w_gate, preferred_element_type=jnp.float32)
+        up_part = jnp.einsum("spkd,pdu->spku", rows_in, w_up, preferred_element_type=jnp.float32)
+        both_parts = jnp.stack([gate_part, up_part], axis=3).astype(jnp.bfloat16)
+        half = both_parts.shape[0] // 2
+        kept = lax.dynamic_slice_in_dim(both_parts, core_bit * half, half, 0)
+        given = lax.dynamic_slice_in_dim(both_parts, (1 - core_bit) * half, half, 0)
+        pair_sum = kept.astype(jnp.float32) + lax.ppermute(given, "kv", flip_core).astype(jnp.float32)
+        pair_sum = pair_sum.astype(jnp.bfloat16)
+        whole = pair_sum.astype(jnp.float32) + lax.ppermute(pair_sum, "kv", flip_chip).astype(jnp.float32)
+        hidden_half = (jax.nn.silu(whole[:, :, :, 0]) * whole[:, :, :, 1]).astype(jnp.bfloat16)
+        hidden_other = lax.ppermute(hidden_half, "kv", flip_core)
+        hidden = jnp.where(
+            core_bit == 0,
+            jnp.concatenate([hidden_half, hidden_other], axis=0),
+            jnp.concatenate([hidden_other, hidden_half], axis=0),
+        )
+        piece_out = jnp.einsum(
+            "spku,pud->spkd", hidden, w_down, preferred_element_type=jnp.float32
+        ).astype(jnp.bfloat16)
+        if paired:
+            half_sum = piece_out.reshape(blk_count, experts_here, 2, chunk_len, feature_part)
+            half_sum = jnp.sum(half_sum.astype(jnp.float32), axis=2).astype(jnp.bfloat16)
+            returned = lax.all_to_all(half_sum, "blk", split_axis=0, concat_axis=0, tiled=True)
+            return returned.reshape(expert_count, chunk_len, feature_part).astype(jnp.float32)
         returned = lax.all_to_all(piece_out, "blk", split_axis=0, concat_axis=0, tiled=True)
-        per_piece = returned.reshape(expert_count, 2, capacity, feature_part).astype(jnp.float32)
-        per_slot = (per_piece[:, 0] + per_piece[:, 1]).reshape(slot_total, feature_part)
+        per_piece = returned.reshape(expert_count, 2, chunk_len, feature_part).astype(jnp.float32)
+        return per_piece[:, 0] + per_piece[:, 1]
+
+    chunk_count = CHUNKS if capacity % CHUNKS == 0 else 1
+    chunk_len = capacity // chunk_count
+    per_chunk = [
+        expert_chunk(outgoing_rows[:, :, i * chunk_len : (i + 1) * chunk_len])
+        for i in range(chunk_count)
+    ]
+    per_slot = jnp.concatenate(per_chunk, axis=1).reshape(slot_total, feature_part)
     routed = per_slot[target].reshape(stretch_len, top_count, feature_part)
     moe_out = jnp.sum(routed * gates[:, :, None], axis=1)
     layer_out = (resid_float + moe_out).astype(jnp.bfloat16)

time: 206 us -> 228 us (1.11)
  matrix products: 26 us -> 49.7 us
  waiting for transfers between devices: 108 us -> 86.2 us
  starting transfers between devices: 26.2 us -> 37.6 us
  other arithmetic: 21.9 us -> 27.1 us
  local copies, waits for them, and re-layouts: 20.6 us -> 23.9 us
    dot_general x3 -> x6, matrix products: 24.7 us -> 48.4 us  [the longest x2 16.1 us: expert_chunk(): jnp.einsum('spkd,pdu->spku', rows_in, w_up, preferred_element_type=jnp.fl...]
    ppermute x3 -> x6, waiting for transfers between devices: 41.1 us -> 28.5 us  [the longest x2 28.5 us: expert_chunk(): lax.ppermute(pair_sum, 'kv', flip_chip).astype(jnp.float32)]
    all_to_all x2 -> x4, starting transfers between devices: 7.33 us -> 17.3 us  [the longest x2 9.99 us: expert_chunk(): lax.all_to_all(half_sum, 'blk', split_axis=0, concat_axis=0, tiled=True)]
    all_to_all x2 -> x4, waiting for transfers between devices: 30.8 us -> 21 us  [the longest x2 11.8 us: expert_chunk(): lax.all_to_all(half_sum, 'blk', split_axis=0, concat_axis=0, tiled=True)]
    convert_element_type x3 -> x4, other arithmetic: 2.58 us -> 5.25 us  [the longest x2 4.41 us: expert_chunk(): pair_sum = pair_sum.astype(jnp.bfloat16)]
  transfers between devices with their start and end apart: 12 -> 17, of which waited for: 11 -> 11; matrix products, arithmetic and copies ran while one was open for 5% -> 32% of each run, Pallas kernels for 0% -> 0%
where the time goes in v6:
time: 228 us; the launch traced here: 227 us
  waiting for transfers between devices  86.2 us (38%)
  matrix products  49.7 us (22%)
  starting transfers between devices  37.6 us (16%)
  other arithmetic  27.1 us (12%)
  local copies, waits for them, and re-layouts  23.9 us (10%)
    ppermute x2, waiting for transfers between devices, expert_chunk(): lax.ppermute(pair_sum, 'kv', flip_chip).astype(jnp.float32)  28.5 us
    dot_general x2, matrix products, expert_chunk(): jnp.einsum('spkd,pdu->spku', rows_in, w_up, preferred_element_type=jnp.fl...  16.1 us
    dot_general x2, matrix products, expert_chunk(): jnp.einsum('spkd,pdu->spku', rows_in, w_gate, preferred_element_type=jnp....  16.1 us
    dot_general x2, matrix products, expert_chunk(): jnp.einsum('spku,pud->spkd', hidden, w_down, preferred_element_type=jnp.f...  16.1 us
    all_to_all x1, waiting for transfers between devices, per_device(): lax.all_to_all(jnp.broadcast_to(attended[None], (blk_count,) + attended.s...  15.8 us
    all_to_all x2, waiting for transfers between devices, expert_chunk(): lax.all_to_all(half_sum, 'blk', split_axis=0, concat_axis=0, tiled=True)  11.8 us
    all_to_all x2, starting transfers between devices, expert_chunk(): lax.all_to_all(half_sum, 'blk', split_axis=0, concat_axis=0, tiled=True)  9.99 us
    all_to_all x1, waiting for transfers between devices, per_device(): lax.all_to_all(column_part, 'blk', split_axis=0, concat_axis=1, tiled=True)  9.85 us
  transfers between devices with their start and end apart: 17, of which 11 were waited for; matrix products, arithmetic and copies ran while one was open for 32% of the time, Pallas kernels for 0%

profile of v6, /device:TPU:0, one launch (start us, length us, event | category | flops | bytes accessed | tf_op | source)
XLA Modules:
  0.0 226.6 jit_solution(10460896517061149520)
XLA Ops:
  14.9 7.3 %all-to-all-start = ((bf16[8,2,16,2,128]{4,2,3,1,0:T(8,128)(2,1)}), bf16[8,2,16,2,128]{4,2,3,1,0:T(8,128)(2,1)S(1)}, u32[]{:S(2)}, u32[]{:S(2)}) async-start(bf16[8,2,16,2,128]{4,2,3,1,0:T(8,128)(2,1)} %copy.165), calls=%async_computation | async-start | bytes 262144 | tf_op jit(solution)/shard_map/all_to_all | solution.py:119
  23.5 6.1 %all-to-all-done = bf16[8,2,16,2,128]{4,2,3,1,0:T(8,128)(2,1)S(1)} async-done(((bf16[8,2,16,2,128]{4,2,3,1,0:T(8,128)(2,1)}), bf16[8,2,16,2,128]{4,2,3,1,0:T(8,128)(2,1)S(1)}, u32[]{:S(2)}, u32[]{:S(2)}) %all-to-all-start) | async-done | bytes 131104 | tf_op jit(solution)/shard_map/all_to_all | solution.py:119
  31.9 3.8 %all-to-all-start.1 = ((bf16[8,64,640]{2,1,0:T(8,128)(2,1)}), bf16[8,64,640]{2,1,0:T(8,128)(2,1)S(1)}, u32[]{:S(2)}, u32[]{:S(2)}) async-start(bf16[8,64,640]{2,1,0:T(8,128)(2,1)} %broadcast_in_dim.169), calls=%async_computation.1 | async-start | bytes 1310720 | tf_op jit(solution)/shard_map/all_to_all | solution.py:149
  36.1 15.8 %all-to-all-done.1 = bf16[8,64,640]{2,1,0:T(8,128)(2,1)S(1)} async-done(((bf16[8,64,640]{2,1,0:T(8,128)(2,1)}), bf16[8,64,640]{2,1,0:T(8,128)(2,1)S(1)}, u32[]{:S(2)}, u32[]{:S(2)}) %all-to-all-start.1) | async-done | bytes 655392 | tf_op jit(solution)/shard_map/all_to_all | solution.py:149
  53.3 3.6 %all-to-all-start.2 = ((bf16[8,64,320]{2,1,0:T(8,128)(2,1)}), bf16[8,64,320]{2,1,0:T(8,128)(2,1)S(1)}, u32[]{:S(2)}, u32[]{:S(2)}) async-start(bf16[8,64,320]{2,1,0:T(8,128)(2,1)} %bitcast.22), calls=%async_computation.2 | async-start | bytes 786432 | tf_op jit(solution)/shard_map/all_to_all | solution.py:155
  58.2 9.8 %all-to-all-done.2 = bf16[8,64,320]{2,1,0:T(8,128)(2,1)S(1)} async-done(((bf16[8,64,320]{2,1,0:T(8,128)(2,1)}), bf16[8,64,320]{2,1,0:T(8,128)(2,1)S(1)}, u32[]{:S(2)}, u32[]{:S(2)}) %all-to-all-start.2) | async-done | bytes 327712 | tf_op jit(solution)/shard_map/all_to_all | solution.py:155
  70.4 3.9 %scatter_custom_fusion.2 = s32[512]{0:T(512)S(1)} fusion(s32[384]{0:T(512)S(1)} %get-tuple-element.185, s32[384]{0:T(512)S(1)} %iota_add_fusion, s32[]{:T(128)} %constant.182.clone.1), kind=kCustom, calls=%fused_computation.200 | custom fusion | flops 384 | bytes 2052 | tf_op jit(solution)/shard_map/scatter-add | solution.py:218
  78.9 2.7 %collective-permute-done.3 = f32[64,65]{1,0:T(8,128)S(1)} collective-permute-done((f32[64,65]{1,0:T(8,128)S(1)}, f32[64,65]{1,0:T(8,128)S(1)}, u32[]{:S(2)}, u32[]{:S(2)}) %collective-permute-start.3) | collective-permute-done | bytes 16672 | tf_op jit(solution)/shard_map/ppermute | solution.py:190
  85.7 3.7 %all-to-all-start.3 = ((bf16[8,8,4,640]{3,2,1,0:T(4,128)(2,1)}), bf16[8,8,4,640]{3,2,1,0:T(4,128)(2,1)S(1)}, u32[]{:S(2)}, u32[]{:S(2)}) async-start(bf16[8,8,4,640]{3,2,1,0:T(4,128)(2,1)} %get-tuple-element.210), calls=%async_computation.3 | async-start | bytes 655360 | tf_op jit(solution)/shard_map/all_to_all | solution.py:242
  89.7 9.1 %all-to-all-done.3 = bf16[8,8,4,640]{3,2,1,0:T(4,128)(2,1)S(1)} async-done(((bf16[8,8,4,640]{3,2,1,0:T(4,128)(2,1)}), bf16[8,8,4,640]{3,2,1,0:T(4,128)(2,1)S(1)}, u32[]{:S(2)}, u32[]{:S(2)}) %all-to-all-start.3) | async-done | bytes 327712 | tf_op jit(solution)/shard_map/all_to_all | solution.py:242
  98.8 3.6 %all-to-all-start.5 = ((bf16[8,8,4,640]{3,2,1,0:T(4,128)(2,1)}), bf16[8,8,4,640]{3,2,1,0:T(4,128)(2,1)S(1)}, u32[]{:S(2)}, u32[]{:S(2)}) async-start(bf16[8,8,4,640]{3,2,1,0:T(4,128)(2,1)} %get-tuple-element.211), calls=%async_computation.5 | async-start | bytes 655360 | tf_op jit(solution)/shard_map/all_to_all | solution.py:242
  102.6 8.1 %fusion.40 = bf16[8,16,4,1,768]{4,0,2,1,3:T(8,128)(2,1)S(1)} fusion(bf16[8,16,4,640]{3,0,2,1:T(8,128)(2,1)S(1)} %bitcast.201, bf16[16,640,768]{2,1,0:T(8,128)(2,1)} %param.32), kind=kOutput, calls=%fused_computation.64 | convolution fusion | flops 503709696 | bytes 17170432 | tf_op jit(solution)/shard_map/spkd,pdu->spku/dot_general | solution.py:250
  110.7 8.1 %fusion.46 = bf16[8,16,4,1,768]{4,0,2,1,3:T(8,128)(2,1)S(1)} fusion(bf16[8,16,4,640]{3,0,2,1:T(8,128)(2,1)S(1)} %bitcast.202, bf16[16,640,768]{2,1,0:T(8,128)(2,1)} %param.31), kind=kOutput, calls=%fused_computation.66 | convolution fusion | flops 503709696 | bytes 17170432 | tf_op jit(solution)/shard_map/spkd,pdu->spku/dot_general | solution.py:249
  120.3 8.1 %fusion.37 = bf16[8,16,4,1,768]{4,0,2,1,3:T(8,128)(2,1)S(1)} fusion(bf16[8,16,4,640]{3,0,2,1:T(8,128)(2,1)S(1)} %bitcast.203, bf16[16,640,768]{2,1,0:T(8,128)(2,1)} %param.32), kind=kOutput, calls=%fused_computation.63 | convolution fusion | flops 503709696 | bytes 17170432 | tf_op jit(solution)/shard_map/spkd,pdu->spku/dot_general | solution.py:250
  128.4 8.1 %fusion.43 = bf16[8,16,4,1,768]{4,0,2,1,3:T(8,128)(2,1)S(1)} fusion(bf16[8,16,4,640]{3,0,2,1:T(8,128)(2,1)S(1)} %bitcast.204, bf16[16,640,768]{2,1,0:T(8,128)(2,1)} %param.31), kind=kOutput, calls=%fused_computation.65 | convolution fusion | flops 503709696 | bytes 17170432 | tf_op jit(solution)/shard_map/spkd,pdu->spku/dot_general | solution.py:249
  140.4 2.7 %add_convert_fusion.1 = bf16[4,16,4,2,768]{4,0,2,1,3:T(4,128)(2,1)} fusion(bf16[4,16,4,2,768]{4,0,2,1,3:T(4,128)(2,1)} %collective-permute-done.4, s32[]{:T(128)S(6)} %select_n.194, bf16[8,16,4,1,768]{4,0,2,1,3:T(8,128)(2,1)S(1)} %fusion.46, bf16[8,16,4,1,768]{4,0,2,1,3:T(8,128)(2,1)S(1)} %fusion.40), kind=kLoop, calls=%fused_computation.54 | loop fusion | flops 2752512 | bytes 3145732 | tf_op jit(solution)/shard_map/convert_element_type | solution.py:256
  148.5 15.3 %collective-permute-done.5 = bf16[4,16,4,2,768]{4,0,2,1,3:T(4,128)(2,1)} collective-permute-done((bf16[4,16,4,2,768]{4,0,2,1,3:T(4,128)(2,1)}, bf16[4,16,4,2,768]{4,0,2,1,3:T(4,128)(2,1)}, u32[]{:S(2)}, u32[]{:S(2)}) %collective-permute-start.5) | collective-permute-done | bytes 786464 | tf_op jit(solution)/shard_map/ppermute | solution.py:257
  163.8 2.1 convert_add_fusion.1
  166.4 13.2 %collective-permute-done.8 = bf16[4,16,4,2,768]{4,0,2,1,3:T(4,128)(2,1)S(1)} collective-permute-done((bf16[4,16,4,2,768]{4,0,2,1,3:T(4,128)(2,1)S(1)}, bf16[4,16,4,2,768]{4,0,2,1,3:T(4,128)(2,1)S(1)}, u32[]{:S(2)}, u32[]{:S(2)}) %collective-permute-start.8) | collective-permute-done | bytes 786464 | tf_op jit(solution)/shard_map/ppermute | solution.py:257
  182.1 8.1 %bitcast_reduce_fusion.1 = bf16[8,8,4,640]{3,0,2,1:T(8,128)(2,1)S(1)} fusion(bf16[16,768,640]{2,1,0:T(8,128)(2,1)} %param.33, bf16[4,16,4,768]{3,0,2,1:T(4,128)(2,1)S(1)} %collective-permute-done.6, bf16[4,16,4,768]{3,0,2,1:T(4,128)(2,1)S(1)} %fusion.67, pred[]{:T(512)S(6)} %eq.109), kind=kOutput, calls=%fused_computation.101 | convolution fusion | flops 507346944 | bytes 16842752 | tf_op jit(solution)/shard_map/spku,pud->spkd/dot_general | solution.py:265
  191.0 6.0 %all-to-all-start.4 = ((bf16[8,8,4,640]{3,2,1,0:T(4,128)(2,1)}), bf16[8,8,4,640]{3,2,1,0:T(4,128)(2,1)S(1)}, u32[]{:S(2)}, u32[]{:S(2)}) async-start(bf16[8,8,4,640]{3,2,1,0:T(4,128)(2,1)} %copy.177), calls=%async_computation.4 | async-start | bytes 655360 | tf_op jit(solution)/shard_map/all_to_all | solution.py:271
  197.0 8.1 %bitcast_reduce_fusion = bf16[8,8,4,640]{3,0,2,1:T(8,128)(2,1)S(1)} fusion(bf16[16,768,640]{2,1,0:T(8,128)(2,1)} %param.33, bf16[4,16,4,768]{3,0,2,1:T(4,128)(2,1)S(1)} %collective-permute-done.9, bf16[4,16,4,768]{3,0,2,1:T(4,128)(2,1)S(1)} %fusion.66, pred[]{:T(512)S(6)} %eq.109), kind=kOutput, calls=%fused_computation.100 | convolution fusion | flops 507346944 | bytes 16842752 | tf_op jit(solution)/shard_map/spku,pud->spkd/dot_general | solution.py:265
  207.9 4.0 %all-to-all-start.6 = ((bf16[8,8,4,640]{3,2,1,0:T(4,128)(2,1)}), bf16[8,8,4,640]{3,2,1,0:T(4,128)(2,1)S(1)}, u32[]{:S(2)}, u32[]{:S(2)}) async-start(bf16[8,8,4,640]{3,2,1,0:T(4,128)(2,1)} %copy.180), calls=%async_computation.6 | async-start | bytes 655360 | tf_op jit(solution)/shard_map/all_to_all | solution.py:271
  212.4 9.9 %all-to-all-done.6 = bf16[8,8,4,640]{3,2,1,0:T(4,128)(2,1)S(1)} async-done(((bf16[8,8,4,640]{3,2,1,0:T(4,128)(2,1)}), bf16[8,8,4,640]{3,2,1,0:T(4,128)(2,1)S(1)}, u32[]{:S(2)}, u32[]{:S(2)}) %all-to-all-start.6) | async-done | bytes 327712 | tf_op jit(solution)/shard_map/all_to_all | solution.py:271
  (185 shorter events, 53.6 us)
Async XLA Ops:
  0.6 51.3 %copy-start = (bf16[640,320]{0,1:T(8,128)(2,1)S(1)}, bf16[640,320]{0,1:T(8,128)(2,1)}, u32[]{:S(2)}) copy-start(bf16[640,320]{0,1:T(8,128)(2,1)} %param.27) | copy-start | bytes 1228804
  0.6 22.1 %copy-start.8 = (bf16[64,1,2,128]{3,2,1,0:T(2,128)(2,1)S(1)}, bf16[64,1,2,128]{3,2,1,0:T(2,128)(2,1)}, u32[]{:S(2)}) copy-start(bf16[64,1,2,128]{3,2,1,0:T(2,128)(2,1)} %param.20) | copy-start | bytes 98308
  0.7 22.2 %copy-start.9 = (bf16[64,640]{1,0:T(8,128)(2,1)S(1)}, bf16[64,640]{1,0:T(8,128)(2,1)}, u32[]{:S(2)}) copy-start(bf16[64,640]{1,0:T(8,128)(2,1)} %param.19) | copy-start | bytes 245764
  14.9 14.6 %all-to-all-start = ((bf16[8,2,16,2,128]{4,2,3,1,0:T(8,128)(2,1)}), bf16[8,2,16,2,128]{4,2,3,1,0:T(8,128)(2,1)S(1)}, u32[]{:S(2)}, u32[]{:S(2)}) async-start(bf16[8,2,16,2,128]{4,2,3,1,0:T(8,128)(2,1)} %copy.165), calls=%async_computation | async-start | bytes 262144 | tf_op jit(solution)/shard_map/all_to_all | solution.py:119
  31.9 20.0 %all-to-all-start.1 = ((bf16[8,64,640]{2,1,0:T(8,128)(2,1)}), bf16[8,64,640]{2,1,0:T(8,128)(2,1)S(1)}, u32[]{:S(2)}, u32[]{:S(2)}) async-start(bf16[8,64,640]{2,1,0:T(8,128)(2,1)} %broadcast_in_dim.169), calls=%async_computation.1 | async-start | bytes 1310720 | tf_op jit(solution)/shard_map/all_to_all | solution.py:149
  53.3 14.8 %all-to-all-start.2 = ((bf16[8,64,320]{2,1,0:T(8,128)(2,1)}), bf16[8,64,320]{2,1,0:T(8,128)(2,1)S(1)}, u32[]{:S(2)}, u32[]{:S(2)}) async-start(bf16[8,64,320]{2,1,0:T(8,128)(2,1)} %bitcast.22), calls=%async_computation.2 | async-start | bytes 786432 | tf_op jit(solution)/shard_map/all_to_all | solution.py:155
  56.9 17.6 %copy-start.16 = (bf16[640]{0:T(1024)(128)(2,1)S(1)}, bf16[640]{0:T(1024)(128)(2,1)}, u32[]{:S(2)}) copy-start(bf16[640]{0:T(1024)(128)(2,1)} %param.28) | copy-start | bytes 3844
  56.9 18.8 %copy-start.10 = (bf16[64,640]{1,0:T(8,128)(2,1)S(1)}, bf16[64,640]{1,0:T(8,128)(2,1)}, u32[]{:S(2)}) copy-start(bf16[64,640]{1,0:T(8,128)(2,1)} %param.18) | copy-start | bytes 245764
  68.6 5.7 %collective-permute-start = (bf16[64,1280]{1,0:T(8,128)(2,1)S(1)}, bf16[64,1280]{1,0:T(8,128)(2,1)S(1)}, u32[]{:S(2)}, u32[]{:S(2)}) collective-permute-start(bf16[64,1280]{1,0:T(8,128)(2,1)S(1)} %constant_dynamic-slice_fusion), channel_id=1, source_target_pairs={{0,16},{8,24},{16,0},{24,8},{1,17},{9,25},{17,1},{25,9},{2,18},{10... | collective-permute-start | bytes 491528 | tf_op jit(solution)/shard_map/ppermute | solution.py:165
  74.4 1.3 collective-permute-start.1
  76.4 1.2 collective-permute-start.2
  77.7 3.9 %collective-permute-start.3 = (f32[64,65]{1,0:T(8,128)S(1)}, f32[64,65]{1,0:T(8,128)S(1)}, u32[]{:S(2)}, u32[]{:S(2)}) collective-permute-start(f32[64,65]{1,0:T(8,128)S(1)} %fusion.133), channel_id=1, source_target_pairs={{0,16},{8,24},{16,0},{24,8},{1,17},{9,25},{17,1},{25,9},{2,18},{10... | collective-permute-start | bytes 49928 | tf_op jit(solution)/shard_map/ppermute | solution.py:190
  85.7 13.2 %all-to-all-start.3 = ((bf16[8,8,4,640]{3,2,1,0:T(4,128)(2,1)}), bf16[8,8,4,640]{3,2,1,0:T(4,128)(2,1)S(1)}, u32[]{:S(2)}, u32[]{:S(2)}) async-start(bf16[8,8,4,640]{3,2,1,0:T(4,128)(2,1)} %get-tuple-element.210), calls=%async_computation.3 | async-start | bytes 655360 | tf_op jit(solution)/shard_map/all_to_all | solution.py:242
  98.8 21.3 %all-to-all-start.5 = ((bf16[8,8,4,640]{3,2,1,0:T(4,128)(2,1)}), bf16[8,8,4,640]{3,2,1,0:T(4,128)(2,1)S(1)}, u32[]{:S(2)}, u32[]{:S(2)}) async-start(bf16[8,8,4,640]{3,2,1,0:T(4,128)(2,1)} %get-tuple-element.211), calls=%async_computation.5 | async-start | bytes 655360 | tf_op jit(solution)/shard_map/all_to_all | solution.py:242
  120.1 20.3 %collective-permute-start.4 = (bf16[4,16,4,2,768]{4,0,2,1,3:T(4,128)(2,1)}, bf16[4,16,4,2,768]{4,0,2,1,3:T(4,128)(2,1)}, u32[]{:S(2)}, u32[]{:S(2)}) collective-permute-start(bf16[4,16,4,2,768]{4,0,2,1,3:T(4,128)(2,1)} %fusion.54), channel_id=1, source_target_pairs={{0,8},{8,0},{16,24},{24,16},{1,9},{9,1},{17,25},{25,17},{2,10},{10... | collective-permute-start | bytes 2359304 | tf_op jit(solution)/shard_map/ppermute | solution.py:255
  137.7 7.2 %collective-permute-start.7 = (bf16[4,16,4,2,768]{4,0,2,1,3:T(4,128)(2,1)}, bf16[4,16,4,2,768]{4,0,2,1,3:T(4,128)(2,1)}, u32[]{:S(2)}, u32[]{:S(2)}) collective-permute-start(bf16[4,16,4,2,768]{4,0,2,1,3:T(4,128)(2,1)} %fusion.52), channel_id=1, source_target_pairs={{0,8},{8,0},{16,24},{24,16},{1,9},{9,1},{17,25},{25,17},{2,10},{10... | collective-permute-start | bytes 2359304 | tf_op jit(solution)/shard_map/ppermute | solution.py:255
  143.1 20.7 %collective-permute-start.5 = (bf16[4,16,4,2,768]{4,0,2,1,3:T(4,128)(2,1)}, bf16[4,16,4,2,768]{4,0,2,1,3:T(4,128)(2,1)}, u32[]{:S(2)}, u32[]{:S(2)}) collective-permute-start(bf16[4,16,4,2,768]{4,0,2,1,3:T(4,128)(2,1)} %add_convert_fusion.1), channel_id=1, source_target_pairs={{0,16},{8,24},{16,0},{24,8},{1,17},{9,25},{17,1},{25,9},{2,18},{10... | collective-permute-start | bytes 2359304 | tf_op jit(solution)/shard_map/ppermute | solution.py:257
  146.7 32.9 %collective-permute-start.8 = (bf16[4,16,4,2,768]{4,0,2,1,3:T(4,128)(2,1)S(1)}, bf16[4,16,4,2,768]{4,0,2,1,3:T(4,128)(2,1)S(1)}, u32[]{:S(2)}, u32[]{:S(2)}) collective-permute-start(bf16[4,16,4,2,768]{4,0,2,1,3:T(4,128)(2,1)S(1)} %add_convert_fusion), channel_id=1, source_target_pairs={{0,16},{8,24},{16,0},{24,8},{1,17},{9,25},{17,1},{25,9},{2,18},{10... | collective-permute-start | bytes 2359304 | tf_op jit(solution)/shard_map/ppermute | solution.py:257
  166.3 15.8 %collective-permute-start.6 = (bf16[4,16,4,768]{3,0,2,1:T(4,128)(2,1)S(1)}, bf16[4,16,4,768]{3,0,2,1:T(4,128)(2,1)S(1)}, u32[]{:S(2)}, u32[]{:S(2)}) collective-permute-start(bf16[4,16,4,768]{3,0,2,1:T(4,128)(2,1)S(1)} %fusion.67), channel_id=1, source_target_pairs={{0,8},{8,0},{16,24},{24,16},{1,9},{9,1},{17,25},{25,17},{2,10},{10... | collective-permute-start | bytes 1179656 | tf_op jit(solution)/shard_map/ppermute | solution.py:259
  182.0 15.0 %collective-permute-start.9 = (bf16[4,16,4,768]{3,0,2,1:T(4,128)(2,1)S(1)}, bf16[4,16,4,768]{3,0,2,1:T(4,128)(2,1)S(1)}, u32[]{:S(2)}, u32[]{:S(2)}) collective-permute-start(bf16[4,16,4,768]{3,0,2,1:T(4,128)(2,1)S(1)} %fusion.66), channel_id=1, source_target_pairs={{0,8},{8,0},{16,24},{24,16},{1,9},{9,1},{17,25},{25,17},{2,10},{10... | collective-permute-start | bytes 1179656 | tf_op jit(solution)/shard_map/ppermute | solution.py:259
  191.0 16.9 %all-to-all-start.4 = ((bf16[8,8,4,640]{3,2,1,0:T(4,128)(2,1)}), bf16[8,8,4,640]{3,2,1,0:T(4,128)(2,1)S(1)}, u32[]{:S(2)}, u32[]{:S(2)}) async-start(bf16[8,8,4,640]{3,2,1,0:T(4,128)(2,1)} %copy.177), calls=%async_computation.4 | async-start | bytes 655360 | tf_op jit(solution)/shard_map/all_to_all | solution.py:271
  197.0 14.9 %copy-start.5 = (f32[64,65]{1,0:T(8,128)S(1)}, f32[64,65]{1,0:T(8,128)}, u32[]{:S(2)}) copy-start(f32[64,65]{1,0:T(8,128)} %copy-done.4) | copy-start | bytes 49924
  197.0 15.0 %copy-start.12 = (s32[64,6]{0,1:T(8,128)S(1)}, s32[64,6]{0,1:T(8,128)}, u32[]{:S(2)}) copy-start(s32[64,6]{0,1:T(8,128)} %param.30) | copy-start | bytes 4612
  207.9 14.4 %all-to-all-start.6 = ((bf16[8,8,4,640]{3,2,1,0:T(4,128)(2,1)}), bf16[8,8,4,640]{3,2,1,0:T(4,128)(2,1)S(1)}, u32[]{:S(2)}, u32[]{:S(2)}) async-start(bf16[8,8,4,640]{3,2,1,0:T(4,128)(2,1)} %copy.180), calls=%async_computation.6 | async-start | bytes 655360 | tf_op jit(solution)/shard_map/all_to_all | solution.py:271
  (10 other events, 41.6 us)

commit v7 on v6

--- a/solution.py
+++ b/solution.py
@@ -232,22 +232,24 @@
         experts_here = pieces_here // 2
         outgoing_rows = packed_rows.reshape(blk_count, experts_here, capacity, feature_part)
     else:
+        experts_here = 1
         outgoing_rows = jnp.broadcast_to(
             packed_rows.reshape(expert_count, 1, capacity, feature_part),
             (expert_count, 2, capacity, feature_part),
         ).reshape(blk_count, pieces_here, capacity, feature_part)
 
-    def expert_chunk(chunk_rows):
-        chunk_len = chunk_rows.shape[2]
+    def expert_chunk(chunk_rows, gate_w, up_w, down_w):
+        chunk_pieces = gate_w.shape[0]
         landed_rows = lax.all_to_all(chunk_rows, "blk", split_axis=0, concat_axis=0, tiled=True)
         if paired:
             rows_in = jnp.broadcast_to(
-                landed_rows[:, :, None], (blk_count, experts_here, 2, chunk_len, feature_part)
-            ).reshape(blk_count, pieces_here, chunk_len, feature_part)
+                landed_rows[:, :, None],
+                (blk_count, chunk_pieces // 2, 2, capacity, feature_part),
+            ).reshape(blk_count, chunk_pieces, capacity, feature_part)
         else:
             rows_in = landed_rows
-        gate_part = jnp.einsum("spkd,pdu->spku", rows_in, w_gate, preferred_element_type=jnp.float32)
-        up_part = jnp.einsum("spkd,pdu->spku", rows_in, w_up, preferred_element_type=jnp.float32)
+        gate_part = jnp.einsum("spkd,pdu->spku", rows_in, gate_w, preferred_element_type=jnp.float32)
+        up_part = jnp.einsum("spkd,pdu->spku", rows_in, up_w, preferred_element_type=jnp.float32)
         both_parts = jnp.stack([gate_part, up_part], axis=3).astype(jnp.bfloat16)
         half = both_parts.shape[0] // 2
         kept = lax.dynamic_slice_in_dim(both_parts, core_bit * half, half, 0)
@@ -263,24 +265,35 @@
             jnp.concatenate([hidden_other, hidden_half], axis=0),
         )
         piece_out = jnp.einsum(
-            "spku,pud->spkd", hidden, w_down, preferred_element_type=jnp.float32
+            "spku,pud->spkd", hidden, down_w, preferred_element_type=jnp.float32
         ).astype(jnp.bfloat16)
         if paired:
-            half_sum = piece_out.reshape(blk_count, experts_here, 2, chunk_len, feature_part)
+            half_sum = piece_out.reshape(blk_count, chunk_pieces // 2, 2, capacity, feature_part)
             half_sum = jnp.sum(half_sum.astype(jnp.float32), axis=2).astype(jnp.bfloat16)
-            returned = lax.all_to_all(half_sum, "blk", split_axis=0, concat_axis=0, tiled=True)
-            return returned.reshape(expert_count, chunk_len, feature_part).astype(jnp.float32)
+            return lax.all_to_all(half_sum, "blk", split_axis=0, concat_axis=0, tiled=True)
         returned = lax.all_to_all(piece_out, "blk", split_axis=0, concat_axis=0, tiled=True)
-        per_piece = returned.reshape(expert_count, 2, chunk_len, feature_part).astype(jnp.float32)
-        return per_piece[:, 0] + per_piece[:, 1]
-
-    chunk_count = CHUNKS if capacity % CHUNKS == 0 else 1
-    chunk_len = capacity // chunk_count
-    per_chunk = [
-        expert_chunk(outgoing_rows[:, :, i * chunk_len : (i + 1) * chunk_len])
-        for i in range(chunk_count)
-    ]
-    per_slot = jnp.concatenate(per_chunk, axis=1).reshape(slot_total, feature_part)
+        per_piece = returned.reshape(expert_count, 2, capacity, feature_part).astype(jnp.float32)
+        return (per_piece[:, 0] + per_piece[:, 1]).astype(jnp.bfloat16)
+
+    chunk_count = CHUNKS if paired and experts_here % CHUNKS == 0 else 1
+    chunk_experts = experts_here // chunk_count
+    chunk_pieces = pieces_here // chunk_count
+    per_chunk = []
+    for i in range(chunk_count):
+        pieces_of = slice(i * chunk_pieces, (i + 1) * chunk_pieces)
+        per_chunk.append(
+            expert_chunk(
+                outgoing_rows[:, i * chunk_experts : (i + 1) * chunk_experts],
+                w_gate[pieces_of],
+                w_up[pieces_of],
+                w_down[pieces_of],
+            )
+        )
+    if paired:
+        per_slot = jnp.concatenate(per_chunk, axis=1).reshape(slot_total, feature_part)
+    else:
+        per_slot = per_chunk[0].reshape(slot_total, feature_part)
+    per_slot = per_slot.astype(jnp.float32)
     routed = per_slot[target].reshape(stretch_len, top_count, feature_part)
     moe_out = jnp.sum(routed * gates[:, :, None], axis=1)
     layer_out = (resid_float + moe_out).astype(jnp.bfloat16)

time: 228 us -> 207 us (0.908)
  matrix products: 49.7 us -> 29.3 us
  waiting for transfers between devices: 86.2 us -> 91 us
  local copies, waits for them, and re-layouts: 23.9 us -> 21.1 us
  other arithmetic: 27.1 us -> 24.8 us
    dot_general x6, matrix products: 48.4 us -> 28 us  [the longest x2 9.4 us: expert_chunk(): jnp.einsum('spkd,pdu->spku', rows_in, up_w, preferred_element_type=jnp.fl...]
    all_to_all x2, waiting for transfers between devices: 11.8 us -> 15.6 us  [expert_chunk(): lax.all_to_all(half_sum, 'blk', split_axis=0, concat_axis=0, tiled=True)]
  transfers between devices with their start and end apart: 17 -> 17, of which waited for: 11 -> 11; matrix products, arithmetic and copies ran while one was open for 32% -> 24% of each run, Pallas kernels for 0% -> 0%
where the time goes in v7:
time: 207 us; the launch traced here: 205 us
  waiting for transfers between devices  91 us (44%)
  starting transfers between devices  37.3 us (18%)
  matrix products  29.3 us (14%)
  other arithmetic  24.8 us (12%)
  local copies, waits for them, and re-layouts  21.1 us (10%)
    ppermute x2, waiting for transfers between devices, expert_chunk(): lax.ppermute(pair_sum, 'kv', flip_chip).astype(jnp.float32)  29.4 us
    all_to_all x1, waiting for transfers between devices, per_device(): lax.all_to_all(jnp.broadcast_to(attended[None], (blk_count,) + attended.s...  15.8 us
    all_to_all x2, waiting for transfers between devices, expert_chunk(): lax.all_to_all(half_sum, 'blk', split_axis=0, concat_axis=0, tiled=True)  15.6 us
    all_to_all x1, waiting for transfers between devices, per_device(): lax.all_to_all(column_part, 'blk', split_axis=0, concat_axis=1, tiled=True)  9.85 us
    all_to_all x2, starting transfers between devices, expert_chunk(): lax.all_to_all(half_sum, 'blk', split_axis=0, concat_axis=0, tiled=True)  9.61 us
    all_to_all x2, waiting for transfers between devices, expert_chunk(): lax.all_to_all(chunk_rows, 'blk', split_axis=0, concat_axis=0, tiled=True)  9.41 us
    dot_general x2, matrix products, expert_chunk(): jnp.einsum('spkd,pdu->spku', rows_in, up_w, preferred_element_type=jnp.fl...  9.4 us
    dot_general x2, matrix products, expert_chunk(): jnp.einsum('spkd,pdu->spku', rows_in, gate_w, preferred_element_type=jnp....  9.4 us
  transfers between devices with their start and end apart: 17, of which 11 were waited for; matrix products, arithmetic and copies ran while one was open for 24% of the time, Pallas kernels for 0%

profile of v7, /device:TPU:0, one launch (start us, length us, event | category | flops | bytes accessed | tf_op | source)
XLA Modules:
  0.0 205.5 jit_solution(17188765904113002392)
XLA Ops:
  14.9 7.3 %all-to-all-start = ((bf16[8,2,16,2,128]{4,2,3,1,0:T(8,128)(2,1)}), bf16[8,2,16,2,128]{4,2,3,1,0:T(8,128)(2,1)S(1)}, u32[]{:S(2)}, u32[]{:S(2)}) async-start(bf16[8,2,16,2,128]{4,2,3,1,0:T(8,128)(2,1)} %copy.139), calls=%async_computation | async-start | bytes 262144 | tf_op jit(solution)/shard_map/all_to_all | solution.py:119
  23.6 6.0 %all-to-all-done = bf16[8,2,16,2,128]{4,2,3,1,0:T(8,128)(2,1)S(1)} async-done(((bf16[8,2,16,2,128]{4,2,3,1,0:T(8,128)(2,1)}), bf16[8,2,16,2,128]{4,2,3,1,0:T(8,128)(2,1)S(1)}, u32[]{:S(2)}, u32[]{:S(2)}) %all-to-all-start) | async-done | bytes 131104 | tf_op jit(solution)/shard_map/all_to_all | solution.py:119
  31.3 3.9 %all-to-all-start.1 = ((bf16[8,64,640]{2,1,0:T(8,128)(2,1)}), bf16[8,64,640]{2,1,0:T(8,128)(2,1)S(1)}, u32[]{:S(2)}, u32[]{:S(2)}) async-start(bf16[8,64,640]{2,1,0:T(8,128)(2,1)} %broadcast_in_dim.169), calls=%async_computation.1 | async-start | bytes 1310720 | tf_op jit(solution)/shard_map/all_to_all | solution.py:149
  35.6 15.8 %all-to-all-done.1 = bf16[8,64,640]{2,1,0:T(8,128)(2,1)S(1)} async-done(((bf16[8,64,640]{2,1,0:T(8,128)(2,1)}), bf16[8,64,640]{2,1,0:T(8,128)(2,1)S(1)}, u32[]{:S(2)}, u32[]{:S(2)}) %all-to-all-start.1) | async-done | bytes 655392 | tf_op jit(solution)/shard_map/all_to_all | solution.py:149
  52.7 3.6 %all-to-all-start.2 = ((bf16[8,64,320]{2,1,0:T(8,128)(2,1)}), bf16[8,64,320]{2,1,0:T(8,128)(2,1)S(1)}, u32[]{:S(2)}, u32[]{:S(2)}) async-start(bf16[8,64,320]{2,1,0:T(8,128)(2,1)} %bitcast.22), calls=%async_computation.2 | async-start | bytes 786432 | tf_op jit(solution)/shard_map/all_to_all | solution.py:155
  57.7 9.8 %all-to-all-done.2 = bf16[8,64,320]{2,1,0:T(8,128)(2,1)S(1)} async-done(((bf16[8,64,320]{2,1,0:T(8,128)(2,1)}), bf16[8,64,320]{2,1,0:T(8,128)(2,1)S(1)}, u32[]{:S(2)}, u32[]{:S(2)}) %all-to-all-start.2) | async-done | bytes 327712 | tf_op jit(solution)/shard_map/all_to_all | solution.py:155
  69.9 3.9 %scatter_custom_fusion.2 = s32[512]{0:T(512)S(1)} fusion(s32[384]{0:T(512)S(1)} %get-tuple-element.175, s32[384]{0:T(512)S(1)} %iota_add_fusion, s32[]{:T(128)} %constant.182.clone.1), kind=kCustom, calls=%fused_computation.202 | custom fusion | flops 384 | bytes 2052 | tf_op jit(solution)/shard_map/scatter-add | solution.py:218
  78.4 2.7 %collective-permute-done.3 = f32[64,65]{1,0:T(8,128)S(1)} collective-permute-done((f32[64,65]{1,0:T(8,128)S(1)}, f32[64,65]{1,0:T(8,128)S(1)}, u32[]{:S(2)}, u32[]{:S(2)}) %collective-permute-start.3) | collective-permute-done | bytes 16672 | tf_op jit(solution)/shard_map/ppermute | solution.py:190
  84.4 3.6 %all-to-all-start.3 = ((bf16[8,4,8,640]{3,2,1,0:T(8,128)(2,1)}), bf16[8,4,8,640]{3,2,1,0:T(8,128)(2,1)S(1)}, u32[]{:S(2)}, u32[]{:S(2)}) async-start(bf16[8,4,8,640]{3,2,1,0:T(8,128)(2,1)} %get-tuple-element.200), calls=%async_computation.3 | async-start | bytes 655360 | tf_op jit(solution)/shard_map/all_to_all | solution.py:243
  88.2 9.4 %all-to-all-done.3 = bf16[8,4,8,640]{3,2,1,0:T(8,128)(2,1)S(1)} async-done(((bf16[8,4,8,640]{3,2,1,0:T(8,128)(2,1)}), bf16[8,4,8,640]{3,2,1,0:T(8,128)(2,1)S(1)}, u32[]{:S(2)}, u32[]{:S(2)}) %all-to-all-start.3) | async-done | bytes 327712 | tf_op jit(solution)/shard_map/all_to_all | solution.py:243
  97.6 3.6 %all-to-all-start.5 = ((bf16[8,4,8,640]{3,2,1,0:T(8,128)(2,1)}), bf16[8,4,8,640]{3,2,1,0:T(8,128)(2,1)S(1)}, u32[]{:S(2)}, u32[]{:S(2)}) async-start(bf16[8,4,8,640]{3,2,1,0:T(8,128)(2,1)} %get-tuple-element.201), calls=%async_computation.5 | async-start | bytes 655360 | tf_op jit(solution)/shard_map/all_to_all | solution.py:243
  101.3 4.7 %fusion.49 = bf16[8,8,8,1,768]{4,2,0,1,3:T(8,128)(2,1)S(1)} fusion(bf16[8,8,8,640]{3,2,0,1:T(8,128)(2,1)S(1)} %bitcast.206, bf16[16,640,768]{2,1,0:T(8,128)(2,1)} %param.32), kind=kOutput, calls=%fused_computation.70 | convolution fusion | flops 503709696 | bytes 9306112 | tf_op jit(solution)/shard_map/spkd,pdu->spku/dot_general | solution.py:252
  106.0 4.7 %fusion.52 = bf16[8,8,8,1,768]{4,2,0,1,3:T(8,128)(2,1)S(1)} fusion(bf16[8,8,8,640]{3,2,0,1:T(8,128)(2,1)S(1)} %bitcast.207, bf16[16,640,768]{2,1,0:T(8,128)(2,1)} %param.31), kind=kOutput, calls=%fused_computation.71 | convolution fusion | flops 503709696 | bytes 9306112 | tf_op jit(solution)/shard_map/spkd,pdu->spku/dot_general | solution.py:251
  111.8 4.7 %fusion.43 = bf16[8,8,8,1,768]{4,2,0,1,3:T(8,128)(2,1)S(1)} fusion(bf16[8,8,8,640]{3,2,0,1:T(8,128)(2,1)S(1)} %bitcast.208, bf16[16,640,768]{2,1,0:T(8,128)(2,1)} %param.32), kind=kOutput, calls=%fused_computation.68 | convolution fusion | flops 503709696 | bytes 9306112 | tf_op jit(solution)/shard_map/spkd,pdu->spku/dot_general | solution.py:252
  116.5 4.7 %fusion.46 = bf16[8,8,8,1,768]{4,2,0,1,3:T(8,128)(2,1)S(1)} fusion(bf16[8,8,8,640]{3,2,0,1:T(8,128)(2,1)S(1)} %bitcast.209, bf16[16,640,768]{2,1,0:T(8,128)(2,1)} %param.31), kind=kOutput, calls=%fused_computation.69 | convolution fusion | flops 503709696 | bytes 9306112 | tf_op jit(solution)/shard_map/spkd,pdu->spku/dot_general | solution.py:251
  124.9 2.2 %add_convert_fusion.1 = bf16[4,8,8,2,768]{4,2,0,1,3:T(8,128)(2,1)} fusion(bf16[4,8,8,2,768]{4,2,0,1,3:T(8,128)(2,1)} %collective-permute-done.4, s32[]{:T(128)S(6)} %select_n.194, bf16[8,8,8,1,768]{4,2,0,1,3:T(8,128)(2,1)S(1)} %fusion.52, bf16[8,8,8,1,768]{4,2,0,1,3:T(8,128)(2,1)S(1)} %fusion.49), kind=kLoop, calls=%fused_computation.60 | loop fusion | flops 1966080 | bytes 3145732 | tf_op jit(solution)/shard_map/convert_element_type | solution.py:258
  132.2 15.5 %collective-permute-done.5 = bf16[4,8,8,2,768]{4,2,0,1,3:T(8,128)(2,1)} collective-permute-done((bf16[4,8,8,2,768]{4,2,0,1,3:T(8,128)(2,1)}, bf16[4,8,8,2,768]{4,2,0,1,3:T(8,128)(2,1)}, u32[]{:S(2)}, u32[]{:S(2)}) %collective-permute-start.5) | collective-permute-done | bytes 786464 | tf_op jit(solution)/shard_map/ppermute | solution.py:259
  149.8 13.9 %collective-permute-done.8 = bf16[4,8,8,2,768]{4,2,0,1,3:T(8,128)(2,1)} collective-permute-done((bf16[4,8,8,2,768]{4,2,0,1,3:T(8,128)(2,1)}, bf16[4,8,8,2,768]{4,2,0,1,3:T(8,128)(2,1)}, u32[]{:S(2)}, u32[]{:S(2)}) %collective-permute-start.8) | collective-permute-done | bytes 786464 | tf_op jit(solution)/shard_map/ppermute | solution.py:259
  165.7 4.6 %bitcast_reduce_fusion.1 = bf16[8,4,8,640]{3,2,0,1:T(8,128)(2,1)S(1)} fusion(bf16[16,768,640]{2,1,0:T(8,128)(2,1)} %param.33, bf16[4,8,8,768]{3,2,0,1:T(8,128)(2,1)S(1)} %collective-permute-done.6, bf16[4,8,8,768]{3,2,0,1:T(8,128)(2,1)S(1)} %fusion.63, pred[]{:T(512)S(6)} %eq.109), kind=kOutput, calls=%fused_computation.105 | convolution fusion | flops 504987648 | bytes 8978433 | tf_op jit(solution)/shard_map/spku,pud->spkd/dot_general | solution.py:267
  171.1 6.0 %all-to-all-start.4 = ((bf16[8,4,8,640]{3,2,1,0:T(8,128)(2,1)}), bf16[8,4,8,640]{3,2,1,0:T(8,128)(2,1)S(1)}, u32[]{:S(2)}, u32[]{:S(2)}) async-start(bf16[8,4,8,640]{3,2,1,0:T(8,128)(2,1)} %copy.151), calls=%async_computation.4 | async-start | bytes 655360 | tf_op jit(solution)/shard_map/all_to_all | solution.py:273
  177.1 4.6 %bitcast_reduce_fusion = bf16[8,4,8,640]{3,2,0,1:T(8,128)(2,1)S(1)} fusion(bf16[16,768,640]{2,1,0:T(8,128)(2,1)} %param.33, bf16[4,8,8,768]{3,2,0,1:T(8,128)(2,1)S(1)} %collective-permute-done.9, bf16[4,8,8,768]{3,2,0,1:T(8,128)(2,1)S(1)} %fusion.61, pred[]{:T(512)S(6)} %eq.109), kind=kOutput, calls=%fused_computation.104 | convolution fusion | flops 504987648 | bytes 8978433 | tf_op jit(solution)/shard_map/spku,pud->spkd/dot_general | solution.py:267
  182.4 5.6 %all-to-all-done.4 = bf16[8,4,8,640]{3,2,1,0:T(8,128)(2,1)S(1)} async-done(((bf16[8,4,8,640]{3,2,1,0:T(8,128)(2,1)}), bf16[8,4,8,640]{3,2,1,0:T(8,128)(2,1)S(1)}, u32[]{:S(2)}, u32[]{:S(2)}) %all-to-all-start.4) | async-done | bytes 327712 | tf_op jit(solution)/shard_map/all_to_all | solution.py:273
  188.0 3.6 %all-to-all-start.6 = ((bf16[8,4,8,640]{3,2,1,0:T(8,128)(2,1)}), bf16[8,4,8,640]{3,2,1,0:T(8,128)(2,1)S(1)}, u32[]{:S(2)}, u32[]{:S(2)}) async-start(bf16[8,4,8,640]{3,2,1,0:T(8,128)(2,1)} %copy.153), calls=%async_computation.6 | async-start | bytes 655360 | tf_op jit(solution)/shard_map/all_to_all | solution.py:273
  192.1 10.0 %all-to-all-done.6 = bf16[8,4,8,640]{3,2,1,0:T(8,128)(2,1)S(1)} async-done(((bf16[8,4,8,640]{3,2,1,0:T(8,128)(2,1)}), bf16[8,4,8,640]{3,2,1,0:T(8,128)(2,1)S(1)}, u32[]{:S(2)}, u32[]{:S(2)}) %all-to-all-start.6) | async-done | bytes 327712 | tf_op jit(solution)/shard_map/all_to_all | solution.py:273
  (169 shorter events, 48.9 us)
Async XLA Ops:
  0.6 50.7 %copy-start = (bf16[640,320]{0,1:T(8,128)(2,1)S(1)}, bf16[640,320]{0,1:T(8,128)(2,1)}, u32[]{:S(2)}) copy-start(bf16[640,320]{0,1:T(8,128)(2,1)} %param.27) | copy-start | bytes 1228804
  0.6 22.2 %copy-start.3 = (bf16[64,1,2,128]{3,2,1,0:T(2,128)(2,1)S(1)}, bf16[64,1,2,128]{3,2,1,0:T(2,128)(2,1)}, u32[]{:S(2)}) copy-start(bf16[64,1,2,128]{3,2,1,0:T(2,128)(2,1)} %param.20) | copy-start | bytes 98308
  0.7 22.3 %copy-start.4 = (bf16[64,640]{1,0:T(8,128)(2,1)S(1)}, bf16[64,640]{1,0:T(8,128)(2,1)}, u32[]{:S(2)}) copy-start(bf16[64,640]{1,0:T(8,128)(2,1)} %param.19) | copy-start | bytes 245764
  14.9 14.6 %all-to-all-start = ((bf16[8,2,16,2,128]{4,2,3,1,0:T(8,128)(2,1)}), bf16[8,2,16,2,128]{4,2,3,1,0:T(8,128)(2,1)S(1)}, u32[]{:S(2)}, u32[]{:S(2)}) async-start(bf16[8,2,16,2,128]{4,2,3,1,0:T(8,128)(2,1)} %copy.139), calls=%async_computation | async-start | bytes 262144 | tf_op jit(solution)/shard_map/all_to_all | solution.py:119
  30.2 5.0 %copy-start.6 = (s32[64,6]{0,1:T(8,128)S(1)}, s32[64,6]{0,1:T(8,128)}, u32[]{:S(2)}) copy-start(s32[64,6]{0,1:T(8,128)} %param.30) | copy-start | bytes 4612
  31.3 20.1 %all-to-all-start.1 = ((bf16[8,64,640]{2,1,0:T(8,128)(2,1)}), bf16[8,64,640]{2,1,0:T(8,128)(2,1)S(1)}, u32[]{:S(2)}, u32[]{:S(2)}) async-start(bf16[8,64,640]{2,1,0:T(8,128)(2,1)} %broadcast_in_dim.169), calls=%async_computation.1 | async-start | bytes 1310720 | tf_op jit(solution)/shard_map/all_to_all | solution.py:149
  52.7 14.8 %all-to-all-start.2 = ((bf16[8,64,320]{2,1,0:T(8,128)(2,1)}), bf16[8,64,320]{2,1,0:T(8,128)(2,1)S(1)}, u32[]{:S(2)}, u32[]{:S(2)}) async-start(bf16[8,64,320]{2,1,0:T(8,128)(2,1)} %bitcast.22), calls=%async_computation.2 | async-start | bytes 786432 | tf_op jit(solution)/shard_map/all_to_all | solution.py:155
  56.4 17.6 %copy-start.9 = (bf16[640]{0:T(1024)(128)(2,1)S(1)}, bf16[640]{0:T(1024)(128)(2,1)}, u32[]{:S(2)}) copy-start(bf16[640]{0:T(1024)(128)(2,1)} %param.28) | copy-start | bytes 3844
  56.4 18.9 %copy-start.5 = (bf16[64,640]{1,0:T(8,128)(2,1)S(1)}, bf16[64,640]{1,0:T(8,128)(2,1)}, u32[]{:S(2)}) copy-start(bf16[64,640]{1,0:T(8,128)(2,1)} %param.18) | copy-start | bytes 245764
  67.6 7.9 %copy-start.2 = (f32[640,64]{0,1:T(8,128)S(1)}, f32[640,64]{0,1:T(8,128)}, u32[]{:S(2)}) copy-start(f32[640,64]{0,1:T(8,128)} %param.29) | copy-start | bytes 491524
  68.1 5.7 %collective-permute-start = (bf16[64,1280]{1,0:T(8,128)(2,1)S(1)}, bf16[64,1280]{1,0:T(8,128)(2,1)S(1)}, u32[]{:S(2)}, u32[]{:S(2)}) collective-permute-start(bf16[64,1280]{1,0:T(8,128)(2,1)S(1)} %constant_dynamic-slice_fusion), channel_id=1, source_target_pairs={{0,16},{8,24},{16,0},{24,8},{1,17},{9,25},{17,1},{25,9},{2,18},{10... | collective-permute-start | bytes 491528 | tf_op jit(solution)/shard_map/ppermute | solution.py:165
  73.9 1.3 collective-permute-start.1
  75.9 1.2 collective-permute-start.2
  77.2 3.9 %collective-permute-start.3 = (f32[64,65]{1,0:T(8,128)S(1)}, f32[64,65]{1,0:T(8,128)S(1)}, u32[]{:S(2)}, u32[]{:S(2)}) collective-permute-start(f32[64,65]{1,0:T(8,128)S(1)} %fusion.139), channel_id=1, source_target_pairs={{0,16},{8,24},{16,0},{24,8},{1,17},{9,25},{17,1},{25,9},{2,18},{10... | collective-permute-start | bytes 49928 | tf_op jit(solution)/shard_map/ppermute | solution.py:190
  84.4 13.1 %all-to-all-start.3 = ((bf16[8,4,8,640]{3,2,1,0:T(8,128)(2,1)}), bf16[8,4,8,640]{3,2,1,0:T(8,128)(2,1)S(1)}, u32[]{:S(2)}, u32[]{:S(2)}) async-start(bf16[8,4,8,640]{3,2,1,0:T(8,128)(2,1)} %get-tuple-element.200), calls=%async_computation.3 | async-start | bytes 655360 | tf_op jit(solution)/shard_map/all_to_all | solution.py:243
  97.6 14.1 %all-to-all-start.5 = ((bf16[8,4,8,640]{3,2,1,0:T(8,128)(2,1)}), bf16[8,4,8,640]{3,2,1,0:T(8,128)(2,1)S(1)}, u32[]{:S(2)}, u32[]{:S(2)}) async-start(bf16[8,4,8,640]{3,2,1,0:T(8,128)(2,1)} %get-tuple-element.201), calls=%async_computation.5 | async-start | bytes 655360 | tf_op jit(solution)/shard_map/all_to_all | solution.py:243
  111.7 13.2 %collective-permute-start.4 = (bf16[4,8,8,2,768]{4,2,0,1,3:T(8,128)(2,1)}, bf16[4,8,8,2,768]{4,2,0,1,3:T(8,128)(2,1)}, u32[]{:S(2)}, u32[]{:S(2)}) collective-permute-start(bf16[4,8,8,2,768]{4,2,0,1,3:T(8,128)(2,1)} %fusion.58), channel_id=1, source_target_pairs={{0,8},{8,0},{16,24},{24,16},{1,9},{9,1},{17,25},{25,17},{2,10},{10... | collective-permute-start | bytes 2359304 | tf_op jit(solution)/shard_map/ppermute | solution.py:257
  122.2 6.1 %collective-permute-start.7 = (bf16[4,8,8,2,768]{4,2,0,1,3:T(8,128)(2,1)}, bf16[4,8,8,2,768]{4,2,0,1,3:T(8,128)(2,1)}, u32[]{:S(2)}, u32[]{:S(2)}) collective-permute-start(bf16[4,8,8,2,768]{4,2,0,1,3:T(8,128)(2,1)} %fusion.56), channel_id=1, source_target_pairs={{0,8},{8,0},{16,24},{24,16},{1,9},{9,1},{17,25},{25,17},{2,10},{10... | collective-permute-start | bytes 2359304 | tf_op jit(solution)/shard_map/ppermute | solution.py:257
  127.1 20.7 %collective-permute-start.5 = (bf16[4,8,8,2,768]{4,2,0,1,3:T(8,128)(2,1)}, bf16[4,8,8,2,768]{4,2,0,1,3:T(8,128)(2,1)}, u32[]{:S(2)}, u32[]{:S(2)}) collective-permute-start(bf16[4,8,8,2,768]{4,2,0,1,3:T(8,128)(2,1)} %add_convert_fusion.1), channel_id=1, source_target_pairs={{0,16},{8,24},{16,0},{24,8},{1,17},{9,25},{17,1},{25,9},{2,18},{10... | collective-permute-start | bytes 2359304 | tf_op jit(solution)/shard_map/ppermute | solution.py:259
  130.5 33.2 %collective-permute-start.8 = (bf16[4,8,8,2,768]{4,2,0,1,3:T(8,128)(2,1)}, bf16[4,8,8,2,768]{4,2,0,1,3:T(8,128)(2,1)}, u32[]{:S(2)}, u32[]{:S(2)}) collective-permute-start(bf16[4,8,8,2,768]{4,2,0,1,3:T(8,128)(2,1)} %add_convert_fusion), channel_id=1, source_target_pairs={{0,16},{8,24},{16,0},{24,8},{1,17},{9,25},{17,1},{25,9},{2,18},{10... | collective-permute-start | bytes 2359304 | tf_op jit(solution)/shard_map/ppermute | solution.py:259
  149.7 16.0 %collective-permute-start.6 = (bf16[4,8,8,768]{3,2,0,1:T(8,128)(2,1)S(1)}, bf16[4,8,8,768]{3,2,0,1:T(8,128)(2,1)S(1)}, u32[]{:S(2)}, u32[]{:S(2)}) collective-permute-start(bf16[4,8,8,768]{3,2,0,1:T(8,128)(2,1)S(1)} %fusion.63), channel_id=1, source_target_pairs={{0,8},{8,0},{16,24},{24,16},{1,9},{9,1},{17,25},{25,17},{2,10},{10... | collective-permute-start | bytes 1179656 | tf_op jit(solution)/shard_map/ppermute | solution.py:261
  165.6 11.4 %collective-permute-start.9 = (bf16[4,8,8,768]{3,2,0,1:T(8,128)(2,1)S(1)}, bf16[4,8,8,768]{3,2,0,1:T(8,128)(2,1)S(1)}, u32[]{:S(2)}, u32[]{:S(2)}) collective-permute-start(bf16[4,8,8,768]{3,2,0,1:T(8,128)(2,1)S(1)} %fusion.61), channel_id=1, source_target_pairs={{0,8},{8,0},{16,24},{24,16},{1,9},{9,1},{17,25},{25,17},{2,10},{10... | collective-permute-start | bytes 1179656 | tf_op jit(solution)/shard_map/ppermute | solution.py:261
  171.1 16.9 %all-to-all-start.4 = ((bf16[8,4,8,640]{3,2,1,0:T(8,128)(2,1)}), bf16[8,4,8,640]{3,2,1,0:T(8,128)(2,1)S(1)}, u32[]{:S(2)}, u32[]{:S(2)}) async-start(bf16[8,4,8,640]{3,2,1,0:T(8,128)(2,1)} %copy.151), calls=%async_computation.4 | async-start | bytes 655360 | tf_op jit(solution)/shard_map/all_to_all | solution.py:273
  188.0 14.1 %all-to-all-start.6 = ((bf16[8,4,8,640]{3,2,1,0:T(8,128)(2,1)}), bf16[8,4,8,640]{3,2,1,0:T(8,128)(2,1)S(1)}, u32[]{:S(2)}, u32[]{:S(2)}) async-start(bf16[8,4,8,640]{3,2,1,0:T(8,128)(2,1)} %copy.153), calls=%async_computation.6 | async-start | bytes 655360 | tf_op jit(solution)/shard_map/all_to_all | solution.py:273
  (3 other events, 9.3 us)

commit v8 on v7

--- a/solution.py
+++ b/solution.py
@@ -7,7 +7,7 @@
 
 D = 2560
 CAP = 8
-CHUNKS = 2
+CHUNKS = 1
 
 
 EPSILON = 1e-05
@@ -226,6 +226,7 @@
     paired = pieces_here % 2 == 0
     kv_count = lax.axis_size("kv")
     core_bit = lax.axis_index("kv") % 2
+    chip_bit = lax.axis_index("kv") // 2
     flip_core = [(i, i ^ 1) for i in range(kv_count)]
     flip_chip = [(i, i ^ 2) for i in range(kv_count)]
     if paired:
@@ -238,9 +239,8 @@
             (expert_count, 2, capacity, feature_part),
         ).reshape(blk_count, pieces_here, capacity, feature_part)
 
-    def expert_chunk(chunk_rows, gate_w, up_w, down_w):
+    def pair_stage(landed_rows, gate_w, up_w):
         chunk_pieces = gate_w.shape[0]
-        landed_rows = lax.all_to_all(chunk_rows, "blk", split_axis=0, concat_axis=0, tiled=True)
         if paired:
             rows_in = jnp.broadcast_to(
                 landed_rows[:, :, None],
@@ -255,9 +255,23 @@
         kept = lax.dynamic_slice_in_dim(both_parts, core_bit * half, half, 0)
         given = lax.dynamic_slice_in_dim(both_parts, (1 - core_bit) * half, half, 0)
         pair_sum = kept.astype(jnp.float32) + lax.ppermute(given, "kv", flip_core).astype(jnp.float32)
-        pair_sum = pair_sum.astype(jnp.bfloat16)
-        whole = pair_sum.astype(jnp.float32) + lax.ppermute(pair_sum, "kv", flip_chip).astype(jnp.float32)
-        hidden_half = (jax.nn.silu(whole[:, :, :, 0]) * whole[:, :, :, 1]).astype(jnp.bfloat16)
+        return pair_sum.astype(jnp.bfloat16)
+
+    def out_stage(pair_sum, down_w):
+        chunk_pieces = down_w.shape[0]
+        quarter = pair_sum.shape[0] // 2
+        chip_kept = lax.dynamic_slice_in_dim(pair_sum, chip_bit * quarter, quarter, 0)
+        chip_given = lax.dynamic_slice_in_dim(pair_sum, (1 - chip_bit) * quarter, quarter, 0)
+        whole = chip_kept.astype(jnp.float32) + lax.ppermute(
+            chip_given, "kv", flip_chip
+        ).astype(jnp.float32)
+        hidden_quarter = (jax.nn.silu(whole[:, :, :, 0]) * whole[:, :, :, 1]).astype(jnp.bfloat16)
+        hidden_far = lax.ppermute(hidden_quarter, "kv", flip_chip)
+        hidden_half = jnp.where(
+            chip_bit == 0,
+            jnp.concatenate([hidden_quarter, hidden_far], axis=0),
+            jnp.concatenate([hidden_far, hidden_quarter], axis=0),
+        )
         hidden_other = lax.ppermute(hidden_half, "kv", flip_core)
         hidden = jnp.where(
             core_bit == 0,
@@ -278,17 +292,24 @@
     chunk_count = CHUNKS if paired and experts_here % CHUNKS == 0 else 1
     chunk_experts = experts_here // chunk_count
     chunk_pieces = pieces_here // chunk_count
-    per_chunk = []
+    piece_sets = [slice(i * chunk_pieces, (i + 1) * chunk_pieces) for i in range(chunk_count)]
+    landed_sets = [
+        lax.all_to_all(
+            outgoing_rows[:, i * chunk_experts : (i + 1) * chunk_experts],
+            "blk",
+            split_axis=0,
+            concat_axis=0,
+            tiled=True,
+        )
+        for i in range(chunk_count)
+    ]
+    pair_sets = []
     for i in range(chunk_count):
-        pieces_of = slice(i * chunk_pieces, (i + 1) * chunk_pieces)
-        per_chunk.append(
-            expert_chunk(
-                outgoing_rows[:, i * chunk_experts : (i + 1) * chunk_experts],
-                w_gate[pieces_of],
-                w_up[pieces_of],
-                w_down[pieces_of],
-            )
-        )
+        landed_now = landed_sets[i]
+        if pair_sets:
+            pair_sets[-1], landed_now = lax.optimization_barrier((pair_sets[-1], landed_now))
+        pair_sets.append(pair_stage(landed_now, w_gate[piece_sets[i]], w_up[piece_sets[i]]))
+    per_chunk = [out_stage(pair_sets[i], w_down[piece_sets[i]]) for i in range(chunk_count)]
     if paired:
         per_slot = jnp.concatenate(per_chunk, axis=1).reshape(slot_total, feature_part)
     else:

time: 207 us -> 201 us (0.971)
  starting transfers between devices: 37.3 us -> 25.4 us
  waiting for transfers between devices: 91 us -> 102 us
  other arithmetic: 24.8 us -> 21.4 us
  matrix products: 29.3 us -> 26 us
    all_to_all x4 -> x2, starting transfers between devices: 16.9 us -> 7.33 us  [the longest x1 3.72 us: per_device(): lax.all_to_all(outgoing_rows[:, i * chunk_experts:(i + 1) * chunk_experts...]
    all_to_all x4 -> x2, waiting for transfers between devices: 25 us -> 30.7 us  [the longest x1 16.5 us: per_device(): lax.all_to_all(outgoing_rows[:, i * chunk_experts:(i + 1) * chunk_experts...]
    ppermute x6 -> x4, waiting for transfers between devices: 29.5 us -> 34.7 us  [the longest x1 19 us: out_stage(): lax.ppermute(chip_given, 'kv', flip_chip).astype(jnp.float32)]
    dot_general x6 -> x3, matrix products: 28 us -> 24.7 us  [the longest x1 8.3 us: pair_stage(): jnp.einsum('spkd,pdu->spku', rows_in, gate_w, preferred_element_type=jnp....]
    convert_element_type x4 -> x2, other arithmetic: 4.9 us -> 2.19 us  [the longest x1 1.96 us: pair_stage(): return pair_sum.astype(jnp.bfloat16)]
  transfers between devices with their start and end apart: 17 -> 13, of which waited for: 11 -> 12; matrix products, arithmetic and copies ran while one was open for 24% -> 5% of each run, Pallas kernels for 0% -> 0%
where the time goes in v8:
time: 201 us; the launch traced here: 200 us
  waiting for transfers between devices  102 us (51%)
  matrix products  26 us (13%)
  starting transfers between devices  25.4 us (13%)
  local copies, waits for them, and re-layouts  22.4 us (11%)
  other arithmetic  21.4 us (11%)
  between operations  2.04 us (1%)
    ppermute x1, waiting for transfers between devices, out_stage(): lax.ppermute(chip_given, 'kv', flip_chip).astype(jnp.float32)  19 us
    all_to_all x1, waiting for transfers between devices, per_device(): lax.all_to_all(outgoing_rows[:, i * chunk_experts:(i + 1) * chunk_experts...  16.5 us
    all_to_all x1, waiting for transfers between devices, per_device(): lax.all_to_all(jnp.broadcast_to(attended[None], (blk_count,) + attended.s...  15.7 us
    all_to_all x1, waiting for transfers between devices, out_stage(): lax.all_to_all(half_sum, 'blk', split_axis=0, concat_axis=0, tiled=True)  14.2 us
    all_to_all x1, waiting for transfers between devices, per_device(): lax.all_to_all(column_part, 'blk', split_axis=0, concat_axis=1, tiled=True)  9.78 us
    ppermute x1, waiting for transfers between devices, out_stage(): hidden_far = lax.ppermute(hidden_quarter, 'kv', flip_chip)  9.77 us
    dot_general x1, matrix products, pair_stage(): jnp.einsum('spkd,pdu->spku', rows_in, gate_w, preferred_element_type=jnp....  8.3 us
    dot_general x1, matrix products, pair_stage(): jnp.einsum('spkd,pdu->spku', rows_in, up_w, preferred_element_type=jnp.fl...  8.3 us
  transfers between devices with their start and end apart: 13, of which 12 were waited for; matrix products, arithmetic and copies ran while one was open for 5% of the time, Pallas kernels for 0%

profile of v8, /device:TPU:0, one launch (start us, length us, event | category | flops | bytes accessed | tf_op | source)
XLA Modules:
  0.0 199.7 jit_solution(13424411933030251894)
XLA Ops:
  7.8 1.4 and_select_fusion.1
  15.5 7.3 %all-to-all-start = ((bf16[8,2,16,2,128]{4,2,3,1,0:T(8,128)(2,1)}), bf16[8,2,16,2,128]{4,2,3,1,0:T(8,128)(2,1)S(1)}, u32[]{:S(2)}, u32[]{:S(2)}) async-start(bf16[8,2,16,2,128]{4,2,3,1,0:T(8,128)(2,1)} %copy.131), calls=%async_computation | async-start | bytes 262144 | tf_op jit(solution)/shard_map/all_to_all | solution.py:119
  24.1 6.1 %all-to-all-done = bf16[8,2,16,2,128]{4,2,3,1,0:T(8,128)(2,1)S(1)} async-done(((bf16[8,2,16,2,128]{4,2,3,1,0:T(8,128)(2,1)}), bf16[8,2,16,2,128]{4,2,3,1,0:T(8,128)(2,1)S(1)}, u32[]{:S(2)}, u32[]{:S(2)}) %all-to-all-start) | async-done | bytes 131104 | tf_op jit(solution)/shard_map/all_to_all | solution.py:119
  32.5 3.5 %all-to-all-start.1 = ((bf16[8,64,640]{2,1,0:T(8,128)(2,1)}), bf16[8,64,640]{2,1,0:T(8,128)(2,1)S(1)}, u32[]{:S(2)}, u32[]{:S(2)}) async-start(bf16[8,64,640]{2,1,0:T(8,128)(2,1)} %broadcast_in_dim.163), calls=%async_computation.1 | async-start | bytes 1310720 | tf_op jit(solution)/shard_map/all_to_all | solution.py:149
  36.5 15.7 %all-to-all-done.1 = bf16[8,64,640]{2,1,0:T(8,128)(2,1)S(1)} async-done(((bf16[8,64,640]{2,1,0:T(8,128)(2,1)}), bf16[8,64,640]{2,1,0:T(8,128)(2,1)S(1)}, u32[]{:S(2)}, u32[]{:S(2)}) %all-to-all-start.1) | async-done | bytes 655392 | tf_op jit(solution)/shard_map/all_to_all | solution.py:149
  53.5 3.6 %all-to-all-start.2 = ((bf16[8,64,320]{2,1,0:T(8,128)(2,1)}), bf16[8,64,320]{2,1,0:T(8,128)(2,1)S(1)}, u32[]{:S(2)}, u32[]{:S(2)}) async-start(bf16[8,64,320]{2,1,0:T(8,128)(2,1)} %bitcast.22), calls=%async_computation.2 | async-start | bytes 786432 | tf_op jit(solution)/shard_map/all_to_all | solution.py:155
  58.5 9.8 %all-to-all-done.2 = bf16[8,64,320]{2,1,0:T(8,128)(2,1)S(1)} async-done(((bf16[8,64,320]{2,1,0:T(8,128)(2,1)}), bf16[8,64,320]{2,1,0:T(8,128)(2,1)S(1)}, u32[]{:S(2)}, u32[]{:S(2)}) %all-to-all-start.2) | async-done | bytes 327712 | tf_op jit(solution)/shard_map/all_to_all | solution.py:155
  68.8 1.6 collective-permute-start
  71.3 3.9 %scatter_custom_fusion.2 = s32[512]{0:T(512)S(1)} fusion(s32[384]{0:T(512)S(1)} %get-tuple-element.175, s32[384]{0:T(512)S(1)} %iota_add_fusion, s32[]{:T(128)} %constant.182.clone.1), kind=kCustom, calls=%fused_computation.166 | custom fusion | flops 384 | bytes 2052 | tf_op jit(solution)/shard_map/scatter-add | solution.py:218
  79.2 3.3 %collective-permute-done.3 = f32[64,65]{1,0:T(8,128)S(1)} collective-permute-done((f32[64,65]{1,0:T(8,128)S(1)}, f32[64,65]{1,0:T(8,128)S(1)}, u32[]{:S(2)}, u32[]{:S(2)}) %collective-permute-start.3) | collective-permute-done | bytes 16672 | tf_op jit(solution)/shard_map/ppermute | solution.py:190
  83.2 2.0 %gather_fusion.8 = bf16[512,640]{1,0:T(8,128)(2,1)S(1)} fusion(bf16[64,640]{1,0:T(8,128)(2,1)S(1)} %fusion.41, s32[1024]{0:T(1024)S(1)} %pad_clamp_fusion.1), kind=kCustom, calls=%fused_computation.8 | custom fusion | bytes 1312768 | tf_op jit(solution)/shard_map/gather | solution.py:221
  86.3 3.7 %all-to-all-start.3 = ((bf16[8,8,8,640]{3,2,1,0:T(8,128)(2,1)}), bf16[8,8,8,640]{3,2,1,0:T(8,128)(2,1)S(1)}, u32[]{:S(2)}, u32[]{:S(2)}) async-start(bf16[8,8,8,640]{3,2,1,0:T(8,128)(2,1)} %broadcast_select_fusion), calls=%async_computation.3 | async-start | bytes 1310720 | tf_op jit(solution)/shard_map/all_to_all | solution.py:297
  90.0 16.5 %all-to-all-done.3 = bf16[8,8,8,640]{3,2,1,0:T(8,128)(2,1)S(1)} async-done(((bf16[8,8,8,640]{3,2,1,0:T(8,128)(2,1)}), bf16[8,8,8,640]{3,2,1,0:T(8,128)(2,1)S(1)}, u32[]{:S(2)}, u32[]{:S(2)}) %all-to-all-start.3) | async-done | bytes 655392 | tf_op jit(solution)/shard_map/all_to_all | solution.py:297
  106.8 8.3 %fusion.30 = bf16[8,16,8,1,768]{4,2,0,1,3:T(8,128)(2,1)S(1)} fusion(bf16[8,16,8,640]{3,2,0,1:T(8,128)(2,1)S(1)} %bitcast.147, bf16[16,640,768]{2,1,0:T(8,128)(2,1)} %param.32), kind=kOutput, calls=%fused_computation.55 | convolution fusion | flops 1007419392 | bytes 18612224 | tf_op jit(solution)/shard_map/spkd,pdu->spku/dot_general | solution.py:252
  115.1 8.3 %fusion.33 = bf16[8,16,8,1,768]{4,2,0,1,3:T(8,128)(2,1)S(1)} fusion(bf16[8,16,8,640]{3,2,0,1:T(8,128)(2,1)S(1)} %bitcast.148, bf16[16,640,768]{2,1,0:T(8,128)(2,1)} %param.31), kind=kOutput, calls=%fused_computation.56 | convolution fusion | flops 1007419392 | bytes 18612224 | tf_op jit(solution)/shard_map/spkd,pdu->spku/dot_general | solution.py:251
  124.7 3.7 %collective-permute-done.4 = bf16[4,16,8,2,768]{4,2,0,1,3:T(8,128)(2,1)} collective-permute-done((bf16[4,16,8,2,768]{4,2,0,1,3:T(8,128)(2,1)}, bf16[4,16,8,2,768]{4,2,0,1,3:T(8,128)(2,1)}, u32[]{:S(2)}, u32[]{:S(2)}) %collective-permute-start.4) | collective-permute-done | bytes 1572896 | tf_op jit(solution)/shard_map/ppermute | solution.py:257
  128.5 2.0 add_convert_fusion
  132.3 19.0 %collective-permute-done.5 = bf16[2,16,8,2,768]{4,2,0,1,3:T(8,128)(2,1)S(1)} collective-permute-done((bf16[2,16,8,2,768]{4,2,0,1,3:T(8,128)(2,1)S(1)}, bf16[2,16,8,2,768]{4,2,0,1,3:T(8,128)(2,1)S(1)}, u32[]{:S(2)}, u32[]{:S(2)}) %collective-permute-start.5) | collective-permute-done | bytes 786464 | tf_op jit(solution)/shard_map/ppermute | solution.py:265
  153.5 9.8 %collective-permute-done.6 = bf16[2,16,8,768]{3,2,0,1:T(8,128)(2,1)S(1)} collective-permute-done((bf16[2,16,8,768]{3,2,0,1:T(8,128)(2,1)S(1)}, bf16[2,16,8,768]{3,2,0,1:T(8,128)(2,1)S(1)}, u32[]{:S(2)}, u32[]{:S(2)}) %collective-permute-start.6) | collective-permute-done | bytes 393248 | tf_op jit(solution)/shard_map/ppermute | solution.py:269
  163.6 2.1 %collective-permute-done.7 = bf16[4,16,8,768]{3,2,0,1:T(8,128)(2,1)S(1)} collective-permute-done((bf16[4,16,8,768]{3,2,0,1:T(8,128)(2,1)S(1)}, bf16[4,16,8,768]{3,2,0,1:T(8,128)(2,1)S(1)}, u32[]{:S(2)}, u32[]{:S(2)}) %collective-permute-start.7) | collective-permute-done | bytes 786464 | tf_op jit(solution)/shard_map/ppermute | solution.py:275
  165.7 8.1 %bitcast_reduce_fusion = bf16[8,8,8,640]{3,2,0,1:T(8,128)(2,1)S(1)} fusion(bf16[16,768,640]{2,1,0:T(8,128)(2,1)} %param.33, bf16[4,16,8,768]{3,2,0,1:T(8,128)(2,1)S(1)} %collective-permute-done.7, bf16[4,16,8,768]{3,2,0,1:T(8,128)(2,1)S(1)} %maximum_select_fusion.2, pred[]{:T(512)S(6)} %eq.111), kind=kOutput, calls=%fused_computation.57 | convolution fusion | flops 1009975296 | bytes 17956864 | tf_op jit(solution)/shard_map/spku,pud->spkd/dot_general | solution.py:281
  174.8 3.6 %all-to-all-start.4 = ((bf16[8,8,8,640]{3,2,1,0:T(8,128)(2,1)}), bf16[8,8,8,640]{3,2,1,0:T(8,128)(2,1)S(1)}, u32[]{:S(2)}, u32[]{:S(2)}) async-start(bf16[8,8,8,640]{3,2,1,0:T(8,128)(2,1)} %copy.143), calls=%async_computation.4 | async-start | bytes 1310720 | tf_op jit(solution)/shard_map/all_to_all | solution.py:287
  181.9 14.2 %all-to-all-done.4 = bf16[8,8,8,640]{3,2,1,0:T(8,128)(2,1)S(1)} async-done(((bf16[8,8,8,640]{3,2,1,0:T(8,128)(2,1)}), bf16[8,8,8,640]{3,2,1,0:T(8,128)(2,1)S(1)}, u32[]{:S(2)}, u32[]{:S(2)}) %all-to-all-start.4) | async-done | bytes 655392 | tf_op jit(solution)/shard_map/all_to_all | solution.py:287
  196.3 1.9 gather_fusion.9
  (173 shorter events, 38.4 us)
Async XLA Ops:
  0.6 51.5 %copy-start = (bf16[640,320]{0,1:T(8,128)(2,1)S(1)}, bf16[640,320]{0,1:T(8,128)(2,1)}, u32[]{:S(2)}) copy-start(bf16[640,320]{0,1:T(8,128)(2,1)} %param.27) | copy-start | bytes 1228804
  0.6 22.7 %copy-start.9 = (bf16[64,1,2,128]{3,2,1,0:T(2,128)(2,1)S(1)}, bf16[64,1,2,128]{3,2,1,0:T(2,128)(2,1)}, u32[]{:S(2)}) copy-start(bf16[64,1,2,128]{3,2,1,0:T(2,128)(2,1)} %param.20) | copy-start | bytes 98308
  0.7 22.8 %copy-start.10 = (bf16[64,640]{1,0:T(8,128)(2,1)S(1)}, bf16[64,640]{1,0:T(8,128)(2,1)}, u32[]{:S(2)}) copy-start(bf16[64,640]{1,0:T(8,128)(2,1)} %param.19) | copy-start | bytes 245764
  15.5 14.6 %all-to-all-start = ((bf16[8,2,16,2,128]{4,2,3,1,0:T(8,128)(2,1)}), bf16[8,2,16,2,128]{4,2,3,1,0:T(8,128)(2,1)S(1)}, u32[]{:S(2)}, u32[]{:S(2)}) async-start(bf16[8,2,16,2,128]{4,2,3,1,0:T(8,128)(2,1)} %copy.131), calls=%async_computation | async-start | bytes 262144 | tf_op jit(solution)/shard_map/all_to_all | solution.py:119
  32.5 19.7 %all-to-all-start.1 = ((bf16[8,64,640]{2,1,0:T(8,128)(2,1)}), bf16[8,64,640]{2,1,0:T(8,128)(2,1)S(1)}, u32[]{:S(2)}, u32[]{:S(2)}) async-start(bf16[8,64,640]{2,1,0:T(8,128)(2,1)} %broadcast_in_dim.163), calls=%async_computation.1 | async-start | bytes 1310720 | tf_op jit(solution)/shard_map/all_to_all | solution.py:149
  53.5 14.7 %all-to-all-start.2 = ((bf16[8,64,320]{2,1,0:T(8,128)(2,1)}), bf16[8,64,320]{2,1,0:T(8,128)(2,1)S(1)}, u32[]{:S(2)}, u32[]{:S(2)}) async-start(bf16[8,64,320]{2,1,0:T(8,128)(2,1)} %bitcast.22), calls=%async_computation.2 | async-start | bytes 786432 | tf_op jit(solution)/shard_map/all_to_all | solution.py:155
  57.2 18.2 %copy-start.20 = (bf16[640]{0:T(1024)(128)(2,1)S(1)}, bf16[640]{0:T(1024)(128)(2,1)}, u32[]{:S(2)}) copy-start(bf16[640]{0:T(1024)(128)(2,1)} %param.28) | copy-start | bytes 3844
  57.2 19.4 %copy-start.11 = (bf16[64,640]{1,0:T(8,128)(2,1)S(1)}, bf16[64,640]{1,0:T(8,128)(2,1)}, u32[]{:S(2)}) copy-start(bf16[64,640]{1,0:T(8,128)(2,1)} %param.18) | copy-start | bytes 245764
  68.3 8.5 %copy-start.8 = (f32[640,64]{0,1:T(8,128)S(1)}, f32[640,64]{0,1:T(8,128)}, u32[]{:S(2)}) copy-start(f32[640,64]{0,1:T(8,128)} %param.29) | copy-start | bytes 491524
  68.8 6.3 %collective-permute-start = (bf16[64,1280]{1,0:T(8,128)(2,1)S(1)}, bf16[64,1280]{1,0:T(8,128)(2,1)S(1)}, u32[]{:S(2)}, u32[]{:S(2)}) collective-permute-start(bf16[64,1280]{1,0:T(8,128)(2,1)S(1)} %constant_dynamic-slice_fusion.1), channel_id=1, source_target_pairs={{0,16},{8,24},{16,0},{24,8},{1,17},{9,25},{17,1},{25,9},{2,18},{10... | collective-permute-start | bytes 491528 | tf_op jit(solution)/shard_map/ppermute | solution.py:165
  75.2 1.3 collective-permute-start.1
  76.7 8.6 %copy-start.3 = (bf16[64,640]{1,0:T(8,128)(2,1)}, bf16[64,640]{1,0:T(8,128)(2,1)S(1)}, u32[]{:S(2)}) copy-start(bf16[64,640]{1,0:T(8,128)(2,1)S(1)} %get-tuple-element.195) | copy-start | bytes 245764
  77.2 1.2 collective-permute-start.2
  78.5 3.9 %collective-permute-start.3 = (f32[64,65]{1,0:T(8,128)S(1)}, f32[64,65]{1,0:T(8,128)S(1)}, u32[]{:S(2)}, u32[]{:S(2)}) collective-permute-start(f32[64,65]{1,0:T(8,128)S(1)} %fusion.96), channel_id=1, source_target_pairs={{0,16},{8,24},{16,0},{24,8},{1,17},{9,25},{17,1},{25,9},{2,18},{10... | collective-permute-start | bytes 49928 | tf_op jit(solution)/shard_map/ppermute | solution.py:190
  86.3 20.3 %all-to-all-start.3 = ((bf16[8,8,8,640]{3,2,1,0:T(8,128)(2,1)}), bf16[8,8,8,640]{3,2,1,0:T(8,128)(2,1)S(1)}, u32[]{:S(2)}, u32[]{:S(2)}) async-start(bf16[8,8,8,640]{3,2,1,0:T(8,128)(2,1)} %broadcast_select_fusion), calls=%async_computation.3 | async-start | bytes 1310720 | tf_op jit(solution)/shard_map/all_to_all | solution.py:297
  124.7 3.8 %collective-permute-start.4 = (bf16[4,16,8,2,768]{4,2,0,1,3:T(8,128)(2,1)}, bf16[4,16,8,2,768]{4,2,0,1,3:T(8,128)(2,1)}, u32[]{:S(2)}, u32[]{:S(2)}) collective-permute-start(bf16[4,16,8,2,768]{4,2,0,1,3:T(8,128)(2,1)} %fusion.22), channel_id=1, source_target_pairs={{0,8},{8,0},{16,24},{24,16},{1,9},{9,1},{17,25},{25,17},{2,10},{10... | collective-permute-start | bytes 4718600 | tf_op jit(solution)/shard_map/ppermute | solution.py:257
  131.6 19.6 %collective-permute-start.5 = (bf16[2,16,8,2,768]{4,2,0,1,3:T(8,128)(2,1)S(1)}, bf16[2,16,8,2,768]{4,2,0,1,3:T(8,128)(2,1)S(1)}, u32[]{:S(2)}, u32[]{:S(2)}) collective-permute-start(bf16[2,16,8,2,768]{4,2,0,1,3:T(8,128)(2,1)S(1)} %constant_dynamic-slice_fusion), channel_id=1, source_target_pairs={{0,16},{8,24},{16,0},{24,8},{1,17},{9,25},{17,1},{25,9},{2,18},{10... | collective-permute-start | bytes 2359304 | tf_op jit(solution)/shard_map/ppermute | solution.py:265
  152.7 10.8 %copy-start.16 = (s32[8,12]{1,0:T(8,128)S(1)}, s32[8,12]{1,0:T(8,128)}, u32[]{:S(2)}) copy-start(s32[8,12]{1,0:T(8,128)} %param.26) | copy-start | bytes 1156
  152.7 10.9 %copy-start.14 = (s32[8,12]{1,0:T(8,128)S(1)}, s32[8,12]{1,0:T(8,128)}, u32[]{:S(2)}) copy-start(s32[8,12]{1,0:T(8,128)} %param.25) | copy-start | bytes 1156
  152.9 10.4 %collective-permute-start.6 = (bf16[2,16,8,768]{3,2,0,1:T(8,128)(2,1)S(1)}, bf16[2,16,8,768]{3,2,0,1:T(8,128)(2,1)S(1)}, u32[]{:S(2)}, u32[]{:S(2)}) collective-permute-start(bf16[2,16,8,768]{3,2,0,1:T(8,128)(2,1)S(1)} %fusion.38), channel_id=1, source_target_pairs={{0,16},{8,24},{16,0},{24,8},{1,17},{9,25},{17,1},{25,9},{2,18},{10... | collective-permute-start | bytes 1179656 | tf_op jit(solution)/shard_map/ppermute | solution.py:269
  163.4 2.4 %collective-permute-start.7 = (bf16[4,16,8,768]{3,2,0,1:T(8,128)(2,1)S(1)}, bf16[4,16,8,768]{3,2,0,1:T(8,128)(2,1)S(1)}, u32[]{:S(2)}, u32[]{:S(2)}) collective-permute-start(bf16[4,16,8,768]{3,2,0,1:T(8,128)(2,1)S(1)} %maximum_select_fusion.2), channel_id=1, source_target_pairs={{0,8},{8,0},{16,24},{24,16},{1,9},{9,1},{17,25},{25,17},{2,10},{10... | collective-permute-start | bytes 2359304 | tf_op jit(solution)/shard_map/ppermute | solution.py:275
  173.9 7.6 %copy-start.6 = (f32[64,65]{1,0:T(8,128)S(1)}, f32[64,65]{1,0:T(8,128)}, u32[]{:S(2)}) copy-start(f32[64,65]{1,0:T(8,128)} %copy-done.5) | copy-start | bytes 49924
  173.9 7.7 %copy-start.13 = (s32[64,6]{0,1:T(8,128)S(1)}, s32[64,6]{0,1:T(8,128)}, u32[]{:S(2)}) copy-start(s32[64,6]{0,1:T(8,128)} %param.30) | copy-start | bytes 4612
  174.8 21.3 %all-to-all-start.4 = ((bf16[8,8,8,640]{3,2,1,0:T(8,128)(2,1)}), bf16[8,8,8,640]{3,2,1,0:T(8,128)(2,1)S(1)}, u32[]{:S(2)}, u32[]{:S(2)}) async-start(bf16[8,8,8,640]{3,2,1,0:T(8,128)(2,1)} %copy.143), calls=%async_computation.4 | async-start | bytes 1310720 | tf_op jit(solution)/shard_map/all_to_all | solution.py:287
  (10 other events, 36.6 us)

commit v9 on v8

--- a/solution.py
+++ b/solution.py
@@ -7,7 +7,7 @@
 
 D = 2560
 CAP = 8
-CHUNKS = 1
+CHUNKS = 2
 
 
 EPSILON = 1e-05
@@ -257,11 +257,14 @@
         pair_sum = kept.astype(jnp.float32) + lax.ppermute(given, "kv", flip_core).astype(jnp.float32)
         return pair_sum.astype(jnp.bfloat16)
 
-    def out_stage(pair_sum, down_w):
-        chunk_pieces = down_w.shape[0]
+    def chip_split(pair_sum):
         quarter = pair_sum.shape[0] // 2
         chip_kept = lax.dynamic_slice_in_dim(pair_sum, chip_bit * quarter, quarter, 0)
         chip_given = lax.dynamic_slice_in_dim(pair_sum, (1 - chip_bit) * quarter, quarter, 0)
+        return chip_kept, chip_given
+
+    def out_stage(chip_kept, chip_given, down_w):
+        chunk_pieces = down_w.shape[0]
         whole = chip_kept.astype(jnp.float32) + lax.ppermute(
             chip_given, "kv", flip_chip
         ).astype(jnp.float32)
@@ -293,23 +296,20 @@
     chunk_experts = experts_here // chunk_count
     chunk_pieces = pieces_here // chunk_count
     piece_sets = [slice(i * chunk_pieces, (i + 1) * chunk_pieces) for i in range(chunk_count)]
-    landed_sets = [
-        lax.all_to_all(
-            outgoing_rows[:, i * chunk_experts : (i + 1) * chunk_experts],
-            "blk",
-            split_axis=0,
-            concat_axis=0,
-            tiled=True,
-        )
+    split_sets = []
+    for i in range(chunk_count):
+        rows_now = outgoing_rows[:, i * chunk_experts : (i + 1) * chunk_experts]
+        if split_sets:
+            last_kept, last_given = split_sets[-1]
+            last_given, rows_now = lax.optimization_barrier((last_given, rows_now))
+            split_sets[-1] = (last_kept, last_given)
+        landed_now = lax.all_to_all(rows_now, "blk", split_axis=0, concat_axis=0, tiled=True)
+        pair_now = pair_stage(landed_now, w_gate[piece_sets[i]], w_up[piece_sets[i]])
+        split_sets.append(chip_split(pair_now))
+    per_chunk = [
+        out_stage(split_sets[i][0], split_sets[i][1], w_down[piece_sets[i]])
         for i in range(chunk_count)
     ]
-    pair_sets = []
-    for i in range(chunk_count):
-        landed_now = landed_sets[i]
-        if pair_sets:
-            pair_sets[-1], landed_now = lax.optimization_barrier((pair_sets[-1], landed_now))
-        pair_sets.append(pair_stage(landed_now, w_gate[piece_sets[i]], w_up[piece_sets[i]]))
-    per_chunk = [out_stage(pair_sets[i], w_down[piece_sets[i]]) for i in range(chunk_count)]
     if paired:
         per_slot = jnp.concatenate(per_chunk, axis=1).reshape(slot_total, feature_part)
     else:

time: 201 us -> 203 us (level)
  waiting for transfers between devices: 102 us -> 90.4 us
  starting transfers between devices: 25.4 us -> 36.8 us
  matrix products: 26 us -> 29.3 us
    ppermute x1 -> x2, waiting for transfers between devices: 19 us -> 0.01 us  [out_stage(): lax.ppermute(chip_given, 'kv', flip_chip).astype(jnp.float32)]
    ppermute x1 -> x2, waiting for transfers between devices: 9.77 us -> 18.7 us  [out_stage(): hidden_far = lax.ppermute(hidden_quarter, 'kv', flip_chip)]
    all_to_all x1 -> x2, starting transfers between devices: 3.61 us -> 7.24 us  [out_stage(): lax.all_to_all(half_sum, 'blk', split_axis=0, concat_axis=0, tiled=True)]
    all_to_all x1 -> x2, starting transfers between devices: 3.72 us -> 7.26 us  [per_device(): lax.all_to_all(rows_now, 'blk', split_axis=0, concat_axis=0, tiled=True)]
    all_to_all x1 -> x2, waiting for transfers between devices: 16.5 us -> 18.8 us  [per_device(): lax.all_to_all(rows_now, 'blk', split_axis=0, concat_axis=0, tiled=True)]
    ppermute x1 -> x2, waiting for transfers between devices: 2.1 us -> 0.01 us  [out_stage(): hidden_other = lax.ppermute(hidden_half, 'kv', flip_core)]
    all_to_all x1 -> x2, waiting for transfers between devices: 14.2 us -> 15.6 us  [out_stage(): lax.all_to_all(half_sum, 'blk', split_axis=0, concat_axis=0, tiled=True)]
    dot_general x1 -> x2, matrix products: 8.3 us -> 9.43 us  [pair_stage(): jnp.einsum('spkd,pdu->spku', rows_in, gate_w, preferred_element_type=jnp....]
  transfers between devices with their start and end apart: 13 -> 19, of which waited for: 12 -> 13; matrix products, arithmetic and copies ran while one was open for 5% -> 17% of each run, Pallas kernels for 0% -> 0%
where the time goes in v9:
time: 203 us; the launch traced here: 201 us
  waiting for transfers between devices  90.4 us (45%)
  starting transfers between devices  36.8 us (18%)
  matrix products  29.3 us (14%)
  local copies, waits for them, and re-layouts  22.8 us (11%)
  other arithmetic  19.9 us (10%)
  between operations  2.11 us (1%)
    all_to_all x2, waiting for transfers between devices, per_device(): lax.all_to_all(rows_now, 'blk', split_axis=0, concat_axis=0, tiled=True)  18.8 us
    ppermute x2, waiting for transfers between devices, out_stage(): hidden_far = lax.ppermute(hidden_quarter, 'kv', flip_chip)  18.7 us
    all_to_all x1, waiting for transfers between devices, per_device(): lax.all_to_all(jnp.broadcast_to(attended[None], (blk_count,) + attended.s...  15.8 us
    all_to_all x2, waiting for transfers between devices, out_stage(): lax.all_to_all(half_sum, 'blk', split_axis=0, concat_axis=0, tiled=True)  15.6 us
    all_to_all x1, waiting for transfers between devices, per_device(): lax.all_to_all(column_part, 'blk', split_axis=0, concat_axis=1, tiled=True)  9.82 us
    dot_general x2, matrix products, pair_stage(): jnp.einsum('spkd,pdu->spku', rows_in, gate_w, preferred_element_type=jnp....  9.43 us
    dot_general x2, matrix products, pair_stage(): jnp.einsum('spkd,pdu->spku', rows_in, up_w, preferred_element_type=jnp.fl...  9.42 us
    dot_general x2, matrix products, out_stage(): jnp.einsum('spku,pud->spkd', hidden, down_w, preferred_element_type=jnp.f...  9.18 us
  transfers between devices with their start and end apart: 19, of which 13 were waited for; matrix products, arithmetic and copies ran while one was open for 17% of the time, Pallas kernels for 0%

profile of v9, /device:TPU:0, one launch (start us, length us, event | category | flops | bytes accessed | tf_op | source)
XLA Modules:
  0.0 201.3 jit_solution(9622124190654022374)
XLA Ops:
  14.9 7.3 %all-to-all-start = ((bf16[8,2,16,2,128]{4,2,3,1,0:T(8,128)(2,1)}), bf16[8,2,16,2,128]{4,2,3,1,0:T(8,128)(2,1)S(1)}, u32[]{:S(2)}, u32[]{:S(2)}) async-start(bf16[8,2,16,2,128]{4,2,3,1,0:T(8,128)(2,1)} %copy.139), calls=%async_computation | async-start | bytes 262144 | tf_op jit(solution)/shard_map/all_to_all | solution.py:119
  25.2 4.4 %all-to-all-done = bf16[8,2,16,2,128]{4,2,3,1,0:T(8,128)(2,1)S(1)} async-done(((bf16[8,2,16,2,128]{4,2,3,1,0:T(8,128)(2,1)}), bf16[8,2,16,2,128]{4,2,3,1,0:T(8,128)(2,1)S(1)}, u32[]{:S(2)}, u32[]{:S(2)}) %all-to-all-start) | async-done | bytes 131104 | tf_op jit(solution)/shard_map/all_to_all | solution.py:119
  31.3 3.5 %all-to-all-start.1 = ((bf16[8,64,640]{2,1,0:T(8,128)(2,1)}), bf16[8,64,640]{2,1,0:T(8,128)(2,1)S(1)}, u32[]{:S(2)}, u32[]{:S(2)}) async-start(bf16[8,64,640]{2,1,0:T(8,128)(2,1)} %broadcast_in_dim.169), calls=%async_computation.1 | async-start | bytes 1310720 | tf_op jit(solution)/shard_map/all_to_all | solution.py:149
  35.2 15.8 %all-to-all-done.1 = bf16[8,64,640]{2,1,0:T(8,128)(2,1)S(1)} async-done(((bf16[8,64,640]{2,1,0:T(8,128)(2,1)}), bf16[8,64,640]{2,1,0:T(8,128)(2,1)S(1)}, u32[]{:S(2)}, u32[]{:S(2)}) %all-to-all-start.1) | async-done | bytes 655392 | tf_op jit(solution)/shard_map/all_to_all | solution.py:149
  52.4 3.6 %all-to-all-start.2 = ((bf16[8,64,320]{2,1,0:T(8,128)(2,1)}), bf16[8,64,320]{2,1,0:T(8,128)(2,1)S(1)}, u32[]{:S(2)}, u32[]{:S(2)}) async-start(bf16[8,64,320]{2,1,0:T(8,128)(2,1)} %bitcast.22), calls=%async_computation.2 | async-start | bytes 786432 | tf_op jit(solution)/shard_map/all_to_all | solution.py:155
  57.3 9.8 %all-to-all-done.2 = bf16[8,64,320]{2,1,0:T(8,128)(2,1)S(1)} async-done(((bf16[8,64,320]{2,1,0:T(8,128)(2,1)}), bf16[8,64,320]{2,1,0:T(8,128)(2,1)S(1)}, u32[]{:S(2)}, u32[]{:S(2)}) %all-to-all-start.2) | async-done | bytes 327712 | tf_op jit(solution)/shard_map/all_to_all | solution.py:155
  69.6 3.9 %scatter_custom_fusion.2 = s32[512]{0:T(512)S(1)} fusion(s32[384]{0:T(512)S(1)} %get-tuple-element.179, s32[384]{0:T(512)S(1)} %iota_add_fusion, s32[]{:T(128)} %constant.184.clone.1), kind=kCustom, calls=%fused_computation.206 | custom fusion | flops 384 | bytes 2052 | tf_op jit(solution)/shard_map/scatter-add | solution.py:218
  78.1 2.7 %collective-permute-done.3 = f32[64,65]{1,0:T(8,128)S(1)} collective-permute-done((f32[64,65]{1,0:T(8,128)S(1)}, f32[64,65]{1,0:T(8,128)S(1)}, u32[]{:S(2)}, u32[]{:S(2)}) %collective-permute-start.3) | collective-permute-done | bytes 16672 | tf_op jit(solution)/shard_map/ppermute | solution.py:190
  84.1 3.6 %all-to-all-start.3 = ((bf16[8,4,8,640]{3,2,1,0:T(8,128)(2,1)}), bf16[8,4,8,640]{3,2,1,0:T(8,128)(2,1)S(1)}, u32[]{:S(2)}, u32[]{:S(2)}) async-start(bf16[8,4,8,640]{3,2,1,0:T(8,128)(2,1)} %get-tuple-element.205), calls=%async_computation.3 | async-start | bytes 655360 | tf_op jit(solution)/shard_map/all_to_all | solution.py:306
  87.7 9.5 %all-to-all-done.3 = bf16[8,4,8,640]{3,2,1,0:T(8,128)(2,1)S(1)} async-done(((bf16[8,4,8,640]{3,2,1,0:T(8,128)(2,1)}), bf16[8,4,8,640]{3,2,1,0:T(8,128)(2,1)S(1)}, u32[]{:S(2)}, u32[]{:S(2)}) %all-to-all-start.3) | async-done | bytes 327712 | tf_op jit(solution)/shard_map/all_to_all | solution.py:306
  97.3 4.7 %fusion.49 = bf16[8,8,8,1,768]{4,2,0,1,3:T(8,128)(2,1)S(1)} fusion(bf16[8,8,8,640]{3,2,0,1:T(8,128)(2,1)S(1)} %bitcast.206, bf16[16,640,768]{2,1,0:T(8,128)(2,1)} %param.32), kind=kOutput, calls=%fused_computation.68 | convolution fusion | flops 503709696 | bytes 9306112 | tf_op jit(solution)/shard_map/spkd,pdu->spku/dot_general | solution.py:252
  102.0 4.7 %fusion.52 = bf16[8,8,8,1,768]{4,2,0,1,3:T(8,128)(2,1)S(1)} fusion(bf16[8,8,8,640]{3,2,0,1:T(8,128)(2,1)S(1)} %bitcast.207, bf16[16,640,768]{2,1,0:T(8,128)(2,1)} %param.31), kind=kOutput, calls=%fused_computation.69 | convolution fusion | flops 503709696 | bytes 9306112 | tf_op jit(solution)/shard_map/spkd,pdu->spku/dot_general | solution.py:251
  110.8 3.6 %all-to-all-start.5 = ((bf16[8,4,8,640]{3,2,1,0:T(8,128)(2,1)}), bf16[8,4,8,640]{3,2,1,0:T(8,128)(2,1)S(1)}, u32[]{:S(2)}, u32[]{:S(2)}) async-start(bf16[8,4,8,640]{3,2,1,0:T(8,128)(2,1)} %get-tuple-element.113), calls=%async_computation.5 | async-start | bytes 655360 | tf_op jit(solution)/shard_map/all_to_all | solution.py:306
  115.7 9.3 %all-to-all-done.5 = bf16[8,4,8,640]{3,2,1,0:T(8,128)(2,1)S(1)} async-done(((bf16[8,4,8,640]{3,2,1,0:T(8,128)(2,1)}), bf16[8,4,8,640]{3,2,1,0:T(8,128)(2,1)S(1)}, u32[]{:S(2)}, u32[]{:S(2)}) %all-to-all-start.5) | async-done | bytes 327712 | tf_op jit(solution)/shard_map/all_to_all | solution.py:306
  125.1 4.7 %fusion.43 = bf16[8,8,8,1,768]{4,2,0,1,3:T(8,128)(2,1)S(1)} fusion(bf16[8,8,8,640]{3,2,0,1:T(8,128)(2,1)S(1)} %bitcast.208, bf16[16,640,768]{2,1,0:T(8,128)(2,1)} %param.32), kind=kOutput, calls=%fused_computation.66 | convolution fusion | flops 503709696 | bytes 9306112 | tf_op jit(solution)/shard_map/spkd,pdu->spku/dot_general | solution.py:252
  129.8 4.7 %fusion.46 = bf16[8,8,8,1,768]{4,2,0,1,3:T(8,128)(2,1)S(1)} fusion(bf16[8,8,8,640]{3,2,0,1:T(8,128)(2,1)S(1)} %bitcast.209, bf16[16,640,768]{2,1,0:T(8,128)(2,1)} %param.31), kind=kOutput, calls=%fused_computation.67 | convolution fusion | flops 503709696 | bytes 9306112 | tf_op jit(solution)/shard_map/spkd,pdu->spku/dot_general | solution.py:251
  142.6 13.4 %collective-permute-done.6 = bf16[2,8,8,768]{3,2,0,1:T(8,128)(2,1)S(1)} collective-permute-done((bf16[2,8,8,768]{3,2,0,1:T(8,128)(2,1)S(1)}, bf16[2,8,8,768]{3,2,0,1:T(8,128)(2,1)S(1)}, u32[]{:S(2)}, u32[]{:S(2)}) %collective-permute-start.6) | collective-permute-done | bytes 196640 | tf_op jit(solution)/shard_map/ppermute | solution.py:272
  158.5 5.3 %collective-permute-done.10 = bf16[2,8,8,768]{3,2,0,1:T(8,128)(2,1)S(1)} collective-permute-done((bf16[2,8,8,768]{3,2,0,1:T(8,128)(2,1)S(1)}, bf16[2,8,8,768]{3,2,0,1:T(8,128)(2,1)S(1)}, u32[]{:S(2)}, u32[]{:S(2)}) %collective-permute-start.10) | collective-permute-done | bytes 196640 | tf_op jit(solution)/shard_map/ppermute | solution.py:272
  163.9 4.6 %bitcast_reduce_fusion.1 = bf16[8,4,8,640]{3,2,0,1:T(8,128)(2,1)S(1)} fusion(bf16[16,768,640]{2,1,0:T(8,128)(2,1)} %param.33, bf16[4,8,8,768]{3,2,0,1:T(8,128)(2,1)S(1)} %collective-permute-done.7, bf16[4,8,8,768]{3,2,0,1:T(8,128)(2,1)S(1)} %maximum_select_fusion.4, pred[]{:T(512)S(6)} %eq.113), kind=kOutput, calls=%fused_computation.97 | convolution fusion | flops 504987648 | bytes 8978433 | tf_op jit(solution)/shard_map/spku,pud->spkd/dot_general | solution.py:284
  169.3 3.6 %all-to-all-start.4 = ((bf16[8,4,8,640]{3,2,1,0:T(8,128)(2,1)}), bf16[8,4,8,640]{3,2,1,0:T(8,128)(2,1)S(1)}, u32[]{:S(2)}, u32[]{:S(2)}) async-start(bf16[8,4,8,640]{3,2,1,0:T(8,128)(2,1)} %copy.151), calls=%async_computation.4 | async-start | bytes 655360 | tf_op jit(solution)/shard_map/all_to_all | solution.py:290
  172.9 4.6 %bitcast_reduce_fusion = bf16[8,4,8,640]{3,2,0,1:T(8,128)(2,1)S(1)} fusion(bf16[16,768,640]{2,1,0:T(8,128)(2,1)} %param.33, bf16[4,8,8,768]{3,2,0,1:T(8,128)(2,1)S(1)} %collective-permute-done.11, bf16[4,8,8,768]{3,2,0,1:T(8,128)(2,1)S(1)} %maximum_select_fusion.5, pred[]{:T(512)S(6)} %eq.113), kind=kOutput, calls=%fused_computation.96 | convolution fusion | flops 504987648 | bytes 8978433 | tf_op jit(solution)/shard_map/spku,pud->spkd/dot_general | solution.py:284
  178.2 5.6 %all-to-all-done.4 = bf16[8,4,8,640]{3,2,1,0:T(8,128)(2,1)S(1)} async-done(((bf16[8,4,8,640]{3,2,1,0:T(8,128)(2,1)}), bf16[8,4,8,640]{3,2,1,0:T(8,128)(2,1)S(1)}, u32[]{:S(2)}, u32[]{:S(2)}) %all-to-all-start.4) | async-done | bytes 327712 | tf_op jit(solution)/shard_map/all_to_all | solution.py:290
  183.8 3.6 %all-to-all-start.6 = ((bf16[8,4,8,640]{3,2,1,0:T(8,128)(2,1)}), bf16[8,4,8,640]{3,2,1,0:T(8,128)(2,1)S(1)}, u32[]{:S(2)}, u32[]{:S(2)}) async-start(bf16[8,4,8,640]{3,2,1,0:T(8,128)(2,1)} %copy.153), calls=%async_computation.6 | async-start | bytes 655360 | tf_op jit(solution)/shard_map/all_to_all | solution.py:290
  187.9 10.0 %all-to-all-done.6 = bf16[8,4,8,640]{3,2,1,0:T(8,128)(2,1)S(1)} async-done(((bf16[8,4,8,640]{3,2,1,0:T(8,128)(2,1)}), bf16[8,4,8,640]{3,2,1,0:T(8,128)(2,1)S(1)}, u32[]{:S(2)}, u32[]{:S(2)}) %all-to-all-start.6) | async-done | bytes 327712 | tf_op jit(solution)/shard_map/all_to_all | solution.py:290
  (173 shorter events, 52.6 us)
Async XLA Ops:
  0.6 50.4 %copy-start = (bf16[640,320]{0,1:T(8,128)(2,1)S(1)}, bf16[640,320]{0,1:T(8,128)(2,1)}, u32[]{:S(2)}) copy-start(bf16[640,320]{0,1:T(8,128)(2,1)} %param.27) | copy-start | bytes 1228804
  0.6 34.2 %copy-start.4 = (s32[64,6]{0,1:T(8,128)S(1)}, s32[64,6]{0,1:T(8,128)}, u32[]{:S(2)}) copy-start(s32[64,6]{0,1:T(8,128)} %param.30) | copy-start | bytes 4612
  14.9 14.6 %all-to-all-start = ((bf16[8,2,16,2,128]{4,2,3,1,0:T(8,128)(2,1)}), bf16[8,2,16,2,128]{4,2,3,1,0:T(8,128)(2,1)S(1)}, u32[]{:S(2)}, u32[]{:S(2)}) async-start(bf16[8,2,16,2,128]{4,2,3,1,0:T(8,128)(2,1)} %copy.139), calls=%async_computation | async-start | bytes 262144 | tf_op jit(solution)/shard_map/all_to_all | solution.py:119
  25.0 48.7 %copy-start.7 = (bf16[640]{0:T(1024)(128)(2,1)S(1)}, bf16[640]{0:T(1024)(128)(2,1)}, u32[]{:S(2)}) copy-start(bf16[640]{0:T(1024)(128)(2,1)} %param.28) | copy-start | bytes 3844
  25.0 49.9 %copy-start.3 = (bf16[64,640]{1,0:T(8,128)(2,1)S(1)}, bf16[64,640]{1,0:T(8,128)(2,1)}, u32[]{:S(2)}) copy-start(bf16[64,640]{1,0:T(8,128)(2,1)} %param.18) | copy-start | bytes 245764
  29.6 45.6 %copy-start.2 = (f32[640,64]{0,1:T(8,128)S(1)}, f32[640,64]{0,1:T(8,128)}, u32[]{:S(2)}) copy-start(f32[640,64]{0,1:T(8,128)} %param.29) | copy-start | bytes 491524
  31.3 19.7 %all-to-all-start.1 = ((bf16[8,64,640]{2,1,0:T(8,128)(2,1)}), bf16[8,64,640]{2,1,0:T(8,128)(2,1)S(1)}, u32[]{:S(2)}, u32[]{:S(2)}) async-start(bf16[8,64,640]{2,1,0:T(8,128)(2,1)} %broadcast_in_dim.169), calls=%async_computation.1 | async-start | bytes 1310720 | tf_op jit(solution)/shard_map/all_to_all | solution.py:149
  52.4 14.8 %all-to-all-start.2 = ((bf16[8,64,320]{2,1,0:T(8,128)(2,1)}), bf16[8,64,320]{2,1,0:T(8,128)(2,1)S(1)}, u32[]{:S(2)}, u32[]{:S(2)}) async-start(bf16[8,64,320]{2,1,0:T(8,128)(2,1)} %bitcast.22), calls=%async_computation.2 | async-start | bytes 786432 | tf_op jit(solution)/shard_map/all_to_all | solution.py:155
  67.7 5.8 %collective-permute-start = (bf16[64,1280]{1,0:T(8,128)(2,1)S(1)}, bf16[64,1280]{1,0:T(8,128)(2,1)S(1)}, u32[]{:S(2)}, u32[]{:S(2)}) collective-permute-start(bf16[64,1280]{1,0:T(8,128)(2,1)S(1)} %constant_dynamic-slice_fusion.2), channel_id=1, source_target_pairs={{0,16},{8,24},{16,0},{24,8},{1,17},{9,25},{17,1},{25,9},{2,18},{10... | collective-permute-start | bytes 491528 | tf_op jit(solution)/shard_map/ppermute | solution.py:165
  73.6 1.3 collective-permute-start.1
  75.5 1.2 collective-permute-start.2
  76.8 3.9 %collective-permute-start.3 = (f32[64,65]{1,0:T(8,128)S(1)}, f32[64,65]{1,0:T(8,128)S(1)}, u32[]{:S(2)}, u32[]{:S(2)}) collective-permute-start(f32[64,65]{1,0:T(8,128)S(1)} %fusion.139), channel_id=1, source_target_pairs={{0,16},{8,24},{16,0},{24,8},{1,17},{9,25},{17,1},{25,9},{2,18},{10... | collective-permute-start | bytes 49928 | tf_op jit(solution)/shard_map/ppermute | solution.py:190
  84.1 13.1 %all-to-all-start.3 = ((bf16[8,4,8,640]{3,2,1,0:T(8,128)(2,1)}), bf16[8,4,8,640]{3,2,1,0:T(8,128)(2,1)S(1)}, u32[]{:S(2)}, u32[]{:S(2)}) async-start(bf16[8,4,8,640]{3,2,1,0:T(8,128)(2,1)} %get-tuple-element.205), calls=%async_computation.3 | async-start | bytes 655360 | tf_op jit(solution)/shard_map/all_to_all | solution.py:306
  106.8 2.5 %collective-permute-start.4 = (bf16[4,8,8,2,768]{4,2,0,1,3:T(8,128)(2,1)S(1)}, bf16[4,8,8,2,768]{4,2,0,1,3:T(8,128)(2,1)}, u32[]{:S(2)}, u32[]{:S(2)}) collective-permute-start(bf16[4,8,8,2,768]{4,2,0,1,3:T(8,128)(2,1)S(1)} %fusion.58), channel_id=1, source_target_pairs={{0,8},{8,0},{16,24},{24,16},{1,9},{9,1},{17,25},{25,17},{2,10},{10... | collective-permute-start | bytes 2359304 | tf_op jit(solution)/shard_map/ppermute | solution.py:257
  110.8 14.2 %all-to-all-start.5 = ((bf16[8,4,8,640]{3,2,1,0:T(8,128)(2,1)}), bf16[8,4,8,640]{3,2,1,0:T(8,128)(2,1)S(1)}, u32[]{:S(2)}, u32[]{:S(2)}) async-start(bf16[8,4,8,640]{3,2,1,0:T(8,128)(2,1)} %get-tuple-element.113), calls=%async_computation.5 | async-start | bytes 655360 | tf_op jit(solution)/shard_map/all_to_all | solution.py:306
  114.5 23.2 %collective-permute-start.5 = (bf16[2,8,8,2,768]{4,2,0,1,3:T(8,128)(2,1)S(1)}, bf16[2,8,8,2,768]{4,2,0,1,3:T(8,128)(2,1)}, u32[]{:S(2)}, u32[]{:S(2)}) collective-permute-start(bf16[2,8,8,2,768]{4,2,0,1,3:T(8,128)(2,1)S(1)} %constant_dynamic-slice_fusion.1), channel_id=1, source_target_pairs={{0,16},{8,24},{16,0},{24,8},{1,17},{9,25},{17,1},{25,9},{2,18},{10... | collective-permute-start | bytes 1179656 | tf_op jit(solution)/shard_map/ppermute | solution.py:268
  135.5 3.3 %collective-permute-start.8 = (bf16[4,8,8,2,768]{4,2,0,1,3:T(8,128)(2,1)}, bf16[4,8,8,2,768]{4,2,0,1,3:T(8,128)(2,1)}, u32[]{:S(2)}, u32[]{:S(2)}) collective-permute-start(bf16[4,8,8,2,768]{4,2,0,1,3:T(8,128)(2,1)} %fusion.56), channel_id=1, source_target_pairs={{0,8},{8,0},{16,24},{24,16},{1,9},{9,1},{17,25},{25,17},{2,10},{10... | collective-permute-start | bytes 2359304 | tf_op jit(solution)/shard_map/ppermute | solution.py:257
  140.2 15.9 %collective-permute-start.9 = (bf16[2,8,8,2,768]{4,2,0,1,3:T(8,128)(2,1)S(1)}, bf16[2,8,8,2,768]{4,2,0,1,3:T(8,128)(2,1)S(1)}, u32[]{:S(2)}, u32[]{:S(2)}) collective-permute-start(bf16[2,8,8,2,768]{4,2,0,1,3:T(8,128)(2,1)S(1)} %constant_dynamic-slice_fusion), channel_id=1, source_target_pairs={{0,16},{8,24},{16,0},{24,8},{1,17},{9,25},{17,1},{25,9},{2,18},{10... | collective-permute-start | bytes 1179656 | tf_op jit(solution)/shard_map/ppermute | solution.py:268
  141.6 14.4 %collective-permute-start.6 = (bf16[2,8,8,768]{3,2,0,1:T(8,128)(2,1)S(1)}, bf16[2,8,8,768]{3,2,0,1:T(8,128)(2,1)S(1)}, u32[]{:S(2)}, u32[]{:S(2)}) collective-permute-start(bf16[2,8,8,768]{3,2,0,1:T(8,128)(2,1)S(1)} %fusion.75), channel_id=1, source_target_pairs={{0,16},{8,24},{16,0},{24,8},{1,17},{9,25},{17,1},{25,9},{2,18},{10... | collective-permute-start | bytes 589832 | tf_op jit(solution)/shard_map/ppermute | solution.py:272
  156.1 7.8 %collective-permute-start.7 = (bf16[4,8,8,768]{3,2,0,1:T(8,128)(2,1)S(1)}, bf16[4,8,8,768]{3,2,0,1:T(8,128)(2,1)S(1)}, u32[]{:S(2)}, u32[]{:S(2)}) collective-permute-start(bf16[4,8,8,768]{3,2,0,1:T(8,128)(2,1)S(1)} %maximum_select_fusion.4), channel_id=1, source_target_pairs={{0,8},{8,0},{16,24},{24,16},{1,9},{9,1},{17,25},{25,17},{2,10},{10... | collective-permute-start | bytes 1179656 | tf_op jit(solution)/shard_map/ppermute | solution.py:278
  156.4 7.4 %collective-permute-start.10 = (bf16[2,8,8,768]{3,2,0,1:T(8,128)(2,1)S(1)}, bf16[2,8,8,768]{3,2,0,1:T(8,128)(2,1)S(1)}, u32[]{:S(2)}, u32[]{:S(2)}) collective-permute-start(bf16[2,8,8,768]{3,2,0,1:T(8,128)(2,1)S(1)} %fusion.73), channel_id=1, source_target_pairs={{0,16},{8,24},{16,0},{24,8},{1,17},{9,25},{17,1},{25,9},{2,18},{10... | collective-permute-start | bytes 589832 | tf_op jit(solution)/shard_map/ppermute | solution.py:272
  163.8 9.1 %collective-permute-start.11 = (bf16[4,8,8,768]{3,2,0,1:T(8,128)(2,1)S(1)}, bf16[4,8,8,768]{3,2,0,1:T(8,128)(2,1)S(1)}, u32[]{:S(2)}, u32[]{:S(2)}) collective-permute-start(bf16[4,8,8,768]{3,2,0,1:T(8,128)(2,1)S(1)} %maximum_select_fusion.5), channel_id=1, source_target_pairs={{0,8},{8,0},{16,24},{24,16},{1,9},{9,1},{17,25},{25,17},{2,10},{10... | collective-permute-start | bytes 1179656 | tf_op jit(solution)/shard_map/ppermute | solution.py:278
  169.3 14.6 %all-to-all-start.4 = ((bf16[8,4,8,640]{3,2,1,0:T(8,128)(2,1)}), bf16[8,4,8,640]{3,2,1,0:T(8,128)(2,1)S(1)}, u32[]{:S(2)}, u32[]{:S(2)}) async-start(bf16[8,4,8,640]{3,2,1,0:T(8,128)(2,1)} %copy.151), calls=%async_computation.4 | async-start | bytes 655360 | tf_op jit(solution)/shard_map/all_to_all | solution.py:290
  183.8 14.1 %all-to-all-start.6 = ((bf16[8,4,8,640]{3,2,1,0:T(8,128)(2,1)}), bf16[8,4,8,640]{3,2,1,0:T(8,128)(2,1)S(1)}, u32[]{:S(2)}, u32[]{:S(2)}) async-start(bf16[8,4,8,640]{3,2,1,0:T(8,128)(2,1)} %copy.153), calls=%async_computation.6 | async-start | bytes 655360 | tf_op jit(solution)/shard_map/all_to_all | solution.py:290
  (3 other events, 31.7 us)

commit v10 on v8

--- a/solution.py
+++ b/solution.py
@@ -116,11 +116,19 @@
     source_request = jnp.zeros_like(devices) + own_index
     match_here = (block_holder[devices] == own_index) & in_use[devices]
     outgoing = pool_rows[jnp.sum(jnp.where(match_here, block_slot[devices], 0), axis=1)]
+    block_shape = sending.shape[1:]
     both_blocks = lax.all_to_all(
-        jnp.stack([sending, outgoing], axis=1), "blk", split_axis=0, concat_axis=0, tiled=True
-    )
-    landed = both_blocks[:, 0]
-    arrived = both_blocks[:, 1]
+        jnp.stack(
+            [sending.reshape(blk_count, -1, head_dim), outgoing.reshape(blk_count, -1, head_dim)],
+            axis=1,
+        ),
+        "blk",
+        split_axis=0,
+        concat_axis=0,
+        tiled=True,
+    )
+    landed = both_blocks[:, 0].reshape((blk_count,) + block_shape)
+    arrived = both_blocks[:, 1].reshape((blk_count,) + block_shape)
     present = jnp.any(
         (block_holder[source_request] == devices[:, None]) & in_use[source_request], axis=1
     )

time: 201 us -> 201 us (level)
    unnamed x47 -> x44, local copies, waits for them, and re-layouts: 3.7 us -> 4.35 us
  transfers between devices with their start and end apart: 13 -> 13, of which waited for: 12 -> 12; matrix products, arithmetic and copies ran while one was open for 5% -> 6% of each run, Pallas kernels for 0% -> 0%
where the time goes in v10:
time: 201 us; the launch traced here: 200 us
  waiting for transfers between devices  101 us (50%)
  matrix products  26 us (13%)
  starting transfers between devices  25.7 us (13%)
  other arithmetic  22.9 us (11%)
  local copies, waits for them, and re-layouts  22.8 us (11%)
    ppermute x1, waiting for transfers between devices, out_stage(): lax.ppermute(chip_given, 'kv', flip_chip).astype(jnp.float32)  19 us
    all_to_all x1, waiting for transfers between devices, per_device(): lax.all_to_all(outgoing_rows[:, i * chunk_experts:(i + 1) * chunk_experts...  16.5 us
    all_to_all x1, waiting for transfers between devices, per_device(): lax.all_to_all(jnp.broadcast_to(attended[None], (blk_count,) + attended.s...  15.8 us
    all_to_all x1, waiting for transfers between devices, out_stage(): lax.all_to_all(half_sum, 'blk', split_axis=0, concat_axis=0, tiled=True)  14.3 us
    all_to_all x1, waiting for transfers between devices, per_device(): lax.all_to_all(column_part, 'blk', split_axis=0, concat_axis=1, tiled=True)  9.85 us
    ppermute x1, waiting for transfers between devices, out_stage(): hidden_far = lax.ppermute(hidden_quarter, 'kv', flip_chip)  9.77 us
    dot_general x1, matrix products, pair_stage(): jnp.einsum('spkd,pdu->spku', rows_in, gate_w, preferred_element_type=jnp....  8.3 us
    dot_general x1, matrix products, pair_stage(): jnp.einsum('spkd,pdu->spku', rows_in, up_w, preferred_element_type=jnp.fl...  8.3 us
  transfers between devices with their start and end apart: 13, of which 12 were waited for; matrix products, arithmetic and copies ran while one was open for 6% of the time, Pallas kernels for 0%

profile of v10, /device:TPU:0, one launch (start us, length us, event | category | flops | bytes accessed | tf_op | source)
XLA Modules:
  0.0 200.5 jit_solution(3158408718464588555)
XLA Ops:
  12.1 1.4 gather_fusion.6
  15.8 7.3 %all-to-all-start = ((bf16[8,2,32,128]{3,2,1,0:T(8,128)(2,1)}), bf16[8,2,32,128]{3,2,1,0:T(8,128)(2,1)S(1)}, u32[]{:S(2)}, u32[]{:S(2)}) async-start(bf16[8,2,32,128]{3,2,1,0:T(8,128)(2,1)} %pad_maximum_fusion), calls=%async_computation | async-start | bytes 262144 | tf_op jit(solution)/shard_map/all_to_all | solution.py:120
  26.0 4.5 %all-to-all-done = bf16[8,2,32,128]{3,2,1,0:T(8,128)(2,1)S(1)} async-done(((bf16[8,2,32,128]{3,2,1,0:T(8,128)(2,1)}), bf16[8,2,32,128]{3,2,1,0:T(8,128)(2,1)S(1)}, u32[]{:S(2)}, u32[]{:S(2)}) %all-to-all-start) | async-done | bytes 131104 | tf_op jit(solution)/shard_map/all_to_all | solution.py:120
  32.8 3.8 %all-to-all-start.1 = ((bf16[8,64,640]{2,1,0:T(8,128)(2,1)}), bf16[8,64,640]{2,1,0:T(8,128)(2,1)S(1)}, u32[]{:S(2)}, u32[]{:S(2)}) async-start(bf16[8,64,640]{2,1,0:T(8,128)(2,1)} %broadcast_in_dim.163), calls=%async_computation.1 | async-start | bytes 1310720 | tf_op jit(solution)/shard_map/all_to_all | solution.py:157
  37.0 15.8 %all-to-all-done.1 = bf16[8,64,640]{2,1,0:T(8,128)(2,1)S(1)} async-done(((bf16[8,64,640]{2,1,0:T(8,128)(2,1)}), bf16[8,64,640]{2,1,0:T(8,128)(2,1)S(1)}, u32[]{:S(2)}, u32[]{:S(2)}) %all-to-all-start.1) | async-done | bytes 655392 | tf_op jit(solution)/shard_map/all_to_all | solution.py:157
  54.2 3.6 %all-to-all-start.2 = ((bf16[8,64,320]{2,1,0:T(8,128)(2,1)}), bf16[8,64,320]{2,1,0:T(8,128)(2,1)S(1)}, u32[]{:S(2)}, u32[]{:S(2)}) async-start(bf16[8,64,320]{2,1,0:T(8,128)(2,1)} %bitcast.22), calls=%async_computation.2 | async-start | bytes 786432 | tf_op jit(solution)/shard_map/all_to_all | solution.py:163
  59.2 9.8 %all-to-all-done.2 = bf16[8,64,320]{2,1,0:T(8,128)(2,1)S(1)} async-done(((bf16[8,64,320]{2,1,0:T(8,128)(2,1)}), bf16[8,64,320]{2,1,0:T(8,128)(2,1)S(1)}, u32[]{:S(2)}, u32[]{:S(2)}) %all-to-all-start.2) | async-done | bytes 327712 | tf_op jit(solution)/shard_map/all_to_all | solution.py:163
  69.6 1.6 collective-permute-start
  72.0 3.9 %scatter_custom_fusion.2 = s32[512]{0:T(512)S(1)} fusion(s32[384]{0:T(512)S(1)} %get-tuple-element.165, s32[384]{0:T(512)S(1)} %iota_add_fusion, s32[]{:T(128)} %constant.182.clone.1), kind=kCustom, calls=%fused_computation.167 | custom fusion | flops 384 | bytes 2052 | tf_op jit(solution)/shard_map/scatter-add | solution.py:226
  79.9 3.3 %collective-permute-done.3 = f32[64,65]{1,0:T(8,128)S(1)} collective-permute-done((f32[64,65]{1,0:T(8,128)S(1)}, f32[64,65]{1,0:T(8,128)S(1)}, u32[]{:S(2)}, u32[]{:S(2)}) %collective-permute-start.3) | collective-permute-done | bytes 16672 | tf_op jit(solution)/shard_map/ppermute | solution.py:198
  84.0 2.0 %gather_fusion.8 = bf16[512,640]{1,0:T(8,128)(2,1)S(1)} fusion(bf16[64,640]{1,0:T(8,128)(2,1)S(1)} %fusion.41, s32[1024]{0:T(1024)S(1)} %pad_clamp_fusion.1), kind=kCustom, calls=%fused_computation.8 | custom fusion | bytes 1312768 | tf_op jit(solution)/shard_map/gather | solution.py:229
  87.0 3.7 %all-to-all-start.3 = ((bf16[8,8,8,640]{3,2,1,0:T(8,128)(2,1)}), bf16[8,8,8,640]{3,2,1,0:T(8,128)(2,1)S(1)}, u32[]{:S(2)}, u32[]{:S(2)}) async-start(bf16[8,8,8,640]{3,2,1,0:T(8,128)(2,1)} %broadcast_select_fusion), calls=%async_computation.3 | async-start | bytes 1310720 | tf_op jit(solution)/shard_map/all_to_all | solution.py:305
  90.8 16.5 %all-to-all-done.3 = bf16[8,8,8,640]{3,2,1,0:T(8,128)(2,1)S(1)} async-done(((bf16[8,8,8,640]{3,2,1,0:T(8,128)(2,1)}), bf16[8,8,8,640]{3,2,1,0:T(8,128)(2,1)S(1)}, u32[]{:S(2)}, u32[]{:S(2)}) %all-to-all-start.3) | async-done | bytes 655392 | tf_op jit(solution)/shard_map/all_to_all | solution.py:305
  107.5 8.3 %fusion.30 = bf16[8,16,8,1,768]{4,2,0,1,3:T(8,128)(2,1)S(1)} fusion(bf16[8,16,8,640]{3,2,0,1:T(8,128)(2,1)S(1)} %bitcast.146, bf16[16,640,768]{2,1,0:T(8,128)(2,1)} %param.32), kind=kOutput, calls=%fused_computation.55 | convolution fusion | flops 1007419392 | bytes 18612224 | tf_op jit(solution)/shard_map/spkd,pdu->spku/dot_general | solution.py:260
  115.8 8.3 %fusion.33 = bf16[8,16,8,1,768]{4,2,0,1,3:T(8,128)(2,1)S(1)} fusion(bf16[8,16,8,640]{3,2,0,1:T(8,128)(2,1)S(1)} %bitcast.147, bf16[16,640,768]{2,1,0:T(8,128)(2,1)} %param.31), kind=kOutput, calls=%fused_computation.56 | convolution fusion | flops 1007419392 | bytes 18612224 | tf_op jit(solution)/shard_map/spkd,pdu->spku/dot_general | solution.py:259
  125.5 3.7 %collective-permute-done.4 = bf16[4,16,8,2,768]{4,2,0,1,3:T(8,128)(2,1)} collective-permute-done((bf16[4,16,8,2,768]{4,2,0,1,3:T(8,128)(2,1)}, bf16[4,16,8,2,768]{4,2,0,1,3:T(8,128)(2,1)}, u32[]{:S(2)}, u32[]{:S(2)}) %collective-permute-start.4) | collective-permute-done | bytes 1572896 | tf_op jit(solution)/shard_map/ppermute | solution.py:265
  129.2 2.0 add_convert_fusion
  133.0 19.0 %collective-permute-done.5 = bf16[2,16,8,2,768]{4,2,0,1,3:T(8,128)(2,1)S(1)} collective-permute-done((bf16[2,16,8,2,768]{4,2,0,1,3:T(8,128)(2,1)S(1)}, bf16[2,16,8,2,768]{4,2,0,1,3:T(8,128)(2,1)S(1)}, u32[]{:S(2)}, u32[]{:S(2)}) %collective-permute-start.5) | collective-permute-done | bytes 786464 | tf_op jit(solution)/shard_map/ppermute | solution.py:273
  154.3 9.8 %collective-permute-done.6 = bf16[2,16,8,768]{3,2,0,1:T(8,128)(2,1)S(1)} collective-permute-done((bf16[2,16,8,768]{3,2,0,1:T(8,128)(2,1)S(1)}, bf16[2,16,8,768]{3,2,0,1:T(8,128)(2,1)S(1)}, u32[]{:S(2)}, u32[]{:S(2)}) %collective-permute-start.6) | collective-permute-done | bytes 393248 | tf_op jit(solution)/shard_map/ppermute | solution.py:277
  164.4 2.1 %collective-permute-done.7 = bf16[4,16,8,768]{3,2,0,1:T(8,128)(2,1)S(1)} collective-permute-done((bf16[4,16,8,768]{3,2,0,1:T(8,128)(2,1)S(1)}, bf16[4,16,8,768]{3,2,0,1:T(8,128)(2,1)S(1)}, u32[]{:S(2)}, u32[]{:S(2)}) %collective-permute-start.7) | collective-permute-done | bytes 786464 | tf_op jit(solution)/shard_map/ppermute | solution.py:283
  166.5 8.1 %bitcast_reduce_fusion = bf16[8,8,8,640]{3,2,0,1:T(8,128)(2,1)S(1)} fusion(bf16[16,768,640]{2,1,0:T(8,128)(2,1)} %param.33, bf16[4,16,8,768]{3,2,0,1:T(8,128)(2,1)S(1)} %collective-permute-done.7, bf16[4,16,8,768]{3,2,0,1:T(8,128)(2,1)S(1)} %maximum_select_fusion.2, pred[]{:T(512)S(6)} %eq.111), kind=kOutput, calls=%fused_computation.57 | convolution fusion | flops 1009975296 | bytes 17956864 | tf_op jit(solution)/shard_map/spku,pud->spkd/dot_general | solution.py:289
  175.5 3.6 %all-to-all-start.4 = ((bf16[8,8,8,640]{3,2,1,0:T(8,128)(2,1)}), bf16[8,8,8,640]{3,2,1,0:T(8,128)(2,1)S(1)}, u32[]{:S(2)}, u32[]{:S(2)}) async-start(bf16[8,8,8,640]{3,2,1,0:T(8,128)(2,1)} %copy.115), calls=%async_computation.4 | async-start | bytes 1310720 | tf_op jit(solution)/shard_map/all_to_all | solution.py:295
  182.6 14.3 %all-to-all-done.4 = bf16[8,8,8,640]{3,2,1,0:T(8,128)(2,1)S(1)} async-done(((bf16[8,8,8,640]{3,2,1,0:T(8,128)(2,1)}), bf16[8,8,8,640]{3,2,1,0:T(8,128)(2,1)S(1)}, u32[]{:S(2)}, u32[]{:S(2)}) %all-to-all-start.4) | async-done | bytes 655392 | tf_op jit(solution)/shard_map/all_to_all | solution.py:295
  197.0 1.9 gather_fusion.9
  (166 shorter events, 40.2 us)
Async XLA Ops:
  0.6 52.2 %copy-start = (bf16[640,320]{0,1:T(8,128)(2,1)S(1)}, bf16[640,320]{0,1:T(8,128)(2,1)}, u32[]{:S(2)}) copy-start(bf16[640,320]{0,1:T(8,128)(2,1)} %param.27) | copy-start | bytes 1228804
  15.8 14.6 %all-to-all-start = ((bf16[8,2,32,128]{3,2,1,0:T(8,128)(2,1)}), bf16[8,2,32,128]{3,2,1,0:T(8,128)(2,1)S(1)}, u32[]{:S(2)}, u32[]{:S(2)}) async-start(bf16[8,2,32,128]{3,2,1,0:T(8,128)(2,1)} %pad_maximum_fusion), calls=%async_computation | async-start | bytes 262144 | tf_op jit(solution)/shard_map/all_to_all | solution.py:120
  32.8 20.0 %all-to-all-start.1 = ((bf16[8,64,640]{2,1,0:T(8,128)(2,1)}), bf16[8,64,640]{2,1,0:T(8,128)(2,1)S(1)}, u32[]{:S(2)}, u32[]{:S(2)}) async-start(bf16[8,64,640]{2,1,0:T(8,128)(2,1)} %broadcast_in_dim.163), calls=%async_computation.1 | async-start | bytes 1310720 | tf_op jit(solution)/shard_map/all_to_all | solution.py:157
  54.2 14.8 %all-to-all-start.2 = ((bf16[8,64,320]{2,1,0:T(8,128)(2,1)}), bf16[8,64,320]{2,1,0:T(8,128)(2,1)S(1)}, u32[]{:S(2)}, u32[]{:S(2)}) async-start(bf16[8,64,320]{2,1,0:T(8,128)(2,1)} %bitcast.22), calls=%async_computation.2 | async-start | bytes 786432 | tf_op jit(solution)/shard_map/all_to_all | solution.py:163
  57.8 18.2 %copy-start.18 = (bf16[640]{0:T(1024)(128)(2,1)S(1)}, bf16[640]{0:T(1024)(128)(2,1)}, u32[]{:S(2)}) copy-start(bf16[640]{0:T(1024)(128)(2,1)} %param.28) | copy-start | bytes 3844
  57.9 19.4 %copy-start.9 = (bf16[64,640]{1,0:T(8,128)(2,1)S(1)}, bf16[64,640]{1,0:T(8,128)(2,1)}, u32[]{:S(2)}) copy-start(bf16[64,640]{1,0:T(8,128)(2,1)} %param.18) | copy-start | bytes 245764
  69.0 8.5 %copy-start.8 = (f32[640,64]{0,1:T(8,128)S(1)}, f32[640,64]{0,1:T(8,128)}, u32[]{:S(2)}) copy-start(f32[640,64]{0,1:T(8,128)} %param.29) | copy-start | bytes 491524
  69.6 6.3 %collective-permute-start = (bf16[64,1280]{1,0:T(8,128)(2,1)S(1)}, bf16[64,1280]{1,0:T(8,128)(2,1)S(1)}, u32[]{:S(2)}, u32[]{:S(2)}) collective-permute-start(bf16[64,1280]{1,0:T(8,128)(2,1)S(1)} %constant_dynamic-slice_fusion.1), channel_id=1, source_target_pairs={{0,16},{8,24},{16,0},{24,8},{1,17},{9,25},{17,1},{25,9},{2,18},{10... | collective-permute-start | bytes 491528 | tf_op jit(solution)/shard_map/ppermute | solution.py:173
  76.0 1.3 collective-permute-start.1
  77.4 8.6 %copy-start.3 = (bf16[64,640]{1,0:T(8,128)(2,1)}, bf16[64,640]{1,0:T(8,128)(2,1)S(1)}, u32[]{:S(2)}) copy-start(bf16[64,640]{1,0:T(8,128)(2,1)S(1)} %get-tuple-element.185) | copy-start | bytes 245764
  77.9 1.2 collective-permute-start.2
  79.2 3.9 %collective-permute-start.3 = (f32[64,65]{1,0:T(8,128)S(1)}, f32[64,65]{1,0:T(8,128)S(1)}, u32[]{:S(2)}, u32[]{:S(2)}) collective-permute-start(f32[64,65]{1,0:T(8,128)S(1)} %fusion.96), channel_id=1, source_target_pairs={{0,16},{8,24},{16,0},{24,8},{1,17},{9,25},{17,1},{25,9},{2,18},{10... | collective-permute-start | bytes 49928 | tf_op jit(solution)/shard_map/ppermute | solution.py:198
  87.0 20.3 %all-to-all-start.3 = ((bf16[8,8,8,640]{3,2,1,0:T(8,128)(2,1)}), bf16[8,8,8,640]{3,2,1,0:T(8,128)(2,1)S(1)}, u32[]{:S(2)}, u32[]{:S(2)}) async-start(bf16[8,8,8,640]{3,2,1,0:T(8,128)(2,1)} %broadcast_select_fusion), calls=%async_computation.3 | async-start | bytes 1310720 | tf_op jit(solution)/shard_map/all_to_all | solution.py:305
  125.5 3.8 %collective-permute-start.4 = (bf16[4,16,8,2,768]{4,2,0,1,3:T(8,128)(2,1)}, bf16[4,16,8,2,768]{4,2,0,1,3:T(8,128)(2,1)}, u32[]{:S(2)}, u32[]{:S(2)}) collective-permute-start(bf16[4,16,8,2,768]{4,2,0,1,3:T(8,128)(2,1)} %fusion.22), channel_id=1, source_target_pairs={{0,8},{8,0},{16,24},{24,16},{1,9},{9,1},{17,25},{25,17},{2,10},{10... | collective-permute-start | bytes 4718600 | tf_op jit(solution)/shard_map/ppermute | solution.py:265
  132.4 19.6 %collective-permute-start.5 = (bf16[2,16,8,2,768]{4,2,0,1,3:T(8,128)(2,1)S(1)}, bf16[2,16,8,2,768]{4,2,0,1,3:T(8,128)(2,1)S(1)}, u32[]{:S(2)}, u32[]{:S(2)}) collective-permute-start(bf16[2,16,8,2,768]{4,2,0,1,3:T(8,128)(2,1)S(1)} %constant_dynamic-slice_fusion), channel_id=1, source_target_pairs={{0,16},{8,24},{16,0},{24,8},{1,17},{9,25},{17,1},{25,9},{2,18},{10... | collective-permute-start | bytes 2359304 | tf_op jit(solution)/shard_map/ppermute | solution.py:273
  153.4 10.8 %copy-start.14 = (s32[8,12]{1,0:T(8,128)S(1)}, s32[8,12]{1,0:T(8,128)}, u32[]{:S(2)}) copy-start(s32[8,12]{1,0:T(8,128)} %param.26) | copy-start | bytes 1156
  153.4 10.9 %copy-start.12 = (s32[8,12]{1,0:T(8,128)S(1)}, s32[8,12]{1,0:T(8,128)}, u32[]{:S(2)}) copy-start(s32[8,12]{1,0:T(8,128)} %param.25) | copy-start | bytes 1156
  153.7 10.4 %collective-permute-start.6 = (bf16[2,16,8,768]{3,2,0,1:T(8,128)(2,1)S(1)}, bf16[2,16,8,768]{3,2,0,1:T(8,128)(2,1)S(1)}, u32[]{:S(2)}, u32[]{:S(2)}) collective-permute-start(bf16[2,16,8,768]{3,2,0,1:T(8,128)(2,1)S(1)} %fusion.38), channel_id=1, source_target_pairs={{0,16},{8,24},{16,0},{24,8},{1,17},{9,25},{17,1},{25,9},{2,18},{10... | collective-permute-start | bytes 1179656 | tf_op jit(solution)/shard_map/ppermute | solution.py:277
  164.1 2.4 %collective-permute-start.7 = (bf16[4,16,8,768]{3,2,0,1:T(8,128)(2,1)S(1)}, bf16[4,16,8,768]{3,2,0,1:T(8,128)(2,1)S(1)}, u32[]{:S(2)}, u32[]{:S(2)}) collective-permute-start(bf16[4,16,8,768]{3,2,0,1:T(8,128)(2,1)S(1)} %maximum_select_fusion.2), channel_id=1, source_target_pairs={{0,8},{8,0},{16,24},{24,16},{1,9},{9,1},{17,25},{25,17},{2,10},{10... | collective-permute-start | bytes 2359304 | tf_op jit(solution)/shard_map/ppermute | solution.py:283
  174.6 6.7 %copy-start.7 = (bf16[1,8,32,128]{3,2,1,0:T(8,128)(2,1)S(1)}, bf16[1,8,32,128]{3,2,1,0:T(8,128)(2,1)}, u32[]{:S(2)}) copy-start(bf16[1,8,32,128]{3,2,1,0:T(8,128)(2,1)} %get-tuple-element.190) | copy-start | bytes 196612
  174.6 7.5 %copy-start.6 = (f32[64,65]{1,0:T(8,128)S(1)}, f32[64,65]{1,0:T(8,128)}, u32[]{:S(2)}) copy-start(f32[64,65]{1,0:T(8,128)} %copy-done.5) | copy-start | bytes 49924
  174.6 7.5 %copy-start.17 = (f32[64]{0:T(128)S(1)}, f32[64]{0:T(128)}, u32[]{:S(2)}) copy-start(f32[64]{0:T(128)} %copy-done.16) | copy-start | bytes 772
  174.6 7.6 %copy-start.11 = (s32[64,6]{0,1:T(8,128)S(1)}, s32[64,6]{0,1:T(8,128)}, u32[]{:S(2)}) copy-start(s32[64,6]{0,1:T(8,128)} %param.30) | copy-start | bytes 4612
  175.5 21.3 %all-to-all-start.4 = ((bf16[8,8,8,640]{3,2,1,0:T(8,128)(2,1)}), bf16[8,8,8,640]{3,2,1,0:T(8,128)(2,1)S(1)}, u32[]{:S(2)}, u32[]{:S(2)}) async-start(bf16[8,8,8,640]{3,2,1,0:T(8,128)(2,1)} %copy.115), calls=%async_computation.4 | async-start | bytes 1310720 | tf_op jit(solution)/shard_map/all_to_all | solution.py:295
  (8 other events, 22.5 us)

commit v11 on v10

--- a/solution.py
+++ b/solution.py
@@ -108,14 +108,22 @@
         num_segments=blk_count,
     )
     picked = pick_old + pick_new
-    sending = jnp.where(
-        (picked > 0)[:, None, None, None],
-        sources[jnp.maximum(picked - 1, 0)],
-        jnp.zeros((), jnp.bfloat16),
+    source_count = sources.shape[0]
+    send_pick = (jnp.arange(source_count)[None, :] == (picked - 1)[:, None]).astype(jnp.bfloat16)
+    sending = (
+        jnp.dot(send_pick, sources.reshape(source_count, -1), preferred_element_type=jnp.float32)
+        .astype(jnp.bfloat16)
+        .reshape((blk_count,) + sources.shape[1:])
     )
     source_request = jnp.zeros_like(devices) + own_index
     match_here = (block_holder[devices] == own_index) & in_use[devices]
-    outgoing = pool_rows[jnp.sum(jnp.where(match_here, block_slot[devices], 0), axis=1)]
+    out_slot = jnp.sum(jnp.where(match_here, block_slot[devices], 0), axis=1)
+    out_pick = (jnp.arange(pool_size)[None, :] == out_slot[:, None]).astype(jnp.bfloat16)
+    outgoing = (
+        jnp.dot(out_pick, pool_rows.reshape(pool_size, -1), preferred_element_type=jnp.float32)
+        .astype(jnp.bfloat16)
+        .reshape((blk_count,) + pool_rows.shape[1:])
+    )
     block_shape = sending.shape[1:]
     both_blocks = lax.all_to_all(
         jnp.stack(
@@ -224,11 +232,12 @@
     target = flat_routes * capacity + slot_rank
     slot_total = expert_count * capacity
     source_item = jax.ops.segment_sum(jnp.arange(assign_count) + 1, target, num_segments=slot_total)
-    packed_rows = jnp.where(
-        (source_item > 0)[:, None],
-        normed[jnp.maximum(source_item - 1, 0) // top_count],
-        jnp.zeros((), jnp.bfloat16),
-    )
+    row_pick = (
+        jnp.arange(stretch_len)[None, :] == ((source_item - 1) // top_count)[:, None]
+    ) & (source_item > 0)[:, None]
+    packed_rows = jnp.dot(
+        row_pick.astype(jnp.bfloat16), normed, preferred_element_type=jnp.float32
+    ).astype(jnp.bfloat16)
     pieces_here = w_gate.shape[0]
     feature_part = normed.shape[1]
     paired = pieces_here % 2 == 0
@@ -323,8 +332,17 @@
     else:
         per_slot = per_chunk[0].reshape(slot_total, feature_part)
     per_slot = per_slot.astype(jnp.float32)
-    routed = per_slot[target].reshape(stretch_len, top_count, feature_part)
-    moe_out = jnp.sum(routed * gates[:, :, None], axis=1)
+    slot_weight = jnp.sum(
+        jnp.where(
+            target.reshape(stretch_len, top_count, 1) == jnp.arange(slot_total)[None, None, :],
+            gates[:, :, None],
+            0.0,
+        ),
+        axis=1,
+    )
+    moe_out = jnp.dot(
+        slot_weight, per_slot, precision=lax.Precision.HIGHEST, preferred_element_type=jnp.float32
+    )
     layer_out = (resid_float + moe_out).astype(jnp.bfloat16)
     here_old = in_use & (decode_holder[:, :max_blocks] == own_index)
     from_old = jnp.where(here_old, block_holder, blk_count).reshape(-1)

time: 201 us -> 197 us (0.980)
  blocking collectives: 0 us -> 19 us
  waiting for transfers between devices: 101 us -> 83.6 us
  local copies, waits for them, and re-layouts: 22.8 us -> 16.4 us
  matrix products: 26 us -> 29.3 us
  other arithmetic: 22.9 us -> 20.6 us
    all_to_all x0 -> x1, blocking collectives: none -> 19 us  [per_device(): lax.all_to_all(jnp.broadcast_to(attended[None], (blk_count,) + attended.s...]
    all_to_all x1 -> x0, waiting for transfers between devices: 15.8 us -> none  [per_device(): lax.all_to_all(jnp.broadcast_to(attended[None], (blk_count,) + attended.s...]
    gather x5 -> x1, local copies, waits for them, and re-layouts: 7.26 us -> 1.24 us  [per_device(): out_slot = jnp.sum(jnp.where(match_here, block_slot[devices], 0), axis=1)]
    all_to_all x1 -> x0, starting transfers between devices: 3.78 us -> none  [per_device(): lax.all_to_all(jnp.broadcast_to(attended[None], (blk_count,) + attended.s...]
    ppermute x1, waiting for transfers between devices: 0.01 us -> 3.11 us  [per_device(): lax.ppermute(chip_given, 'kv', swap_chip).astype(jnp.float32)]
    dot_general x0 -> x5, matrix products: none -> 3.04 us  [the longest x1 1.24 us: per_device(): jnp.dot(row_pick.astype(jnp.bfloat16), normed, preferred_element_type=jnp...]
    all_to_all x1, waiting for transfers between devices: 14.3 us -> 16.6 us  [out_stage(): lax.all_to_all(half_sum, 'blk', split_axis=0, concat_axis=0, tiled=True)]
    ppermute x1, waiting for transfers between devices: 2.1 us -> 0.01 us  [out_stage(): hidden_other = lax.ppermute(hidden_half, 'kv', flip_core)]
  transfers between devices with their start and end apart: 13 -> 12, of which waited for: 12 -> 10; matrix products, arithmetic and copies ran while one was open for 6% -> 7% of each run, Pallas kernels for 0% -> 0%
where the time goes in v11:
time: 197 us; the launch traced here: 196 us
  waiting for transfers between devices  83.6 us (42%)
  matrix products  29.3 us (15%)
  starting transfers between devices  24.7 us (13%)
  other arithmetic  20.6 us (10%)
  blocking collectives  19 us (10%)
  local copies, waits for them, and re-layouts  16.4 us (8%)
    all_to_all x1, blocking collectives, per_device(): lax.all_to_all(jnp.broadcast_to(attended[None], (blk_count,) + attended.s...  19 us
    ppermute x1, waiting for transfers between devices, out_stage(): lax.ppermute(chip_given, 'kv', flip_chip).astype(jnp.float32)  18.2 us
    all_to_all x1, waiting for transfers between devices, per_device(): lax.all_to_all(outgoing_rows[:, i * chunk_experts:(i + 1) * chunk_experts...  16.7 us
    all_to_all x1, waiting for transfers between devices, out_stage(): lax.all_to_all(half_sum, 'blk', split_axis=0, concat_axis=0, tiled=True)  16.6 us
    all_to_all x1, waiting for transfers between devices, per_device(): lax.all_to_all(column_part, 'blk', split_axis=0, concat_axis=1, tiled=True)  9.11 us
    ppermute x1, waiting for transfers between devices, out_stage(): hidden_far = lax.ppermute(hidden_quarter, 'kv', flip_chip)  8.92 us
    dot_general x1, matrix products, pair_stage(): jnp.einsum('spkd,pdu->spku', rows_in, gate_w, preferred_element_type=jnp....  8.3 us
    dot_general x1, matrix products, pair_stage(): jnp.einsum('spkd,pdu->spku', rows_in, up_w, preferred_element_type=jnp.fl...  8.3 us
  transfers between devices with their start and end apart: 12, of which 10 were waited for; matrix products, arithmetic and copies ran while one was open for 7% of the time, Pallas kernels for 0%

profile of v11, /device:TPU:0, one launch (start us, length us, event | category | flops | bytes accessed | tf_op | source)
XLA Modules:
  0.0 195.6 jit_solution(11619914984979872237)
XLA Ops:
  14.1 7.3 %all-to-all-start = ((bf16[8,2,32,128]{3,2,1,0:T(8,128)(2,1)}), bf16[8,2,32,128]{3,2,1,0:T(8,128)(2,1)S(1)}, u32[]{:S(2)}, u32[]{:S(2)}) async-start(bf16[8,2,32,128]{3,2,1,0:T(8,128)(2,1)} %pad_maximum_fusion), calls=%async_computation | async-start | bytes 262144 | tf_op jit(solution)/shard_map/all_to_all | solution.py:128
  24.8 3.9 %all-to-all-done = bf16[8,2,32,128]{3,2,1,0:T(8,128)(2,1)S(1)} async-done(((bf16[8,2,32,128]{3,2,1,0:T(8,128)(2,1)}), bf16[8,2,32,128]{3,2,1,0:T(8,128)(2,1)S(1)}, u32[]{:S(2)}, u32[]{:S(2)}) %all-to-all-start) | async-done | bytes 131104 | tf_op jit(solution)/shard_map/all_to_all | solution.py:128
  30.0 1.4 while.16
  31.7 19.0 %all_to_all.39 = bf16[8,64,640]{2,1,0:T(8,128)(2,1)S(1)} all-to-all(bf16[8,64,640]{2,1,0:T(8,128)(2,1)S(1)} %broadcast_in_dim.85), channel_id=1, replica_groups=mesh['kv'=4,'blk'=8] {'blk'}, dimensions={0} | all-to-all | bytes 1310720 | tf_op jit(solution)/shard_map/all_to_all | solution.py:165
  52.1 3.6 %all-to-all-start.2 = ((bf16[8,64,320]{2,1,0:T(8,128)(2,1)}), bf16[8,64,320]{2,1,0:T(8,128)(2,1)S(1)}, u32[]{:S(2)}, u32[]{:S(2)}) async-start(bf16[8,64,320]{2,1,0:T(8,128)(2,1)} %bitcast.18), calls=%async_computation.2 | async-start | bytes 786432 | tf_op jit(solution)/shard_map/all_to_all | solution.py:171
  57.6 9.1 %all-to-all-done.2 = bf16[8,64,320]{2,1,0:T(8,128)(2,1)S(1)} async-done(((bf16[8,64,320]{2,1,0:T(8,128)(2,1)}), bf16[8,64,320]{2,1,0:T(8,128)(2,1)S(1)}, u32[]{:S(2)}, u32[]{:S(2)}) %all-to-all-start.2) | async-done | bytes 327712 | tf_op jit(solution)/shard_map/all_to_all | solution.py:171
  67.2 1.5 collective-permute-start
  69.5 3.1 %collective-permute-done = bf16[64,1280]{1,0:T(8,128)(2,1)S(1)} collective-permute-done((bf16[64,1280]{1,0:T(8,128)(2,1)S(1)}, bf16[64,1280]{1,0:T(8,128)(2,1)S(1)}, u32[]{:S(2)}, u32[]{:S(2)}) %collective-permute-start) | collective-permute-done | bytes 163872 | tf_op jit(solution)/shard_map/ppermute | solution.py:181
  72.8 3.9 %scatter_custom_fusion.2 = s32[512]{0:T(512)S(1)} fusion(s32[384]{0:T(512)S(1)} %add_reduce_fusion, s32[384]{0:T(512)S(1)} %iota_add_fusion, s32[]{:T(128)} %constant.176.clone.1), kind=kCustom, calls=%fused_computation.169 | custom fusion | flops 384 | bytes 2052 | tf_op jit(solution)/shard_map/scatter-add | solution.py:234
  78.7 1.4 collective-permute-start.3
  80.2 2.5 %collective-permute-done.3 = f32[64,65]{1,0:T(8,128)S(1)} collective-permute-done((f32[64,65]{1,0:T(8,128)S(1)}, f32[64,65]{1,0:T(8,128)S(1)}, u32[]{:S(2)}, u32[]{:S(2)}) %collective-permute-start.3) | collective-permute-done | bytes 16672 | tf_op jit(solution)/shard_map/ppermute | solution.py:206
  84.0 3.7 %all-to-all-start.3 = ((bf16[8,8,8,640]{3,2,1,0:T(8,128)(2,1)}), bf16[8,8,8,640]{3,2,1,0:T(8,128)(2,1)S(1)}, u32[]{:S(2)}, u32[]{:S(2)}) async-start(bf16[8,8,8,640]{3,2,1,0:T(8,128)(2,1)} %bitcast.22), calls=%async_computation.3 | async-start | bytes 1310720 | tf_op jit(solution)/shard_map/all_to_all | solution.py:314
  87.8 16.7 %all-to-all-done.3 = bf16[8,8,8,640]{3,2,1,0:T(8,128)(2,1)S(1)} async-done(((bf16[8,8,8,640]{3,2,1,0:T(8,128)(2,1)}), bf16[8,8,8,640]{3,2,1,0:T(8,128)(2,1)S(1)}, u32[]{:S(2)}, u32[]{:S(2)}) %all-to-all-start.3) | async-done | bytes 655392 | tf_op jit(solution)/shard_map/all_to_all | solution.py:314
  104.7 8.3 %fusion.30 = bf16[8,16,8,1,768]{4,2,0,1,3:T(8,128)(2,1)S(1)} fusion(bf16[8,16,8,640]{3,2,0,1:T(8,128)(2,1)S(1)} %bitcast.141, bf16[16,640,768]{2,1,0:T(8,128)(2,1)} %param.32), kind=kOutput, calls=%fused_computation.53 | convolution fusion | flops 1007419392 | bytes 18612224 | tf_op jit(solution)/shard_map/spkd,pdu->spku/dot_general | solution.py:269
  113.0 8.3 %fusion.33 = bf16[8,16,8,1,768]{4,2,0,1,3:T(8,128)(2,1)S(1)} fusion(bf16[8,16,8,640]{3,2,0,1:T(8,128)(2,1)S(1)} %bitcast.142, bf16[16,640,768]{2,1,0:T(8,128)(2,1)} %param.31), kind=kOutput, calls=%fused_computation.54 | convolution fusion | flops 1007419392 | bytes 18612224 | tf_op jit(solution)/shard_map/spkd,pdu->spku/dot_general | solution.py:268
  122.7 3.7 %collective-permute-done.4 = bf16[4,16,8,2,768]{4,2,0,1,3:T(8,128)(2,1)} collective-permute-done((bf16[4,16,8,2,768]{4,2,0,1,3:T(8,128)(2,1)}, bf16[4,16,8,2,768]{4,2,0,1,3:T(8,128)(2,1)}, u32[]{:S(2)}, u32[]{:S(2)}) %collective-permute-start.4) | collective-permute-done | bytes 1572896 | tf_op jit(solution)/shard_map/ppermute | solution.py:274
  126.4 2.0 add_convert_fusion
  129.6 1.5 collective-permute-start.5
  131.1 18.2 %collective-permute-done.5 = bf16[2,16,8,2,768]{4,2,0,1,3:T(8,128)(2,1)S(1)} collective-permute-done((bf16[2,16,8,2,768]{4,2,0,1,3:T(8,128)(2,1)S(1)}, bf16[2,16,8,2,768]{4,2,0,1,3:T(8,128)(2,1)S(1)}, u32[]{:S(2)}, u32[]{:S(2)}) %collective-permute-start.5) | collective-permute-done | bytes 786464 | tf_op jit(solution)/shard_map/ppermute | solution.py:282
  150.9 1.5 collective-permute-start.6
  152.4 8.9 %collective-permute-done.6 = bf16[2,16,8,768]{3,2,0,1:T(8,128)(2,1)S(1)} collective-permute-done((bf16[2,16,8,768]{3,2,0,1:T(8,128)(2,1)S(1)}, bf16[2,16,8,768]{3,2,0,1:T(8,128)(2,1)S(1)}, u32[]{:S(2)}, u32[]{:S(2)}) %collective-permute-start.6) | collective-permute-done | bytes 393248 | tf_op jit(solution)/shard_map/ppermute | solution.py:286
  163.7 8.1 %bitcast_reduce_fusion = bf16[8,8,8,640]{3,2,0,1:T(8,128)(2,1)S(1)} fusion(bf16[16,768,640]{2,1,0:T(8,128)(2,1)} %param.33, bf16[4,16,8,768]{3,2,0,1:T(8,128)(2,1)S(1)} %collective-permute-done.7, bf16[4,16,8,768]{3,2,0,1:T(8,128)(2,1)S(1)} %maximum_select_fusion.2, pred[]{:T(512)S(6)} %eq.180), kind=kOutput, calls=%fused_computation.56 | convolution fusion | flops 1009975296 | bytes 17956864 | tf_op jit(solution)/shard_map/spku,pud->spkd/dot_general | solution.py:298
  172.8 3.6 %all-to-all-start.4 = ((bf16[8,8,8,640]{3,2,1,0:T(8,128)(2,1)}), bf16[8,8,8,640]{3,2,1,0:T(8,128)(2,1)S(1)}, u32[]{:S(2)}, u32[]{:S(2)}) async-start(bf16[8,8,8,640]{3,2,1,0:T(8,128)(2,1)} %copy.126), calls=%async_computation.4 | async-start | bytes 1310720 | tf_op jit(solution)/shard_map/all_to_all | solution.py:304
  177.9 16.6 %all-to-all-done.4 = bf16[8,8,8,640]{3,2,1,0:T(8,128)(2,1)S(1)} async-done(((bf16[8,8,8,640]{3,2,1,0:T(8,128)(2,1)}), bf16[8,8,8,640]{3,2,1,0:T(8,128)(2,1)S(1)}, u32[]{:S(2)}, u32[]{:S(2)}) %all-to-all-start.4) | async-done | bytes 655392 | tf_op jit(solution)/shard_map/all_to_all | solution.py:304
  (164 shorter events, 37.3 us)
Async XLA Ops:
  0.6 50.1 %copy-start = (bf16[640,320]{0,1:T(8,128)(2,1)S(1)}, bf16[640,320]{0,1:T(8,128)(2,1)}, u32[]{:S(2)}) copy-start(bf16[640,320]{0,1:T(8,128)(2,1)} %param.27) | copy-start | bytes 1228804
  14.1 14.6 %all-to-all-start = ((bf16[8,2,32,128]{3,2,1,0:T(8,128)(2,1)}), bf16[8,2,32,128]{3,2,1,0:T(8,128)(2,1)S(1)}, u32[]{:S(2)}, u32[]{:S(2)}) async-start(bf16[8,2,32,128]{3,2,1,0:T(8,128)(2,1)} %pad_maximum_fusion), calls=%async_computation | async-start | bytes 262144 | tf_op jit(solution)/shard_map/all_to_all | solution.py:128
  52.1 17.2 %copy-start.18 = (bf16[640]{0:T(1024)(128)(2,1)S(1)}, bf16[640]{0:T(1024)(128)(2,1)}, u32[]{:S(2)}) copy-start(bf16[640]{0:T(1024)(128)(2,1)} %param.28) | copy-start | bytes 3844
  52.1 14.6 %all-to-all-start.2 = ((bf16[8,64,320]{2,1,0:T(8,128)(2,1)}), bf16[8,64,320]{2,1,0:T(8,128)(2,1)S(1)}, u32[]{:S(2)}, u32[]{:S(2)}) async-start(bf16[8,64,320]{2,1,0:T(8,128)(2,1)} %bitcast.18), calls=%async_computation.2 | async-start | bytes 786432 | tf_op jit(solution)/shard_map/all_to_all | solution.py:171
  57.0 19.6 %copy-start.10 = (bf16[64,640]{1,0:T(8,128)(2,1)S(1)}, bf16[64,640]{1,0:T(8,128)(2,1)}, u32[]{:S(2)}) copy-start(bf16[64,640]{1,0:T(8,128)(2,1)} %param.18) | copy-start | bytes 245764
  66.7 10.2 %copy-start.8 = (f32[640,64]{0,1:T(8,128)S(1)}, f32[640,64]{0,1:T(8,128)}, u32[]{:S(2)}) copy-start(f32[640,64]{0,1:T(8,128)} %param.29) | copy-start | bytes 491524
  67.2 5.4 %collective-permute-start = (bf16[64,1280]{1,0:T(8,128)(2,1)S(1)}, bf16[64,1280]{1,0:T(8,128)(2,1)S(1)}, u32[]{:S(2)}, u32[]{:S(2)}) collective-permute-start(bf16[64,1280]{1,0:T(8,128)(2,1)S(1)} %constant_dynamic-slice_fusion.1), channel_id=1, source_target_pairs={{0,16},{8,24},{16,0},{24,8},{1,17},{9,25},{17,1},{25,9},{2,18},{10... | collective-permute-start | bytes 491528 | tf_op jit(solution)/shard_map/ppermute | solution.py:181
  72.7 4.0 %collective-permute-start.1 = (bf16[64,640]{1,0:T(8,128)(2,1)S(1)}, bf16[64,640]{1,0:T(8,128)(2,1)S(1)}, u32[]{:S(2)}, u32[]{:S(2)}) collective-permute-start(bf16[64,640]{1,0:T(8,128)(2,1)S(1)} %dynamic-slice_convert_fusion), channel_id=1, source_target_pairs={{0,8},{8,0},{16,24},{24,16},{1,9},{9,1},{17,25},{25,17},{2,10},{10... | collective-permute-start | bytes 245768 | tf_op jit(solution)/shard_map/ppermute | solution.py:189
  76.8 27.7 %copy-start.3 = (bf16[64,640]{1,0:T(8,128)(2,1)}, bf16[64,640]{1,0:T(8,128)(2,1)S(1)}, u32[]{:S(2)}) copy-start(bf16[64,640]{1,0:T(8,128)(2,1)S(1)} %get-tuple-element.191) | copy-start | bytes 245764
  77.3 1.4 collective-permute-start.2
  78.7 3.9 %collective-permute-start.3 = (f32[64,65]{1,0:T(8,128)S(1)}, f32[64,65]{1,0:T(8,128)S(1)}, u32[]{:S(2)}, u32[]{:S(2)}) collective-permute-start(f32[64,65]{1,0:T(8,128)S(1)} %fusion.112), channel_id=1, source_target_pairs={{0,16},{8,24},{16,0},{24,8},{1,17},{9,25},{17,1},{25,9},{2,18},{10... | collective-permute-start | bytes 49928 | tf_op jit(solution)/shard_map/ppermute | solution.py:206
  82.7 21.9 %copy-start.5 = (f32[64,65]{1,0:T(8,128)}, f32[64,65]{1,0:T(8,128)S(1)}, u32[]{:S(2)}) copy-start(f32[64,65]{1,0:T(8,128)S(1)} %add.227) | copy-start | bytes 49924
  82.8 21.8 %copy-start.16 = (f32[64]{0:T(128)}, f32[64]{0:T(128)S(1)}, u32[]{:S(2)}) copy-start(f32[64]{0:T(128)S(1)} %fusion.69) | copy-start | bytes 772
  84.0 20.5 %all-to-all-start.3 = ((bf16[8,8,8,640]{3,2,1,0:T(8,128)(2,1)}), bf16[8,8,8,640]{3,2,1,0:T(8,128)(2,1)S(1)}, u32[]{:S(2)}, u32[]{:S(2)}) async-start(bf16[8,8,8,640]{3,2,1,0:T(8,128)(2,1)} %bitcast.22), calls=%async_computation.3 | async-start | bytes 1310720 | tf_op jit(solution)/shard_map/all_to_all | solution.py:314
  122.7 3.8 %collective-permute-start.4 = (bf16[4,16,8,2,768]{4,2,0,1,3:T(8,128)(2,1)}, bf16[4,16,8,2,768]{4,2,0,1,3:T(8,128)(2,1)}, u32[]{:S(2)}, u32[]{:S(2)}) collective-permute-start(bf16[4,16,8,2,768]{4,2,0,1,3:T(8,128)(2,1)} %fusion.22), channel_id=1, source_target_pairs={{0,8},{8,0},{16,24},{24,16},{1,9},{9,1},{17,25},{25,17},{2,10},{10... | collective-permute-start | bytes 4718600 | tf_op jit(solution)/shard_map/ppermute | solution.py:274
  129.6 19.6 %collective-permute-start.5 = (bf16[2,16,8,2,768]{4,2,0,1,3:T(8,128)(2,1)S(1)}, bf16[2,16,8,2,768]{4,2,0,1,3:T(8,128)(2,1)S(1)}, u32[]{:S(2)}, u32[]{:S(2)}) collective-permute-start(bf16[2,16,8,2,768]{4,2,0,1,3:T(8,128)(2,1)S(1)} %constant_dynamic-slice_fusion), channel_id=1, source_target_pairs={{0,16},{8,24},{16,0},{24,8},{1,17},{9,25},{17,1},{25,9},{2,18},{10... | collective-permute-start | bytes 2359304 | tf_op jit(solution)/shard_map/ppermute | solution.py:282
  150.6 10.8 %copy-start.14 = (s32[8,8]{1,0:T(8,128)S(1)}, s32[8,8]{1,0:T(8,128)}, u32[]{:S(2)}) copy-start(s32[8,8]{1,0:T(8,128)} %get-tuple-element.200) | copy-start | bytes 772
  150.6 10.9 %copy-start.15 = (s32[8,12]{1,0:T(8,128)S(1)}, s32[8,12]{1,0:T(8,128)}, u32[]{:S(2)}) copy-start(s32[8,12]{1,0:T(8,128)} %param.26) | copy-start | bytes 1156
  150.6 11.0 %copy-start.13 = (s32[8,12]{1,0:T(8,128)S(1)}, s32[8,12]{1,0:T(8,128)}, u32[]{:S(2)}) copy-start(s32[8,12]{1,0:T(8,128)} %param.25) | copy-start | bytes 1156
  150.9 10.4 %collective-permute-start.6 = (bf16[2,16,8,768]{3,2,0,1:T(8,128)(2,1)S(1)}, bf16[2,16,8,768]{3,2,0,1:T(8,128)(2,1)S(1)}, u32[]{:S(2)}, u32[]{:S(2)}) collective-permute-start(bf16[2,16,8,768]{3,2,0,1:T(8,128)(2,1)S(1)} %fusion.41), channel_id=1, source_target_pairs={{0,16},{8,24},{16,0},{24,8},{1,17},{9,25},{17,1},{25,9},{2,18},{10... | collective-permute-start | bytes 1179656 | tf_op jit(solution)/shard_map/ppermute | solution.py:286
  161.4 2.4 %collective-permute-start.7 = (bf16[4,16,8,768]{3,2,0,1:T(8,128)(2,1)S(1)}, bf16[4,16,8,768]{3,2,0,1:T(8,128)(2,1)S(1)}, u32[]{:S(2)}, u32[]{:S(2)}) collective-permute-start(bf16[4,16,8,768]{3,2,0,1:T(8,128)(2,1)S(1)} %maximum_select_fusion.2), channel_id=1, source_target_pairs={{0,8},{8,0},{16,24},{24,16},{1,9},{9,1},{17,25},{25,17},{2,10},{10... | collective-permute-start | bytes 2359304 | tf_op jit(solution)/shard_map/ppermute | solution.py:292
  171.8 22.7 %copy-start.4 = (bf16[64,640]{1,0:T(8,128)(2,1)S(1)}, bf16[64,640]{1,0:T(8,128)(2,1)}, u32[]{:S(2)}) copy-start(bf16[64,640]{1,0:T(8,128)(2,1)} %copy-done.3) | copy-start | bytes 245764
  171.9 23.7 %copy-start.1 = (bf16[640,320]{0,1:T(8,128)(2,1)S(1)}, bf16[640,320]{0,1:T(8,128)(2,1)}, u32[]{:S(2)}) copy-start(bf16[640,320]{0,1:T(8,128)(2,1)} %param.27) | copy-start | bytes 1228804
  172.8 21.7 %all-to-all-start.4 = ((bf16[8,8,8,640]{3,2,1,0:T(8,128)(2,1)}), bf16[8,8,8,640]{3,2,1,0:T(8,128)(2,1)S(1)}, u32[]{:S(2)}, u32[]{:S(2)}) async-start(bf16[8,8,8,640]{3,2,1,0:T(8,128)(2,1)} %copy.126), calls=%async_computation.4 | async-start | bytes 1310720 | tf_op jit(solution)/shard_map/all_to_all | solution.py:304
  (7 other events, 32.0 us)

commit v12 on v11

--- a/solution.py
+++ b/solution.py
@@ -115,9 +115,8 @@
         .astype(jnp.bfloat16)
         .reshape((blk_count,) + sources.shape[1:])
     )
-    source_request = jnp.zeros_like(devices) + own_index
-    match_here = (block_holder[devices] == own_index) & in_use[devices]
-    out_slot = jnp.sum(jnp.where(match_here, block_slot[devices], 0), axis=1)
+    match_here = (block_holder[:blk_count] == own_index) & in_use[:blk_count]
+    out_slot = jnp.sum(jnp.where(match_here, block_slot[:blk_count], 0), axis=1)
     out_pick = (jnp.arange(pool_size)[None, :] == out_slot[:, None]).astype(jnp.bfloat16)
     outgoing = (
         jnp.dot(out_pick, pool_rows.reshape(pool_size, -1), preferred_element_type=jnp.float32)
@@ -138,7 +137,9 @@
     landed = both_blocks[:, 0].reshape((blk_count,) + block_shape)
     arrived = both_blocks[:, 1].reshape((blk_count,) + block_shape)
     present = jnp.any(
-        (block_holder[source_request] == devices[:, None]) & in_use[source_request], axis=1
+        (lax.dynamic_index_in_dim(block_holder, own_index, 0, keepdims=False)[None, :] == devices[:, None])
+        & lax.dynamic_index_in_dim(in_use, own_index, 0, keepdims=False)[None, :],
+        axis=1,
     )
     own_rows = head_rows(queries, head_count, head_dim)
     row_count = head_count * stretch_len
@@ -231,12 +232,10 @@
     slot_rank = jnp.sum(earlier * onehot, axis=1)
     target = flat_routes * capacity + slot_rank
     slot_total = expert_count * capacity
-    source_item = jax.ops.segment_sum(jnp.arange(assign_count) + 1, target, num_segments=slot_total)
-    row_pick = (
-        jnp.arange(stretch_len)[None, :] == ((source_item - 1) // top_count)[:, None]
-    ) & (source_item > 0)[:, None]
-    packed_rows = jnp.dot(
-        row_pick.astype(jnp.bfloat16), normed, preferred_element_type=jnp.float32
+    slot_hit = target.reshape(stretch_len, top_count, 1) == jnp.arange(slot_total)[None, None, :]
+    token_slot = jnp.any(slot_hit, axis=1).astype(jnp.bfloat16)
+    packed_rows = lax.dot_general(
+        token_slot, normed, (((0,), (0,)), ((), ())), preferred_element_type=jnp.float32
     ).astype(jnp.bfloat16)
     pieces_here = w_gate.shape[0]
     feature_part = normed.shape[1]
@@ -332,14 +331,7 @@
     else:
         per_slot = per_chunk[0].reshape(slot_total, feature_part)
     per_slot = per_slot.astype(jnp.float32)
-    slot_weight = jnp.sum(
-        jnp.where(
-            target.reshape(stretch_len, top_count, 1) == jnp.arange(slot_total)[None, None, :],
-            gates[:, :, None],
-            0.0,
-        ),
-        axis=1,
-    )
+    slot_weight = jnp.sum(jnp.where(slot_hit, gates[:, :, None], 0.0), axis=1)
     moe_out = jnp.dot(
         slot_weight, per_slot, precision=lax.Precision.HIGHEST, preferred_element_type=jnp.float32
     )

time: 197 us -> 190 us (0.964)
  other arithmetic: 20.6 us -> 16.2 us
  local copies, waits for them, and re-layouts: 16.4 us -> 12.2 us
    gather x5 -> x0, local copies, waits for them, and re-layouts: 4.85 us -> none  [the longest x2 1.81 us: per_device(): match_here = (block_holder[devices] == own_index) & in_use[devices]]
    scatter-add x1 -> x0, other arithmetic: 3.88 us -> none  [per_device(): jax.ops.segment_sum(jnp.arange(assign_count) + 1, target, num_segments=sl...]
  transfers between devices with their start and end apart: 12 -> 12, of which waited for: 10 -> 11; matrix products, arithmetic and copies ran while one was open for 7% -> 5% of each run, Pallas kernels for 0% -> 0%
where the time goes in v12:
time: 190 us; the launch traced here: 188 us
  waiting for transfers between devices  85.5 us (45%)
  matrix products  29.2 us (15%)
  starting transfers between devices  24.3 us (13%)
  blocking collectives  19 us (10%)
  other arithmetic  16.2 us (9%)
  local copies, waits for them, and re-layouts  12.2 us (6%)
    all_to_all x1, blocking collectives, per_device(): lax.all_to_all(jnp.broadcast_to(attended[None], (blk_count,) + attended.s...  19 us
    ppermute x1, waiting for transfers between devices, out_stage(): lax.ppermute(chip_given, 'kv', flip_chip).astype(jnp.float32)  18.2 us
    all_to_all x1, waiting for transfers between devices, out_stage(): lax.all_to_all(half_sum, 'blk', split_axis=0, concat_axis=0, tiled=True)  16.7 us
    all_to_all x1, waiting for transfers between devices, per_device(): lax.all_to_all(outgoing_rows[:, i * chunk_experts:(i + 1) * chunk_experts...  16.5 us
    all_to_all x1, waiting for transfers between devices, per_device(): lax.all_to_all(column_part, 'blk', split_axis=0, concat_axis=1, tiled=True)  10.7 us
    ppermute x1, waiting for transfers between devices, out_stage(): hidden_far = lax.ppermute(hidden_quarter, 'kv', flip_chip)  8.93 us
    dot_general x1, matrix products, pair_stage(): jnp.einsum('spkd,pdu->spku', rows_in, up_w, preferred_element_type=jnp.fl...  8.3 us
    dot_general x1, matrix products, pair_stage(): jnp.einsum('spkd,pdu->spku', rows_in, gate_w, preferred_element_type=jnp....  8.3 us
  transfers between devices with their start and end apart: 12, of which 11 were waited for; matrix products, arithmetic and copies ran while one was open for 5% of the time, Pallas kernels for 0%

profile of v12, /device:TPU:0, one launch (start us, length us, event | category | flops | bytes accessed | tf_op | source)
XLA Modules:
  0.0 188.4 jit_solution(10134519291029563821)
XLA Ops:
  2.1 1.4 slice_select_fusion
  9.9 7.3 %all-to-all-start = ((bf16[8,2,32,128]{3,2,1,0:T(8,128)(2,1)}), bf16[8,2,32,128]{3,2,1,0:T(8,128)(2,1)S(1)}, u32[]{:S(2)}, u32[]{:S(2)}) async-start(bf16[8,2,32,128]{3,2,1,0:T(8,128)(2,1)} %pad_maximum_fusion), calls=%async_computation | async-start | bytes 262144 | tf_op jit(solution)/shard_map/all_to_all | solution.py:127
  20.6 3.8 %all-to-all-done = bf16[8,2,32,128]{3,2,1,0:T(8,128)(2,1)S(1)} async-done(((bf16[8,2,32,128]{3,2,1,0:T(8,128)(2,1)}), bf16[8,2,32,128]{3,2,1,0:T(8,128)(2,1)S(1)}, u32[]{:S(2)}, u32[]{:S(2)}) %all-to-all-start) | async-done | bytes 131104 | tf_op jit(solution)/shard_map/all_to_all | solution.py:127
  25.8 1.4 while.16
  27.5 19.0 %all_to_all.39 = bf16[8,64,640]{2,1,0:T(8,128)(2,1)S(1)} all-to-all(bf16[8,64,640]{2,1,0:T(8,128)(2,1)S(1)} %broadcast_in_dim.86), channel_id=1, replica_groups=mesh['kv'=4,'blk'=8] {'blk'}, dimensions={0} | all-to-all | bytes 1310720 | tf_op jit(solution)/shard_map/all_to_all | solution.py:166
  47.9 3.6 %all-to-all-start.2 = ((bf16[8,64,320]{2,1,0:T(8,128)(2,1)}), bf16[8,64,320]{2,1,0:T(8,128)(2,1)S(1)}, u32[]{:S(2)}, u32[]{:S(2)}) async-start(bf16[8,64,320]{2,1,0:T(8,128)(2,1)} %bitcast.20), calls=%async_computation.2 | async-start | bytes 786432 | tf_op jit(solution)/shard_map/all_to_all | solution.py:172
  51.7 10.7 %all-to-all-done.2 = bf16[8,64,320]{2,1,0:T(8,128)(2,1)S(1)} async-done(((bf16[8,64,320]{2,1,0:T(8,128)(2,1)}), bf16[8,64,320]{2,1,0:T(8,128)(2,1)S(1)}, u32[]{:S(2)}, u32[]{:S(2)}) %all-to-all-start.2) | async-done | bytes 327712 | tf_op jit(solution)/shard_map/all_to_all | solution.py:172
  63.0 1.5 collective-permute-start
  65.8 2.5 %collective-permute-done = bf16[64,1280]{1,0:T(8,128)(2,1)S(1)} collective-permute-done((bf16[64,1280]{1,0:T(8,128)(2,1)S(1)}, bf16[64,1280]{1,0:T(8,128)(2,1)S(1)}, u32[]{:S(2)}, u32[]{:S(2)}) %collective-permute-start) | collective-permute-done | bytes 163872 | tf_op jit(solution)/shard_map/ppermute | solution.py:182
  71.7 1.4 collective-permute-start.3
  73.3 2.3 %collective-permute-done.3 = f32[64,65]{1,0:T(8,128)S(1)} collective-permute-done((f32[64,65]{1,0:T(8,128)S(1)}, f32[64,65]{1,0:T(8,128)S(1)}, u32[]{:S(2)}, u32[]{:S(2)}) %collective-permute-start.3) | collective-permute-done | bytes 16672 | tf_op jit(solution)/shard_map/ppermute | solution.py:207
  77.0 3.7 %all-to-all-start.3 = ((bf16[8,8,8,640]{3,2,1,0:T(8,128)(2,1)}), bf16[8,8,8,640]{3,2,1,0:T(8,128)(2,1)S(1)}, u32[]{:S(2)}, u32[]{:S(2)}) async-start(bf16[8,8,8,640]{3,2,1,0:T(8,128)(2,1)} %bitcast.24), calls=%async_computation.3 | async-start | bytes 1310720 | tf_op jit(solution)/shard_map/all_to_all | solution.py:313
  80.8 16.5 %all-to-all-done.3 = bf16[8,8,8,640]{3,2,1,0:T(8,128)(2,1)S(1)} async-done(((bf16[8,8,8,640]{3,2,1,0:T(8,128)(2,1)}), bf16[8,8,8,640]{3,2,1,0:T(8,128)(2,1)S(1)}, u32[]{:S(2)}, u32[]{:S(2)}) %all-to-all-start.3) | async-done | bytes 655392 | tf_op jit(solution)/shard_map/all_to_all | solution.py:313
  97.6 8.3 %fusion.30 = bf16[8,16,8,1,768]{4,2,0,1,3:T(8,128)(2,1)S(1)} fusion(bf16[8,16,8,640]{3,2,0,1:T(8,128)(2,1)S(1)} %bitcast.146, bf16[16,640,768]{2,1,0:T(8,128)(2,1)} %param.32), kind=kOutput, calls=%fused_computation.47 | convolution fusion | flops 1007419392 | bytes 18612224 | tf_op jit(solution)/shard_map/spkd,pdu->spku/dot_general | solution.py:268
  105.9 8.3 %fusion.33 = bf16[8,16,8,1,768]{4,2,0,1,3:T(8,128)(2,1)S(1)} fusion(bf16[8,16,8,640]{3,2,0,1:T(8,128)(2,1)S(1)} %bitcast.147, bf16[16,640,768]{2,1,0:T(8,128)(2,1)} %param.31), kind=kOutput, calls=%fused_computation.48 | convolution fusion | flops 1007419392 | bytes 18612224 | tf_op jit(solution)/shard_map/spkd,pdu->spku/dot_general | solution.py:267
  115.5 3.7 %collective-permute-done.4 = bf16[4,16,8,2,768]{4,2,0,1,3:T(8,128)(2,1)} collective-permute-done((bf16[4,16,8,2,768]{4,2,0,1,3:T(8,128)(2,1)}, bf16[4,16,8,2,768]{4,2,0,1,3:T(8,128)(2,1)}, u32[]{:S(2)}, u32[]{:S(2)}) %collective-permute-start.4) | collective-permute-done | bytes 1572896 | tf_op jit(solution)/shard_map/ppermute | solution.py:273
  119.2 2.0 %add_convert_fusion = bf16[4,16,8,2,768]{4,2,0,1,3:T(8,128)(2,1)S(1)} fusion(bf16[4,16,8,2,768]{4,2,0,1,3:T(8,128)(2,1)} %collective-permute-done.4, s32[]{:T(128)S(6)} %select_n.158, bf16[8,16,8,1,768]{4,2,0,1,3:T(8,128)(2,1)S(1)} %fusion.33, bf16[8,16,8,1,768]{4,2,0,1,3:T(8,128)(2,1)S(1)} %fusion.30), kind=kLoop, calls=%fused_computation.33 | loop fusion | flops 3932160 | bytes 6291460 | tf_op jit(solution)/shard_map/convert_element_type | solution.py:274
  122.4 1.5 collective-permute-start.5
  123.9 18.2 %collective-permute-done.5 = bf16[2,16,8,2,768]{4,2,0,1,3:T(8,128)(2,1)S(1)} collective-permute-done((bf16[2,16,8,2,768]{4,2,0,1,3:T(8,128)(2,1)S(1)}, bf16[2,16,8,2,768]{4,2,0,1,3:T(8,128)(2,1)S(1)}, u32[]{:S(2)}, u32[]{:S(2)}) %collective-permute-start.5) | collective-permute-done | bytes 786464 | tf_op jit(solution)/shard_map/ppermute | solution.py:281
  143.7 1.5 collective-permute-start.6
  145.2 8.9 %collective-permute-done.6 = bf16[2,16,8,768]{3,2,0,1:T(8,128)(2,1)S(1)} collective-permute-done((bf16[2,16,8,768]{3,2,0,1:T(8,128)(2,1)S(1)}, bf16[2,16,8,768]{3,2,0,1:T(8,128)(2,1)S(1)}, u32[]{:S(2)}, u32[]{:S(2)}) %collective-permute-start.6) | collective-permute-done | bytes 393248 | tf_op jit(solution)/shard_map/ppermute | solution.py:285
  156.5 8.1 %bitcast_reduce_fusion = bf16[8,8,8,640]{3,2,0,1:T(8,128)(2,1)S(1)} fusion(bf16[16,768,640]{2,1,0:T(8,128)(2,1)} %param.33, bf16[4,16,8,768]{3,2,0,1:T(8,128)(2,1)S(1)} %collective-permute-done.7, bf16[4,16,8,768]{3,2,0,1:T(8,128)(2,1)S(1)} %maximum_select_fusion.2, pred[]{:T(512)S(6)} %eq.173), kind=kOutput, calls=%fused_computation.50 | convolution fusion | flops 1009975296 | bytes 17956864 | tf_op jit(solution)/shard_map/spku,pud->spkd/dot_general | solution.py:297
  165.6 3.6 %all-to-all-start.4 = ((bf16[8,8,8,640]{3,2,1,0:T(8,128)(2,1)}), bf16[8,8,8,640]{3,2,1,0:T(8,128)(2,1)S(1)}, u32[]{:S(2)}, u32[]{:S(2)}) async-start(bf16[8,8,8,640]{3,2,1,0:T(8,128)(2,1)} %copy.150), calls=%async_computation.4 | async-start | bytes 1310720 | tf_op jit(solution)/shard_map/all_to_all | solution.py:303
  170.6 16.7 %all-to-all-done.4 = bf16[8,8,8,640]{3,2,1,0:T(8,128)(2,1)S(1)} async-done(((bf16[8,8,8,640]{3,2,1,0:T(8,128)(2,1)}), bf16[8,8,8,640]{3,2,1,0:T(8,128)(2,1)S(1)}, u32[]{:S(2)}, u32[]{:S(2)}) %all-to-all-start.4) | async-done | bytes 655392 | tf_op jit(solution)/shard_map/all_to_all | solution.py:303
  (153 shorter events, 31.9 us)
Async XLA Ops:
  0.6 45.9 %copy-start = (bf16[640,320]{0,1:T(8,128)(2,1)S(1)}, bf16[640,320]{0,1:T(8,128)(2,1)}, u32[]{:S(2)}) copy-start(bf16[640,320]{0,1:T(8,128)(2,1)} %param.27) | copy-start | bytes 1228804
  9.9 14.6 %all-to-all-start = ((bf16[8,2,32,128]{3,2,1,0:T(8,128)(2,1)}), bf16[8,2,32,128]{3,2,1,0:T(8,128)(2,1)S(1)}, u32[]{:S(2)}, u32[]{:S(2)}) async-start(bf16[8,2,32,128]{3,2,1,0:T(8,128)(2,1)} %pad_maximum_fusion), calls=%async_computation | async-start | bytes 262144 | tf_op jit(solution)/shard_map/all_to_all | solution.py:127
  47.9 16.8 %copy-start.19 = (bf16[640]{0:T(1024)(128)(2,1)S(1)}, bf16[640]{0:T(1024)(128)(2,1)}, u32[]{:S(2)}) copy-start(bf16[640]{0:T(1024)(128)(2,1)} %param.28) | copy-start | bytes 3844
  47.9 14.6 %all-to-all-start.2 = ((bf16[8,64,320]{2,1,0:T(8,128)(2,1)}), bf16[8,64,320]{2,1,0:T(8,128)(2,1)S(1)}, u32[]{:S(2)}, u32[]{:S(2)}) async-start(bf16[8,64,320]{2,1,0:T(8,128)(2,1)} %bitcast.20), calls=%async_computation.2 | async-start | bytes 786432 | tf_op jit(solution)/shard_map/all_to_all | solution.py:172
  62.7 7.4 %copy-start.8 = (f32[640,64]{0,1:T(8,128)S(1)}, f32[640,64]{0,1:T(8,128)}, u32[]{:S(2)}) copy-start(f32[640,64]{0,1:T(8,128)} %param.29) | copy-start | bytes 491524
  63.0 5.4 %collective-permute-start = (bf16[64,1280]{1,0:T(8,128)(2,1)S(1)}, bf16[64,1280]{1,0:T(8,128)(2,1)S(1)}, u32[]{:S(2)}, u32[]{:S(2)}) collective-permute-start(bf16[64,1280]{1,0:T(8,128)(2,1)S(1)} %constant_dynamic-slice_fusion.1), channel_id=1, source_target_pairs={{0,16},{8,24},{16,0},{24,8},{1,17},{9,25},{17,1},{25,9},{2,18},{10... | collective-permute-start | bytes 491528 | tf_op jit(solution)/shard_map/ppermute | solution.py:182
  68.5 1.3 collective-permute-start.1
  69.9 27.4 %copy-start.3 = (bf16[64,640]{1,0:T(8,128)(2,1)}, bf16[64,640]{1,0:T(8,128)(2,1)S(1)}, u32[]{:S(2)}) copy-start(bf16[64,640]{1,0:T(8,128)(2,1)S(1)} %get-tuple-element.201) | copy-start | bytes 245764
  70.4 1.2 collective-permute-start.2
  70.6 26.8 %copy-start.12 = (s32[64,6]{0,1:T(8,128)}, s32[64,6]{0,1:T(8,128)S(1)}, u32[]{:S(2)}) copy-start(s32[64,6]{0,1:T(8,128)S(1)} %multiply_add_fusion.1) | copy-start | bytes 4612
  71.7 3.9 %collective-permute-start.3 = (f32[64,65]{1,0:T(8,128)S(1)}, f32[64,65]{1,0:T(8,128)S(1)}, u32[]{:S(2)}, u32[]{:S(2)}) collective-permute-start(f32[64,65]{1,0:T(8,128)S(1)} %fusion.108), channel_id=1, source_target_pairs={{0,16},{8,24},{16,0},{24,8},{1,17},{9,25},{17,1},{25,9},{2,18},{10... | collective-permute-start | bytes 49928 | tf_op jit(solution)/shard_map/ppermute | solution.py:207
  75.7 21.7 %copy-start.5 = (f32[64,65]{1,0:T(8,128)}, f32[64,65]{1,0:T(8,128)S(1)}, u32[]{:S(2)}) copy-start(f32[64,65]{1,0:T(8,128)S(1)} %add.205) | copy-start | bytes 49924
  75.8 21.6 %copy-start.17 = (f32[64]{0:T(128)}, f32[64]{0:T(128)S(1)}, u32[]{:S(2)}) copy-start(f32[64]{0:T(128)S(1)} %fusion.66) | copy-start | bytes 772
  77.0 20.3 %all-to-all-start.3 = ((bf16[8,8,8,640]{3,2,1,0:T(8,128)(2,1)}), bf16[8,8,8,640]{3,2,1,0:T(8,128)(2,1)S(1)}, u32[]{:S(2)}, u32[]{:S(2)}) async-start(bf16[8,8,8,640]{3,2,1,0:T(8,128)(2,1)} %bitcast.24), calls=%async_computation.3 | async-start | bytes 1310720 | tf_op jit(solution)/shard_map/all_to_all | solution.py:313
  115.5 3.8 %collective-permute-start.4 = (bf16[4,16,8,2,768]{4,2,0,1,3:T(8,128)(2,1)}, bf16[4,16,8,2,768]{4,2,0,1,3:T(8,128)(2,1)}, u32[]{:S(2)}, u32[]{:S(2)}) collective-permute-start(bf16[4,16,8,2,768]{4,2,0,1,3:T(8,128)(2,1)} %fusion.22), channel_id=1, source_target_pairs={{0,8},{8,0},{16,24},{24,16},{1,9},{9,1},{17,25},{25,17},{2,10},{10... | collective-permute-start | bytes 4718600 | tf_op jit(solution)/shard_map/ppermute | solution.py:273
  122.4 19.6 %collective-permute-start.5 = (bf16[2,16,8,2,768]{4,2,0,1,3:T(8,128)(2,1)S(1)}, bf16[2,16,8,2,768]{4,2,0,1,3:T(8,128)(2,1)S(1)}, u32[]{:S(2)}, u32[]{:S(2)}) collective-permute-start(bf16[2,16,8,2,768]{4,2,0,1,3:T(8,128)(2,1)S(1)} %constant_dynamic-slice_fusion), channel_id=1, source_target_pairs={{0,16},{8,24},{16,0},{24,8},{1,17},{9,25},{17,1},{25,9},{2,18},{10... | collective-permute-start | bytes 2359304 | tf_op jit(solution)/shard_map/ppermute | solution.py:281
  143.4 10.8 %copy-start.16 = (s32[8,8]{1,0:T(8,128)S(1)}, s32[8,8]{1,0:T(8,128)}, u32[]{:S(2)}) copy-start(s32[8,8]{1,0:T(8,128)} %get-tuple-element.210) | copy-start | bytes 772
  143.4 10.9 %copy-start.14 = (s32[8,12]{1,0:T(8,128)S(1)}, s32[8,12]{1,0:T(8,128)}, u32[]{:S(2)}) copy-start(s32[8,12]{1,0:T(8,128)} %param.26) | copy-start | bytes 1156
  143.5 11.0 %copy-start.15 = (s32[8,12]{1,0:T(8,128)S(1)}, s32[8,12]{1,0:T(8,128)}, u32[]{:S(2)}) copy-start(s32[8,12]{1,0:T(8,128)} %param.25) | copy-start | bytes 1156
  143.7 10.4 %collective-permute-start.6 = (bf16[2,16,8,768]{3,2,0,1:T(8,128)(2,1)S(1)}, bf16[2,16,8,768]{3,2,0,1:T(8,128)(2,1)S(1)}, u32[]{:S(2)}, u32[]{:S(2)}) collective-permute-start(bf16[2,16,8,768]{3,2,0,1:T(8,128)(2,1)S(1)} %fusion.41), channel_id=1, source_target_pairs={{0,16},{8,24},{16,0},{24,8},{1,17},{9,25},{17,1},{25,9},{2,18},{10... | collective-permute-start | bytes 1179656 | tf_op jit(solution)/shard_map/ppermute | solution.py:285
  154.2 2.4 %collective-permute-start.7 = (bf16[4,16,8,768]{3,2,0,1:T(8,128)(2,1)S(1)}, bf16[4,16,8,768]{3,2,0,1:T(8,128)(2,1)S(1)}, u32[]{:S(2)}, u32[]{:S(2)}) collective-permute-start(bf16[4,16,8,768]{3,2,0,1:T(8,128)(2,1)S(1)} %maximum_select_fusion.2), channel_id=1, source_target_pairs={{0,8},{8,0},{16,24},{24,16},{1,9},{9,1},{17,25},{25,17},{2,10},{10... | collective-permute-start | bytes 2359304 | tf_op jit(solution)/shard_map/ppermute | solution.py:291
  164.7 22.7 %copy-start.4 = (bf16[64,640]{1,0:T(8,128)(2,1)S(1)}, bf16[64,640]{1,0:T(8,128)(2,1)}, u32[]{:S(2)}) copy-start(bf16[64,640]{1,0:T(8,128)(2,1)} %copy-done.3) | copy-start | bytes 245764
  164.7 23.7 %copy-start.1 = (bf16[640,320]{0,1:T(8,128)(2,1)S(1)}, bf16[640,320]{0,1:T(8,128)(2,1)}, u32[]{:S(2)}) copy-start(bf16[640,320]{0,1:T(8,128)(2,1)} %param.27) | copy-start | bytes 1228804
  165.6 21.7 %all-to-all-start.4 = ((bf16[8,8,8,640]{3,2,1,0:T(8,128)(2,1)}), bf16[8,8,8,640]{3,2,1,0:T(8,128)(2,1)S(1)}, u32[]{:S(2)}, u32[]{:S(2)}) async-start(bf16[8,8,8,640]{3,2,1,0:T(8,128)(2,1)} %copy.150), calls=%async_computation.4 | async-start | bytes 1310720 | tf_op jit(solution)/shard_map/all_to_all | solution.py:303
  (8 other events, 40.2 us)

commit v13 on v12

--- a/solution.py
+++ b/solution.py
@@ -96,25 +96,34 @@
     in_use = jnp.arange(max_blocks)[None, :] < (cache_len // block_len)[:, None]
     pool_rows = cache_pool[:, :, 0]
     fresh_rows = new_kv[:, 0]
-    sources = jnp.concatenate(
-        [pool_rows, fresh_rows.reshape(fresh_count, block_len, 2, head_dim)], axis=0
-    )
     held_here = in_use & (block_holder == own_index)
     old_target = jnp.where(held_here, decode_holder[:, :max_blocks], blk_count).reshape(-1)
-    pick_old = jax.ops.segment_sum((block_slot + 1).reshape(-1), old_target, num_segments=blk_count)
-    pick_new = jax.ops.segment_sum(
-        pool_size + 1 + jnp.arange(fresh_count),
-        decode_holder[own_index, max_blocks:],
-        num_segments=blk_count,
+    pick_old = jnp.sum(
+        jnp.where(
+            old_target[None, :] == devices[:, None], (block_slot + 1).reshape(-1)[None, :], 0
+        ),
+        axis=1,
+    )
+    new_dest = lax.dynamic_index_in_dim(decode_holder, own_index, 0, keepdims=False)[max_blocks:]
+    pick_new = jnp.sum(
+        jnp.where(
+            new_dest[None, :] == devices[:, None],
+            (pool_size + 1 + jnp.arange(fresh_count))[None, :],
+            0,
+        ),
+        axis=1,
     )
     picked = pick_old + pick_new
-    source_count = sources.shape[0]
+    source_count = pool_size + fresh_count
     send_pick = (jnp.arange(source_count)[None, :] == (picked - 1)[:, None]).astype(jnp.bfloat16)
     sending = (
-        jnp.dot(send_pick, sources.reshape(source_count, -1), preferred_element_type=jnp.float32)
-        .astype(jnp.bfloat16)
-        .reshape((blk_count,) + sources.shape[1:])
-    )
+        jnp.dot(send_pick[:, :pool_size], pool_rows.reshape(pool_size, -1), preferred_element_type=jnp.float32)
+        + jnp.dot(
+            send_pick[:, pool_size:],
+            fresh_rows.reshape(fresh_count, -1),
+            preferred_element_type=jnp.float32,
+        )
+    ).astype(jnp.bfloat16).reshape((blk_count,) + pool_rows.shape[1:])
     match_here = (block_holder[:blk_count] == own_index) & in_use[:blk_count]
     out_slot = jnp.sum(jnp.where(match_here, block_slot[:blk_count], 0), axis=1)
     out_pick = (jnp.arange(pool_size)[None, :] == out_slot[:, None]).astype(jnp.bfloat16)

time: 190 us -> 188 us (0.989)
  transfers between devices with their start and end apart: 12 -> 12, of which waited for: 11 -> 11; matrix products, arithmetic and copies ran while one was open for 5% -> 4% of each run, Pallas kernels for 0% -> 0%
where the time goes in v13:
time: 188 us; the launch traced here: 187 us
  waiting for transfers between devices  86.1 us (46%)
  matrix products  29.4 us (16%)
  starting transfers between devices  24.7 us (13%)
  blocking collectives  18.9 us (10%)
  other arithmetic  15.1 us (8%)
  local copies, waits for them, and re-layouts  11.3 us (6%)
    all_to_all x1, blocking collectives, per_device(): lax.all_to_all(jnp.broadcast_to(attended[None], (blk_count,) + attended.s...  18.9 us
    ppermute x1, waiting for transfers between devices, out_stage(): lax.ppermute(chip_given, 'kv', flip_chip).astype(jnp.float32)  18.1 us
    all_to_all x1, waiting for transfers between devices, out_stage(): lax.all_to_all(half_sum, 'blk', split_axis=0, concat_axis=0, tiled=True)  16.7 us
    all_to_all x1, waiting for transfers between devices, per_device(): lax.all_to_all(outgoing_rows[:, i * chunk_experts:(i + 1) * chunk_experts...  16.5 us
    all_to_all x1, waiting for transfers between devices, per_device(): lax.all_to_all(column_part, 'blk', split_axis=0, concat_axis=1, tiled=True)  10.7 us
    ppermute x1, waiting for transfers between devices, out_stage(): hidden_far = lax.ppermute(hidden_quarter, 'kv', flip_chip)  8.85 us
    dot_general x1, matrix products, pair_stage(): jnp.einsum('spkd,pdu->spku', rows_in, up_w, preferred_element_type=jnp.fl...  8.31 us
    dot_general x1, matrix products, pair_stage(): jnp.einsum('spkd,pdu->spku', rows_in, gate_w, preferred_element_type=jnp....  8.3 us
  transfers between devices with their start and end apart: 12, of which 11 were waited for; matrix products, arithmetic and copies ran while one was open for 4% of the time, Pallas kernels for 0%

profile of v13, /device:TPU:0, one launch (start us, length us, event | category | flops | bytes accessed | tf_op | source)
XLA Modules:
  0.0 187.4 jit_solution(3012879775769449475)
XLA Ops:
  2.2 1.4 slice_select_fusion
  8.7 7.3 %all-to-all-start = ((bf16[8,2,32,128]{3,2,1,0:T(8,128)(2,1)}), bf16[8,2,32,128]{3,2,1,0:T(8,128)(2,1)S(1)}, u32[]{:S(2)}, u32[]{:S(2)}) async-start(bf16[8,2,32,128]{3,2,1,0:T(8,128)(2,1)} %pad_maximum_fusion), calls=%async_computation | async-start | bytes 262144 | tf_op jit(solution)/shard_map/all_to_all | solution.py:136
  18.6 4.7 %all-to-all-done = bf16[8,2,32,128]{3,2,1,0:T(8,128)(2,1)S(1)} async-done(((bf16[8,2,32,128]{3,2,1,0:T(8,128)(2,1)}), bf16[8,2,32,128]{3,2,1,0:T(8,128)(2,1)S(1)}, u32[]{:S(2)}, u32[]{:S(2)}) %all-to-all-start) | async-done | bytes 131104 | tf_op jit(solution)/shard_map/all_to_all | solution.py:136
  24.6 1.4 while.16
  26.4 18.9 %all_to_all.39 = bf16[8,64,640]{2,1,0:T(8,128)(2,1)S(1)} all-to-all(bf16[8,64,640]{2,1,0:T(8,128)(2,1)S(1)} %broadcast_in_dim.167), channel_id=1, replica_groups=mesh['kv'=4,'blk'=8] {'blk'}, dimensions={0} | all-to-all | bytes 1310720 | tf_op jit(solution)/shard_map/all_to_all | solution.py:175
  46.7 3.6 %all-to-all-start.2 = ((bf16[8,64,320]{2,1,0:T(8,128)(2,1)}), bf16[8,64,320]{2,1,0:T(8,128)(2,1)S(1)}, u32[]{:S(2)}, u32[]{:S(2)}) async-start(bf16[8,64,320]{2,1,0:T(8,128)(2,1)} %bitcast.20), calls=%async_computation.2 | async-start | bytes 786432 | tf_op jit(solution)/shard_map/all_to_all | solution.py:181
  50.5 10.7 %all-to-all-done.2 = bf16[8,64,320]{2,1,0:T(8,128)(2,1)S(1)} async-done(((bf16[8,64,320]{2,1,0:T(8,128)(2,1)}), bf16[8,64,320]{2,1,0:T(8,128)(2,1)S(1)}, u32[]{:S(2)}, u32[]{:S(2)}) %all-to-all-start.2) | async-done | bytes 327712 | tf_op jit(solution)/shard_map/all_to_all | solution.py:181
  61.8 1.6 collective-permute-start
  64.7 2.5 %collective-permute-done = bf16[64,1280]{1,0:T(8,128)(2,1)S(1)} collective-permute-done((bf16[64,1280]{1,0:T(8,128)(2,1)S(1)}, bf16[64,1280]{1,0:T(8,128)(2,1)S(1)}, u32[]{:S(2)}, u32[]{:S(2)}) %collective-permute-start) | collective-permute-done | bytes 163872 | tf_op jit(solution)/shard_map/ppermute | solution.py:191
  70.5 1.5 collective-permute-start.3
  72.2 2.3 %collective-permute-done.3 = f32[64,65]{1,0:T(8,128)S(1)} collective-permute-done((f32[64,65]{1,0:T(8,128)S(1)}, f32[64,65]{1,0:T(8,128)S(1)}, u32[]{:S(2)}, u32[]{:S(2)}) %collective-permute-start.3) | collective-permute-done | bytes 16672 | tf_op jit(solution)/shard_map/ppermute | solution.py:216
  75.8 3.7 %all-to-all-start.3 = ((bf16[8,8,8,640]{3,2,1,0:T(8,128)(2,1)}), bf16[8,8,8,640]{3,2,1,0:T(8,128)(2,1)S(1)}, u32[]{:S(2)}, u32[]{:S(2)}) async-start(bf16[8,8,8,640]{3,2,1,0:T(8,128)(2,1)} %bitcast.24), calls=%async_computation.3 | async-start | bytes 1310720 | tf_op jit(solution)/shard_map/all_to_all | solution.py:322
  79.6 16.5 %all-to-all-done.3 = bf16[8,8,8,640]{3,2,1,0:T(8,128)(2,1)S(1)} async-done(((bf16[8,8,8,640]{3,2,1,0:T(8,128)(2,1)}), bf16[8,8,8,640]{3,2,1,0:T(8,128)(2,1)S(1)}, u32[]{:S(2)}, u32[]{:S(2)}) %all-to-all-start.3) | async-done | bytes 655392 | tf_op jit(solution)/shard_map/all_to_all | solution.py:322
  96.4 8.3 %fusion.31 = bf16[8,16,8,1,768]{4,2,0,1,3:T(8,128)(2,1)S(1)} fusion(bf16[8,16,8,640]{3,2,0,1:T(8,128)(2,1)S(1)} %bitcast.148, bf16[16,640,768]{2,1,0:T(8,128)(2,1)} %param.32), kind=kOutput, calls=%fused_computation.46 | convolution fusion | flops 1007419392 | bytes 18612224 | tf_op jit(solution)/shard_map/spkd,pdu->spku/dot_general | solution.py:277
  104.7 8.3 %fusion.34 = bf16[8,16,8,1,768]{4,2,0,1,3:T(8,128)(2,1)S(1)} fusion(bf16[8,16,8,640]{3,2,0,1:T(8,128)(2,1)S(1)} %bitcast.149, bf16[16,640,768]{2,1,0:T(8,128)(2,1)} %param.31), kind=kOutput, calls=%fused_computation.47 | convolution fusion | flops 1007419392 | bytes 18612224 | tf_op jit(solution)/shard_map/spkd,pdu->spku/dot_general | solution.py:276
  114.3 3.7 %collective-permute-done.4 = bf16[4,16,8,2,768]{4,2,0,1,3:T(8,128)(2,1)} collective-permute-done((bf16[4,16,8,2,768]{4,2,0,1,3:T(8,128)(2,1)}, bf16[4,16,8,2,768]{4,2,0,1,3:T(8,128)(2,1)}, u32[]{:S(2)}, u32[]{:S(2)}) %collective-permute-start.4) | collective-permute-done | bytes 1572896 | tf_op jit(solution)/shard_map/ppermute | solution.py:282
  118.0 2.0 %add_convert_fusion = bf16[4,16,8,2,768]{4,2,0,1,3:T(8,128)(2,1)S(1)} fusion(bf16[4,16,8,2,768]{4,2,0,1,3:T(8,128)(2,1)} %collective-permute-done.4, s32[]{:T(128)S(6)} %select_n.169, bf16[8,16,8,1,768]{4,2,0,1,3:T(8,128)(2,1)S(1)} %fusion.34, bf16[8,16,8,1,768]{4,2,0,1,3:T(8,128)(2,1)S(1)} %fusion.31), kind=kLoop, calls=%fused_computation.32 | loop fusion | flops 3932160 | bytes 6291460 | tf_op jit(solution)/shard_map/convert_element_type | solution.py:283
  121.2 1.5 collective-permute-start.5
  122.8 18.1 %collective-permute-done.5 = bf16[2,16,8,2,768]{4,2,0,1,3:T(8,128)(2,1)S(1)} collective-permute-done((bf16[2,16,8,2,768]{4,2,0,1,3:T(8,128)(2,1)S(1)}, bf16[2,16,8,2,768]{4,2,0,1,3:T(8,128)(2,1)S(1)}, u32[]{:S(2)}, u32[]{:S(2)}) %collective-permute-start.5) | collective-permute-done | bytes 786464 | tf_op jit(solution)/shard_map/ppermute | solution.py:290
  142.5 1.5 collective-permute-start.6
  144.0 8.8 %collective-permute-done.6 = bf16[2,16,8,768]{3,2,0,1:T(8,128)(2,1)S(1)} collective-permute-done((bf16[2,16,8,768]{3,2,0,1:T(8,128)(2,1)S(1)}, bf16[2,16,8,768]{3,2,0,1:T(8,128)(2,1)S(1)}, u32[]{:S(2)}, u32[]{:S(2)}) %collective-permute-start.6) | collective-permute-done | bytes 393248 | tf_op jit(solution)/shard_map/ppermute | solution.py:294
  155.5 8.1 %bitcast_reduce_fusion = bf16[8,8,8,640]{3,2,0,1:T(8,128)(2,1)S(1)} fusion(bf16[16,768,640]{2,1,0:T(8,128)(2,1)} %param.33, bf16[4,16,8,768]{3,2,0,1:T(8,128)(2,1)S(1)} %collective-permute-done.7, bf16[4,16,8,768]{3,2,0,1:T(8,128)(2,1)S(1)} %maximum_select_fusion.2, pred[]{:T(512)S(6)} %eq.213), kind=kOutput, calls=%fused_computation.49 | convolution fusion | flops 1009975296 | bytes 17956864 | tf_op jit(solution)/shard_map/spku,pud->spkd/dot_general | solution.py:306
  164.6 3.6 %all-to-all-start.4 = ((bf16[8,8,8,640]{3,2,1,0:T(8,128)(2,1)}), bf16[8,8,8,640]{3,2,1,0:T(8,128)(2,1)S(1)}, u32[]{:S(2)}, u32[]{:S(2)}) async-start(bf16[8,8,8,640]{3,2,1,0:T(8,128)(2,1)} %copy.150), calls=%async_computation.4 | async-start | bytes 1310720 | tf_op jit(solution)/shard_map/all_to_all | solution.py:312
  169.6 16.7 %all-to-all-done.4 = bf16[8,8,8,640]{3,2,1,0:T(8,128)(2,1)S(1)} async-done(((bf16[8,8,8,640]{3,2,1,0:T(8,128)(2,1)}), bf16[8,8,8,640]{3,2,1,0:T(8,128)(2,1)S(1)}, u32[]{:S(2)}, u32[]{:S(2)}) %all-to-all-start.4) | async-done | bytes 655392 | tf_op jit(solution)/shard_map/all_to_all | solution.py:312
  (158 shorter events, 30.1 us)
Async XLA Ops:
  0.6 44.7 %copy-start = (bf16[640,320]{0,1:T(8,128)(2,1)S(1)}, bf16[640,320]{0,1:T(8,128)(2,1)}, u32[]{:S(2)}) copy-start(bf16[640,320]{0,1:T(8,128)(2,1)} %param.27) | copy-start | bytes 1228804
  0.6 17.4 %copy-start.9 = (bf16[64,640]{1,0:T(8,128)(2,1)S(1)}, bf16[64,640]{1,0:T(8,128)(2,1)}, u32[]{:S(2)}) copy-start(bf16[64,640]{1,0:T(8,128)(2,1)} %param.19) | copy-start | bytes 245764
  8.7 14.6 %all-to-all-start = ((bf16[8,2,32,128]{3,2,1,0:T(8,128)(2,1)}), bf16[8,2,32,128]{3,2,1,0:T(8,128)(2,1)S(1)}, u32[]{:S(2)}, u32[]{:S(2)}) async-start(bf16[8,2,32,128]{3,2,1,0:T(8,128)(2,1)} %pad_maximum_fusion), calls=%async_computation | async-start | bytes 262144 | tf_op jit(solution)/shard_map/all_to_all | solution.py:136
  46.7 16.9 %copy-start.20 = (bf16[640]{0:T(1024)(128)(2,1)S(1)}, bf16[640]{0:T(1024)(128)(2,1)}, u32[]{:S(2)}) copy-start(bf16[640]{0:T(1024)(128)(2,1)} %param.28) | copy-start | bytes 3844
  46.7 14.6 %all-to-all-start.2 = ((bf16[8,64,320]{2,1,0:T(8,128)(2,1)}), bf16[8,64,320]{2,1,0:T(8,128)(2,1)S(1)}, u32[]{:S(2)}, u32[]{:S(2)}) async-start(bf16[8,64,320]{2,1,0:T(8,128)(2,1)} %bitcast.20), calls=%async_computation.2 | async-start | bytes 786432 | tf_op jit(solution)/shard_map/all_to_all | solution.py:181
  61.8 5.4 %collective-permute-start = (bf16[64,1280]{1,0:T(8,128)(2,1)S(1)}, bf16[64,1280]{1,0:T(8,128)(2,1)S(1)}, u32[]{:S(2)}, u32[]{:S(2)}) collective-permute-start(bf16[64,1280]{1,0:T(8,128)(2,1)S(1)} %constant_dynamic-slice_fusion.1), channel_id=1, source_target_pairs={{0,16},{8,24},{16,0},{24,8},{1,17},{9,25},{17,1},{25,9},{2,18},{10... | collective-permute-start | bytes 491528 | tf_op jit(solution)/shard_map/ppermute | solution.py:191
  67.3 1.3 collective-permute-start.1
  68.7 27.4 %copy-start.3 = (bf16[64,640]{1,0:T(8,128)(2,1)}, bf16[64,640]{1,0:T(8,128)(2,1)S(1)}, u32[]{:S(2)}) copy-start(bf16[64,640]{1,0:T(8,128)(2,1)S(1)} %get-tuple-element.201) | copy-start | bytes 245764
  69.2 1.2 collective-permute-start.2
  69.4 26.8 %copy-start.13 = (s32[64,6]{0,1:T(8,128)}, s32[64,6]{0,1:T(8,128)S(1)}, u32[]{:S(2)}) copy-start(s32[64,6]{0,1:T(8,128)S(1)} %multiply_add_fusion.1) | copy-start | bytes 4612
  70.5 3.9 %collective-permute-start.3 = (f32[64,65]{1,0:T(8,128)S(1)}, f32[64,65]{1,0:T(8,128)S(1)}, u32[]{:S(2)}, u32[]{:S(2)}) collective-permute-start(f32[64,65]{1,0:T(8,128)S(1)} %fusion.105), channel_id=1, source_target_pairs={{0,16},{8,24},{16,0},{24,8},{1,17},{9,25},{17,1},{25,9},{2,18},{10... | collective-permute-start | bytes 49928 | tf_op jit(solution)/shard_map/ppermute | solution.py:216
  74.5 21.7 %copy-start.5 = (f32[64,65]{1,0:T(8,128)}, f32[64,65]{1,0:T(8,128)S(1)}, u32[]{:S(2)}) copy-start(f32[64,65]{1,0:T(8,128)S(1)} %add.218) | copy-start | bytes 49924
  74.6 21.6 %copy-start.18 = (f32[64]{0:T(128)}, f32[64]{0:T(128)S(1)}, u32[]{:S(2)}) copy-start(f32[64]{0:T(128)S(1)} %fusion.64) | copy-start | bytes 772
  75.8 20.3 %all-to-all-start.3 = ((bf16[8,8,8,640]{3,2,1,0:T(8,128)(2,1)}), bf16[8,8,8,640]{3,2,1,0:T(8,128)(2,1)S(1)}, u32[]{:S(2)}, u32[]{:S(2)}) async-start(bf16[8,8,8,640]{3,2,1,0:T(8,128)(2,1)} %bitcast.24), calls=%async_computation.3 | async-start | bytes 1310720 | tf_op jit(solution)/shard_map/all_to_all | solution.py:322
  114.3 3.8 %collective-permute-start.4 = (bf16[4,16,8,2,768]{4,2,0,1,3:T(8,128)(2,1)}, bf16[4,16,8,2,768]{4,2,0,1,3:T(8,128)(2,1)}, u32[]{:S(2)}, u32[]{:S(2)}) collective-permute-start(bf16[4,16,8,2,768]{4,2,0,1,3:T(8,128)(2,1)} %fusion.23), channel_id=1, source_target_pairs={{0,8},{8,0},{16,24},{24,16},{1,9},{9,1},{17,25},{25,17},{2,10},{10... | collective-permute-start | bytes 4718600 | tf_op jit(solution)/shard_map/ppermute | solution.py:282
  121.2 19.6 %collective-permute-start.5 = (bf16[2,16,8,2,768]{4,2,0,1,3:T(8,128)(2,1)S(1)}, bf16[2,16,8,2,768]{4,2,0,1,3:T(8,128)(2,1)S(1)}, u32[]{:S(2)}, u32[]{:S(2)}) collective-permute-start(bf16[2,16,8,2,768]{4,2,0,1,3:T(8,128)(2,1)S(1)} %constant_dynamic-slice_fusion), channel_id=1, source_target_pairs={{0,16},{8,24},{16,0},{24,8},{1,17},{9,25},{17,1},{25,9},{2,18},{10... | collective-permute-start | bytes 2359304 | tf_op jit(solution)/shard_map/ppermute | solution.py:290
  142.2 10.8 %copy-start.17 = (s32[8,8]{1,0:T(8,128)S(1)}, s32[8,8]{1,0:T(8,128)}, u32[]{:S(2)}) copy-start(s32[8,8]{1,0:T(8,128)} %get-tuple-element.210) | copy-start | bytes 772
  142.2 10.9 %copy-start.15 = (s32[8,12]{1,0:T(8,128)S(1)}, s32[8,12]{1,0:T(8,128)}, u32[]{:S(2)}) copy-start(s32[8,12]{1,0:T(8,128)} %param.26) | copy-start | bytes 1156
  142.3 11.0 %copy-start.16 = (s32[8,12]{1,0:T(8,128)S(1)}, s32[8,12]{1,0:T(8,128)}, u32[]{:S(2)}) copy-start(s32[8,12]{1,0:T(8,128)} %param.25) | copy-start | bytes 1156
  142.5 10.4 %collective-permute-start.6 = (bf16[2,16,8,768]{3,2,0,1:T(8,128)(2,1)S(1)}, bf16[2,16,8,768]{3,2,0,1:T(8,128)(2,1)S(1)}, u32[]{:S(2)}, u32[]{:S(2)}) collective-permute-start(bf16[2,16,8,768]{3,2,0,1:T(8,128)(2,1)S(1)} %fusion.42), channel_id=1, source_target_pairs={{0,16},{8,24},{16,0},{24,8},{1,17},{9,25},{17,1},{25,9},{2,18},{10... | collective-permute-start | bytes 1179656 | tf_op jit(solution)/shard_map/ppermute | solution.py:294
  153.0 2.5 %collective-permute-start.7 = (bf16[4,16,8,768]{3,2,0,1:T(8,128)(2,1)S(1)}, bf16[4,16,8,768]{3,2,0,1:T(8,128)(2,1)S(1)}, u32[]{:S(2)}, u32[]{:S(2)}) collective-permute-start(bf16[4,16,8,768]{3,2,0,1:T(8,128)(2,1)S(1)} %maximum_select_fusion.2), channel_id=1, source_target_pairs={{0,8},{8,0},{16,24},{24,16},{1,9},{9,1},{17,25},{25,17},{2,10},{10... | collective-permute-start | bytes 2359304 | tf_op jit(solution)/shard_map/ppermute | solution.py:300
  163.7 22.7 %copy-start.4 = (bf16[64,640]{1,0:T(8,128)(2,1)S(1)}, bf16[64,640]{1,0:T(8,128)(2,1)}, u32[]{:S(2)}) copy-start(bf16[64,640]{1,0:T(8,128)(2,1)} %copy-done.3) | copy-start | bytes 245764
  163.7 23.7 %copy-start.1 = (bf16[640,320]{0,1:T(8,128)(2,1)S(1)}, bf16[640,320]{0,1:T(8,128)(2,1)}, u32[]{:S(2)}) copy-start(bf16[640,320]{0,1:T(8,128)(2,1)} %param.27) | copy-start | bytes 1228804
  164.6 21.7 %all-to-all-start.4 = ((bf16[8,8,8,640]{3,2,1,0:T(8,128)(2,1)}), bf16[8,8,8,640]{3,2,1,0:T(8,128)(2,1)S(1)}, u32[]{:S(2)}, u32[]{:S(2)}) async-start(bf16[8,8,8,640]{3,2,1,0:T(8,128)(2,1)} %copy.150), calls=%async_computation.4 | async-start | bytes 1310720 | tf_op jit(solution)/shard_map/all_to_all | solution.py:312
  (9 other events, 47.6 us)

commit v14 on v13

--- a/solution.py
+++ b/solution.py
@@ -172,13 +172,28 @@
         .transpose(1, 0, 2)
     )
     attended = attended.reshape(stretch_len, head_count * head_dim).astype(jnp.bfloat16)
-    every_token = lax.all_to_all(
-        jnp.broadcast_to(attended[None], (blk_count,) + attended.shape), "blk", 0, 0, tiled=True
-    ).reshape(-1, attended.shape[1])
-    column_part = jnp.dot(
-        every_token, out_weight, preferred_element_type=jnp.float32
-    ).astype(jnp.bfloat16)
-    projected = lax.all_to_all(column_part, "blk", split_axis=0, concat_axis=1, tiled=True)
+    if blk_count <= 8:
+        back_parts = []
+        for shift in range(blk_count):
+            there = [(i, (i + shift) % blk_count) for i in range(blk_count)]
+            back = [(i, (i - shift) % blk_count) for i in range(blk_count)]
+            rows_from = attended if shift == 0 else lax.ppermute(attended, "blk", there)
+            part = jnp.dot(rows_from, out_weight, preferred_element_type=jnp.float32)
+            part = part.astype(jnp.bfloat16)
+            back_parts.append(part if shift == 0 else lax.ppermute(part, "blk", back))
+        by_shift = jnp.concatenate(back_parts + back_parts, axis=1)
+        col_width = out_weight.shape[1]
+        projected = lax.dynamic_slice_in_dim(
+            by_shift, (blk_count - own_index) % blk_count * col_width, blk_count * col_width, 1
+        )
+    else:
+        every_token = lax.all_to_all(
+            jnp.broadcast_to(attended[None], (blk_count,) + attended.shape), "blk", 0, 0, tiled=True
+        ).reshape(-1, attended.shape[1])
+        column_part = jnp.dot(
+            every_token, out_weight, preferred_element_type=jnp.float32
+        ).astype(jnp.bfloat16)
+        projected = lax.all_to_all(column_part, "blk", split_axis=0, concat_axis=1, tiled=True)
     kv_index = lax.axis_index("kv")
     if lax.axis_size("kv") == 4:
         chip_bit = kv_index // 2

time: 188 us -> 183 us (0.973)
  blocking collectives: 18.9 us -> 0 us
  starting transfers between devices: 24.7 us -> 43.4 us
  waiting for transfers between devices: 86.1 us -> 82.2 us
    ppermute x0 -> x14, starting transfers between devices: none -> 21.8 us  [the longest x7 11.4 us: per_device(): back_parts.append(part if shift == 0 else lax.ppermute(part, 'blk', back))]
    all_to_all x1 -> x0, blocking collectives: 18.9 us -> none  [per_device(): lax.all_to_all(jnp.broadcast_to(attended[None], (blk_count,) + attended.s...]
    all_to_all x1 -> x0, waiting for transfers between devices: 10.7 us -> none  [per_device(): lax.all_to_all(column_part, 'blk', split_axis=0, concat_axis=1, tiled=True)]
    ppermute x0 -> x14, waiting for transfers between devices: none -> 6.93 us  [the longest x7 5.03 us: per_device(): back_parts.append(part if shift == 0 else lax.ppermute(part, 'blk', back))]
    all_to_all x1 -> x0, starting transfers between devices: 3.58 us -> none  [per_device(): lax.all_to_all(column_part, 'blk', split_axis=0, concat_axis=1, tiled=True)]
  transfers between devices with their start and end apart: 12 -> 25, of which waited for: 11 -> 15; matrix products, arithmetic and copies ran while one was open for 4% -> 5% of each run, Pallas kernels for 0% -> 0%
where the time goes in v14:
time: 183 us
  waiting for transfers between devices  82.2 us (45%)
  starting transfers between devices  43.4 us (24%)
  matrix products  30.4 us (17%)
  other arithmetic  14.2 us (8%)
  local copies, waits for them, and re-layouts  10.5 us (6%)
  between operations  1.95 us (1%)
    ppermute x1, waiting for transfers between devices, out_stage(): lax.ppermute(chip_given, 'kv', flip_chip).astype(jnp.float32)  18.1 us
    all_to_all x1, waiting for transfers between devices, out_stage(): lax.all_to_all(half_sum, 'blk', split_axis=0, concat_axis=0, tiled=True)  16.7 us
    all_to_all x1, waiting for transfers between devices, per_device(): lax.all_to_all(outgoing_rows[:, i * chunk_experts:(i + 1) * chunk_experts...  16.5 us
    ppermute x7, starting transfers between devices, per_device(): back_parts.append(part if shift == 0 else lax.ppermute(part, 'blk', back))  11.4 us
    ppermute x7, starting transfers between devices, per_device(): rows_from = attended if shift == 0 else lax.ppermute(attended, 'blk', there)  10.4 us
    ppermute x1, waiting for transfers between devices, out_stage(): hidden_far = lax.ppermute(hidden_quarter, 'kv', flip_chip)  8.82 us
    dot_general x1, matrix products, pair_stage(): jnp.einsum('spkd,pdu->spku', rows_in, gate_w, preferred_element_type=jnp....  8.3 us
    dot_general x1, matrix products, pair_stage(): jnp.einsum('spkd,pdu->spku', rows_in, up_w, preferred_element_type=jnp.fl...  8.3 us
  transfers between devices with their start and end apart: 25, of which 15 were waited for; matrix products, arithmetic and copies ran while one was open for 5% of the time, Pallas kernels for 0%

profile of v14, /device:TPU:0, one launch (start us, length us, event | category | flops | bytes accessed | tf_op | source)
XLA Modules:
  0.0 182.6 jit_solution(7633405353709044751)
XLA Ops:
  8.7 7.3 %all-to-all-start = ((bf16[8,2,32,128]{3,2,1,0:T(8,128)(2,1)}), bf16[8,2,32,128]{3,2,1,0:T(8,128)(2,1)S(1)}, u32[]{:S(2)}, u32[]{:S(2)}) async-start(bf16[8,2,32,128]{3,2,1,0:T(8,128)(2,1)} %pad_maximum_fusion), calls=%async_computation | async-start | bytes 262144 | tf_op jit(solution)/shard_map/all_to_all | solution.py:136
  18.6 4.7 %all-to-all-done = bf16[8,2,32,128]{3,2,1,0:T(8,128)(2,1)S(1)} async-done(((bf16[8,2,32,128]{3,2,1,0:T(8,128)(2,1)}), bf16[8,2,32,128]{3,2,1,0:T(8,128)(2,1)S(1)}, u32[]{:S(2)}, u32[]{:S(2)}) %all-to-all-start) | async-done | bytes 131104 | tf_op jit(solution)/shard_map/all_to_all | solution.py:136
  25.6 2.7 %collective-permute-start.10 = (bf16[64,640]{1,0:T(8,128)(2,1)S(1)}, bf16[64,640]{1,0:T(8,128)(2,1)S(1)}, u32[]{:S(2)}, u32[]{:S(2)}) collective-permute-start(bf16[64,640]{1,0:T(8,128)(2,1)S(1)} %bitcast.170), channel_id=1, source_target_pairs={{0,6},{1,7},{2,0},{3,1},{4,2},{5,3},{6,4},{7,5},{8,14},{9,15},{10,... | collective-permute-start | bytes 245768 | tf_op jit(solution)/shard_map/ppermute | solution.py:180
  28.3 1.8 %collective-permute-start.12 = (bf16[64,640]{1,0:T(8,128)(2,1)S(1)}, bf16[64,640]{1,0:T(8,128)(2,1)S(1)}, u32[]{:S(2)}, u32[]{:S(2)}) collective-permute-start(bf16[64,640]{1,0:T(8,128)(2,1)S(1)} %bitcast.171), channel_id=1, source_target_pairs={{0,7},{1,0},{2,1},{3,2},{4,3},{5,4},{6,5},{7,6},{8,15},{9,8},{10,9... | collective-permute-start | bytes 245768 | tf_op jit(solution)/shard_map/ppermute | solution.py:180
  30.1 1.8 %collective-permute-start.2 = (bf16[64,640]{1,0:T(8,128)(2,1)S(1)}, bf16[64,640]{1,0:T(8,128)(2,1)S(1)}, u32[]{:S(2)}, u32[]{:S(2)}) collective-permute-start(bf16[64,640]{1,0:T(8,128)(2,1)S(1)} %bitcast.172), channel_id=1, source_target_pairs={{0,2},{1,3},{2,4},{3,5},{4,6},{5,7},{6,0},{7,1},{8,10},{9,11},{10,... | collective-permute-start | bytes 245768 | tf_op jit(solution)/shard_map/ppermute | solution.py:180
  32.2 2.2 %collective-permute-start.6 = (bf16[64,640]{1,0:T(8,128)(2,1)S(1)}, bf16[64,640]{1,0:T(8,128)(2,1)S(1)}, u32[]{:S(2)}, u32[]{:S(2)}) collective-permute-start(bf16[64,640]{1,0:T(8,128)(2,1)S(1)} %bitcast.174), channel_id=1, source_target_pairs={{0,4},{1,5},{2,6},{3,7},{4,0},{5,1},{6,2},{7,3},{8,12},{9,13},{10,... | collective-permute-start | bytes 245768 | tf_op jit(solution)/shard_map/ppermute | solution.py:180
  36.4 2.1 %collective-permute-start.1 = (bf16[64,320]{1,0:T(8,128)(2,1)S(1)}, bf16[64,320]{1,0:T(8,128)(2,1)S(1)}, u32[]{:S(2)}, u32[]{:S(2)}) collective-permute-start(bf16[64,320]{1,0:T(8,128)(2,1)S(1)} %convolution_convert_fusion.9), channel_id=1, source_target_pairs={{0,7},{1,0},{2,1},{3,2},{4,3},{5,4},{6,5},{7,6},{8,15},{9,8},{10,9... | collective-permute-start | bytes 122888 | tf_op jit(solution)/shard_map/ppermute | solution.py:183
  41.3 2.7 %collective-permute-start.13 = (bf16[64,320]{1,0:T(8,128)(2,1)S(1)}, bf16[64,320]{1,0:T(8,128)(2,1)S(1)}, u32[]{:S(2)}, u32[]{:S(2)}) collective-permute-start(bf16[64,320]{1,0:T(8,128)(2,1)S(1)} %convolution_convert_fusion.3), channel_id=1, source_target_pairs={{0,1},{1,2},{2,3},{3,4},{4,5},{5,6},{6,7},{7,0},{8,9},{9,10},{10,1... | collective-permute-start | bytes 122888 | tf_op jit(solution)/shard_map/ppermute | solution.py:183
  44.3 2.2 %collective-permute-start.3 = (bf16[64,320]{1,0:T(8,128)(2,1)S(1)}, bf16[64,320]{1,0:T(8,128)(2,1)S(1)}, u32[]{:S(2)}, u32[]{:S(2)}) collective-permute-start(bf16[64,320]{1,0:T(8,128)(2,1)S(1)} %convolution_convert_fusion.8), channel_id=1, source_target_pairs={{0,6},{1,7},{2,0},{3,1},{4,2},{5,3},{6,4},{7,5},{8,14},{9,15},{10,... | collective-permute-start | bytes 122888 | tf_op jit(solution)/shard_map/ppermute | solution.py:183
  51.8 2.2 %collective-permute-done.7 = bf16[64,320]{1,0:T(8,128)(2,1)S(1)} collective-permute-done((bf16[64,320]{1,0:T(8,128)(2,1)S(1)}, bf16[64,320]{1,0:T(8,128)(2,1)S(1)}, u32[]{:S(2)}, u32[]{:S(2)}) %collective-permute-start.7) | collective-permute-done | bytes 40992 | tf_op jit(solution)/shard_map/ppermute | solution.py:183
  54.0 2.2 %collective-permute-done.9 = bf16[64,320]{1,0:T(8,128)(2,1)S(1)} collective-permute-done((bf16[64,320]{1,0:T(8,128)(2,1)S(1)}, bf16[64,320]{1,0:T(8,128)(2,1)S(1)}, u32[]{:S(2)}, u32[]{:S(2)}) %collective-permute-start.9) | collective-permute-done | bytes 40992 | tf_op jit(solution)/shard_map/ppermute | solution.py:183
  59.7 2.4 %collective-permute-done.14 = bf16[64,1280]{1,0:T(8,128)(2,1)S(1)} collective-permute-done((bf16[64,1280]{1,0:T(8,128)(2,1)S(1)}, bf16[64,1280]{1,0:T(8,128)(2,1)S(1)}, u32[]{:S(2)}, u32[]{:S(2)}) %collective-permute-start.14) | collective-permute-done | bytes 163872 | tf_op jit(solution)/shard_map/ppermute | solution.py:206
  67.2 2.2 %collective-permute-done.17 = f32[64,65]{1,0:T(8,128)S(1)} collective-permute-done((f32[64,65]{1,0:T(8,128)S(1)}, f32[64,65]{1,0:T(8,128)S(1)}, u32[]{:S(2)}, u32[]{:S(2)}) %collective-permute-start.17) | collective-permute-done | bytes 16672 | tf_op jit(solution)/shard_map/ppermute | solution.py:231
  70.8 4.2 %all-to-all-start.1 = ((bf16[8,8,8,640]{3,2,1,0:T(8,128)(2,1)}), bf16[8,8,8,640]{3,2,1,0:T(8,128)(2,1)S(1)}, u32[]{:S(2)}, u32[]{:S(2)}) async-start(bf16[8,8,8,640]{3,2,1,0:T(8,128)(2,1)} %bitcast.21), calls=%async_computation.1 | async-start | bytes 1310720 | tf_op jit(solution)/shard_map/all_to_all | solution.py:337
  75.0 16.5 %all-to-all-done.1 = bf16[8,8,8,640]{3,2,1,0:T(8,128)(2,1)S(1)} async-done(((bf16[8,8,8,640]{3,2,1,0:T(8,128)(2,1)}), bf16[8,8,8,640]{3,2,1,0:T(8,128)(2,1)S(1)}, u32[]{:S(2)}, u32[]{:S(2)}) %all-to-all-start.1) | async-done | bytes 655392 | tf_op jit(solution)/shard_map/all_to_all | solution.py:337
  91.8 8.3 %fusion.31 = bf16[8,16,8,1,768]{4,2,0,1,3:T(8,128)(2,1)S(1)} fusion(bf16[8,16,8,640]{3,2,0,1:T(8,128)(2,1)S(1)} %bitcast.159, bf16[16,640,768]{2,1,0:T(8,128)(2,1)} %param.32), kind=kOutput, calls=%fused_computation.46 | convolution fusion | flops 1007419392 | bytes 18612224 | tf_op jit(solution)/shard_map/spkd,pdu->spku/dot_general | solution.py:292
  100.1 8.3 %fusion.34 = bf16[8,16,8,1,768]{4,2,0,1,3:T(8,128)(2,1)S(1)} fusion(bf16[8,16,8,640]{3,2,0,1:T(8,128)(2,1)S(1)} %bitcast.160, bf16[16,640,768]{2,1,0:T(8,128)(2,1)} %param.31), kind=kOutput, calls=%fused_computation.47 | convolution fusion | flops 1007419392 | bytes 18612224 | tf_op jit(solution)/shard_map/spkd,pdu->spku/dot_general | solution.py:291
  109.7 3.7 %collective-permute-done.18 = bf16[4,16,8,2,768]{4,2,0,1,3:T(8,128)(2,1)} collective-permute-done((bf16[4,16,8,2,768]{4,2,0,1,3:T(8,128)(2,1)}, bf16[4,16,8,2,768]{4,2,0,1,3:T(8,128)(2,1)}, u32[]{:S(2)}, u32[]{:S(2)}) %collective-permute-start.18) | collective-permute-done | bytes 1572896 | tf_op jit(solution)/shard_map/ppermute | solution.py:297
  113.5 2.0 %add_convert_fusion = bf16[4,16,8,2,768]{4,2,0,1,3:T(8,128)(2,1)S(1)} fusion(bf16[4,16,8,2,768]{4,2,0,1,3:T(8,128)(2,1)} %collective-permute-done.18, s32[]{:T(128)S(6)} %select_n.187, bf16[8,16,8,1,768]{4,2,0,1,3:T(8,128)(2,1)S(1)} %fusion.34, bf16[8,16,8,1,768]{4,2,0,1,3:T(8,128)(2,1)S(1)} %fusion.31), kind=kLoop, calls=%fused_computation.32 | loop fusion | flops 3932160 | bytes 6291460 | tf_op jit(solution)/shard_map/convert_element_type | solution.py:298
  118.2 18.1 %collective-permute-done.19 = bf16[2,16,8,2,768]{4,2,0,1,3:T(8,128)(2,1)S(1)} collective-permute-done((bf16[2,16,8,2,768]{4,2,0,1,3:T(8,128)(2,1)S(1)}, bf16[2,16,8,2,768]{4,2,0,1,3:T(8,128)(2,1)S(1)}, u32[]{:S(2)}, u32[]{:S(2)}) %collective-permute-start.19) | collective-permute-done | bytes 786464 | tf_op jit(solution)/shard_map/ppermute | solution.py:305
  139.5 8.8 %collective-permute-done.20 = bf16[2,16,8,768]{3,2,0,1:T(8,128)(2,1)S(1)} collective-permute-done((bf16[2,16,8,768]{3,2,0,1:T(8,128)(2,1)S(1)}, bf16[2,16,8,768]{3,2,0,1:T(8,128)(2,1)S(1)}, u32[]{:S(2)}, u32[]{:S(2)}) %collective-permute-start.20) | collective-permute-done | bytes 393248 | tf_op jit(solution)/shard_map/ppermute | solution.py:309
  150.8 8.1 %bitcast_reduce_fusion = bf16[8,8,8,640]{3,2,0,1:T(8,128)(2,1)S(1)} fusion(bf16[16,768,640]{2,1,0:T(8,128)(2,1)} %param.33, bf16[4,16,8,768]{3,2,0,1:T(8,128)(2,1)S(1)} %collective-permute-done.21, bf16[4,16,8,768]{3,2,0,1:T(8,128)(2,1)S(1)} %maximum_select_fusion.2, pred[]{:T(512)S(6)} %eq.214), kind=kOutput, calls=%fused_computation.49 | convolution fusion | flops 1009975296 | bytes 17956864 | tf_op jit(solution)/shard_map/spku,pud->spkd/dot_general | solution.py:321
  159.8 3.6 %all-to-all-start.2 = ((bf16[8,8,8,640]{3,2,1,0:T(8,128)(2,1)}), bf16[8,8,8,640]{3,2,1,0:T(8,128)(2,1)S(1)}, u32[]{:S(2)}, u32[]{:S(2)}) async-start(bf16[8,8,8,640]{3,2,1,0:T(8,128)(2,1)} %copy.135), calls=%async_computation.2 | async-start | bytes 1310720 | tf_op jit(solution)/shard_map/all_to_all | solution.py:327
  164.9 16.7 %all-to-all-done.2 = bf16[8,8,8,640]{3,2,1,0:T(8,128)(2,1)S(1)} async-done(((bf16[8,8,8,640]{3,2,1,0:T(8,128)(2,1)}), bf16[8,8,8,640]{3,2,1,0:T(8,128)(2,1)S(1)}, u32[]{:S(2)}, u32[]{:S(2)}) %all-to-all-start.2) | async-done | bytes 655392 | tf_op jit(solution)/shard_map/all_to_all | solution.py:327
  (179 shorter events, 45.8 us)
Async XLA Ops:
  8.7 14.6 %all-to-all-start = ((bf16[8,2,32,128]{3,2,1,0:T(8,128)(2,1)}), bf16[8,2,32,128]{3,2,1,0:T(8,128)(2,1)S(1)}, u32[]{:S(2)}, u32[]{:S(2)}) async-start(bf16[8,2,32,128]{3,2,1,0:T(8,128)(2,1)} %pad_maximum_fusion), calls=%async_computation | async-start | bytes 262144 | tf_op jit(solution)/shard_map/all_to_all | solution.py:136
  24.9 7.3 %collective-permute-start = (bf16[64,640]{1,0:T(8,128)(2,1)S(1)}, bf16[64,640]{1,0:T(8,128)(2,1)S(1)}, u32[]{:S(2)}, u32[]{:S(2)}) collective-permute-start(bf16[64,640]{1,0:T(8,128)(2,1)S(1)} %bitcast.169), channel_id=1, source_target_pairs={{0,1},{1,2},{2,3},{3,4},{4,5},{5,6},{6,7},{7,0},{8,9},{9,10},{10,1... | collective-permute-start | bytes 245768 | tf_op jit(solution)/shard_map/ppermute | solution.py:180
  25.6 9.0 %collective-permute-start.10 = (bf16[64,640]{1,0:T(8,128)(2,1)S(1)}, bf16[64,640]{1,0:T(8,128)(2,1)S(1)}, u32[]{:S(2)}, u32[]{:S(2)}) collective-permute-start(bf16[64,640]{1,0:T(8,128)(2,1)S(1)} %bitcast.170), channel_id=1, source_target_pairs={{0,6},{1,7},{2,0},{3,1},{4,2},{5,3},{6,4},{7,5},{8,14},{9,15},{10,... | collective-permute-start | bytes 245768 | tf_op jit(solution)/shard_map/ppermute | solution.py:180
  28.3 8.1 %collective-permute-start.12 = (bf16[64,640]{1,0:T(8,128)(2,1)S(1)}, bf16[64,640]{1,0:T(8,128)(2,1)S(1)}, u32[]{:S(2)}, u32[]{:S(2)}) collective-permute-start(bf16[64,640]{1,0:T(8,128)(2,1)S(1)} %bitcast.171), channel_id=1, source_target_pairs={{0,7},{1,0},{2,1},{3,2},{4,3},{5,4},{6,5},{7,6},{8,15},{9,8},{10,9... | collective-permute-start | bytes 245768 | tf_op jit(solution)/shard_map/ppermute | solution.py:180
  30.1 8.6 %collective-permute-start.2 = (bf16[64,640]{1,0:T(8,128)(2,1)S(1)}, bf16[64,640]{1,0:T(8,128)(2,1)S(1)}, u32[]{:S(2)}, u32[]{:S(2)}) collective-permute-start(bf16[64,640]{1,0:T(8,128)(2,1)S(1)} %bitcast.172), channel_id=1, source_target_pairs={{0,2},{1,3},{2,4},{3,5},{4,6},{5,7},{6,0},{7,1},{8,10},{9,11},{10,... | collective-permute-start | bytes 245768 | tf_op jit(solution)/shard_map/ppermute | solution.py:180
  32.0 9.3 %collective-permute-start.4 = (bf16[64,640]{1,0:T(8,128)(2,1)S(1)}, bf16[64,640]{1,0:T(8,128)(2,1)S(1)}, u32[]{:S(2)}, u32[]{:S(2)}) collective-permute-start(bf16[64,640]{1,0:T(8,128)(2,1)S(1)} %bitcast.173), channel_id=1, source_target_pairs={{0,3},{1,4},{2,5},{3,6},{4,7},{5,0},{6,1},{7,2},{8,11},{9,12},{10,... | collective-permute-start | bytes 245768 | tf_op jit(solution)/shard_map/ppermute | solution.py:180
  32.2 12.1 %collective-permute-start.6 = (bf16[64,640]{1,0:T(8,128)(2,1)S(1)}, bf16[64,640]{1,0:T(8,128)(2,1)S(1)}, u32[]{:S(2)}, u32[]{:S(2)}) collective-permute-start(bf16[64,640]{1,0:T(8,128)(2,1)S(1)} %bitcast.174), channel_id=1, source_target_pairs={{0,4},{1,5},{2,6},{3,7},{4,0},{5,1},{6,2},{7,3},{8,12},{9,13},{10,... | collective-permute-start | bytes 245768 | tf_op jit(solution)/shard_map/ppermute | solution.py:180
  34.6 12.2 %collective-permute-start.8 = (bf16[64,640]{1,0:T(8,128)(2,1)S(1)}, bf16[64,640]{1,0:T(8,128)(2,1)S(1)}, u32[]{:S(2)}, u32[]{:S(2)}) collective-permute-start(bf16[64,640]{1,0:T(8,128)(2,1)S(1)} %bitcast.175), channel_id=1, source_target_pairs={{0,5},{1,6},{2,7},{3,0},{4,1},{5,2},{6,3},{7,4},{8,13},{9,14},{10,... | collective-permute-start | bytes 245768 | tf_op jit(solution)/shard_map/ppermute | solution.py:180
  36.4 12.3 %collective-permute-start.1 = (bf16[64,320]{1,0:T(8,128)(2,1)S(1)}, bf16[64,320]{1,0:T(8,128)(2,1)S(1)}, u32[]{:S(2)}, u32[]{:S(2)}) collective-permute-start(bf16[64,320]{1,0:T(8,128)(2,1)S(1)} %convolution_convert_fusion.9), channel_id=1, source_target_pairs={{0,7},{1,0},{2,1},{3,2},{4,3},{5,4},{6,5},{7,6},{8,15},{9,8},{10,9... | collective-permute-start | bytes 122888 | tf_op jit(solution)/shard_map/ppermute | solution.py:183
  38.7 11.6 %collective-permute-start.11 = (bf16[64,320]{1,0:T(8,128)(2,1)S(1)}, bf16[64,320]{1,0:T(8,128)(2,1)S(1)}, u32[]{:S(2)}, u32[]{:S(2)}) collective-permute-start(bf16[64,320]{1,0:T(8,128)(2,1)S(1)} %convolution_convert_fusion.4), channel_id=1, source_target_pairs={{0,2},{1,3},{2,4},{3,5},{4,6},{5,7},{6,0},{7,1},{8,10},{9,11},{10,... | collective-permute-start | bytes 122888 | tf_op jit(solution)/shard_map/ppermute | solution.py:183
  41.3 9.9 %collective-permute-start.13 = (bf16[64,320]{1,0:T(8,128)(2,1)S(1)}, bf16[64,320]{1,0:T(8,128)(2,1)S(1)}, u32[]{:S(2)}, u32[]{:S(2)}) collective-permute-start(bf16[64,320]{1,0:T(8,128)(2,1)S(1)} %convolution_convert_fusion.3), channel_id=1, source_target_pairs={{0,1},{1,2},{2,3},{3,4},{4,5},{5,6},{6,7},{7,0},{8,9},{9,10},{10,1... | collective-permute-start | bytes 122888 | tf_op jit(solution)/shard_map/ppermute | solution.py:183
  44.3 6.9 %collective-permute-start.3 = (bf16[64,320]{1,0:T(8,128)(2,1)S(1)}, bf16[64,320]{1,0:T(8,128)(2,1)S(1)}, u32[]{:S(2)}, u32[]{:S(2)}) collective-permute-start(bf16[64,320]{1,0:T(8,128)(2,1)S(1)} %convolution_convert_fusion.8), channel_id=1, source_target_pairs={{0,6},{1,7},{2,0},{3,1},{4,2},{5,3},{6,4},{7,5},{8,14},{9,15},{10,... | collective-permute-start | bytes 122888 | tf_op jit(solution)/shard_map/ppermute | solution.py:183
  46.8 5.0 %collective-permute-start.5 = (bf16[64,320]{1,0:T(8,128)(2,1)S(1)}, bf16[64,320]{1,0:T(8,128)(2,1)S(1)}, u32[]{:S(2)}, u32[]{:S(2)}) collective-permute-start(bf16[64,320]{1,0:T(8,128)(2,1)S(1)} %convolution_convert_fusion.7), channel_id=1, source_target_pairs={{0,5},{1,6},{2,7},{3,0},{4,1},{5,2},{6,3},{7,4},{8,13},{9,14},{10,... | collective-permute-start | bytes 122888 | tf_op jit(solution)/shard_map/ppermute | solution.py:183
  48.7 5.2 %collective-permute-start.7 = (bf16[64,320]{1,0:T(8,128)(2,1)S(1)}, bf16[64,320]{1,0:T(8,128)(2,1)S(1)}, u32[]{:S(2)}, u32[]{:S(2)}) collective-permute-start(bf16[64,320]{1,0:T(8,128)(2,1)S(1)} %convolution_convert_fusion.6), channel_id=1, source_target_pairs={{0,4},{1,5},{2,6},{3,7},{4,0},{5,1},{6,2},{7,3},{8,12},{9,13},{10,... | collective-permute-start | bytes 122888 | tf_op jit(solution)/shard_map/ppermute | solution.py:183
  50.3 5.9 %collective-permute-start.9 = (bf16[64,320]{1,0:T(8,128)(2,1)S(1)}, bf16[64,320]{1,0:T(8,128)(2,1)S(1)}, u32[]{:S(2)}, u32[]{:S(2)}) collective-permute-start(bf16[64,320]{1,0:T(8,128)(2,1)S(1)} %convolution_convert_fusion.5), channel_id=1, source_target_pairs={{0,3},{1,4},{2,5},{3,6},{4,7},{5,0},{6,1},{7,2},{8,11},{9,12},{10,... | collective-permute-start | bytes 122888 | tf_op jit(solution)/shard_map/ppermute | solution.py:183
  56.7 5.4 %collective-permute-start.14 = (bf16[64,1280]{1,0:T(8,128)(2,1)S(1)}, bf16[64,1280]{1,0:T(8,128)(2,1)S(1)}, u32[]{:S(2)}, u32[]{:S(2)}) collective-permute-start(bf16[64,1280]{1,0:T(8,128)(2,1)S(1)} %constant_dynamic-slice_fusion.1), channel_id=1, source_target_pairs={{0,16},{8,24},{16,0},{24,8},{1,17},{9,25},{17,1},{25,9},{2,18},{10... | collective-permute-start | bytes 491528 | tf_op jit(solution)/shard_map/ppermute | solution.py:206
  62.3 1.3 collective-permute-start.15
  65.6 3.9 %collective-permute-start.17 = (f32[64,65]{1,0:T(8,128)S(1)}, f32[64,65]{1,0:T(8,128)S(1)}, u32[]{:S(2)}, u32[]{:S(2)}) collective-permute-start(f32[64,65]{1,0:T(8,128)S(1)} %fusion.119), channel_id=1, source_target_pairs={{0,16},{8,24},{16,0},{24,8},{1,17},{9,25},{17,1},{25,9},{2,18},{10... | collective-permute-start | bytes 49928 | tf_op jit(solution)/shard_map/ppermute | solution.py:231
  70.8 20.7 %all-to-all-start.1 = ((bf16[8,8,8,640]{3,2,1,0:T(8,128)(2,1)}), bf16[8,8,8,640]{3,2,1,0:T(8,128)(2,1)S(1)}, u32[]{:S(2)}, u32[]{:S(2)}) async-start(bf16[8,8,8,640]{3,2,1,0:T(8,128)(2,1)} %bitcast.21), calls=%async_computation.1 | async-start | bytes 1310720 | tf_op jit(solution)/shard_map/all_to_all | solution.py:337
  109.7 3.8 %collective-permute-start.18 = (bf16[4,16,8,2,768]{4,2,0,1,3:T(8,128)(2,1)}, bf16[4,16,8,2,768]{4,2,0,1,3:T(8,128)(2,1)}, u32[]{:S(2)}, u32[]{:S(2)}) collective-permute-start(bf16[4,16,8,2,768]{4,2,0,1,3:T(8,128)(2,1)} %fusion.23), channel_id=1, source_target_pairs={{0,8},{8,0},{16,24},{24,16},{1,9},{9,1},{17,25},{25,17},{2,10},{10... | collective-permute-start | bytes 4718600 | tf_op jit(solution)/shard_map/ppermute | solution.py:297
  116.7 19.6 %collective-permute-start.19 = (bf16[2,16,8,2,768]{4,2,0,1,3:T(8,128)(2,1)S(1)}, bf16[2,16,8,2,768]{4,2,0,1,3:T(8,128)(2,1)S(1)}, u32[]{:S(2)}, u32[]{:S(2)}) collective-permute-start(bf16[2,16,8,2,768]{4,2,0,1,3:T(8,128)(2,1)S(1)} %constant_dynamic-slice_fusion), channel_id=1, source_target_pairs={{0,16},{8,24},{16,0},{24,8},{1,17},{9,25},{17,1},{25,9},{2,18},{10... | collective-permute-start | bytes 2359304 | tf_op jit(solution)/shard_map/ppermute | solution.py:305
  137.9 10.4 %collective-permute-start.20 = (bf16[2,16,8,768]{3,2,0,1:T(8,128)(2,1)S(1)}, bf16[2,16,8,768]{3,2,0,1:T(8,128)(2,1)S(1)}, u32[]{:S(2)}, u32[]{:S(2)}) collective-permute-start(bf16[2,16,8,768]{3,2,0,1:T(8,128)(2,1)S(1)} %fusion.42), channel_id=1, source_target_pairs={{0,16},{8,24},{16,0},{24,8},{1,17},{9,25},{17,1},{25,9},{2,18},{10... | collective-permute-start | bytes 1179656 | tf_op jit(solution)/shard_map/ppermute | solution.py:309
  148.4 2.4 %collective-permute-start.21 = (bf16[4,16,8,768]{3,2,0,1:T(8,128)(2,1)S(1)}, bf16[4,16,8,768]{3,2,0,1:T(8,128)(2,1)S(1)}, u32[]{:S(2)}, u32[]{:S(2)}) collective-permute-start(bf16[4,16,8,768]{3,2,0,1:T(8,128)(2,1)S(1)} %maximum_select_fusion.2), channel_id=1, source_target_pairs={{0,8},{8,0},{16,24},{24,16},{1,9},{9,1},{17,25},{25,17},{2,10},{10... | collective-permute-start | bytes 2359304 | tf_op jit(solution)/shard_map/ppermute | solution.py:315
  159.8 21.7 %all-to-all-start.2 = ((bf16[8,8,8,640]{3,2,1,0:T(8,128)(2,1)}), bf16[8,8,8,640]{3,2,1,0:T(8,128)(2,1)S(1)}, u32[]{:S(2)}, u32[]{:S(2)}) async-start(bf16[8,8,8,640]{3,2,1,0:T(8,128)(2,1)} %copy.135), calls=%async_computation.2 | async-start | bytes 1310720 | tf_op jit(solution)/shard_map/all_to_all | solution.py:327
  (22 other events, 296.4 us)

commit v15 on v14

--- a/solution.py
+++ b/solution.py
@@ -324,23 +324,46 @@
         if paired:
             half_sum = piece_out.reshape(blk_count, chunk_pieces // 2, 2, capacity, feature_part)
             half_sum = jnp.sum(half_sum.astype(jnp.float32), axis=2).astype(jnp.bfloat16)
+            if shifted:
+                back_sets = [half_sum[0]] + [
+                    lax.ppermute(
+                        half_sum[shift],
+                        "blk",
+                        [(i, (i - shift) % blk_count) for i in range(blk_count)],
+                    )
+                    for shift in range(1, blk_count)
+                ]
+                by_shift = jnp.stack(back_sets + back_sets)
+                return lax.dynamic_slice_in_dim(
+                    by_shift, (blk_count - own_index) % blk_count, blk_count, 0
+                )
             return lax.all_to_all(half_sum, "blk", split_axis=0, concat_axis=0, tiled=True)
         returned = lax.all_to_all(piece_out, "blk", split_axis=0, concat_axis=0, tiled=True)
         per_piece = returned.reshape(expert_count, 2, capacity, feature_part).astype(jnp.float32)
         return (per_piece[:, 0] + per_piece[:, 1]).astype(jnp.bfloat16)
 
     chunk_count = CHUNKS if paired and experts_here % CHUNKS == 0 else 1
+    shifted = paired and blk_count <= 8
     chunk_experts = experts_here // chunk_count
     chunk_pieces = pieces_here // chunk_count
     piece_sets = [slice(i * chunk_pieces, (i + 1) * chunk_pieces) for i in range(chunk_count)]
+    def dispatch(rows_now):
+        if not shifted:
+            return lax.all_to_all(rows_now, "blk", split_axis=0, concat_axis=0, tiled=True)
+        arrivals = []
+        for shift in range(blk_count):
+            mine = lax.dynamic_index_in_dim(
+                rows_now, (own_index + shift) % blk_count, 0, keepdims=False
+            )
+            if shift:
+                mine = lax.ppermute(
+                    mine, "blk", [(i, (i + shift) % blk_count) for i in range(blk_count)]
+                )
+            arrivals.append(mine)
+        return jnp.stack(arrivals)
+
     landed_sets = [
-        lax.all_to_all(
-            outgoing_rows[:, i * chunk_experts : (i + 1) * chunk_experts],
-            "blk",
-            split_axis=0,
-            concat_axis=0,
-            tiled=True,
-        )
+        dispatch(outgoing_rows[:, i * chunk_experts : (i + 1) * chunk_experts])
         for i in range(chunk_count)
     ]
     pair_sets = []

time: 183 us -> 185 us (1.011)
  waiting for transfers between devices: 82.2 us -> 56.2 us
  local copies, waits for them, and re-layouts: 10.5 us -> 23.2 us
  starting transfers between devices: 43.4 us -> 55.5 us
  other arithmetic: 14.2 us -> 19.5 us
  matrix products: 30.4 us -> 27.5 us
    all_to_all x2 -> x0, waiting for transfers between devices: 33.2 us -> none  [the longest x1 16.7 us: out_stage(): lax.all_to_all(half_sum, 'blk', split_axis=0, concat_axis=0, tiled=True)]
    ppermute x0 -> x14, starting transfers between devices: none -> 22.3 us  [the longest x7 12.2 us: out_stage(): lax.ppermute(half_sum[shift], 'blk', [(i, (i - shift) % blk_count) for i...]
    ppermute x0 -> x14, waiting for transfers between devices: none -> 12.5 us  [the longest x7 10.3 us: out_stage(): lax.ppermute(half_sum[shift], 'blk', [(i, (i - shift) % blk_count) for i...]
    all_to_all x2 -> x0, starting transfers between devices: 7.81 us -> none  [the longest x1 4.17 us: per_device(): lax.all_to_all(outgoing_rows[:, i * chunk_experts:(i + 1) * chunk_experts...]
    dot_general x1, matrix products: 8.3 us -> 2.84 us  [pair_stage(): jnp.einsum('spkd,pdu->spku', rows_in, gate_w, preferred_element_type=jnp....]
    unnamed x48 -> x85, local copies, waits for them, and re-layouts: 3.66 us -> 8.19 us
    ppermute x1, waiting for transfers between devices: 2.44 us -> 0.01 us  [per_device(): lax.ppermute(chip_given, 'kv', swap_chip).astype(jnp.float32)]
    ppermute x1, waiting for transfers between devices: 18.1 us -> 15.7 us  [out_stage(): lax.ppermute(chip_given, 'kv', flip_chip).astype(jnp.float32)]
  transfers between devices with their start and end apart: 25 -> 37, of which waited for: 15 -> 14; matrix products, arithmetic and copies ran while one was open for 5% -> 13% of each run, Pallas kernels for 0% -> 0%
where the time goes in v15:
time: 185 us; the launch traced here: 184 us
  waiting for transfers between devices  56.2 us (30%)
  starting transfers between devices  55.5 us (30%)
  matrix products  27.5 us (15%)
  local copies, waits for them, and re-layouts  23.2 us (13%)
  other arithmetic  19.5 us (11%)
  between operations  2.39 us (1%)
    ppermute x1, waiting for transfers between devices, out_stage(): lax.ppermute(chip_given, 'kv', flip_chip).astype(jnp.float32)  15.7 us
    ppermute x7, starting transfers between devices, out_stage(): lax.ppermute(half_sum[shift], 'blk', [(i, (i - shift) % blk_count) for i...  12.2 us
    ppermute x7, starting transfers between devices, per_device(): back_parts.append(part if shift == 0 else lax.ppermute(part, 'blk', back))  11.3 us
    ppermute x7, starting transfers between devices, per_device(): rows_from = attended if shift == 0 else lax.ppermute(attended, 'blk', there)  10.8 us
    ppermute x7, waiting for transfers between devices, out_stage(): lax.ppermute(half_sum[shift], 'blk', [(i, (i - shift) % blk_count) for i...  10.3 us
    ppermute x7, starting transfers between devices, dispatch(): lax.ppermute(mine, 'blk', [(i, (i + shift) % blk_count) for i in range(bl...  10.1 us
    ppermute x1, waiting for transfers between devices, out_stage(): hidden_far = lax.ppermute(hidden_quarter, 'kv', flip_chip)  8.96 us
    dot_general x1, matrix products, pair_stage(): jnp.einsum('spkd,pdu->spku', rows_in, up_w, preferred_element_type=jnp.fl...  8.45 us
  transfers between devices with their start and end apart: 37, of which 14 were waited for; matrix products, arithmetic and copies ran while one was open for 13% of the time, Pallas kernels for 0%

profile of v15, /device:TPU:0, one launch (start us, length us, event | category | flops | bytes accessed | tf_op | source)
XLA Modules:
  0.0 184.3 jit_solution(8836439824518522144)
XLA Ops:
  8.7 7.3 %all-to-all-start = ((bf16[8,2,32,128]{3,2,1,0:T(8,128)(2,1)}), bf16[8,2,32,128]{3,2,1,0:T(8,128)(2,1)S(1)}, u32[]{:S(2)}, u32[]{:S(2)}) async-start(bf16[8,2,32,128]{3,2,1,0:T(8,128)(2,1)} %pad_maximum_fusion), calls=%async_computation | async-start | bytes 262144 | tf_op jit(solution)/shard_map/all_to_all | solution.py:136
  18.1 5.2 %all-to-all-done = bf16[8,2,32,128]{3,2,1,0:T(8,128)(2,1)S(1)} async-done(((bf16[8,2,32,128]{3,2,1,0:T(8,128)(2,1)}), bf16[8,2,32,128]{3,2,1,0:T(8,128)(2,1)S(1)}, u32[]{:S(2)}, u32[]{:S(2)}) %all-to-all-start) | async-done | bytes 131104 | tf_op jit(solution)/shard_map/all_to_all | solution.py:136
  27.5 3.0 %collective-permute-start.12 = (bf16[64,640]{1,0:T(8,128)(2,1)S(1)}, bf16[64,640]{1,0:T(8,128)(2,1)S(1)}, u32[]{:S(2)}, u32[]{:S(2)}) collective-permute-start(bf16[64,640]{1,0:T(8,128)(2,1)S(1)} %bitcast.255), channel_id=1, source_target_pairs={{0,7},{1,0},{2,1},{3,2},{4,3},{5,4},{6,5},{7,6},{8,15},{9,8},{10,9... | collective-permute-start | bytes 245768 | tf_op jit(solution)/shard_map/ppermute | solution.py:180
  30.5 2.0 %collective-permute-start.2 = (bf16[64,640]{1,0:T(8,128)(2,1)S(1)}, bf16[64,640]{1,0:T(8,128)(2,1)S(1)}, u32[]{:S(2)}, u32[]{:S(2)}) collective-permute-start(bf16[64,640]{1,0:T(8,128)(2,1)S(1)} %bitcast.256), channel_id=1, source_target_pairs={{0,2},{1,3},{2,4},{3,5},{4,6},{5,7},{6,0},{7,1},{8,10},{9,11},{10,... | collective-permute-start | bytes 245768 | tf_op jit(solution)/shard_map/ppermute | solution.py:180
  32.5 2.4 %collective-permute-start.6 = (bf16[64,640]{1,0:T(8,128)(2,1)S(1)}, bf16[64,640]{1,0:T(8,128)(2,1)S(1)}, u32[]{:S(2)}, u32[]{:S(2)}) collective-permute-start(bf16[64,640]{1,0:T(8,128)(2,1)S(1)} %bitcast.258), channel_id=1, source_target_pairs={{0,4},{1,5},{2,6},{3,7},{4,0},{5,1},{6,2},{7,3},{8,12},{9,13},{10,... | collective-permute-start | bytes 245768 | tf_op jit(solution)/shard_map/ppermute | solution.py:180
  41.8 2.9 %collective-permute-start.13 = (bf16[64,320]{1,0:T(8,128)(2,1)S(1)}, bf16[64,320]{1,0:T(8,128)(2,1)}, u32[]{:S(2)}, u32[]{:S(2)}) collective-permute-start(bf16[64,320]{1,0:T(8,128)(2,1)S(1)} %convolution_convert_fusion.3), channel_id=1, source_target_pairs={{0,1},{1,2},{2,3},{3,4},{4,5},{5,6},{6,7},{7,0},{8,9},{9,10},{10,1... | collective-permute-start | bytes 122888 | tf_op jit(solution)/shard_map/ppermute | solution.py:183
  47.0 2.2 %collective-permute-start.5 = (bf16[64,320]{1,0:T(8,128)(2,1)S(1)}, bf16[64,320]{1,0:T(8,128)(2,1)}, u32[]{:S(2)}, u32[]{:S(2)}) collective-permute-start(bf16[64,320]{1,0:T(8,128)(2,1)S(1)} %convolution_convert_fusion.7), channel_id=1, source_target_pairs={{0,5},{1,6},{2,7},{3,0},{4,1},{5,2},{6,3},{7,4},{8,13},{9,14},{10,... | collective-permute-start | bytes 122888 | tf_op jit(solution)/shard_map/ppermute | solution.py:183
  51.6 1.9 %convolution_convert_fusion.10 = bf16[64,320]{1,0:T(8,128)(2,1)} fusion(bf16[64,640]{1,0:T(8,128)(2,1)} %bitcast.260, bf16[640,320]{0,1:T(8,128)(2,1)S(1)} %copy-done), kind=kOutput, calls=%fused_computation.62 | convolution fusion | flops 26234880 | bytes 532480 | tf_op jit(solution)/shard_map/dot_general | solution.py:181
  57.0 2.2 %concatenate.18 = bf16[64,5120]{1,0:T(8,128)(2,1)} concatenate(bf16[64,320]{1,0:T(8,128)(2,1)} %convolution_convert_fusion.10, bf16[64,320]{1,0:T(8,128)(2,1)} %copy-done.12, bf16[64,320]{1,0:T(8,128)(2,1)} %collective-permute-done.3, bf16[64,320]{1,0:T(8,128)(2,1)} %collective-permute-done.5, bf16[64,320]{1,0:T(8,128)(2,1)} %collective-permute-done.7, ...), dimensions={1} | concatenate | bytes 1310720 | tf_op jit(solution)/shard_map/concatenate | solution.py:184
  76.5 3.1 %collective-permute-done.17 = f32[64,65]{1,0:T(8,128)S(1)} collective-permute-done((f32[64,65]{1,0:T(8,128)S(1)}, f32[64,65]{1,0:T(8,128)S(1)}, u32[]{:S(2)}, u32[]{:S(2)}) %collective-permute-start.17) | collective-permute-done | bytes 16672 | tf_op jit(solution)/shard_map/ppermute | solution.py:231
  83.7 1.9 %collective-permute-start.20 = (bf16[8,8,640]{2,1,0:T(8,128)(2,1)}, bf16[8,8,640]{2,1,0:T(8,128)(2,1)S(1)}, u32[]{:S(2)}, u32[]{:S(2)}) collective-permute-start(bf16[8,8,640]{2,1,0:T(8,128)(2,1)} %get-tuple-element.199), channel_id=1, source_target_pairs={{0,3},{1,4},{2,5},{3,6},{4,7},{5,0},{6,1},{7,2},{8,11},{9,12},{10,... | collective-permute-start | bytes 245768 | tf_op jit(solution)/shard_map/ppermute | solution.py:359
  85.6 3.3 %collective-permute-start.21 = (bf16[8,8,640]{2,1,0:T(8,128)(2,1)}, bf16[8,8,640]{2,1,0:T(8,128)(2,1)S(1)}, u32[]{:S(2)}, u32[]{:S(2)}) collective-permute-start(bf16[8,8,640]{2,1,0:T(8,128)(2,1)} %get-tuple-element.198), channel_id=1, source_target_pairs={{0,4},{1,5},{2,6},{3,7},{4,0},{5,1},{6,2},{7,3},{8,12},{9,13},{10,... | collective-permute-start | bytes 245768 | tf_op jit(solution)/shard_map/ppermute | solution.py:359
  100.7 8.5 %fusion.31 = bf16[8,16,8,1,768]{4,2,0,1,3:T(8,128)(2,1)S(1)} fusion(bf16[8,16,8,640]{3,2,0,1:T(8,128)(2,1)S(1)} %bitcast.242, bf16[16,640,768]{2,1,0:T(8,128)(2,1)} %param.32), kind=kOutput, calls=%fused_computation.46 | convolution fusion | flops 1007419392 | bytes 18612224 | tf_op jit(solution)/shard_map/spkd,pdu->spku/dot_general | solution.py:292
  109.2 2.8 %fusion.34 = bf16[8,16,8,1,768]{4,2,0,1,3:T(8,128)(2,1)S(1)} fusion(bf16[8,16,8,640]{3,2,0,1:T(8,128)(2,1)S(1)} %bitcast.243, bf16[16,640,768]{2,1,0:T(8,128)(2,1)S(1)} %bitcast.241), kind=kOutput, calls=%fused_computation.47 | convolution fusion | flops 1007419392 | bytes 18612224 | tf_op jit(solution)/shard_map/spkd,pdu->spku/dot_general | solution.py:291
  113.2 3.4 %collective-permute-done.25 = bf16[4,16,8,2,768]{4,2,0,1,3:T(8,128)(2,1)S(1)} collective-permute-done((bf16[4,16,8,2,768]{4,2,0,1,3:T(8,128)(2,1)S(1)}, bf16[4,16,8,2,768]{4,2,0,1,3:T(8,128)(2,1)S(1)}, u32[]{:S(2)}, u32[]{:S(2)}) %collective-permute-start.25) | collective-permute-done | bytes 1572896 | tf_op jit(solution)/shard_map/ppermute | solution.py:297
  116.6 1.9 %add_convert_fusion = bf16[4,16,8,2,768]{4,2,0,1,3:T(8,128)(2,1)S(1)} fusion(bf16[4,16,8,2,768]{4,2,0,1,3:T(8,128)(2,1)S(1)} %collective-permute-done.25, s32[]{:T(128)S(6)} %select_n.265, bf16[8,16,8,1,768]{4,2,0,1,3:T(8,128)(2,1)} %copy-done.3, bf16[8,16,8,1,768]{4,2,0,1,3:T(8,128)(2,1)} %copy-done.2), kind=kLoop, calls=%fused_computation.32 | loop fusion | flops 3932160 | bytes 6291460 | tf_op jit(solution)/shard_map/convert_element_type | solution.py:298
  122.5 15.7 %collective-permute-done.26 = bf16[2,16,8,2,768]{4,2,0,1,3:T(8,128)(2,1)S(1)} collective-permute-done((bf16[2,16,8,2,768]{4,2,0,1,3:T(8,128)(2,1)S(1)}, bf16[2,16,8,2,768]{4,2,0,1,3:T(8,128)(2,1)S(1)}, u32[]{:S(2)}, u32[]{:S(2)}) %collective-permute-start.26) | collective-permute-done | bytes 786464 | tf_op jit(solution)/shard_map/ppermute | solution.py:305
  140.2 9.0 %collective-permute-done.27 = bf16[2,16,8,768]{3,2,0,1:T(8,128)(2,1)S(1)} collective-permute-done((bf16[2,16,8,768]{3,2,0,1:T(8,128)(2,1)S(1)}, bf16[2,16,8,768]{3,2,0,1:T(8,128)(2,1)S(1)}, u32[]{:S(2)}, u32[]{:S(2)}) %collective-permute-start.27) | collective-permute-done | bytes 393248 | tf_op jit(solution)/shard_map/ppermute | solution.py:309
  151.6 8.1 %bitcast_reduce_fusion = bf16[8,8,8,640]{3,2,0,1:T(8,128)(2,1)S(1)} fusion(bf16[16,768,640]{2,1,0:T(8,128)(2,1)} %param.33, bf16[4,16,8,768]{3,2,0,1:T(8,128)(2,1)S(1)} %collective-permute-done.28, bf16[4,16,8,768]{3,2,0,1:T(8,128)(2,1)S(1)} %maximum_select_fusion.2, pred[]{:T(512)S(6)} %eq.223), kind=kOutput, calls=%fused_computation.49 | convolution fusion | flops 1009975296 | bytes 17956864 | tf_op jit(solution)/shard_map/spku,pud->spkd/dot_general | solution.py:321
  159.8 5.6 %collective-permute-start.29 = (bf16[8,8,640]{2,1,0:T(8,128)(2,1)S(1)}, bf16[8,8,640]{2,1,0:T(8,128)(2,1)S(1)}, u32[]{:S(2)}, u32[]{:S(2)}) collective-permute-start(bf16[8,8,640]{2,1,0:T(8,128)(2,1)S(1)} %get-tuple-element.193), channel_id=1, source_target_pairs={{0,7},{1,0},{2,1},{3,2},{4,3},{5,4},{6,5},{7,6},{8,15},{9,8},{10,9... | collective-permute-start | bytes 245768 | tf_op jit(solution)/shard_map/ppermute | solution.py:329
  165.6 3.2 %collective-permute-start.32 = (bf16[8,8,640]{2,1,0:T(8,128)(2,1)S(1)}, bf16[8,8,640]{2,1,0:T(8,128)(2,1)S(1)}, u32[]{:S(2)}, u32[]{:S(2)}) collective-permute-start(bf16[8,8,640]{2,1,0:T(8,128)(2,1)S(1)} %get-tuple-element.190), channel_id=1, source_target_pairs={{0,4},{1,5},{2,6},{3,7},{4,0},{5,1},{6,2},{7,3},{8,12},{9,13},{10,... | collective-permute-start | bytes 245768 | tf_op jit(solution)/shard_map/ppermute | solution.py:329
  168.8 2.2 %collective-permute-start.34 = (bf16[8,8,640]{2,1,0:T(8,128)(2,1)S(1)}, bf16[8,8,640]{2,1,0:T(8,128)(2,1)S(1)}, u32[]{:S(2)}, u32[]{:S(2)}) collective-permute-start(bf16[8,8,640]{2,1,0:T(8,128)(2,1)S(1)} %get-tuple-element.194), channel_id=1, source_target_pairs={{0,2},{1,3},{2,4},{3,5},{4,6},{5,7},{6,0},{7,1},{8,10},{9,11},{10,... | collective-permute-start | bytes 245768 | tf_op jit(solution)/shard_map/ppermute | solution.py:329
  172.1 7.7 %collective-permute-done.32 = bf16[8,8,640]{2,1,0:T(8,128)(2,1)S(1)} collective-permute-done((bf16[8,8,640]{2,1,0:T(8,128)(2,1)S(1)}, bf16[8,8,640]{2,1,0:T(8,128)(2,1)S(1)}, u32[]{:S(2)}, u32[]{:S(2)}) %collective-permute-start.32) | collective-permute-done | bytes 81952 | tf_op jit(solution)/shard_map/ppermute | solution.py:329
  179.8 2.5 %collective-permute-done.33 = bf16[8,8,640]{2,1,0:T(8,128)(2,1)S(1)} collective-permute-done((bf16[8,8,640]{2,1,0:T(8,128)(2,1)S(1)}, bf16[8,8,640]{2,1,0:T(8,128)(2,1)S(1)}, u32[]{:S(2)}, u32[]{:S(2)}) %collective-permute-start.33) | collective-permute-done | bytes 81952 | tf_op jit(solution)/shard_map/ppermute | solution.py:329
  (245 shorter events, 74.0 us)
Async XLA Ops:
  8.7 14.6 %all-to-all-start = ((bf16[8,2,32,128]{3,2,1,0:T(8,128)(2,1)}), bf16[8,2,32,128]{3,2,1,0:T(8,128)(2,1)S(1)}, u32[]{:S(2)}, u32[]{:S(2)}) async-start(bf16[8,2,32,128]{3,2,1,0:T(8,128)(2,1)} %pad_maximum_fusion), calls=%async_computation | async-start | bytes 262144 | tf_op jit(solution)/shard_map/all_to_all | solution.py:136
  24.9 7.6 %collective-permute-start = (bf16[64,640]{1,0:T(8,128)(2,1)S(1)}, bf16[64,640]{1,0:T(8,128)(2,1)S(1)}, u32[]{:S(2)}, u32[]{:S(2)}) collective-permute-start(bf16[64,640]{1,0:T(8,128)(2,1)S(1)} %bitcast.253), channel_id=1, source_target_pairs={{0,1},{1,2},{2,3},{3,4},{4,5},{5,6},{6,7},{7,0},{8,9},{9,10},{10,1... | collective-permute-start | bytes 245768 | tf_op jit(solution)/shard_map/ppermute | solution.py:180
  27.5 9.5 %collective-permute-start.12 = (bf16[64,640]{1,0:T(8,128)(2,1)S(1)}, bf16[64,640]{1,0:T(8,128)(2,1)S(1)}, u32[]{:S(2)}, u32[]{:S(2)}) collective-permute-start(bf16[64,640]{1,0:T(8,128)(2,1)S(1)} %bitcast.255), channel_id=1, source_target_pairs={{0,7},{1,0},{2,1},{3,2},{4,3},{5,4},{6,5},{7,6},{8,15},{9,8},{10,9... | collective-permute-start | bytes 245768 | tf_op jit(solution)/shard_map/ppermute | solution.py:180
  30.5 8.6 %collective-permute-start.2 = (bf16[64,640]{1,0:T(8,128)(2,1)S(1)}, bf16[64,640]{1,0:T(8,128)(2,1)S(1)}, u32[]{:S(2)}, u32[]{:S(2)}) collective-permute-start(bf16[64,640]{1,0:T(8,128)(2,1)S(1)} %bitcast.256), channel_id=1, source_target_pairs={{0,2},{1,3},{2,4},{3,5},{4,6},{5,7},{6,0},{7,1},{8,10},{9,11},{10,... | collective-permute-start | bytes 245768 | tf_op jit(solution)/shard_map/ppermute | solution.py:180
  32.5 9.3 %collective-permute-start.4 = (bf16[64,640]{1,0:T(8,128)(2,1)S(1)}, bf16[64,640]{1,0:T(8,128)(2,1)S(1)}, u32[]{:S(2)}, u32[]{:S(2)}) collective-permute-start(bf16[64,640]{1,0:T(8,128)(2,1)S(1)} %bitcast.257), channel_id=1, source_target_pairs={{0,3},{1,4},{2,5},{3,6},{4,7},{5,0},{6,1},{7,2},{8,11},{9,12},{10,... | collective-permute-start | bytes 245768 | tf_op jit(solution)/shard_map/ppermute | solution.py:180
  32.5 12.5 %collective-permute-start.6 = (bf16[64,640]{1,0:T(8,128)(2,1)S(1)}, bf16[64,640]{1,0:T(8,128)(2,1)S(1)}, u32[]{:S(2)}, u32[]{:S(2)}) collective-permute-start(bf16[64,640]{1,0:T(8,128)(2,1)S(1)} %bitcast.258), channel_id=1, source_target_pairs={{0,4},{1,5},{2,6},{3,7},{4,0},{5,1},{6,2},{7,3},{8,12},{9,13},{10,... | collective-permute-start | bytes 245768 | tf_op jit(solution)/shard_map/ppermute | solution.py:180
  35.1 11.9 %collective-permute-start.8 = (bf16[64,640]{1,0:T(8,128)(2,1)S(1)}, bf16[64,640]{1,0:T(8,128)(2,1)S(1)}, u32[]{:S(2)}, u32[]{:S(2)}) collective-permute-start(bf16[64,640]{1,0:T(8,128)(2,1)S(1)} %bitcast.259), channel_id=1, source_target_pairs={{0,5},{1,6},{2,7},{3,0},{4,1},{5,2},{6,3},{7,4},{8,13},{9,14},{10,... | collective-permute-start | bytes 245768 | tf_op jit(solution)/shard_map/ppermute | solution.py:180
  37.1 12.4 %collective-permute-start.1 = (bf16[64,320]{1,0:T(8,128)(2,1)S(1)}, bf16[64,320]{1,0:T(8,128)(2,1)S(1)}, u32[]{:S(2)}, u32[]{:S(2)}) collective-permute-start(bf16[64,320]{1,0:T(8,128)(2,1)S(1)} %convolution_convert_fusion.9), channel_id=1, source_target_pairs={{0,7},{1,0},{2,1},{3,2},{4,3},{5,4},{6,5},{7,6},{8,15},{9,8},{10,9... | collective-permute-start | bytes 122888 | tf_op jit(solution)/shard_map/ppermute | solution.py:183
  39.1 11.9 %collective-permute-start.11 = (bf16[64,320]{1,0:T(8,128)(2,1)S(1)}, bf16[64,320]{1,0:T(8,128)(2,1)S(1)}, u32[]{:S(2)}, u32[]{:S(2)}) collective-permute-start(bf16[64,320]{1,0:T(8,128)(2,1)S(1)} %convolution_convert_fusion.4), channel_id=1, source_target_pairs={{0,2},{1,3},{2,4},{3,5},{4,6},{5,7},{6,0},{7,1},{8,10},{9,11},{10,... | collective-permute-start | bytes 122888 | tf_op jit(solution)/shard_map/ppermute | solution.py:183
  41.8 11.7 %collective-permute-start.13 = (bf16[64,320]{1,0:T(8,128)(2,1)S(1)}, bf16[64,320]{1,0:T(8,128)(2,1)}, u32[]{:S(2)}, u32[]{:S(2)}) collective-permute-start(bf16[64,320]{1,0:T(8,128)(2,1)S(1)} %convolution_convert_fusion.3), channel_id=1, source_target_pairs={{0,1},{1,2},{2,3},{3,4},{4,5},{5,6},{6,7},{7,0},{8,9},{9,10},{10,1... | collective-permute-start | bytes 122888 | tf_op jit(solution)/shard_map/ppermute | solution.py:183
  45.0 8.5 %collective-permute-start.3 = (bf16[64,320]{1,0:T(8,128)(2,1)S(1)}, bf16[64,320]{1,0:T(8,128)(2,1)}, u32[]{:S(2)}, u32[]{:S(2)}) collective-permute-start(bf16[64,320]{1,0:T(8,128)(2,1)S(1)} %convolution_convert_fusion.8), channel_id=1, source_target_pairs={{0,6},{1,7},{2,0},{3,1},{4,2},{5,3},{6,4},{7,5},{8,14},{9,15},{10,... | collective-permute-start | bytes 122888 | tf_op jit(solution)/shard_map/ppermute | solution.py:183
  81.6 8.4 %collective-permute-start.18 = (bf16[8,8,640]{2,1,0:T(8,128)(2,1)}, bf16[8,8,640]{2,1,0:T(8,128)(2,1)}, u32[]{:S(2)}, u32[]{:S(2)}) collective-permute-start(bf16[8,8,640]{2,1,0:T(8,128)(2,1)} %get-tuple-element.201), channel_id=1, source_target_pairs={{0,1},{1,2},{2,3},{3,4},{4,5},{5,6},{6,7},{7,0},{8,9},{9,10},{10,1... | collective-permute-start | bytes 245768 | tf_op jit(solution)/shard_map/ppermute | solution.py:359
  82.2 10.7 %collective-permute-start.19 = (bf16[8,8,640]{2,1,0:T(8,128)(2,1)}, bf16[8,8,640]{2,1,0:T(8,128)(2,1)S(1)}, u32[]{:S(2)}, u32[]{:S(2)}) collective-permute-start(bf16[8,8,640]{2,1,0:T(8,128)(2,1)} %get-tuple-element.200), channel_id=1, source_target_pairs={{0,2},{1,3},{2,4},{3,5},{4,6},{5,7},{6,0},{7,1},{8,10},{9,11},{10,... | collective-permute-start | bytes 245768 | tf_op jit(solution)/shard_map/ppermute | solution.py:359
  83.7 12.4 %collective-permute-start.20 = (bf16[8,8,640]{2,1,0:T(8,128)(2,1)}, bf16[8,8,640]{2,1,0:T(8,128)(2,1)S(1)}, u32[]{:S(2)}, u32[]{:S(2)}) collective-permute-start(bf16[8,8,640]{2,1,0:T(8,128)(2,1)} %get-tuple-element.199), channel_id=1, source_target_pairs={{0,3},{1,4},{2,5},{3,6},{4,7},{5,0},{6,1},{7,2},{8,11},{9,12},{10,... | collective-permute-start | bytes 245768 | tf_op jit(solution)/shard_map/ppermute | solution.py:359
  85.6 11.2 %collective-permute-start.21 = (bf16[8,8,640]{2,1,0:T(8,128)(2,1)}, bf16[8,8,640]{2,1,0:T(8,128)(2,1)S(1)}, u32[]{:S(2)}, u32[]{:S(2)}) collective-permute-start(bf16[8,8,640]{2,1,0:T(8,128)(2,1)} %get-tuple-element.198), channel_id=1, source_target_pairs={{0,4},{1,5},{2,6},{3,7},{4,0},{5,1},{6,2},{7,3},{8,12},{9,13},{10,... | collective-permute-start | bytes 245768 | tf_op jit(solution)/shard_map/ppermute | solution.py:359
  88.9 8.5 %collective-permute-start.22 = (bf16[8,8,640]{2,1,0:T(8,128)(2,1)S(1)}, bf16[8,8,640]{2,1,0:T(8,128)(2,1)S(1)}, u32[]{:S(2)}, u32[]{:S(2)}) collective-permute-start(bf16[8,8,640]{2,1,0:T(8,128)(2,1)S(1)} %get-tuple-element.197), channel_id=1, source_target_pairs={{0,5},{1,6},{2,7},{3,0},{4,1},{5,2},{6,3},{7,4},{8,13},{9,14},{10,... | collective-permute-start | bytes 245768 | tf_op jit(solution)/shard_map/ppermute | solution.py:359
  90.1 8.0 %collective-permute-start.23 = (bf16[8,8,640]{2,1,0:T(8,128)(2,1)S(1)}, bf16[8,8,640]{2,1,0:T(8,128)(2,1)S(1)}, u32[]{:S(2)}, u32[]{:S(2)}) collective-permute-start(bf16[8,8,640]{2,1,0:T(8,128)(2,1)S(1)} %get-tuple-element.196), channel_id=1, source_target_pairs={{0,6},{1,7},{2,0},{3,1},{4,2},{5,3},{6,4},{7,5},{8,14},{9,15},{10,... | collective-permute-start | bytes 245768 | tf_op jit(solution)/shard_map/ppermute | solution.py:359
  118.6 19.6 %collective-permute-start.26 = (bf16[2,16,8,2,768]{4,2,0,1,3:T(8,128)(2,1)S(1)}, bf16[2,16,8,2,768]{4,2,0,1,3:T(8,128)(2,1)S(1)}, u32[]{:S(2)}, u32[]{:S(2)}) collective-permute-start(bf16[2,16,8,2,768]{4,2,0,1,3:T(8,128)(2,1)S(1)} %constant_dynamic-slice_fusion.1), channel_id=1, source_target_pairs={{0,16},{8,24},{16,0},{24,8},{1,17},{9,25},{17,1},{25,9},{2,18},{10... | collective-permute-start | bytes 2359304 | tf_op jit(solution)/shard_map/ppermute | solution.py:305
  138.8 10.4 %collective-permute-start.27 = (bf16[2,16,8,768]{3,2,0,1:T(8,128)(2,1)S(1)}, bf16[2,16,8,768]{3,2,0,1:T(8,128)(2,1)S(1)}, u32[]{:S(2)}, u32[]{:S(2)}) collective-permute-start(bf16[2,16,8,768]{3,2,0,1:T(8,128)(2,1)S(1)} %fusion.42), channel_id=1, source_target_pairs={{0,16},{8,24},{16,0},{24,8},{1,17},{9,25},{17,1},{25,9},{2,18},{10... | collective-permute-start | bytes 1179656 | tf_op jit(solution)/shard_map/ppermute | solution.py:309
  159.8 9.0 %collective-permute-start.29 = (bf16[8,8,640]{2,1,0:T(8,128)(2,1)S(1)}, bf16[8,8,640]{2,1,0:T(8,128)(2,1)S(1)}, u32[]{:S(2)}, u32[]{:S(2)}) collective-permute-start(bf16[8,8,640]{2,1,0:T(8,128)(2,1)S(1)} %get-tuple-element.193), channel_id=1, source_target_pairs={{0,7},{1,0},{2,1},{3,2},{4,3},{5,4},{6,5},{7,6},{8,15},{9,8},{10,9... | collective-permute-start | bytes 245768 | tf_op jit(solution)/shard_map/ppermute | solution.py:329
  165.6 14.2 %collective-permute-start.32 = (bf16[8,8,640]{2,1,0:T(8,128)(2,1)S(1)}, bf16[8,8,640]{2,1,0:T(8,128)(2,1)S(1)}, u32[]{:S(2)}, u32[]{:S(2)}) collective-permute-start(bf16[8,8,640]{2,1,0:T(8,128)(2,1)S(1)} %get-tuple-element.190), channel_id=1, source_target_pairs={{0,4},{1,5},{2,6},{3,7},{4,0},{5,1},{6,2},{7,3},{8,12},{9,13},{10,... | collective-permute-start | bytes 245768 | tf_op jit(solution)/shard_map/ppermute | solution.py:329
  168.8 13.5 %collective-permute-start.33 = (bf16[8,8,640]{2,1,0:T(8,128)(2,1)S(1)}, bf16[8,8,640]{2,1,0:T(8,128)(2,1)S(1)}, u32[]{:S(2)}, u32[]{:S(2)}) collective-permute-start(bf16[8,8,640]{2,1,0:T(8,128)(2,1)S(1)} %get-tuple-element.189), channel_id=1, source_target_pairs={{0,3},{1,4},{2,5},{3,6},{4,7},{5,0},{6,1},{7,2},{8,11},{9,12},{10,... | collective-permute-start | bytes 245768 | tf_op jit(solution)/shard_map/ppermute | solution.py:329
  168.8 13.5 %collective-permute-start.34 = (bf16[8,8,640]{2,1,0:T(8,128)(2,1)S(1)}, bf16[8,8,640]{2,1,0:T(8,128)(2,1)S(1)}, u32[]{:S(2)}, u32[]{:S(2)}) collective-permute-start(bf16[8,8,640]{2,1,0:T(8,128)(2,1)S(1)} %get-tuple-element.194), channel_id=1, source_target_pairs={{0,2},{1,3},{2,4},{3,5},{4,6},{5,7},{6,0},{7,1},{8,10},{9,11},{10,... | collective-permute-start | bytes 245768 | tf_op jit(solution)/shard_map/ppermute | solution.py:329
  171.0 11.4 %collective-permute-start.35 = (bf16[8,8,640]{2,1,0:T(8,128)(2,1)S(1)}, bf16[8,8,640]{2,1,0:T(8,128)(2,1)S(1)}, u32[]{:S(2)}, u32[]{:S(2)}) collective-permute-start(bf16[8,8,640]{2,1,0:T(8,128)(2,1)S(1)} %get-tuple-element.188), channel_id=1, source_target_pairs={{0,1},{1,2},{2,3},{3,4},{4,5},{5,6},{6,7},{7,0},{8,9},{9,10},{10,1... | collective-permute-start | bytes 245768 | tf_op jit(solution)/shard_map/ppermute | solution.py:329
  (42 other events, 353.3 us)

commit v16 on v14

--- a/solution.py
+++ b/solution.py
@@ -133,16 +133,29 @@
         .reshape((blk_count,) + pool_rows.shape[1:])
     )
     block_shape = sending.shape[1:]
-    both_blocks = lax.all_to_all(
-        jnp.stack(
-            [sending.reshape(blk_count, -1, head_dim), outgoing.reshape(blk_count, -1, head_dim)],
-            axis=1,
-        ),
-        "blk",
-        split_axis=0,
-        concat_axis=0,
-        tiled=True,
-    )
+    block_pairs = jnp.stack(
+        [sending.reshape(blk_count, -1, head_dim), outgoing.reshape(blk_count, -1, head_dim)],
+        axis=1,
+    )
+    if blk_count <= 8:
+        block_arrivals = []
+        for shift in range(blk_count):
+            mine = lax.dynamic_index_in_dim(
+                block_pairs, (own_index - shift) % blk_count, 0, keepdims=False
+            )
+            if shift:
+                mine = lax.ppermute(
+                    mine, "blk", [(i, (i - shift) % blk_count) for i in range(blk_count)]
+                )
+            block_arrivals.append(mine)
+        both_blocks = lax.dynamic_slice_in_dim(
+            jnp.stack(block_arrivals + block_arrivals),
+            (blk_count - own_index) % blk_count,
+            blk_count,
+            0,
+        )
+    else:
+        both_blocks = lax.all_to_all(block_pairs, "blk", split_axis=0, concat_axis=0, tiled=True)
     landed = both_blocks[:, 0].reshape((blk_count,) + block_shape)
     arrived = both_blocks[:, 1].reshape((blk_count,) + block_shape)
     present = jnp.any(

time: 183 us -> 191 us (1.044)
  starting transfers between devices: 43.4 us -> 55 us
  waiting for transfers between devices: 82.2 us -> 77.6 us
    ppermute x0 -> x7, starting transfers between devices: none -> 12.5 us  [per_device(): lax.ppermute(mine, 'blk', [(i, (i - shift) % blk_count) for i in range(bl...]
    all_to_all x1 -> x0, starting transfers between devices: 7.28 us -> none  [per_device(): lax.all_to_all(jnp.stack([sending.reshape(blk_count, -1, head_dim), outgo...]
    ppermute x0 -> x7, waiting for transfers between devices: none -> 5.25 us  [per_device(): lax.ppermute(mine, 'blk', [(i, (i - shift) % blk_count) for i in range(bl...]
    ppermute x7, starting transfers between devices: 11.4 us -> 16.6 us  [per_device(): back_parts.append(part if shift == 0 else lax.ppermute(part, 'blk', back))]
    all_to_all x1 -> x0, waiting for transfers between devices: 4.71 us -> none  [per_device(): lax.all_to_all(jnp.stack([sending.reshape(blk_count, -1, head_dim), outgo...]
    ppermute x7, waiting for transfers between devices: 5.03 us -> 1.77 us  [per_device(): back_parts.append(part if shift == 0 else lax.ppermute(part, 'blk', back))]
  transfers between devices with their start and end apart: 25 -> 31, of which waited for: 15 -> 12; matrix products, arithmetic and copies ran while one was open for 5% -> 5% of each run, Pallas kernels for 0% -> 0%
where the time goes in v16:
time: 191 us
  waiting for transfers between devices  77.6 us (41%)
  starting transfers between devices  55 us (29%)
  matrix products  30.9 us (16%)
  other arithmetic  14.5 us (8%)
  local copies, waits for them, and re-layouts  10.5 us (5%)
  between operations  2.42 us (1%)
    ppermute x1, waiting for transfers between devices, out_stage(): lax.ppermute(chip_given, 'kv', flip_chip).astype(jnp.float32)  18.1 us
    all_to_all x1, waiting for transfers between devices, out_stage(): lax.all_to_all(half_sum, 'blk', split_axis=0, concat_axis=0, tiled=True)  16.7 us
    ppermute x7, starting transfers between devices, per_device(): back_parts.append(part if shift == 0 else lax.ppermute(part, 'blk', back))  16.6 us
    all_to_all x1, waiting for transfers between devices, per_device(): lax.all_to_all(outgoing_rows[:, i * chunk_experts:(i + 1) * chunk_experts...  16.5 us
    ppermute x7, starting transfers between devices, per_device(): lax.ppermute(mine, 'blk', [(i, (i - shift) % blk_count) for i in range(bl...  12.5 us
    ppermute x7, starting transfers between devices, per_device(): rows_from = attended if shift == 0 else lax.ppermute(attended, 'blk', there)  9.78 us
    ppermute x1, waiting for transfers between devices, out_stage(): hidden_far = lax.ppermute(hidden_quarter, 'kv', flip_chip)  8.84 us
    dot_general x1, matrix products, pair_stage(): jnp.einsum('spkd,pdu->spku', rows_in, up_w, preferred_element_type=jnp.fl...  8.3 us
  transfers between devices with their start and end apart: 31, of which 12 were waited for; matrix products, arithmetic and copies ran while one was open for 5% of the time, Pallas kernels for 0%

profile of v16, /device:TPU:0, one launch (start us, length us, event | category | flops | bytes accessed | tf_op | source)
XLA Modules:
  0.0 191.1 jit_solution(856461379859614184)
XLA Ops:
  8.3 6.1 %collective-permute-start = (bf16[2,32,128]{2,1,0:T(8,128)(2,1)S(1)}, bf16[2,32,128]{2,1,0:T(8,128)(2,1)S(1)}, u32[]{:S(2)}, u32[]{:S(2)}) collective-permute-start(bf16[2,32,128]{2,1,0:T(8,128)(2,1)S(1)} %get-tuple-element.217), channel_id=1, source_target_pairs={{0,7},{1,0},{2,1},{3,2},{4,3},{5,4},{6,5},{7,6},{8,15},{9,8},{10,9... | collective-permute-start | bytes 49160 | tf_op jit(solution)/shard_map/ppermute | solution.py:147
  14.8 3.0 %collective-permute-start.3 = (bf16[2,32,128]{2,1,0:T(8,128)(2,1)S(1)}, bf16[2,32,128]{2,1,0:T(8,128)(2,1)S(1)}, u32[]{:S(2)}, u32[]{:S(2)}) collective-permute-start(bf16[2,32,128]{2,1,0:T(8,128)(2,1)S(1)} %get-tuple-element.214), channel_id=1, source_target_pairs={{0,4},{1,5},{2,6},{3,7},{4,0},{5,1},{6,2},{7,3},{8,12},{9,13},{10,... | collective-permute-start | bytes 49160 | tf_op jit(solution)/shard_map/ppermute | solution.py:147
  20.6 1.9 collective-permute-start.5
  23.7 3.4 %collective-permute-done.5 = bf16[2,32,128]{2,1,0:T(8,128)(2,1)S(1)} collective-permute-done((bf16[2,32,128]{2,1,0:T(8,128)(2,1)S(1)}, bf16[2,32,128]{2,1,0:T(8,128)(2,1)S(1)}, u32[]{:S(2)}, u32[]{:S(2)}) %collective-permute-start.5) | collective-permute-done | bytes 16416 | tf_op jit(solution)/shard_map/ppermute | solution.py:147
  27.2 1.8 collective-permute-done.6
  32.5 2.5 %collective-permute-start.13 = (bf16[64,640]{1,0:T(8,128)(2,1)S(1)}, bf16[64,640]{1,0:T(8,128)(2,1)S(1)}, u32[]{:S(2)}, u32[]{:S(2)}) collective-permute-start(bf16[64,640]{1,0:T(8,128)(2,1)S(1)} %bitcast.206), channel_id=1, source_target_pairs={{0,4},{1,5},{2,6},{3,7},{4,0},{5,1},{6,2},{7,3},{8,12},{9,13},{10,... | collective-permute-start | bytes 245768 | tf_op jit(solution)/shard_map/ppermute | solution.py:193
  36.8 3.3 %collective-permute-start.17 = (bf16[64,640]{1,0:T(8,128)(2,1)S(1)}, bf16[64,640]{1,0:T(8,128)(2,1)S(1)}, u32[]{:S(2)}, u32[]{:S(2)}) collective-permute-start(bf16[64,640]{1,0:T(8,128)(2,1)S(1)} %bitcast.208), channel_id=1, source_target_pairs={{0,6},{1,7},{2,0},{3,1},{4,2},{5,3},{6,4},{7,5},{8,14},{9,15},{10,... | collective-permute-start | bytes 245768 | tf_op jit(solution)/shard_map/ppermute | solution.py:193
  42.7 5.8 %collective-permute-start.10 = (bf16[64,320]{1,0:T(8,128)(2,1)S(1)}, bf16[64,320]{1,0:T(8,128)(2,1)S(1)}, u32[]{:S(2)}, u32[]{:S(2)}) collective-permute-start(bf16[64,320]{1,0:T(8,128)(2,1)S(1)} %convolution_convert_fusion.8), channel_id=1, source_target_pairs={{0,6},{1,7},{2,0},{3,1},{4,2},{5,3},{6,4},{7,5},{8,14},{9,15},{10,... | collective-permute-start | bytes 122888 | tf_op jit(solution)/shard_map/ppermute | solution.py:196
  49.1 2.4 %collective-permute-start.14 = (bf16[64,320]{1,0:T(8,128)(2,1)S(1)}, bf16[64,320]{1,0:T(8,128)(2,1)S(1)}, u32[]{:S(2)}, u32[]{:S(2)}) collective-permute-start(bf16[64,320]{1,0:T(8,128)(2,1)S(1)} %convolution_convert_fusion.6), channel_id=1, source_target_pairs={{0,4},{1,5},{2,6},{3,7},{4,0},{5,1},{6,2},{7,3},{8,12},{9,13},{10,... | collective-permute-start | bytes 122888 | tf_op jit(solution)/shard_map/ppermute | solution.py:196
  52.7 3.0 %collective-permute-start.18 = (bf16[64,320]{1,0:T(8,128)(2,1)S(1)}, bf16[64,320]{1,0:T(8,128)(2,1)S(1)}, u32[]{:S(2)}, u32[]{:S(2)}) collective-permute-start(bf16[64,320]{1,0:T(8,128)(2,1)S(1)} %convolution_convert_fusion.4), channel_id=1, source_target_pairs={{0,2},{1,3},{2,4},{3,5},{4,6},{5,7},{6,0},{7,1},{8,10},{9,11},{10,... | collective-permute-start | bytes 122888 | tf_op jit(solution)/shard_map/ppermute | solution.py:196
  57.1 3.6 %collective-permute-start.8 = (bf16[64,320]{1,0:T(8,128)(2,1)S(1)}, bf16[64,320]{1,0:T(8,128)(2,1)S(1)}, u32[]{:S(2)}, u32[]{:S(2)}) collective-permute-start(bf16[64,320]{1,0:T(8,128)(2,1)S(1)} %convolution_convert_fusion.9), channel_id=1, source_target_pairs={{0,7},{1,0},{2,1},{3,2},{4,3},{5,4},{6,5},{7,6},{8,15},{9,8},{10,9... | collective-permute-start | bytes 122888 | tf_op jit(solution)/shard_map/ppermute | solution.py:196
  66.3 2.4 %collective-permute-done.21 = bf16[64,1280]{1,0:T(8,128)(2,1)S(1)} collective-permute-done((bf16[64,1280]{1,0:T(8,128)(2,1)S(1)}, bf16[64,1280]{1,0:T(8,128)(2,1)S(1)}, u32[]{:S(2)}, u32[]{:S(2)}) %collective-permute-start.21) | collective-permute-done | bytes 163872 | tf_op jit(solution)/shard_map/ppermute | solution.py:219
  73.9 2.2 %collective-permute-done.24 = f32[64,65]{1,0:T(8,128)S(1)} collective-permute-done((f32[64,65]{1,0:T(8,128)S(1)}, f32[64,65]{1,0:T(8,128)S(1)}, u32[]{:S(2)}, u32[]{:S(2)}) %collective-permute-start.24) | collective-permute-done | bytes 16672 | tf_op jit(solution)/shard_map/ppermute | solution.py:244
  77.5 6.0 %all-to-all-start = ((bf16[8,8,8,640]{3,2,1,0:T(8,128)(2,1)}), bf16[8,8,8,640]{3,2,1,0:T(8,128)(2,1)S(1)}, u32[]{:S(2)}, u32[]{:S(2)}) async-start(bf16[8,8,8,640]{3,2,1,0:T(8,128)(2,1)} %bitcast.35), calls=%async_computation | async-start | bytes 1310720 | tf_op jit(solution)/shard_map/all_to_all | solution.py:350
  83.5 16.5 %all-to-all-done = bf16[8,8,8,640]{3,2,1,0:T(8,128)(2,1)S(1)} async-done(((bf16[8,8,8,640]{3,2,1,0:T(8,128)(2,1)}), bf16[8,8,8,640]{3,2,1,0:T(8,128)(2,1)S(1)}, u32[]{:S(2)}, u32[]{:S(2)}) %all-to-all-start) | async-done | bytes 655392 | tf_op jit(solution)/shard_map/all_to_all | solution.py:350
  100.3 8.3 %fusion.31 = bf16[8,16,8,1,768]{4,2,0,1,3:T(8,128)(2,1)S(1)} fusion(bf16[8,16,8,640]{3,2,0,1:T(8,128)(2,1)S(1)} %bitcast.194, bf16[16,640,768]{2,1,0:T(8,128)(2,1)} %param.32), kind=kOutput, calls=%fused_computation.46 | convolution fusion | flops 1007419392 | bytes 18612224 | tf_op jit(solution)/shard_map/spkd,pdu->spku/dot_general | solution.py:305
  108.6 8.3 %fusion.34 = bf16[8,16,8,1,768]{4,2,0,1,3:T(8,128)(2,1)S(1)} fusion(bf16[8,16,8,640]{3,2,0,1:T(8,128)(2,1)S(1)} %bitcast.195, bf16[16,640,768]{2,1,0:T(8,128)(2,1)} %param.31), kind=kOutput, calls=%fused_computation.47 | convolution fusion | flops 1007419392 | bytes 18612224 | tf_op jit(solution)/shard_map/spkd,pdu->spku/dot_general | solution.py:304
  118.2 3.7 %collective-permute-done.25 = bf16[4,16,8,2,768]{4,2,0,1,3:T(8,128)(2,1)} collective-permute-done((bf16[4,16,8,2,768]{4,2,0,1,3:T(8,128)(2,1)}, bf16[4,16,8,2,768]{4,2,0,1,3:T(8,128)(2,1)}, u32[]{:S(2)}, u32[]{:S(2)}) %collective-permute-start.25) | collective-permute-done | bytes 1572896 | tf_op jit(solution)/shard_map/ppermute | solution.py:310
  122.0 2.0 %add_convert_fusion = bf16[4,16,8,2,768]{4,2,0,1,3:T(8,128)(2,1)S(1)} fusion(bf16[4,16,8,2,768]{4,2,0,1,3:T(8,128)(2,1)} %collective-permute-done.25, s32[]{:T(128)S(6)} %select_n.266, bf16[8,16,8,1,768]{4,2,0,1,3:T(8,128)(2,1)S(1)} %fusion.34, bf16[8,16,8,1,768]{4,2,0,1,3:T(8,128)(2,1)S(1)} %fusion.31), kind=kLoop, calls=%fused_computation.32 | loop fusion | flops 3932160 | bytes 6291460 | tf_op jit(solution)/shard_map/convert_element_type | solution.py:311
  126.7 18.1 %collective-permute-done.26 = bf16[2,16,8,2,768]{4,2,0,1,3:T(8,128)(2,1)S(1)} collective-permute-done((bf16[2,16,8,2,768]{4,2,0,1,3:T(8,128)(2,1)S(1)}, bf16[2,16,8,2,768]{4,2,0,1,3:T(8,128)(2,1)S(1)}, u32[]{:S(2)}, u32[]{:S(2)}) %collective-permute-start.26) | collective-permute-done | bytes 786464 | tf_op jit(solution)/shard_map/ppermute | solution.py:318
  148.0 8.8 %collective-permute-done.27 = bf16[2,16,8,768]{3,2,0,1:T(8,128)(2,1)S(1)} collective-permute-done((bf16[2,16,8,768]{3,2,0,1:T(8,128)(2,1)S(1)}, bf16[2,16,8,768]{3,2,0,1:T(8,128)(2,1)S(1)}, u32[]{:S(2)}, u32[]{:S(2)}) %collective-permute-start.27) | collective-permute-done | bytes 393248 | tf_op jit(solution)/shard_map/ppermute | solution.py:322
  159.2 8.1 %bitcast_reduce_fusion = bf16[8,8,8,640]{3,2,0,1:T(8,128)(2,1)S(1)} fusion(bf16[16,768,640]{2,1,0:T(8,128)(2,1)} %param.33, bf16[4,16,8,768]{3,2,0,1:T(8,128)(2,1)S(1)} %collective-permute-done.28, bf16[4,16,8,768]{3,2,0,1:T(8,128)(2,1)S(1)} %maximum_select_fusion.2, pred[]{:T(512)S(6)} %eq.223), kind=kOutput, calls=%fused_computation.49 | convolution fusion | flops 1009975296 | bytes 17956864 | tf_op jit(solution)/shard_map/spku,pud->spkd/dot_general | solution.py:334
  168.3 3.6 %all-to-all-start.1 = ((bf16[8,8,8,640]{3,2,1,0:T(8,128)(2,1)}), bf16[8,8,8,640]{3,2,1,0:T(8,128)(2,1)S(1)}, u32[]{:S(2)}, u32[]{:S(2)}) async-start(bf16[8,8,8,640]{3,2,1,0:T(8,128)(2,1)} %copy.140), calls=%async_computation.1 | async-start | bytes 1310720 | tf_op jit(solution)/shard_map/all_to_all | solution.py:340
  173.3 16.7 %all-to-all-done.1 = bf16[8,8,8,640]{3,2,1,0:T(8,128)(2,1)S(1)} async-done(((bf16[8,8,8,640]{3,2,1,0:T(8,128)(2,1)}), bf16[8,8,8,640]{3,2,1,0:T(8,128)(2,1)S(1)}, u32[]{:S(2)}, u32[]{:S(2)}) %all-to-all-start.1) | async-done | bytes 655392 | tf_op jit(solution)/shard_map/all_to_all | solution.py:340
  (213 shorter events, 48.5 us)
Async XLA Ops:
  8.3 12.3 %collective-permute-start = (bf16[2,32,128]{2,1,0:T(8,128)(2,1)S(1)}, bf16[2,32,128]{2,1,0:T(8,128)(2,1)S(1)}, u32[]{:S(2)}, u32[]{:S(2)}) collective-permute-start(bf16[2,32,128]{2,1,0:T(8,128)(2,1)S(1)} %get-tuple-element.217), channel_id=1, source_target_pairs={{0,7},{1,0},{2,1},{3,2},{4,3},{5,4},{6,5},{7,6},{8,15},{9,8},{10,9... | collective-permute-start | bytes 49160 | tf_op jit(solution)/shard_map/ppermute | solution.py:147
  14.3 8.2 %collective-permute-start.1 = (bf16[2,32,128]{2,1,0:T(8,128)(2,1)S(1)}, bf16[2,32,128]{2,1,0:T(8,128)(2,1)S(1)}, u32[]{:S(2)}, u32[]{:S(2)}) collective-permute-start(bf16[2,32,128]{2,1,0:T(8,128)(2,1)S(1)} %get-tuple-element.216), channel_id=1, source_target_pairs={{0,6},{1,7},{2,0},{3,1},{4,2},{5,3},{6,4},{7,5},{8,14},{9,15},{10,... | collective-permute-start | bytes 49160 | tf_op jit(solution)/shard_map/ppermute | solution.py:147
  14.8 8.9 %collective-permute-start.2 = (bf16[2,32,128]{2,1,0:T(8,128)(2,1)S(1)}, bf16[2,32,128]{2,1,0:T(8,128)(2,1)S(1)}, u32[]{:S(2)}, u32[]{:S(2)}) collective-permute-start(bf16[2,32,128]{2,1,0:T(8,128)(2,1)S(1)} %get-tuple-element.215), channel_id=1, source_target_pairs={{0,5},{1,6},{2,7},{3,0},{4,1},{5,2},{6,3},{7,4},{8,13},{9,14},{10,... | collective-permute-start | bytes 49160 | tf_op jit(solution)/shard_map/ppermute | solution.py:147
  14.8 8.9 %collective-permute-start.3 = (bf16[2,32,128]{2,1,0:T(8,128)(2,1)S(1)}, bf16[2,32,128]{2,1,0:T(8,128)(2,1)S(1)}, u32[]{:S(2)}, u32[]{:S(2)}) collective-permute-start(bf16[2,32,128]{2,1,0:T(8,128)(2,1)S(1)} %get-tuple-element.214), channel_id=1, source_target_pairs={{0,4},{1,5},{2,6},{3,7},{4,0},{5,1},{6,2},{7,3},{8,12},{9,13},{10,... | collective-permute-start | bytes 49160 | tf_op jit(solution)/shard_map/ppermute | solution.py:147
  17.8 5.9 %collective-permute-start.4 = (bf16[2,32,128]{2,1,0:T(8,128)(2,1)S(1)}, bf16[2,32,128]{2,1,0:T(8,128)(2,1)S(1)}, u32[]{:S(2)}, u32[]{:S(2)}) collective-permute-start(bf16[2,32,128]{2,1,0:T(8,128)(2,1)S(1)} %get-tuple-element.213), channel_id=1, source_target_pairs={{0,3},{1,4},{2,5},{3,6},{4,7},{5,0},{6,1},{7,2},{8,11},{9,12},{10,... | collective-permute-start | bytes 49160 | tf_op jit(solution)/shard_map/ppermute | solution.py:147
  20.6 6.5 %collective-permute-start.5 = (bf16[2,32,128]{2,1,0:T(8,128)(2,1)S(1)}, bf16[2,32,128]{2,1,0:T(8,128)(2,1)S(1)}, u32[]{:S(2)}, u32[]{:S(2)}) collective-permute-start(bf16[2,32,128]{2,1,0:T(8,128)(2,1)S(1)} %get-tuple-element.212), channel_id=1, source_target_pairs={{0,2},{1,3},{2,4},{3,5},{4,6},{5,7},{6,0},{7,1},{8,10},{9,11},{10,... | collective-permute-start | bytes 49160 | tf_op jit(solution)/shard_map/ppermute | solution.py:147
  22.5 6.4 %collective-permute-start.6 = (bf16[2,32,128]{2,1,0:T(8,128)(2,1)S(1)}, bf16[2,32,128]{2,1,0:T(8,128)(2,1)S(1)}, u32[]{:S(2)}, u32[]{:S(2)}) collective-permute-start(bf16[2,32,128]{2,1,0:T(8,128)(2,1)S(1)} %get-tuple-element.210), channel_id=1, source_target_pairs={{0,1},{1,2},{2,3},{3,4},{4,5},{5,6},{6,7},{7,0},{8,9},{9,10},{10,1... | collective-permute-start | bytes 49160 | tf_op jit(solution)/shard_map/ppermute | solution.py:147
  32.1 8.0 %collective-permute-start.9 = (bf16[64,640]{1,0:T(8,128)(2,1)S(1)}, bf16[64,640]{1,0:T(8,128)(2,1)S(1)}, u32[]{:S(2)}, u32[]{:S(2)}) collective-permute-start(bf16[64,640]{1,0:T(8,128)(2,1)S(1)} %bitcast.204), channel_id=1, source_target_pairs={{0,2},{1,3},{2,4},{3,5},{4,6},{5,7},{6,0},{7,1},{8,10},{9,11},{10,... | collective-permute-start | bytes 245768 | tf_op jit(solution)/shard_map/ppermute | solution.py:193
  32.5 8.6 %collective-permute-start.11 = (bf16[64,640]{1,0:T(8,128)(2,1)S(1)}, bf16[64,640]{1,0:T(8,128)(2,1)S(1)}, u32[]{:S(2)}, u32[]{:S(2)}) collective-permute-start(bf16[64,640]{1,0:T(8,128)(2,1)S(1)} %bitcast.205), channel_id=1, source_target_pairs={{0,3},{1,4},{2,5},{3,6},{4,7},{5,0},{6,1},{7,2},{8,11},{9,12},{10,... | collective-permute-start | bytes 245768 | tf_op jit(solution)/shard_map/ppermute | solution.py:193
  32.5 10.2 %collective-permute-start.13 = (bf16[64,640]{1,0:T(8,128)(2,1)S(1)}, bf16[64,640]{1,0:T(8,128)(2,1)S(1)}, u32[]{:S(2)}, u32[]{:S(2)}) collective-permute-start(bf16[64,640]{1,0:T(8,128)(2,1)S(1)} %bitcast.206), channel_id=1, source_target_pairs={{0,4},{1,5},{2,6},{3,7},{4,0},{5,1},{6,2},{7,3},{8,12},{9,13},{10,... | collective-permute-start | bytes 245768 | tf_op jit(solution)/shard_map/ppermute | solution.py:193
  35.1 13.7 %collective-permute-start.15 = (bf16[64,640]{1,0:T(8,128)(2,1)S(1)}, bf16[64,640]{1,0:T(8,128)(2,1)S(1)}, u32[]{:S(2)}, u32[]{:S(2)}) collective-permute-start(bf16[64,640]{1,0:T(8,128)(2,1)S(1)} %bitcast.207), channel_id=1, source_target_pairs={{0,5},{1,6},{2,7},{3,0},{4,1},{5,2},{6,3},{7,4},{8,13},{9,14},{10,... | collective-permute-start | bytes 245768 | tf_op jit(solution)/shard_map/ppermute | solution.py:193
  36.8 12.3 %collective-permute-start.17 = (bf16[64,640]{1,0:T(8,128)(2,1)S(1)}, bf16[64,640]{1,0:T(8,128)(2,1)S(1)}, u32[]{:S(2)}, u32[]{:S(2)}) collective-permute-start(bf16[64,640]{1,0:T(8,128)(2,1)S(1)} %bitcast.208), channel_id=1, source_target_pairs={{0,6},{1,7},{2,0},{3,1},{4,2},{5,3},{6,4},{7,5},{8,14},{9,15},{10,... | collective-permute-start | bytes 245768 | tf_op jit(solution)/shard_map/ppermute | solution.py:193
  40.1 11.7 %collective-permute-start.19 = (bf16[64,640]{1,0:T(8,128)(2,1)S(1)}, bf16[64,640]{1,0:T(8,128)(2,1)S(1)}, u32[]{:S(2)}, u32[]{:S(2)}) collective-permute-start(bf16[64,640]{1,0:T(8,128)(2,1)S(1)} %bitcast.209), channel_id=1, source_target_pairs={{0,7},{1,0},{2,1},{3,2},{4,3},{5,4},{6,5},{7,6},{8,15},{9,8},{10,9... | collective-permute-start | bytes 245768 | tf_op jit(solution)/shard_map/ppermute | solution.py:193
  41.0 11.7 %collective-permute-start.7 = (bf16[64,640]{1,0:T(8,128)(2,1)S(1)}, bf16[64,640]{1,0:T(8,128)(2,1)S(1)}, u32[]{:S(2)}, u32[]{:S(2)}) collective-permute-start(bf16[64,640]{1,0:T(8,128)(2,1)S(1)} %bitcast.210), channel_id=1, source_target_pairs={{0,1},{1,2},{2,3},{3,4},{4,5},{5,6},{6,7},{7,0},{8,9},{9,10},{10,1... | collective-permute-start | bytes 245768 | tf_op jit(solution)/shard_map/ppermute | solution.py:193
  42.7 13.2 %collective-permute-start.10 = (bf16[64,320]{1,0:T(8,128)(2,1)S(1)}, bf16[64,320]{1,0:T(8,128)(2,1)S(1)}, u32[]{:S(2)}, u32[]{:S(2)}) collective-permute-start(bf16[64,320]{1,0:T(8,128)(2,1)S(1)} %convolution_convert_fusion.8), channel_id=1, source_target_pairs={{0,6},{1,7},{2,0},{3,1},{4,2},{5,3},{6,4},{7,5},{8,14},{9,15},{10,... | collective-permute-start | bytes 122888 | tf_op jit(solution)/shard_map/ppermute | solution.py:196
  48.8 8.3 %collective-permute-start.12 = (bf16[64,320]{1,0:T(8,128)(2,1)S(1)}, bf16[64,320]{1,0:T(8,128)(2,1)S(1)}, u32[]{:S(2)}, u32[]{:S(2)}) collective-permute-start(bf16[64,320]{1,0:T(8,128)(2,1)S(1)} %convolution_convert_fusion.7), channel_id=1, source_target_pairs={{0,5},{1,6},{2,7},{3,0},{4,1},{5,2},{6,3},{7,4},{8,13},{9,14},{10,... | collective-permute-start | bytes 122888 | tf_op jit(solution)/shard_map/ppermute | solution.py:196
  49.1 11.9 %collective-permute-start.14 = (bf16[64,320]{1,0:T(8,128)(2,1)S(1)}, bf16[64,320]{1,0:T(8,128)(2,1)S(1)}, u32[]{:S(2)}, u32[]{:S(2)}) collective-permute-start(bf16[64,320]{1,0:T(8,128)(2,1)S(1)} %convolution_convert_fusion.6), channel_id=1, source_target_pairs={{0,4},{1,5},{2,6},{3,7},{4,0},{5,1},{6,2},{7,3},{8,12},{9,13},{10,... | collective-permute-start | bytes 122888 | tf_op jit(solution)/shard_map/ppermute | solution.py:196
  51.8 9.2 %collective-permute-start.16 = (bf16[64,320]{1,0:T(8,128)(2,1)S(1)}, bf16[64,320]{1,0:T(8,128)(2,1)S(1)}, u32[]{:S(2)}, u32[]{:S(2)}) collective-permute-start(bf16[64,320]{1,0:T(8,128)(2,1)S(1)} %convolution_convert_fusion.5), channel_id=1, source_target_pairs={{0,3},{1,4},{2,5},{3,6},{4,7},{5,0},{6,1},{7,2},{8,11},{9,12},{10,... | collective-permute-start | bytes 122888 | tf_op jit(solution)/shard_map/ppermute | solution.py:196
  52.7 8.3 %collective-permute-start.18 = (bf16[64,320]{1,0:T(8,128)(2,1)S(1)}, bf16[64,320]{1,0:T(8,128)(2,1)S(1)}, u32[]{:S(2)}, u32[]{:S(2)}) collective-permute-start(bf16[64,320]{1,0:T(8,128)(2,1)S(1)} %convolution_convert_fusion.4), channel_id=1, source_target_pairs={{0,2},{1,3},{2,4},{3,5},{4,6},{5,7},{6,0},{7,1},{8,10},{9,11},{10,... | collective-permute-start | bytes 122888 | tf_op jit(solution)/shard_map/ppermute | solution.py:196
  55.9 6.8 %collective-permute-start.20 = (bf16[64,320]{1,0:T(8,128)(2,1)S(1)}, bf16[64,320]{1,0:T(8,128)(2,1)S(1)}, u32[]{:S(2)}, u32[]{:S(2)}) collective-permute-start(bf16[64,320]{1,0:T(8,128)(2,1)S(1)} %convolution_convert_fusion.3), channel_id=1, source_target_pairs={{0,1},{1,2},{2,3},{3,4},{4,5},{5,6},{6,7},{7,0},{8,9},{9,10},{10,1... | collective-permute-start | bytes 122888 | tf_op jit(solution)/shard_map/ppermute | solution.py:196
  77.5 22.5 %all-to-all-start = ((bf16[8,8,8,640]{3,2,1,0:T(8,128)(2,1)}), bf16[8,8,8,640]{3,2,1,0:T(8,128)(2,1)S(1)}, u32[]{:S(2)}, u32[]{:S(2)}) async-start(bf16[8,8,8,640]{3,2,1,0:T(8,128)(2,1)} %bitcast.35), calls=%async_computation | async-start | bytes 1310720 | tf_op jit(solution)/shard_map/all_to_all | solution.py:350
  125.1 19.6 %collective-permute-start.26 = (bf16[2,16,8,2,768]{4,2,0,1,3:T(8,128)(2,1)S(1)}, bf16[2,16,8,2,768]{4,2,0,1,3:T(8,128)(2,1)S(1)}, u32[]{:S(2)}, u32[]{:S(2)}) collective-permute-start(bf16[2,16,8,2,768]{4,2,0,1,3:T(8,128)(2,1)S(1)} %constant_dynamic-slice_fusion), channel_id=1, source_target_pairs={{0,16},{8,24},{16,0},{24,8},{1,17},{9,25},{17,1},{25,9},{2,18},{10... | collective-permute-start | bytes 2359304 | tf_op jit(solution)/shard_map/ppermute | solution.py:318
  146.4 10.4 %collective-permute-start.27 = (bf16[2,16,8,768]{3,2,0,1:T(8,128)(2,1)S(1)}, bf16[2,16,8,768]{3,2,0,1:T(8,128)(2,1)S(1)}, u32[]{:S(2)}, u32[]{:S(2)}) collective-permute-start(bf16[2,16,8,768]{3,2,0,1:T(8,128)(2,1)S(1)} %fusion.42), channel_id=1, source_target_pairs={{0,16},{8,24},{16,0},{24,8},{1,17},{9,25},{17,1},{25,9},{2,18},{10... | collective-permute-start | bytes 1179656 | tf_op jit(solution)/shard_map/ppermute | solution.py:322
  168.3 21.7 %all-to-all-start.1 = ((bf16[8,8,8,640]{3,2,1,0:T(8,128)(2,1)}), bf16[8,8,8,640]{3,2,1,0:T(8,128)(2,1)S(1)}, u32[]{:S(2)}, u32[]{:S(2)}) async-start(bf16[8,8,8,640]{3,2,1,0:T(8,128)(2,1)} %copy.140), calls=%async_computation.1 | async-start | bytes 1310720 | tf_op jit(solution)/shard_map/all_to_all | solution.py:340
  (28 other events, 328.4 us)
